TPU v7x, 32 devices: a whole 2x2x4 slice. The times are simulated.
32 devices in a mesh: groups: 2 (over y), cols: 4 (over z), slab: 2 (over x), rep: 2 (over core).
Axes of the slice: x: 2, y: 2, z: 4, core: 2. Of those that a mesh axis runs over, the one named last changes fastest.
Arguments:
- fields: bfloat16 [16, 8, 2048, 512], P('cols', 'groups', 'rep', 'slab'), parts along dimension 1, may hold values from -250 to 250
- stresses: bfloat16 [6, 8, 512, 128], P(None, 'groups', 'rep', 'slab'), parts along dimension 1, may hold values from -750 to 750
- planes: int32 [8], P('groups'), parts along dimension 0, may hold values from 0 to 2047, as said below
- active_masks: int32 [3, 6, 256], replicated, may hold values 0 or 1
Outputs:
- coefficients: float32 [3, 12, 256], P(None, 'groups', 'cols'), parts along dimension 1
- misfit: bfloat16 [6, 8, 512, 128], P(None, 'groups', 'rep', 'slab'), parts along dimension 1
There are 2 independent parts, one for each index of `groups`. A program takes and returns all parts, laid end to end along the dimension named above; an argument that names none is the same for every part. Nothing has to cross between parts.
Inputs may be any that keep to these rules, and one draw needn't show every extreme that they name: `planes`: sorted and distinct; either the first is 0 or the last is 2047.
All inputs are finite; a program needn't handle non-finite values.
Results may differ from a plain program's by a relative error of at most 0.0069.
Values may be sent and summed in bfloat16 or wider, within the bound.
No kernel may reach another device: no remote copies, remote signals or barrier semaphores. Data moves between devices by JAX's collectives and lax.ppermute only.
A program may use at most 128 MiB of HBM per device.

v0:
```python
import math

import jax
import jax.numpy as jnp
import numpy as np
from jax import lax
from jax.sharding import PartitionSpec as P

STRESS = 6
TERMS = 256
NY = 2048
PASSES = 3
ITERS = 3


ridge_weight = 0.05
epsilon = 1e-06


def extended(array, sides, width):
    for axis, dim in sides:
        count, length = (lax.axis_size(axis), array.shape[dim])
        up = [(i, (i + 1) % count) for i in range(count)]
        down = [(j, i) for i, j in up]
        last = lax.slice_in_dim(array, length - width, length, axis=dim)
        leading = lax.slice_in_dim(array, 0, width, axis=dim)
        before = lax.ppermute(last, axis, up)
        after = lax.ppermute(leading, axis, down)
        array = jnp.concatenate([before, array, after], axis=dim)
    return array


def tree_sum(value, axes):
    for axis in axes:
        count = lax.axis_size(axis)
        if count & (count - 1):
            value = lax.psum(value, axis)
            continue
        step = 1
        while step < count:
            partner = [(i, i ^ step) for i in range(count)]
            value = value + lax.ppermute(value, axis, partner)
            step *= 2
    return value


def kernel(spread):
    offsets = np.arange(13) - 6.0
    values = np.exp(-offsets * offsets / (2.0 * spread * spread))
    return values / values.sum()


def filter_table(cells, first_taps, second_taps, guard, order):
    out_count = cells // 4
    shape = tuple((cells + 10, 2, out_count)[d] for d in order)
    where = {d: order.index(d) for d in range(3)}
    position = lax.broadcasted_iota(jnp.int32, shape, where[0])
    which = lax.broadcasted_iota(jnp.int32, shape, where[1])
    out_index = lax.broadcasted_iota(jnp.int32, shape, where[2])
    tap_at = position - 1 - 4 * out_index + guard
    table = jnp.zeros(shape, jnp.float32)
    for tap_index in range(13):
        value = jnp.where(
            which == 0, np.float32(first_taps[tap_index]), np.float32(second_taps[tap_index])
        )
        table = jnp.where(tap_at == tap_index, value, table)
    return table


def library(narrow_part, broad_part):
    product = (
        narrow_part.astype(jnp.float32)[:, None, :] * broad_part.astype(jnp.float32)[None, :, :]
    )
    return product.astype(jnp.bfloat16).reshape(
        narrow_part.shape[0] * broad_part.shape[0], narrow_part.shape[1]
    )


def local(fields, stresses, planes, active_masks):
    chan_dev, plane_count, cells_x, cells_z = fields.shape
    coarse_x = cells_x // 4
    coarse_z = cells_z // 4
    row_count = plane_count * coarse_x * coarse_z
    col_devices = lax.axis_size("cols")
    column_index = lax.axis_index("cols")
    term_dev = TERMS // col_devices
    offset = column_index * term_dev
    samples = float(row_count * lax.axis_size("slab") * lax.axis_size("rep"))
    height = 2.0 * (planes.astype(jnp.float32) + 0.5) / NY - 1.0
    root_weight = jnp.sqrt(1.2 - height * height)
    padded = extended(fields, (("slab", 3), ("rep", 2)), 5)
    widened = padded.astype(jnp.float32)
    narrow_taps = kernel(1.5)
    broad_taps = kernel(3.0)
    guard = jnp.minimum(lax.axis_index("rep"), 0)
    span_table = filter_table(cells_z, narrow_taps, broad_taps, guard, (0, 1, 2))
    stream_table = filter_table(cells_x, narrow_taps, broad_taps, guard, (1, 0, 2))
    along_span = jnp.einsum("cpxz,zsn->cpxsn", widened, span_table, precision=lax.Precision.HIGHEST)
    filtered = jnp.einsum(
        "cpxsn,sxm->scpmn", along_span, stream_table, precision=lax.Precision.HIGHEST
    )
    narrow = filtered[0]
    broader = filtered[1]
    narrow_set = narrow.astype(jnp.bfloat16).reshape(chan_dev, row_count)
    broad_set = (
        (broader * root_weight[None, :, None, None])
        .astype(jnp.bfloat16)
        .reshape(chan_dev, row_count)
    )
    weighted = (stresses.astype(jnp.float32) * root_weight[None, :, None, None]).astype(
        jnp.bfloat16
    )
    weighted = weighted.reshape(STRESS, row_count)
    block_rows = math.gcd(row_count, 4096)
    block_count = row_count // block_rows
    both_sets = lax.all_gather(jnp.stack([narrow_set, broad_set]), "cols", axis=1, tiled=True)
    narrow_all, broad_all = both_sets[0], both_sets[1]

    def gram_step(block_index, carry):
        gram_acc, rhs_acc = carry
        start = block_index * block_rows
        narrow_piece = lax.dynamic_slice_in_dim(narrow_all, start, block_rows, 1)
        broad_piece = lax.dynamic_slice_in_dim(broad_all, start, block_rows, 1)
        own_piece = lax.dynamic_slice_in_dim(narrow_set, start, block_rows, 1)
        all_terms = library(narrow_piece, broad_piece)
        own_terms = library(own_piece, broad_piece)
        weighted_piece = lax.dynamic_slice_in_dim(weighted, start, block_rows, 1)
        gram_acc = gram_acc + jnp.einsum(
            "ir,jr->ij", own_terms, all_terms, preferred_element_type=jnp.float32
        )
        rhs_acc = rhs_acc + jnp.einsum(
            "ir,kr->ik", own_terms, weighted_piece, preferred_element_type=jnp.float32
        )
        return (gram_acc, rhs_acc)

    gram_block, rhs_block = lax.fori_loop(
        0,
        block_count,
        gram_step,
        (jnp.zeros((term_dev, TERMS), jnp.float32), jnp.zeros((term_dev, STRESS), jnp.float32)),
    )
    own_rows = tree_sum(jnp.concatenate([gram_block, rhs_block], axis=1), ("rep", "slab"))
    placed_rows = lax.dynamic_update_slice_in_dim(
        jnp.zeros((TERMS, TERMS + STRESS), jnp.float32), own_rows, offset, 0
    )
    full_rows = tree_sum(placed_rows, ("cols",))
    gram_matrix = full_rows[:, :TERMS]
    rhs_sums = full_rows[:, TERMS:]
    column_scale = 1.0 / jnp.sqrt(jnp.diagonal(gram_matrix) / samples + epsilon)
    normal_gram = column_scale[:, None] * gram_matrix * column_scale[None, :] / samples
    target_norm = column_scale[None, :] * rhs_sums.T / samples

    def apply_normal(vector, active):
        product = jnp.einsum(
            "kl,il->ki", active * vector, normal_gram, precision=lax.Precision.HIGHEST
        )
        return active * product + ridge_weight * vector

    def cg_turn(turn_index, state):
        solution_all, remain, direction, norm_now, active = state
        applied = apply_normal(direction, active)
        curve_sum = jnp.sum(direction * applied, axis=1)
        step_size = norm_now / (curve_sum + epsilon)
        solution_all = solution_all + step_size[:, None] * direction
        remain = remain - step_size[:, None] * applied
        norm_next = jnp.sum(remain * remain, axis=1)
        direction = remain + (norm_next / (norm_now + epsilon))[:, None] * direction
        return (solution_all, remain, direction, norm_next, active)

    def cg_pass(pass_index, state):
        solution_all, coefficients = state
        active = lax.dynamic_index_in_dim(active_masks, pass_index, 0, keepdims=False)
        active = active.astype(jnp.float32)
        solution_all = active * solution_all
        remain = active * target_norm - apply_normal(solution_all, active)
        norm_now = jnp.sum(remain * remain, axis=1)
        solution_all = lax.fori_loop(
            0, ITERS, cg_turn, (solution_all, remain, remain, norm_now, active)
        )[0]
        own_part = lax.dynamic_slice_in_dim(solution_all, offset, term_dev, 1)
        coefficients = lax.dynamic_update_index_in_dim(coefficients, own_part, pass_index, 0)
        return (solution_all, coefficients)

    solution_all, coefficients = lax.fori_loop(
        0,
        PASSES,
        cg_pass,
        (
            jnp.zeros((STRESS, TERMS), jnp.float32),
            jnp.zeros((PASSES, STRESS, term_dev), jnp.float32),
        ),
    )
    final_weights = (column_scale[None, :] * solution_all).astype(jnp.bfloat16)

    def misfit_step(block_index, misfit_acc):
        start = block_index * block_rows
        narrow_piece = lax.dynamic_slice_in_dim(narrow_all, start, block_rows, 1)
        broad_piece = lax.dynamic_slice_in_dim(broad_all, start, block_rows, 1)
        all_terms = library(narrow_piece, broad_piece)
        predicted = jnp.dot(final_weights, all_terms, preferred_element_type=jnp.float32)
        weighted_piece = lax.dynamic_slice_in_dim(weighted, start, block_rows, 1)
        piece_misfit = (weighted_piece.astype(jnp.float32) - predicted).astype(jnp.bfloat16)
        return lax.dynamic_update_slice_in_dim(misfit_acc, piece_misfit, start, 1)

    misfit = lax.fori_loop(
        0, block_count, misfit_step, jnp.zeros((STRESS, row_count), jnp.bfloat16)
    )
    misfit = misfit.reshape(STRESS, plane_count, coarse_x, coarse_z)
    return (coefficients, misfit)


def solution(mesh):
    placed = (
        P("cols", "groups", "rep", "slab"),
        P(None, "groups", "rep", "slab"),
        P("groups"),
        P(),
    )
    return jax.shard_map(
        local,
        mesh=mesh,
        in_specs=placed,
        out_specs=(P(None, "groups", "cols"), P(None, "groups", "rep", "slab")),
        check_vma=False,
    )
```

profile of v0, /device:TPU:0, one launch (start us, length us, event | category | flops | bytes accessed | tf_op | source)
XLA Modules:
  0.0 348.8 jit_solution(8160962072546252235)
XLA Ops:
  7.2 11.5 %copy.40 = bf16[4,4,1024,256]{2,3,1,0:T(8,128)(2,1)} copy(bf16[4,4,1024,256]{3,2,1,0:T(8,128)(2,1)} %param.12) | data formatting | bytes 16777216 | tf_op args[0]
  19.9 3.0 collective-permute-start
  23.0 7.0 %collective-permute-done = bf16[4,4,1024,5]{2,3,1,0:T(8,128)(2,1)S(1)} collective-permute-done((bf16[4,4,1024,5]{2,3,1,0:T(8,128)(2,1)S(1)}, bf16[4,4,1024,5]{2,3,1,0:T(8,128)(2,1)S(1)}, u32[]{:S(2)}, u32[]{:S(2)}) %collective-permute-start) | collective-permute-done | bytes 163872 | tf_op jit(solution)/shard_map/ppermute | solution.py:27
  30.0 4.8 %collective-permute-done.1 = bf16[4,4,1024,5]{2,3,1,0:T(8,128)(2,1)S(1)} collective-permute-done((bf16[4,4,1024,5]{2,3,1,0:T(8,128)(2,1)S(1)}, bf16[4,4,1024,5]{2,3,1,0:T(8,128)(2,1)S(1)}, u32[]{:S(2)}, u32[]{:S(2)}) %collective-permute-start.1) | collective-permute-done | bytes 163872 | tf_op jit(solution)/shard_map/ppermute | solution.py:28
  34.8 5.5 %pad_maximum_fusion = bf16[4,4,1024,266]{2,3,1,0:T(8,128)(2,1)S(1)} fusion(bf16[4,4,1024,5]{2,3,1,0:T(8,128)(2,1)S(1)} %collective-permute-done.1, bf16[4,4,1024,256]{2,3,1,0:T(8,128)(2,1)} %copy.40, bf16[4,4,1024,5]{2,3,1,0:T(8,128)(2,1)S(1)} %collective-permute-done), kind=kLoop, calls=%fused_computation.36 | loop fusion | flops 26148864 | bytes 17432576 | tf_op jit(solution)/shard_map/concatenate | solution.py:29
  40.3 3.5 copy-done
  47.7 18.4 %concatenate.14 = bf16[4,4,1034,266]{2,3,1,0:T(8,128)(2,1)} concatenate(bf16[4,4,5,266]{2,3,1,0:T(8,128)(2,1)S(1)} %copy.45, bf16[4,4,1024,266]{2,3,1,0:T(8,128)(2,1)} %copy-done, bf16[4,4,5,266]{2,3,1,0:T(8,128)(2,1)S(1)} %copy.46), dimensions={2} | concatenate | bytes 17602816 | tf_op jit(solution)/shard_map/concatenate | solution.py:29
  66.1 10.7 %fusion.10 = f32[4,4,1034,2,64]{2,4,1,0,3:T(8,128)S(1)} fusion(bf16[4,4,1034,266]{2,3,1,0:T(8,128)(2,1)} %concatenate.14, f32[2]{0:T(128)S(1)} %get-tuple-element.598, f32[2]{0:T(128)S(1)} %get-tuple-element.599, f32[2]{0:T(128)S(1)} %get-tuple-element.600, f32[2]{0:T(128)S(1)} %get-tuple-element.601, f32[2]{0:T(128)S(1)} %get-tuple-element.602, ...), kind=kOutput, calls=%fused_computation.34 | convolution fusion | flops 6760434688 | bytes 17273316 | tf_op jit(solution)/shard_map/cpxz,zsn->cpxsn/dot_general | solution.py:98
  76.8 10.1 %fusion.53 = f32[2,4,4,256,64]{3,4,2,1,0:T(8,128)S(1)} fusion(f32[4,4,1034,2,64]{2,4,1,0,3:T(8,128)S(1)} %fusion.10, f32[2]{0:T(128)S(1)} %get-tuple-element.598, f32[2]{0:T(128)S(1)} %get-tuple-element.599, f32[2]{0:T(128)S(1)} %get-tuple-element.600, f32[2]{0:T(128)S(1)} %get-tuple-element.601, f32[2]{0:T(128)S(1)} %get-tuple-element.602, ...), kind=kOutput, calls=%fused_computation.68 | convolution fusion | flops 6520188928 | bytes 10572900 | tf_op jit(solution)/shard_map/cpxsn,sxm->scpmn/dot_general | solution.py:99
  89.3 1.5 copy.47
  92.8 2.1 copy.50
  96.1 2.3 reshape.126
  99.1 78.2 %all-gather.2.cloned.1.call-done = bf16[2,16,65536]{2,0,1:T(2,128)(2,1)} async-done(((bf16[2,4,65536]{2,0,1:T(2,128)(2,1)}), bf16[2,16,65536]{2,0,1:T(2,128)(2,1)}) %all-gather.2.cloned.1.call-update) | async-done | bytes 4194320 | tf_op jit(solution)/shard_map/all_gather | solution.py:116
  177.3 9.0 %fusion.185 = (bf16[1,16,65536]{2,0,1:T(2,128)(2,1)S(1)}, bf16[1,16,65536]{2,0,1:T(2,128)(2,1)S(1)}) fusion(bf16[2,16,65536]{2,0,1:T(2,128)(2,1)} %all-gather.2.cloned.1.call-done), kind=kLoop, calls=%fused_computation.204 | loop fusion | bytes 8388608 | tf_op jit(solution)/shard_map/slice | solution.py:117
  186.4 3.6 %copy.63 = bf16[1,16,65536]{2,1,0:T(8,128)(2,1)} copy(bf16[1,16,65536]{2,0,1:T(2,128)(2,1)S(1)} %get-tuple-element.596) | data formatting | bytes 4194304
  190.0 3.6 %copy.64 = bf16[1,16,65536]{2,1,0:T(8,128)(2,1)} copy(bf16[1,16,65536]{2,0,1:T(2,128)(2,1)S(1)} %get-tuple-element.597) | data formatting | bytes 4194304
  193.6 53.2 %while.79 = (s32[]{:T(128)}, f32[64,256]{1,0:T(8,128)S(1)}, f32[64,6]{0,1:T(8,128)S(1)}, bf16[4,65536]{1,0:T(4,128)(2,1)S(1)}, bf16[16,65536]{1,0:T(8,128)(2,1)}...) while((s32[]{:T(128)}, f32[64,256]{1,0:T(8,128)S(1)}, ...), condition=%wide.region_1.2_spmd.clone, body=%wide.region_0.1_spmd.clone.sunk | while | flops 140165888 | bytes 7703730 | solution.py:136
  247.0 1.3 collective-permute-done.4
  248.3 1.6 collective-permute-start.5
  249.9 3.3 collective-permute-done.5
  253.4 10.3 %collective-permute-done.6 = f32[256,262]{1,0:T(8,128)S(1)} collective-permute-done((f32[256,262]{1,0:T(8,128)S(1)}, f32[256,262]{1,0:T(8,128)S(1)}, u32[]{:S(2)}, u32[]{:S(2)}) %collective-permute-start.6) | collective-permute-done | bytes 268320 | tf_op jit(solution)/shard_map/ppermute | solution.py:42
  264.7 17.8 %collective-permute-done.7 = f32[256,262]{1,0:T(8,128)S(1)} collective-permute-done((f32[256,262]{1,0:T(8,128)S(1)}, f32[256,262]{1,0:T(8,128)S(1)}, u32[]{:S(2)}, u32[]{:S(2)}) %collective-permute-start.7) | collective-permute-done | bytes 268320 | tf_op jit(solution)/shard_map/ppermute | solution.py:42
  282.6 2.6 gather_fusion
  285.5 12.1 %while.77 = (s32[]{:T(128)}, f32[6,256]{1,0:T(8,128)S(1)}, f32[3,6,64]{2,1,0:T(8,128)}, s32[3,6,256]{2,1,0:T(8,128)}, f32[6,256]{1,0:T(8,128)S(1)}, /*index=5*/f...) while((s32[]{:T(128)}, f32[6,256]{1,0:T(8,128)S(1)}, f32[3,6,64]{2,1,0:T(8,128)}, ...), condition=%wide.region_8.9_spmd, body=%wide.region_2.8_spmd.sunk | while | flops 9474058 | bytes 660566 | solution.py:184
  286.7 2.2 while.80
  290.7 2.2 while.80
  294.7 2.2 while.80
  297.7 41.2 %while.78 = (s32[]{:T(128)}, bf16[6,65536]{1,0:T(8,128)(2,1)S(1)}, bf16[6,65536]{1,0:T(8,128)(2,1)}, bf16[16,65536]{1,0:T(8,128)(2,1)}, bf16[16,65536]{1,0:T(8,1...) while((s32[]{:T(128)}, bf16[6,65536]{1,0:T(8,128)(2,1)S(1)}, ...), condition=%wide.region_10.11_spmd, body=%wide.region_9.10_spmd.sunk | while | flops 14884870 | bytes 5623963 | solution.py:205
  299.1 1.2 fusion.208
  304.2 1.2 fusion.208
  338.9 1.6 reshape.127
  340.5 1.4 copy.56
  (269 shorter events, 116.2 us)
Async XLA Ops:
  7.2 15.8 %copy-start.2 = (s32[4]{0:T(128)S(1)}, s32[4]{0:T(128)}, u32[]{:S(2)}) copy-start(s32[4]{0:T(128)} %param.14) | copy-start | bytes 52
  7.2 170.2 %all-gather.2.cloned.1.call-start = ((), (), s32[]{:S(2)}) async-start(), calls=%async_computation | async-start | bytes 5242880 | tf_op jit(solution)/shard_map/all_gather | solution.py:116
  19.9 10.1 %collective-permute-start = (bf16[4,4,1024,5]{2,3,1,0:T(8,128)(2,1)S(1)}, bf16[4,4,1024,5]{2,3,1,0:T(8,128)(2,1)S(1)}, u32[]{:S(2)}, u32[]{:S(2)}) collective-permute-start(bf16[4,4,1024,5]{2,3,1,0:T(8,128)(2,1)S(1)} %get-tuple-element.594), channel_id=1, source_target_pairs={{0,2},{2,0},{1,3},{3,1},{4,6},{6,4},{5,7},{7,5},{8,10},{10,8},{9,1... | collective-permute-start | bytes 491528 | tf_op jit(solution)/shard_map/ppermute | solution.py:27
  22.9 11.9 %collective-permute-start.1 = (bf16[4,4,1024,5]{2,3,1,0:T(8,128)(2,1)S(1)}, bf16[4,4,1024,5]{2,3,1,0:T(8,128)(2,1)S(1)}, u32[]{:S(2)}, u32[]{:S(2)}) collective-permute-start(bf16[4,4,1024,5]{2,3,1,0:T(8,128)(2,1)S(1)} %get-tuple-element.595), channel_id=1, source_target_pairs={{2,0},{0,2},{3,1},{1,3},{6,4},{4,6},{7,5},{5,7},{10,8},{8,10},{11,... | collective-permute-start | bytes 491528 | tf_op jit(solution)/shard_map/ppermute | solution.py:28
  40.3 3.5 copy-start
  45.0 1.4 collective-permute-start.2
  45.6 1.4 collective-permute-start.3
  92.8 2.1 copy-start.1
  246.9 1.4 collective-permute-start.4
  248.3 4.9 %collective-permute-start.5 = (f32[64,262]{1,0:T(8,128)S(1)}, f32[64,262]{1,0:T(8,128)S(1)}, u32[]{:S(2)}, u32[]{:S(2)}) collective-permute-start(f32[64,262]{1,0:T(8,128)S(1)} %fusion.181), channel_id=1, source_target_pairs={{0,2},{2,0},{1,3},{3,1},{4,6},{6,4},{5,7},{7,5},{8,10},{10,8},{9,1... | collective-permute-start | bytes 201224 | tf_op jit(solution)/shard_map/ppermute | solution.py:42
  253.3 10.4 %collective-permute-start.6 = (f32[256,262]{1,0:T(8,128)S(1)}, f32[256,262]{1,0:T(8,128)S(1)}, u32[]{:S(2)}, u32[]{:S(2)}) collective-permute-start(f32[256,262]{1,0:T(8,128)S(1)} %get-tuple-element.580), channel_id=1, source_target_pairs={{0,4},{4,0},{8,12},{12,8},{1,5},{5,1},{9,13},{13,9},{2,6},{6,2},{1... | collective-permute-start | bytes 804872 | tf_op jit(solution)/shard_map/ppermute | solution.py:42
  263.7 18.8 %collective-permute-start.7 = (f32[256,262]{1,0:T(8,128)S(1)}, f32[256,262]{1,0:T(8,128)S(1)}, u32[]{:S(2)}, u32[]{:S(2)}) collective-permute-start(f32[256,262]{1,0:T(8,128)S(1)} %add_dynamic-update-slice_fusion), channel_id=1, source_target_pairs={{0,8},{4,12},{8,0},{12,4},{1,9},{5,13},{9,1},{13,5},{2,10},{6,14},... | collective-permute-start | bytes 804872 | tf_op jit(solution)/shard_map/ppermute | solution.py:42
Sparse Core Ops, SparseCore 0:
  95.0 82.2 all-gather.1
where the time goes:
time: 352 us; the launch traced here: 349 us
  waiting for transfers between devices  123 us (35%)
  matrix products  75.5 us (21%)
  local copies, waits for them, and re-layouts  72.5 us (21%)
  other arithmetic  56.2 us (16%)
  between operations  14.4 us (4%)
  starting transfers between devices  6.47 us (2%)
    all_gather x1, waiting for transfers between devices, local(): lax.all_gather(jnp.stack([narrow_set, broad_set]), 'cols', axis=1, tiled=...  78.2 us
    ppermute x4, waiting for transfers between devices, tree_sum(): value = value + lax.ppermute(value, axis, partner)  32.7 us
    unnamed x10, local copies, waits for them, and re-layouts  23.6 us
    dot_general x16, matrix products, misfit_step(): jnp.dot(final_weights, all_terms, preferred_element_type=jnp.float32)  19.7 us
    concatenate x1, local copies, waits for them, and re-layouts, extended(): array = jnp.concatenate([before, array, after], axis=dim)  18.4 us
    dot_general x16, matrix products, gram_step(): jnp.einsum('ir,kr->ik', own_terms, weighted_piece, preferred_element_type...  17.3 us
    convert_element_type x32, other arithmetic, library(): narrow_part.astype(jnp.float32)[:, None, :]  16.6 us
    convert_element_type x16, other arithmetic, library(): broad_part.astype(jnp.float32)[None, :, :]  16.1 us
  transfers between devices with their start and end apart: 9, of which 7 were waited for; matrix products, arithmetic and copies ran while one was open for 2% of the time, Pallas kernels for 0%

commit v1 on v0

--- a/solution.py
+++ b/solution.py
@@ -111,39 +111,39 @@
         jnp.bfloat16
     )
     weighted = weighted.reshape(STRESS, row_count)
-    block_rows = math.gcd(row_count, 4096)
-    block_count = row_count // block_rows
-    both_sets = lax.all_gather(jnp.stack([narrow_set, broad_set]), "cols", axis=1, tiled=True)
+    chunk = row_count // col_devices
+    block_rows = math.gcd(chunk, 4096)
+    block_count = chunk // block_rows
+    both_sets = lax.all_to_all(
+        jnp.stack([narrow_set, broad_set]), "cols", 2, 1, tiled=True
+    )
     narrow_all, broad_all = both_sets[0], both_sets[1]
+    weighted = lax.dynamic_slice_in_dim(weighted, column_index * chunk, chunk, 1)
 
     def gram_step(block_index, carry):
         gram_acc, rhs_acc = carry
         start = block_index * block_rows
         narrow_piece = lax.dynamic_slice_in_dim(narrow_all, start, block_rows, 1)
         broad_piece = lax.dynamic_slice_in_dim(broad_all, start, block_rows, 1)
-        own_piece = lax.dynamic_slice_in_dim(narrow_set, start, block_rows, 1)
         all_terms = library(narrow_piece, broad_piece)
-        own_terms = library(own_piece, broad_piece)
         weighted_piece = lax.dynamic_slice_in_dim(weighted, start, block_rows, 1)
         gram_acc = gram_acc + jnp.einsum(
-            "ir,jr->ij", own_terms, all_terms, preferred_element_type=jnp.float32
+            "ir,jr->ij", all_terms, all_terms, preferred_element_type=jnp.float32
         )
         rhs_acc = rhs_acc + jnp.einsum(
-            "ir,kr->ik", own_terms, weighted_piece, preferred_element_type=jnp.float32
+            "ir,kr->ik", all_terms, weighted_piece, preferred_element_type=jnp.float32
         )
         return (gram_acc, rhs_acc)
 
-    gram_block, rhs_block = lax.fori_loop(
+    gram_part, rhs_part = lax.fori_loop(
         0,
         block_count,
         gram_step,
-        (jnp.zeros((term_dev, TERMS), jnp.float32), jnp.zeros((term_dev, STRESS), jnp.float32)),
-    )
-    own_rows = tree_sum(jnp.concatenate([gram_block, rhs_block], axis=1), ("rep", "slab"))
-    placed_rows = lax.dynamic_update_slice_in_dim(
-        jnp.zeros((TERMS, TERMS + STRESS), jnp.float32), own_rows, offset, 0
-    )
-    full_rows = tree_sum(placed_rows, ("cols",))
+        (jnp.zeros((TERMS, TERMS), jnp.float32), jnp.zeros((TERMS, STRESS), jnp.float32)),
+    )
+    full_rows = tree_sum(
+        jnp.concatenate([gram_part, rhs_part], axis=1), ("rep", "slab", "cols")
+    )
     gram_matrix = full_rows[:, :TERMS]
     rhs_sums = full_rows[:, TERMS:]
     column_scale = 1.0 / jnp.sqrt(jnp.diagonal(gram_matrix) / samples + epsilon)
@@ -203,8 +203,9 @@
         return lax.dynamic_update_slice_in_dim(misfit_acc, piece_misfit, start, 1)
 
     misfit = lax.fori_loop(
-        0, block_count, misfit_step, jnp.zeros((STRESS, row_count), jnp.bfloat16)
-    )
+        0, block_count, misfit_step, jnp.zeros((STRESS, chunk), jnp.bfloat16)
+    )
+    misfit = lax.all_gather(misfit, "cols", axis=1, tiled=True)
     misfit = misfit.reshape(STRESS, plane_count, coarse_x, coarse_z)
     return (coefficients, misfit)
 

time: 352 us -> 654 us (1.86); the launches traced: 349 us -> 642 us
  local copies, waits for them, and re-layouts: 72.5 us -> 476 us
  waiting for transfers between devices: 123 us -> 75.8 us
  other arithmetic: 56.2 us -> 15.8 us
  matrix products: 75.5 us -> 40.1 us
  blocking collectives: 0 us -> 21.5 us
  between operations: 14.4 us -> 1.43 us
    unnamed x10, local copies, waits for them, and re-layouts: 23.6 us -> 201 us
    slice x1 -> x3, local copies, waits for them, and re-layouts: 9.05 us -> 185 us  [local(): narrow_all, broad_all = (both_sets[0], both_sets[1])]
    all_gather x1 -> x0, waiting for transfers between devices: 78.2 us -> none  [local(): lax.all_gather(jnp.stack([narrow_set, broad_set]), 'cols', axis=1, tiled=...]
    another operation x1, local copies, waits for them, and re-layouts: 2.06 us -> 50.9 us  [local(): jnp.stack([narrow_set, broad_set])]
    all_to_all x0 -> x1, waiting for transfers between devices: none -> 24.3 us  [local(): lax.all_to_all(jnp.stack([narrow_set, broad_set]), 'cols', 2, 1, tiled=True)]
    all_gather x0 -> x1, blocking collectives: none -> 21.5 us  [local(): misfit = lax.all_gather(misfit, 'cols', axis=1, tiled=True)]
    dot_general x32 -> x8, matrix products: 29.8 us -> 9.11 us  [the longest x4 5.95 us: gram_step(): jnp.einsum('ir,kr->ik', all_terms, weighted_piece, preferred_element_type...]
    convert_element_type x32 -> x0, other arithmetic: 16.6 us -> none  [library(): narrow_part.astype(jnp.float32)[:, None, :]]
  transfers between devices with their start and end apart: 9 -> 9, of which waited for: 7 -> 7; matrix products, arithmetic and copies ran while one was open for 2% -> 1% of each run, Pallas kernels for 0% -> 0%
where the time goes in v1:
time: 654 us; the launch traced here: 642 us
  local copies, waits for them, and re-layouts  476 us (73%)
  waiting for transfers between devices  75.8 us (12%)
  matrix products  40.1 us (6%)
  blocking collectives  21.5 us (3%)
  other arithmetic  15.8 us (2%)
  starting transfers between devices  10.9 us (2%)
    unnamed x10, local copies, waits for them, and re-layouts  201 us
    slice x3, local copies, waits for them, and re-layouts, local(): narrow_all, broad_all = (both_sets[0], both_sets[1])  185 us
    another operation x1, local copies, waits for them, and re-layouts, local(): jnp.stack([narrow_set, broad_set])  50.9 us
    ppermute x4, waiting for transfers between devices, tree_sum(): value = value + lax.ppermute(value, axis, partner)  40.1 us
    all_to_all x1, waiting for transfers between devices, local(): lax.all_to_all(jnp.stack([narrow_set, broad_set]), 'cols', 2, 1, tiled=True)  24.3 us
    all_gather x1, blocking collectives, local(): misfit = lax.all_gather(misfit, 'cols', axis=1, tiled=True)  21.5 us
    concatenate x1, local copies, waits for them, and re-layouts, extended(): array = jnp.concatenate([before, array, after], axis=dim)  18.4 us
  transfers between devices with their start and end apart: 9, of which 7 were waited for; matrix products, arithmetic and copies ran while one was open for 1% of the time, Pallas kernels for 0%

profile of v1, /device:TPU:0, one launch (start us, length us, event | category | flops | bytes accessed | tf_op | source)
XLA Modules:
  0.0 642.4 jit_solution(13972069590268491912)
XLA Ops:
  0.7 11.6 %copy.29 = bf16[4,4,1024,256]{2,3,1,0:T(8,128)(2,1)} copy(bf16[4,4,1024,256]{3,2,1,0:T(8,128)(2,1)} %param.12) | data formatting | bytes 16777216 | tf_op args[0]
  13.4 3.0 collective-permute-start
  16.9 6.6 %collective-permute-done = bf16[4,4,1024,5]{2,3,1,0:T(8,128)(2,1)S(1)} collective-permute-done((bf16[4,4,1024,5]{2,3,1,0:T(8,128)(2,1)S(1)}, bf16[4,4,1024,5]{2,3,1,0:T(8,128)(2,1)S(1)}, u32[]{:S(2)}, u32[]{:S(2)}) %collective-permute-start) | collective-permute-done | bytes 163872 | tf_op jit(solution)/shard_map/ppermute | solution.py:27
  23.5 4.8 collective-permute-done.1
  28.3 5.5 pad_maximum_fusion
  33.8 3.5 copy-done
  41.5 2.3 reshape.115
  45.0 18.4 %concatenate.14 = bf16[4,4,1034,266]{2,3,1,0:T(8,128)(2,1)} concatenate(bf16[4,4,5,266]{2,3,1,0:T(8,128)(2,1)S(1)} %copy.34, bf16[4,4,1024,266]{2,3,1,0:T(8,128)(2,1)} %copy-done, bf16[4,4,5,266]{2,3,1,0:T(8,128)(2,1)S(1)} %copy.35), dimensions={2} | concatenate | bytes 17602816 | tf_op jit(solution)/shard_map/concatenate | solution.py:29
  63.4 10.7 %fusion.10 = f32[4,4,1034,2,64]{2,4,1,0,3:T(8,128)S(1)} fusion(bf16[4,4,1034,266]{2,3,1,0:T(8,128)(2,1)} %concatenate.14, f32[2]{0:T(128)S(1)} %get-tuple-element.567, f32[2]{0:T(128)S(1)} %get-tuple-element.568, f32[2]{0:T(128)S(1)} %get-tuple-element.569, f32[2]{0:T(128)S(1)} %get-tuple-element.570, f32[2]{0:T(128)S(1)} %get-tuple-element.571, ...), kind=kOutput, calls=%fused_computation.32 | convolution fusion | flops 6760434688 | bytes 17273316 | tf_op jit(solution)/shard_map/cpxz,zsn->cpxsn/dot_general | solution.py:98
  74.2 10.1 %fusion.53 = f32[2,4,4,256,64]{3,4,2,1,0:T(8,128)S(1)} fusion(f32[4,4,1034,2,64]{2,4,1,0,3:T(8,128)S(1)} %fusion.10, f32[2]{0:T(128)S(1)} %get-tuple-element.567, f32[2]{0:T(128)S(1)} %get-tuple-element.568, f32[2]{0:T(128)S(1)} %get-tuple-element.569, f32[2]{0:T(128)S(1)} %get-tuple-element.570, f32[2]{0:T(128)S(1)} %get-tuple-element.571, ...), kind=kOutput, calls=%fused_computation.64 | convolution fusion | flops 6520188928 | bytes 10572900 | tf_op jit(solution)/shard_map/cpxsn,sxm->scpmn/dot_general | solution.py:99
  90.9 50.9 %copy.38 = bf16[2,4,65536]{1,0,2:T(2,128)(2,1)} copy(bf16[2,4,65536]{2,1,0:T(4,128)(2,1)S(1)} %pad_maximum_fusion.1) | data formatting | bytes 2097152 | tf_op jit(solution)/shard_map/stack | solution.py:118
  141.8 99.7 %reshape.126 = bf16[4,2,65536]{2,1,0:T(2,128)(2,1)} reshape(bf16[65536,2,4]{2,1,0:T(2,128)(2,1)} %bitcast.80) | data formatting | bytes 2097152
  241.5 5.1 all-to-all-start
  246.6 1.7 constant_dynamic-slice_fusion
  248.3 24.3 %all-to-all-done = bf16[4,2,65536]{2,1,0:T(2,128)(2,1)S(1)} async-done(((bf16[4,2,65536]{2,1,0:T(2,128)(2,1)}), bf16[4,2,65536]{2,1,0:T(2,128)(2,1)S(1)}, u32[]{:S(2)}, u32[]{:S(2)}) %all-to-all-start) | async-done | bytes 1048608 | tf_op jit(solution)/shard_map/all_to_all | solution.py:117
  272.6 85.1 %reshape.127 = bf16[65536,2,4]{2,1,0:T(2,128)(2,1)} reshape(bf16[4,2,65536]{2,1,0:T(2,128)(2,1)S(1)} %all-to-all-done) | data formatting | bytes 2097152
  357.7 62.4 %fusion.183 = (bf16[1,4,4,16384]{2,0,3,1:T(2,128)(2,1)}, bf16[1,4,4,16384]{2,0,3,1:T(2,128)(2,1)}) fusion(bf16[2,4,4,16384]{2,0,3,1:T(2,128)(2,1)} %bitcast.78), kind=kLoop, calls=%fused_computation.197 | loop fusion | bytes 2097152 | tf_op jit(solution)/shard_map/slice | solution.py:120
  420.1 61.1 %copy.39 = bf16[1,4,4,16384]{3,2,1,0:T(4,128)(2,1)S(1)} copy(bf16[1,4,4,16384]{2,0,3,1:T(2,128)(2,1)} %get-tuple-element.562) | data formatting | bytes 1048576 | tf_op jit(solution)/shard_map/slice | solution.py:120
  481.3 61.1 %copy.40 = bf16[1,4,4,16384]{3,2,1,0:T(4,128)(2,1)S(1)} copy(bf16[1,4,4,16384]{2,0,3,1:T(2,128)(2,1)} %get-tuple-element.561) | data formatting | bytes 1048576 | tf_op jit(solution)/shard_map/slice | solution.py:120
  542.5 11.0 %while.79 = (s32[]{:T(128)}, f32[256,256]{1,0:T(8,128)S(1)}, f32[256,6]{0,1:T(8,128)S(1)}, bf16[16,16384]{1,0:T(8,128)(2,1)S(1)}, bf16[16,16384]{1,0:T(8,128)(2,...) while((s32[]{:T(128)}, f32[256,256]{1,0:T(8,128)S(1)}, ...), condition=%wide.region_1.2_spmd.clone, body=%wide.region_0.1_spmd.clone.sunk | while | flops 551816192 | bytes 8204454 | solution.py:138
  553.8 1.7 collective-permute-done.4
  557.1 9.7 %collective-permute-done.5 = f32[256,262]{1,0:T(8,128)S(1)} collective-permute-done((f32[256,262]{1,0:T(8,128)S(1)}, f32[256,262]{1,0:T(8,128)S(1)}, u32[]{:S(2)}, u32[]{:S(2)}) %collective-permute-start.5) | collective-permute-done | bytes 268320 | tf_op jit(solution)/shard_map/ppermute | solution.py:42
  566.9 10.3 %collective-permute-done.6 = f32[256,262]{1,0:T(8,128)S(1)} collective-permute-done((f32[256,262]{1,0:T(8,128)S(1)}, f32[256,262]{1,0:T(8,128)S(1)}, u32[]{:S(2)}, u32[]{:S(2)}) %collective-permute-start.6) | collective-permute-done | bytes 268320 | tf_op jit(solution)/shard_map/ppermute | solution.py:42
  577.6 18.5 %collective-permute-done.7 = f32[256,262]{1,0:T(8,128)S(1)} collective-permute-done((f32[256,262]{1,0:T(8,128)S(1)}, f32[256,262]{1,0:T(8,128)S(1)}, u32[]{:S(2)}, u32[]{:S(2)}) %collective-permute-start.7) | collective-permute-done | bytes 268320 | tf_op jit(solution)/shard_map/ppermute | solution.py:42
  596.1 2.3 gather_fusion
  598.8 12.1 %while.77 = (s32[]{:T(128)}, f32[6,256]{1,0:T(8,128)S(1)}, f32[3,6,64]{2,1,0:T(8,128)}, s32[3,6,256]{2,1,0:T(8,128)}, f32[6,256]{1,0:T(8,128)S(1)}, /*index=5*/f...) while((s32[]{:T(128)}, f32[6,256]{1,0:T(8,128)S(1)}, f32[3,6,64]{2,1,0:T(8,128)}, ...), condition=%wide.region_8.9_spmd, body=%wide.region_2.8_spmd.sunk | while | flops 9474058 | bytes 660566 | solution.py:184
  599.9 2.2 while.80
  604.0 2.2 while.80
  608.0 2.2 while.80
  610.9 6.4 %while.78 = (s32[]{:T(128)}, bf16[6,16384]{1,0:T(8,128)(2,1)S(1)}, bf16[6,16384]{1,0:T(8,128)(2,1)}, bf16[16,16384]{1,0:T(8,128)(2,1)S(1)}, bf16[16,16384]{1,0:T...) while((s32[]{:T(128)}, bf16[6,16384]{1,0:T(8,128)(2,1)S(1)}, ...), condition=%wide.region_10.11_spmd, body=%wide.region_9.10_spmd.sunk | while | flops 14884870 | bytes 5623963 | solution.py:205
  617.4 21.5 %all_gather.3 = bf16[6,65536]{1,0:T(8,128)(2,1)S(1)} all-gather(bf16[6,16384]{1,0:T(8,128)(2,1)S(1)} %get-tuple-element.439), channel_id=1, replica_groups=mesh['groups'=2,'cols'=4,'slab'=2,'rep'=2] {'cols'}, dimensions={1}, use_global_device_ids=true | all-gather | bytes 983040 | tf_op jit(solution)/shard_map/all_gather | solution.py:208
  638.9 1.6 reshape.116
  (156 shorter events, 46.8 us)
Async XLA Ops:
  0.6 15.8 %copy-start.2 = (s32[4]{0:T(128)S(1)}, s32[4]{0:T(128)}, u32[]{:S(2)}) copy-start(s32[4]{0:T(128)} %param.14) | copy-start | bytes 52
  0.6 15.9 %copy-start.1 = (bf16[6,4,256,64]{2,3,1,0:T(8,128)(2,1)S(1)}, bf16[6,4,256,64]{2,3,1,0:T(8,128)(2,1)}, u32[]{:S(2)}) copy-start(bf16[6,4,256,64]{2,3,1,0:T(8,128)(2,1)} %param.13) | copy-start | bytes 2359300
  13.4 10.1 %collective-permute-start = (bf16[4,4,1024,5]{2,3,1,0:T(8,128)(2,1)S(1)}, bf16[4,4,1024,5]{2,3,1,0:T(8,128)(2,1)S(1)}, u32[]{:S(2)}, u32[]{:S(2)}) collective-permute-start(bf16[4,4,1024,5]{2,3,1,0:T(8,128)(2,1)S(1)} %get-tuple-element.565), channel_id=1, source_target_pairs={{0,2},{2,0},{1,3},{3,1},{4,6},{6,4},{5,7},{7,5},{8,10},{10,8},{9,1... | collective-permute-start | bytes 491528 | tf_op jit(solution)/shard_map/ppermute | solution.py:27
  16.4 11.9 %collective-permute-start.1 = (bf16[4,4,1024,5]{2,3,1,0:T(8,128)(2,1)S(1)}, bf16[4,4,1024,5]{2,3,1,0:T(8,128)(2,1)S(1)}, u32[]{:S(2)}, u32[]{:S(2)}) collective-permute-start(bf16[4,4,1024,5]{2,3,1,0:T(8,128)(2,1)S(1)} %get-tuple-element.566), channel_id=1, source_target_pairs={{2,0},{0,2},{3,1},{1,3},{6,4},{4,6},{7,5},{5,7},{10,8},{8,10},{11,... | collective-permute-start | bytes 491528 | tf_op jit(solution)/shard_map/ppermute | solution.py:28
  33.8 3.5 copy-start
  38.5 5.3 collective-permute-start.2
  39.1 5.3 collective-permute-start.3
  241.5 31.1 %all-to-all-start = ((bf16[4,2,65536]{2,1,0:T(2,128)(2,1)}), bf16[4,2,65536]{2,1,0:T(2,128)(2,1)S(1)}, u32[]{:S(2)}, u32[]{:S(2)}) async-start(bf16[4,2,65536]{2,1,0:T(2,128)(2,1)} %reshape.126), calls=%async_computation | async-start | bytes 2097152 | tf_op jit(solution)/shard_map/all_to_all | solution.py:117
  553.7 1.8 collective-permute-start.4
  555.5 11.2 %collective-permute-start.5 = (f32[256,262]{1,0:T(8,128)S(1)}, f32[256,262]{1,0:T(8,128)S(1)}, u32[]{:S(2)}, u32[]{:S(2)}) collective-permute-start(f32[256,262]{1,0:T(8,128)S(1)} %fusion.181), channel_id=1, source_target_pairs={{0,2},{2,0},{1,3},{3,1},{4,6},{6,4},{5,7},{7,5},{8,10},{10,8},{9,1... | collective-permute-start | bytes 804872 | tf_op jit(solution)/shard_map/ppermute | solution.py:42
  566.8 10.4 %collective-permute-start.6 = (f32[256,262]{1,0:T(8,128)S(1)}, f32[256,262]{1,0:T(8,128)S(1)}, u32[]{:S(2)}, u32[]{:S(2)}) collective-permute-start(f32[256,262]{1,0:T(8,128)S(1)} %add.190), channel_id=1, source_target_pairs={{0,4},{4,0},{8,12},{12,8},{1,5},{5,1},{9,13},{13,9},{2,6},{6,2},{1... | collective-permute-start | bytes 804872 | tf_op jit(solution)/shard_map/ppermute | solution.py:42
  577.2 18.8 %collective-permute-start.7 = (f32[256,262]{1,0:T(8,128)S(1)}, f32[256,262]{1,0:T(8,128)S(1)}, u32[]{:S(2)}, u32[]{:S(2)}) collective-permute-start(f32[256,262]{1,0:T(8,128)S(1)} %add.191), channel_id=1, source_target_pairs={{0,8},{4,12},{8,0},{12,4},{1,9},{5,13},{9,1},{13,5},{2,10},{6,14},... | collective-permute-start | bytes 804872 | tf_op jit(solution)/shard_map/ppermute | solution.py:42

commit v2 on v1

--- a/solution.py
+++ b/solution.py
@@ -69,10 +69,10 @@
 
 def library(narrow_part, broad_part):
     product = (
-        narrow_part.astype(jnp.float32)[:, None, :] * broad_part.astype(jnp.float32)[None, :, :]
+        narrow_part.astype(jnp.float32)[:, None] * broad_part.astype(jnp.float32)[None, :]
     )
     return product.astype(jnp.bfloat16).reshape(
-        narrow_part.shape[0] * broad_part.shape[0], narrow_part.shape[1]
+        (narrow_part.shape[0] * broad_part.shape[0],) + narrow_part.shape[1:]
     )
 
 
@@ -112,13 +112,19 @@
     )
     weighted = weighted.reshape(STRESS, row_count)
     chunk = row_count // col_devices
-    block_rows = math.gcd(chunk, 4096)
-    block_count = chunk // block_rows
-    both_sets = lax.all_to_all(
-        jnp.stack([narrow_set, broad_set]), "cols", 2, 1, tiled=True
-    )
-    narrow_all, broad_all = both_sets[0], both_sets[1]
-    weighted = lax.dynamic_slice_in_dim(weighted, column_index * chunk, chunk, 1)
+    lanes = 128
+    chunk_rows = chunk // lanes
+    channels = chan_dev * col_devices
+    sets = jnp.stack([narrow_set, broad_set]).reshape(2, chan_dev, col_devices, chunk_rows, lanes)
+    sets = jnp.transpose(sets, (2, 0, 1, 3, 4)).reshape(col_devices, 2 * chan_dev * chunk_rows, lanes)
+    sets = lax.all_to_all(sets, "cols", 0, 0, tiled=True)
+    sets = sets.reshape(col_devices, 2, chan_dev, chunk_rows, lanes)
+    sets = jnp.transpose(sets, (1, 0, 2, 3, 4)).reshape(2, channels, chunk_rows, lanes)
+    narrow_all, broad_all = sets[0], sets[1]
+    weighted = weighted.reshape(STRESS, col_devices, chunk_rows, lanes)
+    weighted = lax.dynamic_index_in_dim(weighted, column_index, 1, keepdims=False)
+    block_rows = math.gcd(chunk_rows, 32)
+    block_count = chunk_rows // block_rows
 
     def gram_step(block_index, carry):
         gram_acc, rhs_acc = carry
@@ -128,10 +134,10 @@
         all_terms = library(narrow_piece, broad_piece)
         weighted_piece = lax.dynamic_slice_in_dim(weighted, start, block_rows, 1)
         gram_acc = gram_acc + jnp.einsum(
-            "ir,jr->ij", all_terms, all_terms, preferred_element_type=jnp.float32
+            "iqr,jqr->ij", all_terms, all_terms, preferred_element_type=jnp.float32
         )
         rhs_acc = rhs_acc + jnp.einsum(
-            "ir,kr->ik", all_terms, weighted_piece, preferred_element_type=jnp.float32
+            "iqr,kqr->ik", all_terms, weighted_piece, preferred_element_type=jnp.float32
         )
         return (gram_acc, rhs_acc)
 
@@ -197,13 +203,15 @@
         narrow_piece = lax.dynamic_slice_in_dim(narrow_all, start, block_rows, 1)
         broad_piece = lax.dynamic_slice_in_dim(broad_all, start, block_rows, 1)
         all_terms = library(narrow_piece, broad_piece)
-        predicted = jnp.dot(final_weights, all_terms, preferred_element_type=jnp.float32)
+        predicted = jnp.einsum(
+            "ki,iqr->kqr", final_weights, all_terms, preferred_element_type=jnp.float32
+        )
         weighted_piece = lax.dynamic_slice_in_dim(weighted, start, block_rows, 1)
         piece_misfit = (weighted_piece.astype(jnp.float32) - predicted).astype(jnp.bfloat16)
         return lax.dynamic_update_slice_in_dim(misfit_acc, piece_misfit, start, 1)
 
     misfit = lax.fori_loop(
-        0, block_count, misfit_step, jnp.zeros((STRESS, chunk), jnp.bfloat16)
+        0, block_count, misfit_step, jnp.zeros((STRESS, chunk_rows, lanes), jnp.bfloat16)
     )
     misfit = lax.all_gather(misfit, "cols", axis=1, tiled=True)
     misfit = misfit.reshape(STRESS, plane_count, coarse_x, coarse_z)

time: 654 us -> 216 us (0.33); the launches traced: 642 us -> 215 us
  local copies, waits for them, and re-layouts: 476 us -> 55.2 us
    slice x3 -> x1, local copies, waits for them, and re-layouts: 185 us -> 0.1 us  [local(): narrow_all, broad_all = (sets[0], sets[1])]
    unnamed x10 -> x11, local copies, waits for them, and re-layouts: 201 us -> 17.9 us
    another operation x1, local copies, waits for them, and re-layouts: 50.9 us -> 1.48 us  [local(): weighted = weighted.reshape(STRESS, col_devices, chunk_rows, lanes)]
  transfers between devices with their start and end apart: 9 -> 9, of which waited for: 7 -> 9; matrix products, arithmetic and copies ran while one was open for 1% -> 3% of each run, Pallas kernels for 0% -> 0%
where the time goes in v2:
time: 216 us; the launch traced here: 215 us
  waiting for transfers between devices  72.1 us (33%)
  local copies, waits for them, and re-layouts  55.2 us (26%)
  matrix products  40 us (19%)
  blocking collectives  18 us (8%)
  other arithmetic  17 us (8%)
  starting transfers between devices  10.9 us (5%)
    ppermute x4, waiting for transfers between devices, tree_sum(): value = value + lax.ppermute(value, axis, partner)  40.1 us
    all_to_all x1, waiting for transfers between devices, local(): sets = lax.all_to_all(sets, 'cols', 0, 0, tiled=True)  19.9 us
    concatenate x1, local copies, waits for them, and re-layouts, extended(): array = jnp.concatenate([before, array, after], axis=dim)  18.4 us
    all_gather x1, blocking collectives, local(): misfit = lax.all_gather(misfit, 'cols', axis=1, tiled=True)  18 us
    unnamed x11, local copies, waits for them, and re-layouts  17.9 us
    dot_general x1, matrix products, local(): jnp.einsum('cpxz,zsn->cpxsn', widened, span_table, precision=lax.Precisio...  10.7 us
    dot_general x1, matrix products, local(): jnp.einsum('cpxsn,sxm->scpmn', along_span, stream_table, precision=lax.Pr...  10.1 us
    ppermute x2, waiting for transfers between devices, extended(): before = lax.ppermute(last, axis, up)  7.09 us
  transfers between devices with their start and end apart: 9, of which 9 were waited for; matrix products, arithmetic and copies ran while one was open for 3% of the time, Pallas kernels for 0%

profile of v2, /device:TPU:0, one launch (start us, length us, event | category | flops | bytes accessed | tf_op | source)
XLA Modules:
  0.0 214.6 jit_solution(6035308899534324445)
XLA Ops:
  0.6 11.5 %copy.37 = bf16[4,4,1024,256]{2,3,1,0:T(8,128)(2,1)} copy(bf16[4,4,1024,256]{3,2,1,0:T(8,128)(2,1)} %param.12) | data formatting | bytes 16777216 | tf_op args[0]
  13.3 3.0 %collective-permute-start = (bf16[4,4,1024,5]{2,3,1,0:T(8,128)(2,1)S(1)}, bf16[4,4,1024,5]{2,3,1,0:T(8,128)(2,1)S(1)}, u32[]{:S(2)}, u32[]{:S(2)}) collective-permute-start(bf16[4,4,1024,5]{2,3,1,0:T(8,128)(2,1)S(1)} %get-tuple-element.599), channel_id=1, source_target_pairs={{0,2},{2,0},{1,3},{3,1},{4,6},{6,4},{5,7},{7,5},{8,10},{10,8},{9,1... | collective-permute-start | bytes 491528 | tf_op jit(solution)/shard_map/ppermute | solution.py:27
  16.4 7.0 %collective-permute-done = bf16[4,4,1024,5]{2,3,1,0:T(8,128)(2,1)S(1)} collective-permute-done((bf16[4,4,1024,5]{2,3,1,0:T(8,128)(2,1)S(1)}, bf16[4,4,1024,5]{2,3,1,0:T(8,128)(2,1)S(1)}, u32[]{:S(2)}, u32[]{:S(2)}) %collective-permute-start) | collective-permute-done | bytes 163872 | tf_op jit(solution)/shard_map/ppermute | solution.py:27
  23.4 4.8 %collective-permute-done.1 = bf16[4,4,1024,5]{2,3,1,0:T(8,128)(2,1)S(1)} collective-permute-done((bf16[4,4,1024,5]{2,3,1,0:T(8,128)(2,1)S(1)}, bf16[4,4,1024,5]{2,3,1,0:T(8,128)(2,1)S(1)}, u32[]{:S(2)}, u32[]{:S(2)}) %collective-permute-start.1) | collective-permute-done | bytes 163872 | tf_op jit(solution)/shard_map/ppermute | solution.py:28
  28.2 5.5 %pad_maximum_fusion = bf16[4,4,1024,266]{2,3,1,0:T(8,128)(2,1)S(1)} fusion(bf16[4,4,1024,5]{2,3,1,0:T(8,128)(2,1)S(1)} %collective-permute-done.1, bf16[4,4,1024,256]{2,3,1,0:T(8,128)(2,1)} %copy.37, bf16[4,4,1024,5]{2,3,1,0:T(8,128)(2,1)S(1)} %collective-permute-done), kind=kLoop, calls=%fused_computation.37 | loop fusion | flops 26148864 | bytes 17432576 | tf_op jit(solution)/shard_map/concatenate | solution.py:29
  33.7 3.5 %copy-done = bf16[4,4,1024,266]{2,3,1,0:T(8,128)(2,1)} copy-done((bf16[4,4,1024,266]{2,3,1,0:T(8,128)(2,1)}, bf16[4,4,1024,266]{2,3,1,0:T(8,128)(2,1)S(1)}, u32[]{:S(2)}) %copy-start) | copy-done | bytes 8716312
  41.1 18.4 %concatenate.15 = bf16[4,4,1034,266]{2,3,1,0:T(8,128)(2,1)} concatenate(bf16[4,4,5,266]{2,3,1,0:T(8,128)(2,1)S(1)} %copy.42, bf16[4,4,1024,266]{2,3,1,0:T(8,128)(2,1)} %copy-done, bf16[4,4,5,266]{2,3,1,0:T(8,128)(2,1)S(1)} %copy.43), dimensions={2} | concatenate | bytes 17602816 | tf_op jit(solution)/shard_map/concatenate | solution.py:29
  59.5 10.7 %fusion.12 = f32[4,4,1034,2,64]{2,4,1,0,3:T(8,128)S(1)} fusion(bf16[4,4,1034,266]{2,3,1,0:T(8,128)(2,1)} %concatenate.15, f32[2]{0:T(128)S(1)} %get-tuple-element.603, f32[2]{0:T(128)S(1)} %get-tuple-element.604, f32[2]{0:T(128)S(1)} %get-tuple-element.605, f32[2]{0:T(128)S(1)} %get-tuple-element.606, f32[2]{0:T(128)S(1)} %get-tuple-element.607, ...), kind=kOutput, calls=%fused_computation.35 | convolution fusion | flops 6760434688 | bytes 17273316 | tf_op jit(solution)/shard_map/cpxz,zsn->cpxsn/dot_general | solution.py:98
  70.2 10.1 %fusion.55 = f32[2,4,4,256,64]{3,4,2,1,0:T(8,128)S(1)} fusion(f32[4,4,1034,2,64]{2,4,1,0,3:T(8,128)S(1)} %fusion.12, f32[2]{0:T(128)S(1)} %get-tuple-element.603, f32[2]{0:T(128)S(1)} %get-tuple-element.604, f32[2]{0:T(128)S(1)} %get-tuple-element.605, f32[2]{0:T(128)S(1)} %get-tuple-element.606, f32[2]{0:T(128)S(1)} %get-tuple-element.607, ...), kind=kOutput, calls=%fused_computation.67 | convolution fusion | flops 6520188928 | bytes 10572900 | tf_op jit(solution)/shard_map/cpxsn,sxm->scpmn/dot_general | solution.py:99
  82.2 1.5 copy.44
  85.6 5.1 %all-to-all-start = ((bf16[4,1024,128]{2,1,0:T(8,128)(2,1)}), bf16[4,1024,128]{2,1,0:T(8,128)(2,1)S(1)}, u32[]{:S(2)}, u32[]{:S(2)}) async-start(bf16[4,1024,128]{2,1,0:T(8,128)(2,1)} %bitcast.12), calls=%async_computation | async-start | bytes 2097152 | tf_op jit(solution)/shard_map/all_to_all | solution.py:120
  92.0 1.8 copy.47
  93.8 1.5 reshape_reshape.3
  97.0 19.9 %all-to-all-done = bf16[4,1024,128]{2,1,0:T(8,128)(2,1)S(1)} async-done(((bf16[4,1024,128]{2,1,0:T(8,128)(2,1)}), bf16[4,1024,128]{2,1,0:T(8,128)(2,1)S(1)}, u32[]{:S(2)}, u32[]{:S(2)}) %all-to-all-start) | async-done | bytes 1048608 | tf_op jit(solution)/shard_map/all_to_all | solution.py:120
  117.8 11.7 %while.79 = (s32[]{:T(128)}, f32[256,256]{1,0:T(8,128)S(1)}, f32[256,6]{0,1:T(8,128)S(1)}, bf16[16,128,128]{2,0,1:T(8,128)(2,1)S(1)}, bf16[16,128,128]{2,0,1:T(8...) while((s32[]{:T(128)}, f32[256,256]{1,0:T(8,128)S(1)}, ...), condition=%wide.region_1.2_spmd.clone, body=%wide.region_0.1_spmd.clone.sunk | while | flops 551816192 | bytes 8204454 | solution.py:144
  119.2 1.5 fusion.217
  122.2 1.5 fusion.217
  125.1 1.5 fusion.217
  128.0 1.5 fusion.217
  129.8 1.7 collective-permute-done.4
  131.5 1.6 collective-permute-start.5
  133.1 9.7 %collective-permute-done.5 = f32[256,262]{1,0:T(8,128)S(1)} collective-permute-done((f32[256,262]{1,0:T(8,128)S(1)}, f32[256,262]{1,0:T(8,128)S(1)}, u32[]{:S(2)}, u32[]{:S(2)}) %collective-permute-start.5) | collective-permute-done | bytes 268320 | tf_op jit(solution)/shard_map/ppermute | solution.py:42
  142.9 10.3 %collective-permute-done.6 = f32[256,262]{1,0:T(8,128)S(1)} collective-permute-done((f32[256,262]{1,0:T(8,128)S(1)}, f32[256,262]{1,0:T(8,128)S(1)}, u32[]{:S(2)}, u32[]{:S(2)}) %collective-permute-start.6) | collective-permute-done | bytes 268320 | tf_op jit(solution)/shard_map/ppermute | solution.py:42
  153.6 18.4 %collective-permute-done.7 = f32[256,262]{1,0:T(8,128)S(1)} collective-permute-done((f32[256,262]{1,0:T(8,128)S(1)}, f32[256,262]{1,0:T(8,128)S(1)}, u32[]{:S(2)}, u32[]{:S(2)}) %collective-permute-start.7) | collective-permute-done | bytes 268320 | tf_op jit(solution)/shard_map/ppermute | solution.py:42
  172.1 2.3 %gather_fusion = f32[256]{0:T(256)S(1)} fusion(f32[256,256]{1,0:T(8,128)S(1)} %slice.53, s32[256]{0:T(256)S(1)} %bitcast.96), kind=kCustom, calls=%fused_computation | custom fusion | bytes 4096 | tf_op jit(solution)/shard_map/jit(diagonal)/cond/branch_0_fun/gather | solution.py:155
  174.7 12.1 %while.77 = (s32[]{:T(128)}, f32[6,256]{1,0:T(8,128)S(1)}, f32[3,6,64]{2,1,0:T(8,128)}, s32[3,6,256]{2,1,0:T(8,128)}, f32[6,256]{1,0:T(8,128)S(1)}, /*index=5*/f...) while((s32[]{:T(128)}, f32[6,256]{1,0:T(8,128)S(1)}, f32[3,6,64]{2,1,0:T(8,128)}, ...), condition=%wide.region_8.9_spmd, body=%wide.region_2.8_spmd.sunk | while | flops 9474058 | bytes 660566 | solution.py:190
  175.9 2.2 %while.80 = (s32[]{:T(128)}, f32[6,256]{1,0:T(8,128)S(1)}, f32[6,256]{1,0:T(8,128)S(1)}, f32[6,256]{1,0:T(8,128)S(1)}, f32[6]{0:T(128)S(1)}, /*index=5*/f32[6,256]{1,0:T(8,128)S(1)}, f32[256,256]{1,0:T(8,128)S(1)}, s32[]{:T(128)}) while((s32[]{:T(128)}, f32[6,256]{1,0:T(8,128)S(1)}, f32[6,256]{1,0:T(8,128)S(1)}, f32[6,256]{1,0:T(8,128)S(1)}, ...), condition=%wide.region_7.7_spmd, body=%wide.region_4.6_spmd.sunk | while | flops 4740110 | bytes 330125 | solution.py:183
  179.9 2.2 %while.80 = (s32[]{:T(128)}, f32[6,256]{1,0:T(8,128)S(1)}, f32[6,256]{1,0:T(8,128)S(1)}, f32[6,256]{1,0:T(8,128)S(1)}, f32[6]{0:T(128)S(1)}, /*index=5*/f32[6,256]{1,0:T(8,128)S(1)}, f32[256,256]{1,0:T(8,128)S(1)}, s32[]{:T(128)}) while((s32[]{:T(128)}, f32[6,256]{1,0:T(8,128)S(1)}, f32[6,256]{1,0:T(8,128)S(1)}, f32[6,256]{1,0:T(8,128)S(1)}, ...), condition=%wide.region_7.7_spmd, body=%wide.region_4.6_spmd.sunk | while | flops 4740110 | bytes 330125 | solution.py:183
  184.0 2.2 %while.80 = (s32[]{:T(128)}, f32[6,256]{1,0:T(8,128)S(1)}, f32[6,256]{1,0:T(8,128)S(1)}, f32[6,256]{1,0:T(8,128)S(1)}, f32[6]{0:T(128)S(1)}, /*index=5*/f32[6,256]{1,0:T(8,128)S(1)}, f32[256,256]{1,0:T(8,128)S(1)}, s32[]{:T(128)}) while((s32[]{:T(128)}, f32[6,256]{1,0:T(8,128)S(1)}, f32[6,256]{1,0:T(8,128)S(1)}, f32[6,256]{1,0:T(8,128)S(1)}, ...), condition=%wide.region_7.7_spmd, body=%wide.region_4.6_spmd.sunk | while | flops 4740110 | bytes 330125 | solution.py:183
  186.9 7.6 %while.78 = (s32[]{:T(128)}, bf16[6,128,128]{2,1,0:T(8,128)(2,1)S(1)}, bf16[6,128,128]{2,0,1:T(8,128)(2,1)}, bf16[16,128,128]{2,0,1:T(8,128)(2,1)S(1)}, bf16[16,...) while((s32[]{:T(128)}, ...), condition=%wide.region_10.11_spmd, body=%wide.region_9.10_spmd.sunk | while | flops 14884870 | bytes 5721247 | solution.py:213
  194.5 18.0 %all_gather.3 = bf16[6,512,128]{2,1,0:T(8,128)(2,1)S(1)} all-gather(bf16[6,128,128]{2,1,0:T(8,128)(2,1)S(1)} %get-tuple-element.439), channel_id=1, replica_groups=mesh['groups'=2,'cols'=4,'slab'=2,'rep'=2] {'cols'}, dimensions={1}, use_global_device_ids=true | all-gather | bytes 983040 | tf_op jit(solution)/shard_map/all_gather | solution.py:216
  213.2 1.4 copy.57
  (155 shorter events, 39.5 us)
Async XLA Ops:
  0.6 15.8 %copy-start.2 = (s32[4]{0:T(128)S(1)}, s32[4]{0:T(128)}, u32[]{:S(2)}) copy-start(s32[4]{0:T(128)} %param.14) | copy-start | bytes 52
  13.3 10.1 %collective-permute-start = (bf16[4,4,1024,5]{2,3,1,0:T(8,128)(2,1)S(1)}, bf16[4,4,1024,5]{2,3,1,0:T(8,128)(2,1)S(1)}, u32[]{:S(2)}, u32[]{:S(2)}) collective-permute-start(bf16[4,4,1024,5]{2,3,1,0:T(8,128)(2,1)S(1)} %get-tuple-element.599), channel_id=1, source_target_pairs={{0,2},{2,0},{1,3},{3,1},{4,6},{6,4},{5,7},{7,5},{8,10},{10,8},{9,1... | collective-permute-start | bytes 491528 | tf_op jit(solution)/shard_map/ppermute | solution.py:27
  16.3 11.9 %collective-permute-start.1 = (bf16[4,4,1024,5]{2,3,1,0:T(8,128)(2,1)S(1)}, bf16[4,4,1024,5]{2,3,1,0:T(8,128)(2,1)S(1)}, u32[]{:S(2)}, u32[]{:S(2)}) collective-permute-start(bf16[4,4,1024,5]{2,3,1,0:T(8,128)(2,1)S(1)} %get-tuple-element.600), channel_id=1, source_target_pairs={{2,0},{0,2},{3,1},{1,3},{6,4},{4,6},{7,5},{5,7},{10,8},{8,10},{11,... | collective-permute-start | bytes 491528 | tf_op jit(solution)/shard_map/ppermute | solution.py:28
  33.7 3.5 %copy-start = (bf16[4,4,1024,266]{2,3,1,0:T(8,128)(2,1)}, bf16[4,4,1024,266]{2,3,1,0:T(8,128)(2,1)S(1)}, u32[]{:S(2)}) copy-start(bf16[4,4,1024,266]{2,3,1,0:T(8,128)(2,1)S(1)} %pad_maximum_fusion) | copy-start | bytes 26148868
  38.4 1.3 collective-permute-start.2
  39.0 1.4 collective-permute-start.3
  84.6 6.2 %copy-start.1 = (bf16[6,4,256,64]{2,3,1,0:T(8,128)(2,1)S(1)}, bf16[6,4,256,64]{2,3,1,0:T(8,128)(2,1)}, u32[]{:S(2)}) copy-start(bf16[6,4,256,64]{2,3,1,0:T(8,128)(2,1)} %param.13) | copy-start | bytes 2359300
  85.6 31.4 %all-to-all-start = ((bf16[4,1024,128]{2,1,0:T(8,128)(2,1)}), bf16[4,1024,128]{2,1,0:T(8,128)(2,1)S(1)}, u32[]{:S(2)}, u32[]{:S(2)}) async-start(bf16[4,1024,128]{2,1,0:T(8,128)(2,1)} %bitcast.12), calls=%async_computation | async-start | bytes 2097152 | tf_op jit(solution)/shard_map/all_to_all | solution.py:120
  129.7 1.8 collective-permute-start.4
  131.5 11.2 %collective-permute-start.5 = (f32[256,262]{1,0:T(8,128)S(1)}, f32[256,262]{1,0:T(8,128)S(1)}, u32[]{:S(2)}, u32[]{:S(2)}) collective-permute-start(f32[256,262]{1,0:T(8,128)S(1)} %fusion.183), channel_id=1, source_target_pairs={{0,2},{2,0},{1,3},{3,1},{4,6},{6,4},{5,7},{7,5},{8,10},{10,8},{9,1... | collective-permute-start | bytes 804872 | tf_op jit(solution)/shard_map/ppermute | solution.py:42
  142.8 10.4 %collective-permute-start.6 = (f32[256,262]{1,0:T(8,128)S(1)}, f32[256,262]{1,0:T(8,128)S(1)}, u32[]{:S(2)}, u32[]{:S(2)}) collective-permute-start(f32[256,262]{1,0:T(8,128)S(1)} %add.191), channel_id=1, source_target_pairs={{0,4},{4,0},{8,12},{12,8},{1,5},{5,1},{9,13},{13,9},{2,6},{6,2},{1... | collective-permute-start | bytes 804872 | tf_op jit(solution)/shard_map/ppermute | solution.py:42
  153.2 18.8 %collective-permute-start.7 = (f32[256,262]{1,0:T(8,128)S(1)}, f32[256,262]{1,0:T(8,128)S(1)}, u32[]{:S(2)}, u32[]{:S(2)}) collective-permute-start(f32[256,262]{1,0:T(8,128)S(1)} %add.192), channel_id=1, source_target_pairs={{0,8},{4,12},{8,0},{12,4},{1,9},{5,13},{9,1},{13,5},{2,10},{6,14},... | collective-permute-start | bytes 804872 | tf_op jit(solution)/shard_map/ppermute | solution.py:42

commit v3 on v2

--- a/solution.py
+++ b/solution.py
@@ -42,6 +42,20 @@
             value = value + lax.ppermute(value, axis, partner)
             step *= 2
     return value
+
+
+def split_sum(value, lead, axes):
+    count = lax.axis_size(lead)
+    if count != 2 or value.shape[0] % 2:
+        return tree_sum(value, (lead,) + axes)
+    swap = [(0, 1), (1, 0)]
+    value = value + lax.ppermute(value, lead, swap)
+    half = value.shape[0] // 2
+    first = lax.axis_index(lead) == 0
+    mine = jnp.where(first, value[:half], value[half:])
+    mine = tree_sum(mine, axes)
+    other = lax.ppermute(mine, lead, swap)
+    return jnp.where(first, jnp.concatenate([mine, other]), jnp.concatenate([other, mine]))
 
 
 def kernel(spread):
@@ -147,9 +161,7 @@
         gram_step,
         (jnp.zeros((TERMS, TERMS), jnp.float32), jnp.zeros((TERMS, STRESS), jnp.float32)),
     )
-    full_rows = tree_sum(
-        jnp.concatenate([gram_part, rhs_part], axis=1), ("rep", "slab", "cols")
-    )
+    full_rows = split_sum(jnp.concatenate([gram_part, rhs_part], axis=1), "rep", ("slab", "cols"))
     gram_matrix = full_rows[:, :TERMS]
     rhs_sums = full_rows[:, TERMS:]
     column_scale = 1.0 / jnp.sqrt(jnp.diagonal(gram_matrix) / samples + epsilon)

time: 216 us -> 201 us (0.931)
  waiting for transfers between devices: 72.1 us -> 56.7 us
    ppermute x4 -> x3, waiting for transfers between devices: 40.1 us -> 21.6 us  [tree_sum(): value = value + lax.ppermute(value, axis, partner)]
    ppermute x0 -> x2, waiting for transfers between devices: none -> 3.11 us  [the longest x1 1.7 us: split_sum(): value = value + lax.ppermute(value, lead, swap)]
  transfers between devices with their start and end apart: 9 -> 10, of which waited for: 9 -> 10; matrix products, arithmetic and copies ran while one was open for 3% -> 4% of each run, Pallas kernels for 0% -> 0%
where the time goes in v3:
time: 201 us; the launch traced here: 199 us
  waiting for transfers between devices  56.7 us (28%)
  local copies, waits for them, and re-layouts  55.2 us (27%)
  matrix products  40 us (20%)
  blocking collectives  18 us (9%)
  other arithmetic  17 us (8%)
  starting transfers between devices  10.9 us (5%)
    ppermute x3, waiting for transfers between devices, tree_sum(): value = value + lax.ppermute(value, axis, partner)  21.6 us
    all_to_all x1, waiting for transfers between devices, local(): sets = lax.all_to_all(sets, 'cols', 0, 0, tiled=True)  19.9 us
    concatenate x1, local copies, waits for them, and re-layouts, extended(): array = jnp.concatenate([before, array, after], axis=dim)  18.4 us
    all_gather x1, blocking collectives, local(): misfit = lax.all_gather(misfit, 'cols', axis=1, tiled=True)  18 us
    unnamed x11, local copies, waits for them, and re-layouts  17.9 us
    dot_general x1, matrix products, local(): jnp.einsum('cpxz,zsn->cpxsn', widened, span_table, precision=lax.Precisio...  10.7 us
    dot_general x1, matrix products, local(): jnp.einsum('cpxsn,sxm->scpmn', along_span, stream_table, precision=lax.Pr...  10.1 us
    ppermute x2, waiting for transfers between devices, extended(): before = lax.ppermute(last, axis, up)  7.09 us
  transfers between devices with their start and end apart: 10, of which 10 were waited for; matrix products, arithmetic and copies ran while one was open for 4% of the time, Pallas kernels for 0%

profile of v3, /device:TPU:0, one launch (start us, length us, event | category | flops | bytes accessed | tf_op | source)
XLA Modules:
  0.0 199.2 jit_solution(14642978189339263256)
XLA Ops:
  0.6 11.5 %copy.37 = bf16[4,4,1024,256]{2,3,1,0:T(8,128)(2,1)} copy(bf16[4,4,1024,256]{3,2,1,0:T(8,128)(2,1)} %param.12) | data formatting | bytes 16777216 | tf_op args[0]
  13.3 3.0 %collective-permute-start = (bf16[4,4,1024,5]{2,3,1,0:T(8,128)(2,1)S(1)}, bf16[4,4,1024,5]{2,3,1,0:T(8,128)(2,1)S(1)}, u32[]{:S(2)}, u32[]{:S(2)}) collective-permute-start(bf16[4,4,1024,5]{2,3,1,0:T(8,128)(2,1)S(1)} %get-tuple-element.599), channel_id=1, source_target_pairs={{0,2},{2,0},{1,3},{3,1},{4,6},{6,4},{5,7},{7,5},{8,10},{10,8},{9,1... | collective-permute-start | bytes 491528 | tf_op jit(solution)/shard_map/ppermute | solution.py:27
  16.4 7.0 %collective-permute-done = bf16[4,4,1024,5]{2,3,1,0:T(8,128)(2,1)S(1)} collective-permute-done((bf16[4,4,1024,5]{2,3,1,0:T(8,128)(2,1)S(1)}, bf16[4,4,1024,5]{2,3,1,0:T(8,128)(2,1)S(1)}, u32[]{:S(2)}, u32[]{:S(2)}) %collective-permute-start) | collective-permute-done | bytes 163872 | tf_op jit(solution)/shard_map/ppermute | solution.py:27
  23.4 4.8 %collective-permute-done.1 = bf16[4,4,1024,5]{2,3,1,0:T(8,128)(2,1)S(1)} collective-permute-done((bf16[4,4,1024,5]{2,3,1,0:T(8,128)(2,1)S(1)}, bf16[4,4,1024,5]{2,3,1,0:T(8,128)(2,1)S(1)}, u32[]{:S(2)}, u32[]{:S(2)}) %collective-permute-start.1) | collective-permute-done | bytes 163872 | tf_op jit(solution)/shard_map/ppermute | solution.py:28
  28.2 5.5 %pad_maximum_fusion = bf16[4,4,1024,266]{2,3,1,0:T(8,128)(2,1)S(1)} fusion(bf16[4,4,1024,5]{2,3,1,0:T(8,128)(2,1)S(1)} %collective-permute-done.1, bf16[4,4,1024,256]{2,3,1,0:T(8,128)(2,1)} %copy.37, bf16[4,4,1024,5]{2,3,1,0:T(8,128)(2,1)S(1)} %collective-permute-done), kind=kLoop, calls=%fused_computation.37 | loop fusion | flops 26148864 | bytes 17432576 | tf_op jit(solution)/shard_map/concatenate | solution.py:29
  33.7 3.5 %copy-done = bf16[4,4,1024,266]{2,3,1,0:T(8,128)(2,1)} copy-done((bf16[4,4,1024,266]{2,3,1,0:T(8,128)(2,1)}, bf16[4,4,1024,266]{2,3,1,0:T(8,128)(2,1)S(1)}, u32[]{:S(2)}) %copy-start) | copy-done | bytes 8716312
  41.1 18.4 %concatenate.21 = bf16[4,4,1034,266]{2,3,1,0:T(8,128)(2,1)} concatenate(bf16[4,4,5,266]{2,3,1,0:T(8,128)(2,1)S(1)} %copy.42, bf16[4,4,1024,266]{2,3,1,0:T(8,128)(2,1)} %copy-done, bf16[4,4,5,266]{2,3,1,0:T(8,128)(2,1)S(1)} %copy.43), dimensions={2} | concatenate | bytes 17602816 | tf_op jit(solution)/shard_map/concatenate | solution.py:29
  59.5 10.7 %fusion.12 = f32[4,4,1034,2,64]{2,4,1,0,3:T(8,128)S(1)} fusion(bf16[4,4,1034,266]{2,3,1,0:T(8,128)(2,1)} %concatenate.21, f32[2]{0:T(128)S(1)} %get-tuple-element.603, f32[2]{0:T(128)S(1)} %get-tuple-element.604, f32[2]{0:T(128)S(1)} %get-tuple-element.605, f32[2]{0:T(128)S(1)} %get-tuple-element.606, f32[2]{0:T(128)S(1)} %get-tuple-element.607, ...), kind=kOutput, calls=%fused_computation.35 | convolution fusion | flops 6760434688 | bytes 17273316 | tf_op jit(solution)/shard_map/cpxz,zsn->cpxsn/dot_general | solution.py:112
  70.2 10.1 %fusion.55 = f32[2,4,4,256,64]{3,4,2,1,0:T(8,128)S(1)} fusion(f32[4,4,1034,2,64]{2,4,1,0,3:T(8,128)S(1)} %fusion.12, f32[2]{0:T(128)S(1)} %get-tuple-element.603, f32[2]{0:T(128)S(1)} %get-tuple-element.604, f32[2]{0:T(128)S(1)} %get-tuple-element.605, f32[2]{0:T(128)S(1)} %get-tuple-element.606, f32[2]{0:T(128)S(1)} %get-tuple-element.607, ...), kind=kOutput, calls=%fused_computation.67 | convolution fusion | flops 6520188928 | bytes 10572900 | tf_op jit(solution)/shard_map/cpxsn,sxm->scpmn/dot_general | solution.py:113
  82.2 1.5 copy.44
  85.6 5.1 %all-to-all-start = ((bf16[4,1024,128]{2,1,0:T(8,128)(2,1)}), bf16[4,1024,128]{2,1,0:T(8,128)(2,1)S(1)}, u32[]{:S(2)}, u32[]{:S(2)}) async-start(bf16[4,1024,128]{2,1,0:T(8,128)(2,1)} %bitcast.12), calls=%async_computation | async-start | bytes 2097152 | tf_op jit(solution)/shard_map/all_to_all | solution.py:134
  92.0 1.8 copy.47
  93.8 1.5 reshape_reshape.3
  97.1 19.9 %all-to-all-done = bf16[4,1024,128]{2,1,0:T(8,128)(2,1)S(1)} async-done(((bf16[4,1024,128]{2,1,0:T(8,128)(2,1)}), bf16[4,1024,128]{2,1,0:T(8,128)(2,1)S(1)}, u32[]{:S(2)}, u32[]{:S(2)}) %all-to-all-start) | async-done | bytes 1048608 | tf_op jit(solution)/shard_map/all_to_all | solution.py:134
  117.8 11.7 %while.79 = (s32[]{:T(128)}, f32[256,256]{1,0:T(8,128)S(1)}, f32[256,6]{0,1:T(8,128)S(1)}, bf16[16,128,128]{2,0,1:T(8,128)(2,1)S(1)}, bf16[16,128,128]{2,0,1:T(8...) while((s32[]{:T(128)}, f32[256,256]{1,0:T(8,128)S(1)}, ...), condition=%wide.region_1.2_spmd.clone, body=%wide.region_0.1_spmd.clone.sunk | while | flops 551816192 | bytes 8204454 | solution.py:158
  119.2 1.5 fusion.218
  122.2 1.5 fusion.218
  125.1 1.5 fusion.218
  128.0 1.5 fusion.218
  129.8 1.7 collective-permute-done.4
  131.5 1.6 collective-permute-start.5
  133.1 5.4 %collective-permute-done.5 = f32[128,262]{1,0:T(8,128)S(1)} collective-permute-done((f32[128,262]{1,0:T(8,128)S(1)}, f32[128,262]{1,0:T(8,128)S(1)}, u32[]{:S(2)}, u32[]{:S(2)}) %collective-permute-start.5) | collective-permute-done | bytes 134176 | tf_op jit(solution)/shard_map/ppermute | solution.py:42
  138.7 6.1 %collective-permute-done.6 = f32[128,262]{1,0:T(8,128)S(1)} collective-permute-done((f32[128,262]{1,0:T(8,128)S(1)}, f32[128,262]{1,0:T(8,128)S(1)}, u32[]{:S(2)}, u32[]{:S(2)}) %collective-permute-start.6) | collective-permute-done | bytes 134176 | tf_op jit(solution)/shard_map/ppermute | solution.py:42
  145.1 10.0 %collective-permute-done.7 = f32[128,262]{1,0:T(8,128)S(1)} collective-permute-done((f32[128,262]{1,0:T(8,128)S(1)}, f32[128,262]{1,0:T(8,128)S(1)}, u32[]{:S(2)}, u32[]{:S(2)}) %collective-permute-start.7) | collective-permute-done | bytes 134176 | tf_op jit(solution)/shard_map/ppermute | solution.py:42
  155.3 1.4 collective-permute-done.8
  156.8 2.3 %gather_fusion = f32[256]{0:T(256)S(1)} fusion(f32[256,256]{1,0:T(8,128)S(1)} %slice.63, s32[256]{0:T(256)S(1)} %bitcast.96), kind=kCustom, calls=%fused_computation | custom fusion | bytes 4096 | tf_op jit(solution)/shard_map/jit(diagonal)/cond/branch_0_fun/gather | solution.py:167
  159.4 12.1 %while.77 = (s32[]{:T(128)}, f32[6,256]{1,0:T(8,128)S(1)}, f32[3,6,64]{2,1,0:T(8,128)}, s32[3,6,256]{2,1,0:T(8,128)}, f32[6,256]{1,0:T(8,128)S(1)}, /*index=5*/f...) while((s32[]{:T(128)}, f32[6,256]{1,0:T(8,128)S(1)}, f32[3,6,64]{2,1,0:T(8,128)}, ...), condition=%wide.region_8.9_spmd, body=%wide.region_2.8_spmd.sunk | while | flops 9474058 | bytes 660566 | solution.py:202
  160.6 2.2 %while.80 = (s32[]{:T(128)}, f32[6,256]{1,0:T(8,128)S(1)}, f32[6,256]{1,0:T(8,128)S(1)}, f32[6,256]{1,0:T(8,128)S(1)}, f32[6]{0:T(128)S(1)}, /*index=5*/f32[6,256]{1,0:T(8,128)S(1)}, f32[256,256]{1,0:T(8,128)S(1)}, s32[]{:T(128)}) while((s32[]{:T(128)}, f32[6,256]{1,0:T(8,128)S(1)}, f32[6,256]{1,0:T(8,128)S(1)}, f32[6,256]{1,0:T(8,128)S(1)}, ...), condition=%wide.region_7.7_spmd, body=%wide.region_4.6_spmd.sunk | while | flops 4740110 | bytes 330125 | solution.py:195
  164.6 2.2 %while.80 = (s32[]{:T(128)}, f32[6,256]{1,0:T(8,128)S(1)}, f32[6,256]{1,0:T(8,128)S(1)}, f32[6,256]{1,0:T(8,128)S(1)}, f32[6]{0:T(128)S(1)}, /*index=5*/f32[6,256]{1,0:T(8,128)S(1)}, f32[256,256]{1,0:T(8,128)S(1)}, s32[]{:T(128)}) while((s32[]{:T(128)}, f32[6,256]{1,0:T(8,128)S(1)}, f32[6,256]{1,0:T(8,128)S(1)}, f32[6,256]{1,0:T(8,128)S(1)}, ...), condition=%wide.region_7.7_spmd, body=%wide.region_4.6_spmd.sunk | while | flops 4740110 | bytes 330125 | solution.py:195
  168.6 2.2 %while.80 = (s32[]{:T(128)}, f32[6,256]{1,0:T(8,128)S(1)}, f32[6,256]{1,0:T(8,128)S(1)}, f32[6,256]{1,0:T(8,128)S(1)}, f32[6]{0:T(128)S(1)}, /*index=5*/f32[6,256]{1,0:T(8,128)S(1)}, f32[256,256]{1,0:T(8,128)S(1)}, s32[]{:T(128)}) while((s32[]{:T(128)}, f32[6,256]{1,0:T(8,128)S(1)}, f32[6,256]{1,0:T(8,128)S(1)}, f32[6,256]{1,0:T(8,128)S(1)}, ...), condition=%wide.region_7.7_spmd, body=%wide.region_4.6_spmd.sunk | while | flops 4740110 | bytes 330125 | solution.py:195
  171.6 7.6 %while.78 = (s32[]{:T(128)}, bf16[6,128,128]{2,1,0:T(8,128)(2,1)S(1)}, bf16[6,128,128]{2,0,1:T(8,128)(2,1)}, bf16[16,128,128]{2,0,1:T(8,128)(2,1)S(1)}, bf16[16,...) while((s32[]{:T(128)}, ...), condition=%wide.region_10.11_spmd, body=%wide.region_9.10_spmd.sunk | while | flops 14884870 | bytes 5721247 | solution.py:225
  179.2 18.0 %all_gather.3 = bf16[6,512,128]{2,1,0:T(8,128)(2,1)S(1)} all-gather(bf16[6,128,128]{2,1,0:T(8,128)(2,1)S(1)} %get-tuple-element.439), channel_id=1, replica_groups=mesh['groups'=2,'cols'=4,'slab'=2,'rep'=2] {'cols'}, dimensions={1}, use_global_device_ids=true | all-gather | bytes 983040 | tf_op jit(solution)/shard_map/all_gather | solution.py:228
  (159 shorter events, 41.0 us)
Async XLA Ops:
  0.6 15.8 %copy-start.2 = (s32[4]{0:T(128)S(1)}, s32[4]{0:T(128)}, u32[]{:S(2)}) copy-start(s32[4]{0:T(128)} %param.14) | copy-start | bytes 52
  13.3 10.1 %collective-permute-start = (bf16[4,4,1024,5]{2,3,1,0:T(8,128)(2,1)S(1)}, bf16[4,4,1024,5]{2,3,1,0:T(8,128)(2,1)S(1)}, u32[]{:S(2)}, u32[]{:S(2)}) collective-permute-start(bf16[4,4,1024,5]{2,3,1,0:T(8,128)(2,1)S(1)} %get-tuple-element.599), channel_id=1, source_target_pairs={{0,2},{2,0},{1,3},{3,1},{4,6},{6,4},{5,7},{7,5},{8,10},{10,8},{9,1... | collective-permute-start | bytes 491528 | tf_op jit(solution)/shard_map/ppermute | solution.py:27
  16.3 11.9 %collective-permute-start.1 = (bf16[4,4,1024,5]{2,3,1,0:T(8,128)(2,1)S(1)}, bf16[4,4,1024,5]{2,3,1,0:T(8,128)(2,1)S(1)}, u32[]{:S(2)}, u32[]{:S(2)}) collective-permute-start(bf16[4,4,1024,5]{2,3,1,0:T(8,128)(2,1)S(1)} %get-tuple-element.600), channel_id=1, source_target_pairs={{2,0},{0,2},{3,1},{1,3},{6,4},{4,6},{7,5},{5,7},{10,8},{8,10},{11,... | collective-permute-start | bytes 491528 | tf_op jit(solution)/shard_map/ppermute | solution.py:28
  33.7 3.5 %copy-start = (bf16[4,4,1024,266]{2,3,1,0:T(8,128)(2,1)}, bf16[4,4,1024,266]{2,3,1,0:T(8,128)(2,1)S(1)}, u32[]{:S(2)}) copy-start(bf16[4,4,1024,266]{2,3,1,0:T(8,128)(2,1)S(1)} %pad_maximum_fusion) | copy-start | bytes 26148868
  38.4 1.3 collective-permute-start.2
  39.0 1.4 collective-permute-start.3
  84.6 6.2 %copy-start.1 = (bf16[6,4,256,64]{2,3,1,0:T(8,128)(2,1)S(1)}, bf16[6,4,256,64]{2,3,1,0:T(8,128)(2,1)}, u32[]{:S(2)}) copy-start(bf16[6,4,256,64]{2,3,1,0:T(8,128)(2,1)} %param.13) | copy-start | bytes 2359300
  85.6 31.4 %all-to-all-start = ((bf16[4,1024,128]{2,1,0:T(8,128)(2,1)}), bf16[4,1024,128]{2,1,0:T(8,128)(2,1)S(1)}, u32[]{:S(2)}, u32[]{:S(2)}) async-start(bf16[4,1024,128]{2,1,0:T(8,128)(2,1)} %bitcast.12), calls=%async_computation | async-start | bytes 2097152 | tf_op jit(solution)/shard_map/all_to_all | solution.py:134
  129.7 1.8 collective-permute-start.4
  131.5 7.0 %collective-permute-start.5 = (f32[128,262]{1,0:T(8,128)S(1)}, f32[128,262]{1,0:T(8,128)S(1)}, u32[]{:S(2)}, u32[]{:S(2)}) collective-permute-start(f32[128,262]{1,0:T(8,128)S(1)} %slice_select_fusion), channel_id=1, source_target_pairs={{0,2},{2,0},{1,3},{3,1},{4,6},{6,4},{5,7},{7,5},{8,10},{10,8},{9,1... | collective-permute-start | bytes 402440 | tf_op jit(solution)/shard_map/ppermute | solution.py:42
  138.6 6.2 %collective-permute-start.6 = (f32[128,262]{1,0:T(8,128)S(1)}, f32[128,262]{1,0:T(8,128)S(1)}, u32[]{:S(2)}, u32[]{:S(2)}) collective-permute-start(f32[128,262]{1,0:T(8,128)S(1)} %fusion.195), channel_id=1, source_target_pairs={{0,4},{4,0},{8,12},{12,8},{1,5},{5,1},{9,13},{13,9},{2,6},{6,2},{1... | collective-permute-start | bytes 402440 | tf_op jit(solution)/shard_map/ppermute | solution.py:42
  144.8 10.4 %collective-permute-start.7 = (f32[128,262]{1,0:T(8,128)S(1)}, f32[128,262]{1,0:T(8,128)S(1)}, u32[]{:S(2)}, u32[]{:S(2)}) collective-permute-start(f32[128,262]{1,0:T(8,128)S(1)} %add.192), channel_id=1, source_target_pairs={{0,8},{4,12},{8,0},{12,4},{1,9},{5,13},{9,1},{13,5},{2,10},{6,14},... | collective-permute-start | bytes 402440 | tf_op jit(solution)/shard_map/ppermute | solution.py:42
  155.2 1.5 collective-permute-start.8

commit v4 on v3

--- a/solution.py
+++ b/solution.py
@@ -58,6 +58,15 @@
     return jnp.where(first, jnp.concatenate([mine, other]), jnp.concatenate([other, mine]))
 
 
+def neighbour_edges(array, axis, dim, width):
+    count, length = (lax.axis_size(axis), array.shape[dim])
+    up = [(i, (i + 1) % count) for i in range(count)]
+    down = [(j, i) for i, j in up]
+    last = lax.slice_in_dim(array, length - width, length, axis=dim)
+    leading = lax.slice_in_dim(array, 0, width, axis=dim)
+    return (lax.ppermute(last, axis, up), lax.ppermute(leading, axis, down))
+
+
 def kernel(spread):
     offsets = np.arange(13) - 6.0
     values = np.exp(-offsets * offsets / (2.0 * spread * spread))
@@ -102,16 +111,41 @@
     samples = float(row_count * lax.axis_size("slab") * lax.axis_size("rep"))
     height = 2.0 * (planes.astype(jnp.float32) + 0.5) / NY - 1.0
     root_weight = jnp.sqrt(1.2 - height * height)
-    padded = extended(fields, (("slab", 3), ("rep", 2)), 5)
-    widened = padded.astype(jnp.float32)
+    width = 5
+    top, bottom = neighbour_edges(fields, "rep", 2, width)
     narrow_taps = kernel(1.5)
     broad_taps = kernel(3.0)
     guard = jnp.minimum(lax.axis_index("rep"), 0)
     span_table = filter_table(cells_z, narrow_taps, broad_taps, guard, (0, 1, 2))
     stream_table = filter_table(cells_x, narrow_taps, broad_taps, guard, (1, 0, 2))
-    along_span = jnp.einsum("cpxz,zsn->cpxsn", widened, span_table, precision=lax.Precision.HIGHEST)
-    filtered = jnp.einsum(
-        "cpxsn,sxm->scpmn", along_span, stream_table, precision=lax.Precision.HIGHEST
+    highest = lax.Precision.HIGHEST
+    along_stream = (
+        jnp.einsum(
+            "cpxz,sxm->scpmz",
+            fields.astype(jnp.float32),
+            stream_table[:, width : width + cells_x],
+            precision=highest,
+        )
+        + jnp.einsum(
+            "cpxz,sxm->scpmz", top.astype(jnp.float32), stream_table[:, :width], precision=highest
+        )
+        + jnp.einsum(
+            "cpxz,sxm->scpmz",
+            bottom.astype(jnp.float32),
+            stream_table[:, width + cells_x :],
+            precision=highest,
+        )
+    )
+    left, right = neighbour_edges(along_stream, "slab", 4, width)
+    filtered = (
+        jnp.einsum(
+            "scpmz,zsn->scpmn",
+            along_stream,
+            span_table[width : width + cells_z],
+            precision=highest,
+        )
+        + jnp.einsum("scpmz,zsn->scpmn", left, span_table[:width], precision=highest)
+        + jnp.einsum("scpmz,zsn->scpmn", right, span_table[width + cells_z :], precision=highest)
     )
     narrow = filtered[0]
     broader = filtered[1]

time: 201 us -> 165 us (0.82)
  local copies, waits for them, and re-layouts: 55.2 us -> 18.6 us
  matrix products: 40 us -> 52.8 us
  waiting for transfers between devices: 56.7 us -> 50.1 us
  other arithmetic: 17 us -> 13.2 us
    concatenate x1 -> x0, local copies, waits for them, and re-layouts: 18.4 us -> none  [extended(): array = jnp.concatenate([before, array, after], axis=dim)]
    unnamed x11 -> x8, local copies, waits for them, and re-layouts: 17.9 us -> 2.94 us
    dot_general x2 -> x6, matrix products: 20.8 us -> 33.6 us  [the longest x1 16 us: local(): jnp.einsum('cpxz,sxm->scpmz', fields.astype(jnp.float32), stream_table[:,...]
    ppermute x4, waiting for transfers between devices: 12 us -> 6 us  [neighbour_edges(): return (lax.ppermute(last, axis, up), lax.ppermute(leading, axis, down))]
    concatenate x1 -> x0, other arithmetic: 5.5 us -> none  [extended(): array = jnp.concatenate([before, array, after], axis=dim)]
  transfers between devices with their start and end apart: 10 -> 10, of which waited for: 10 -> 8; matrix products, arithmetic and copies ran while one was open for 4% -> 21% of each run, Pallas kernels for 0% -> 0%
where the time goes in v4:
time: 165 us; the launch traced here: 164 us
  matrix products  52.8 us (32%)
  waiting for transfers between devices  50.1 us (30%)
  local copies, waits for them, and re-layouts  18.6 us (11%)
  blocking collectives  18 us (11%)
  other arithmetic  13.2 us (8%)
  starting transfers between devices  9.69 us (6%)
    ppermute x3, waiting for transfers between devices, tree_sum(): value = value + lax.ppermute(value, axis, partner)  22.5 us
    all_to_all x1, waiting for transfers between devices, local(): sets = lax.all_to_all(sets, 'cols', 0, 0, tiled=True)  18.5 us
    all_gather x1, blocking collectives, local(): misfit = lax.all_gather(misfit, 'cols', axis=1, tiled=True)  18 us
    dot_general x1, matrix products, local(): jnp.einsum('cpxz,sxm->scpmz', fields.astype(jnp.float32), stream_table[:,...  16 us
    ppermute x4, waiting for transfers between devices, neighbour_edges(): return (lax.ppermute(last, axis, up), lax.ppermute(leading, axis, down))  6 us
    dot_general x4, matrix products, gram_step(): jnp.einsum('iqr,kqr->ik', all_terms, weighted_piece, preferred_element_ty...  5.92 us
    dot_general x1, matrix products, local(): jnp.einsum('scpmz,zsn->scpmn', along_stream, span_table[width:width + cel...  5.53 us
    dot_general x12, matrix products, apply_normal(): jnp.einsum('kl,il->ki', active * vector, normal_gram, precision=lax.Preci...  5.26 us
  transfers between devices with their start and end apart: 10, of which 8 were waited for; matrix products, arithmetic and copies ran while one was open for 21% of the time, Pallas kernels for 0%

profile of v4, /device:TPU:0, one launch (start us, length us, event | category | flops | bytes accessed | tf_op | source)
XLA Modules:
  0.0 163.9 jit_solution(15339855423883836964)
XLA Ops:
  2.2 1.5 select_select_fusion
  3.7 16.0 %fusion.12 = f32[2,256,4,4,256]{1,4,3,2,0:T(8,128)S(1)} fusion(bf16[4,4,1024,256]{3,2,1,0:T(8,128)(2,1)} %param.12, f32[2,1034,256]{2,1,0:T(8,128)S(1)} %select_select_fusion), kind=kOutput, calls=%fused_computation.35 | convolution fusion | flops 25769803776 | bytes 18874368 | tf_op jit(solution)/shard_map/cpxz,sxm->scpmz/dot_general | solution.py:123
  20.0 3.5 %fusion.45 = f32[2,256,4,4,256]{1,4,3,2,0:T(8,128)S(1)} fusion(bf16[4,4,5,256]{3,2,1,0:T(8,128)(2,1)S(1)} %collective-permute-done, f32[2,1034,256]{2,1,0:T(8,128)S(1)} %select_select_fusion), kind=kOutput, calls=%fused_computation.88 | convolution fusion | flops 125829120 | bytes 8470528 | tf_op jit(solution)/shard_map/cpxz,sxm->scpmz/dot_general | solution.py:129
  23.5 4.4 %add_bitcast_fusion = f32[2,4,4,256,256]{3,4,2,1,0:T(8,128)S(1)} fusion(f32[2,256,4,4,256]{1,4,3,2,0:T(8,128)S(1)} %fusion.12, f32[2,256,4,4,256]{1,4,3,2,0:T(8,128)S(1)} %fusion.45, bf16[4,4,5,256]{3,2,1,0:T(8,128)(2,1)S(1)} %collective-permute-done.1, f32[2,1034,256]{2,1,0:T(8,128)S(1)} %select_select_fusion), kind=kOutput, calls=%fused_computation.37 | convolution fusion | flops 130023424 | bytes 25247744 | tf_op jit(solution)/shard_map/cpxz,sxm->scpmz/dot_general | solution.py:132
  28.0 3.0 %collective-permute-start.2 = (f32[2,4,4,256,5]{3,4,2,1,0:T(8,128)S(1)}, f32[2,4,4,256,5]{3,4,2,1,0:T(8,128)S(1)}, u32[]{:S(2)}, u32[]{:S(2)}) collective-permute-start(f32[2,4,4,256,5]{3,4,2,1,0:T(8,128)S(1)} %get-tuple-element.598), channel_id=1, source_target_pairs={{0,2},{2,0},{1,3},{3,1},{4,6},{6,4},{5,7},{7,5},{8,10},{10,8},{9,1... | collective-permute-start | bytes 491528 | tf_op jit(solution)/shard_map/ppermute | solution.py:67
  30.9 5.5 %fusion.42 = f32[2,4,4,256,64]{3,4,2,1,0:T(8,128)S(1)} fusion(f32[2,4,4,256,256]{3,4,2,1,0:T(8,128)S(1)} %add_bitcast_fusion, f32[266,2,64]{0,2,1:T(8,128)S(1)} %select_select_fusion.1), kind=kOutput, calls=%fused_computation.83 | convolution fusion | flops 1610612736 | bytes 10616832 | tf_op jit(solution)/shard_map/scpmz,zsn->scpmn/dot_general | solution.py:141
  37.5 2.0 %fusion.43 = f32[2,4,4,256,64]{3,4,2,1,0:T(8,128)S(1)} fusion(f32[2,4,4,256,5]{3,4,2,1,0:T(8,128)S(1)} %collective-permute-done.2, f32[266,2,64]{0,2,1:T(8,128)S(1)} %select_select_fusion.1), kind=kOutput, calls=%fused_computation.86 | convolution fusion | flops 31457280 | bytes 2424832 | tf_op jit(solution)/shard_map/scpmz,zsn->scpmn/dot_general | solution.py:147
  39.5 5.0 %collective-permute-done.3 = f32[2,4,4,256,5]{3,4,2,1,0:T(8,128)S(1)} collective-permute-done((f32[2,4,4,256,5]{3,4,2,1,0:T(8,128)S(1)}, f32[2,4,4,256,5]{3,4,2,1,0:T(8,128)S(1)}, u32[]{:S(2)}, u32[]{:S(2)}) %collective-permute-start.3) | collective-permute-done | bytes 163872 | tf_op jit(solution)/shard_map/ppermute | solution.py:67
  44.6 2.1 %add_add_fusion = f32[2,4,4,256,64]{3,4,2,1,0:T(8,128)S(1)} fusion(f32[2,4,4,256,64]{3,4,2,1,0:T(8,128)S(1)} %fusion.42, f32[2,4,4,256,64]{3,4,2,1,0:T(8,128)S(1)} %fusion.43, f32[2,4,4,256,5]{3,4,2,1,0:T(8,128)S(1)} %collective-permute-done.3, f32[266,2,64]{0,2,1:T(8,128)S(1)} %select_select_fusion.1), kind=kOutput, calls=%fused_computation.54 | convolution fusion | flops 32505856 | bytes 6619136 | tf_op jit(solution)/shard_map/scpmz,zsn->scpmn/dot_general | solution.py:148
  48.6 1.5 copy.50
  52.0 4.9 %all-to-all-start = ((bf16[4,1024,128]{2,1,0:T(8,128)(2,1)}), bf16[4,1024,128]{2,1,0:T(8,128)(2,1)S(1)}, u32[]{:S(2)}, u32[]{:S(2)}) async-start(bf16[4,1024,128]{2,1,0:T(8,128)(2,1)} %bitcast.20), calls=%async_computation | async-start | bytes 2097152 | tf_op jit(solution)/shard_map/all_to_all | solution.py:168
  58.1 1.8 %copy.53 = bf16[6,4,256,64]{3,2,1,0:T(8,128)(2,1)S(1)} copy(bf16[6,4,256,64]{2,3,1,0:T(8,128)(2,1)} %multiply_convert_fusion.2) | data formatting | bytes 1572864 | tf_op jit(solution)/shard_map/convert_element_type | solution.py:158
  59.9 1.5 reshape_reshape.3
  63.2 18.5 %all-to-all-done = bf16[4,1024,128]{2,1,0:T(8,128)(2,1)S(1)} async-done(((bf16[4,1024,128]{2,1,0:T(8,128)(2,1)}), bf16[4,1024,128]{2,1,0:T(8,128)(2,1)S(1)}, u32[]{:S(2)}, u32[]{:S(2)}) %all-to-all-start) | async-done | bytes 1048608 | tf_op jit(solution)/shard_map/all_to_all | solution.py:168
  82.5 11.7 %while.79 = (s32[]{:T(128)}, f32[256,256]{1,0:T(8,128)S(1)}, f32[256,6]{0,1:T(8,128)S(1)}, bf16[16,128,128]{2,0,1:T(8,128)(2,1)S(1)}, bf16[16,128,128]{2,0,1:T(8...) while((s32[]{:T(128)}, f32[256,256]{1,0:T(8,128)S(1)}, ...), condition=%wide.region_1.2_spmd.clone, body=%wide.region_0.1_spmd.clone.sunk | while | flops 551816192 | bytes 8204454 | solution.py:192
  83.9 1.5 fusion.91
  86.8 1.5 fusion.91
  89.8 1.5 fusion.91
  92.7 1.5 fusion.91
  94.4 1.7 %collective-permute-done.4 = f32[256,262]{1,0:T(8,128)S(1)} collective-permute-done((f32[256,262]{1,0:T(8,128)S(1)}, f32[256,262]{1,0:T(8,128)S(1)}, u32[]{:S(2)}, u32[]{:S(2)}) %collective-permute-start.4) | collective-permute-done | bytes 268320 | tf_op jit(solution)/shard_map/ppermute | solution.py:52
  96.9 6.4 %collective-permute-done.5 = f32[128,262]{1,0:T(8,128)S(1)} collective-permute-done((f32[128,262]{1,0:T(8,128)S(1)}, f32[128,262]{1,0:T(8,128)S(1)}, u32[]{:S(2)}, u32[]{:S(2)}) %collective-permute-start.5) | collective-permute-done | bytes 134176 | tf_op jit(solution)/shard_map/ppermute | solution.py:42
  103.3 6.1 %collective-permute-done.6 = f32[128,262]{1,0:T(8,128)S(1)} collective-permute-done((f32[128,262]{1,0:T(8,128)S(1)}, f32[128,262]{1,0:T(8,128)S(1)}, u32[]{:S(2)}, u32[]{:S(2)}) %collective-permute-start.6) | collective-permute-done | bytes 134176 | tf_op jit(solution)/shard_map/ppermute | solution.py:42
  109.8 10.0 %collective-permute-done.7 = f32[128,262]{1,0:T(8,128)S(1)} collective-permute-done((f32[128,262]{1,0:T(8,128)S(1)}, f32[128,262]{1,0:T(8,128)S(1)}, u32[]{:S(2)}, u32[]{:S(2)}) %collective-permute-start.7) | collective-permute-done | bytes 134176 | tf_op jit(solution)/shard_map/ppermute | solution.py:42
  120.0 1.4 collective-permute-done.8
  121.5 2.3 %gather_fusion = f32[256]{0:T(256)S(1)} fusion(f32[256,256]{1,0:T(8,128)S(1)} %slice.91, s32[256]{0:T(256)S(1)} %bitcast.122), kind=kCustom, calls=%fused_computation | custom fusion | bytes 4096 | tf_op jit(solution)/shard_map/jit(diagonal)/cond/branch_0_fun/gather | solution.py:201
  124.1 12.1 %while.77 = (s32[]{:T(128)}, f32[6,256]{1,0:T(8,128)S(1)}, f32[3,6,64]{2,1,0:T(8,128)}, s32[3,6,256]{2,1,0:T(8,128)}, f32[6,256]{1,0:T(8,128)S(1)}, /*index=5*/f...) while((s32[]{:T(128)}, f32[6,256]{1,0:T(8,128)S(1)}, f32[3,6,64]{2,1,0:T(8,128)}, ...), condition=%wide.region_8.9_spmd, body=%wide.region_2.8_spmd.sunk | while | flops 9474058 | bytes 660566 | solution.py:236
  125.3 2.2 %while.80 = (s32[]{:T(128)}, f32[6,256]{1,0:T(8,128)S(1)}, f32[6,256]{1,0:T(8,128)S(1)}, f32[6,256]{1,0:T(8,128)S(1)}, f32[6]{0:T(128)S(1)}, /*index=5*/f32[6,256]{1,0:T(8,128)S(1)}, f32[256,256]{1,0:T(8,128)S(1)}, s32[]{:T(128)}) while((s32[]{:T(128)}, f32[6,256]{1,0:T(8,128)S(1)}, f32[6,256]{1,0:T(8,128)S(1)}, f32[6,256]{1,0:T(8,128)S(1)}, ...), condition=%wide.region_7.7_spmd, body=%wide.region_4.6_spmd.sunk | while | flops 4740110 | bytes 330125 | solution.py:229
  129.3 2.2 %while.80 = (s32[]{:T(128)}, f32[6,256]{1,0:T(8,128)S(1)}, f32[6,256]{1,0:T(8,128)S(1)}, f32[6,256]{1,0:T(8,128)S(1)}, f32[6]{0:T(128)S(1)}, /*index=5*/f32[6,256]{1,0:T(8,128)S(1)}, f32[256,256]{1,0:T(8,128)S(1)}, s32[]{:T(128)}) while((s32[]{:T(128)}, f32[6,256]{1,0:T(8,128)S(1)}, f32[6,256]{1,0:T(8,128)S(1)}, f32[6,256]{1,0:T(8,128)S(1)}, ...), condition=%wide.region_7.7_spmd, body=%wide.region_4.6_spmd.sunk | while | flops 4740110 | bytes 330125 | solution.py:229
  133.3 2.2 %while.80 = (s32[]{:T(128)}, f32[6,256]{1,0:T(8,128)S(1)}, f32[6,256]{1,0:T(8,128)S(1)}, f32[6,256]{1,0:T(8,128)S(1)}, f32[6]{0:T(128)S(1)}, /*index=5*/f32[6,256]{1,0:T(8,128)S(1)}, f32[256,256]{1,0:T(8,128)S(1)}, s32[]{:T(128)}) while((s32[]{:T(128)}, f32[6,256]{1,0:T(8,128)S(1)}, f32[6,256]{1,0:T(8,128)S(1)}, f32[6,256]{1,0:T(8,128)S(1)}, ...), condition=%wide.region_7.7_spmd, body=%wide.region_4.6_spmd.sunk | while | flops 4740110 | bytes 330125 | solution.py:229
  136.3 7.6 %while.78 = (s32[]{:T(128)}, bf16[6,128,128]{2,1,0:T(8,128)(2,1)S(1)}, bf16[6,128,128]{2,0,1:T(8,128)(2,1)}, bf16[16,128,128]{2,0,1:T(8,128)(2,1)S(1)}, bf16[16,...) while((s32[]{:T(128)}, ...), condition=%wide.region_10.11_spmd, body=%wide.region_9.10_spmd.sunk | while | flops 14884870 | bytes 5721247 | solution.py:259
  143.9 18.0 %all_gather.3 = bf16[6,512,128]{2,1,0:T(8,128)(2,1)S(1)} all-gather(bf16[6,128,128]{2,1,0:T(8,128)(2,1)S(1)} %get-tuple-element.439), channel_id=1, replica_groups=mesh['groups'=2,'cols'=4,'slab'=2,'rep'=2] {'cols'}, dimensions={1}, use_global_device_ids=true | all-gather | bytes 983040 | tf_op jit(solution)/shard_map/all_gather | solution.py:262
  162.5 1.4 copy.63
  (156 shorter events, 37.9 us)
Async XLA Ops:
  1.5 18.5 %collective-permute-start = (bf16[4,4,5,256]{3,2,1,0:T(8,128)(2,1)S(1)}, bf16[4,4,5,256]{3,2,1,0:T(8,128)(2,1)S(1)}, u32[]{:S(2)}, u32[]{:S(2)}) collective-permute-start(bf16[4,4,5,256]{3,2,1,0:T(8,128)(2,1)S(1)} %get-tuple-element.600), channel_id=1, source_target_pairs={{0,1},{1,0},{2,3},{3,2},{4,5},{5,4},{6,7},{7,6},{8,9},{9,8},{10,11... | collective-permute-start | bytes 122888 | tf_op jit(solution)/shard_map/ppermute | solution.py:67
  2.0 21.5 %collective-permute-start.1 = (bf16[4,4,5,256]{3,2,1,0:T(8,128)(2,1)S(1)}, bf16[4,4,5,256]{3,2,1,0:T(8,128)(2,1)S(1)}, u32[]{:S(2)}, u32[]{:S(2)}) collective-permute-start(bf16[4,4,5,256]{3,2,1,0:T(8,128)(2,1)S(1)} %get-tuple-element.599), channel_id=1, source_target_pairs={{1,0},{0,1},{3,2},{2,3},{5,4},{4,5},{7,6},{6,7},{9,8},{8,9},{11,10... | collective-permute-start | bytes 122888 | tf_op jit(solution)/shard_map/ppermute | solution.py:67
  3.7 16.3 %copy-start.1 = (s32[4]{0:T(128)S(1)}, s32[4]{0:T(128)}, u32[]{:S(2)}) copy-start(s32[4]{0:T(128)} %param.14) | copy-start | bytes 52
  28.0 9.5 %collective-permute-start.2 = (f32[2,4,4,256,5]{3,4,2,1,0:T(8,128)S(1)}, f32[2,4,4,256,5]{3,4,2,1,0:T(8,128)S(1)}, u32[]{:S(2)}, u32[]{:S(2)}) collective-permute-start(f32[2,4,4,256,5]{3,4,2,1,0:T(8,128)S(1)} %get-tuple-element.598), channel_id=1, source_target_pairs={{0,2},{2,0},{1,3},{3,1},{4,6},{6,4},{5,7},{7,5},{8,10},{10,8},{9,1... | collective-permute-start | bytes 491528 | tf_op jit(solution)/shard_map/ppermute | solution.py:67
  36.5 8.1 %collective-permute-start.3 = (f32[2,4,4,256,5]{3,4,2,1,0:T(8,128)S(1)}, f32[2,4,4,256,5]{3,4,2,1,0:T(8,128)S(1)}, u32[]{:S(2)}, u32[]{:S(2)}) collective-permute-start(f32[2,4,4,256,5]{3,4,2,1,0:T(8,128)S(1)} %get-tuple-element.597), channel_id=1, source_target_pairs={{2,0},{0,2},{3,1},{1,3},{6,4},{4,6},{7,5},{5,7},{10,8},{8,10},{11,... | collective-permute-start | bytes 491528 | tf_op jit(solution)/shard_map/ppermute | solution.py:67
  50.9 6.0 %copy-start = (bf16[6,4,256,64]{2,3,1,0:T(8,128)(2,1)S(1)}, bf16[6,4,256,64]{2,3,1,0:T(8,128)(2,1)}, u32[]{:S(2)}) copy-start(bf16[6,4,256,64]{2,3,1,0:T(8,128)(2,1)} %param.13) | copy-start | bytes 2359300
  52.0 29.7 %all-to-all-start = ((bf16[4,1024,128]{2,1,0:T(8,128)(2,1)}), bf16[4,1024,128]{2,1,0:T(8,128)(2,1)S(1)}, u32[]{:S(2)}, u32[]{:S(2)}) async-start(bf16[4,1024,128]{2,1,0:T(8,128)(2,1)} %bitcast.20), calls=%async_computation | async-start | bytes 2097152 | tf_op jit(solution)/shard_map/all_to_all | solution.py:168
  94.4 1.8 %collective-permute-start.4 = (f32[256,262]{1,0:T(8,128)S(1)}, f32[256,262]{1,0:T(8,128)S(1)}, u32[]{:S(2)}, u32[]{:S(2)}) collective-permute-start(f32[256,262]{1,0:T(8,128)S(1)} %pad_maximum_fusion), channel_id=1, source_target_pairs={{0,1},{1,0},{2,3},{3,2},{4,5},{5,4},{6,7},{7,6},{8,9},{9,8},{10,11... | collective-permute-start | bytes 804872 | tf_op jit(solution)/shard_map/ppermute | solution.py:52
  96.2 7.0 %collective-permute-start.5 = (f32[128,262]{1,0:T(8,128)S(1)}, f32[128,262]{1,0:T(8,128)S(1)}, u32[]{:S(2)}, u32[]{:S(2)}) collective-permute-start(f32[128,262]{1,0:T(8,128)S(1)} %slice_select_fusion), channel_id=1, source_target_pairs={{0,2},{2,0},{1,3},{3,1},{4,6},{6,4},{5,7},{7,5},{8,10},{10,8},{9,1... | collective-permute-start | bytes 402440 | tf_op jit(solution)/shard_map/ppermute | solution.py:42
  103.3 6.2 %collective-permute-start.6 = (f32[128,262]{1,0:T(8,128)S(1)}, f32[128,262]{1,0:T(8,128)S(1)}, u32[]{:S(2)}, u32[]{:S(2)}) collective-permute-start(f32[128,262]{1,0:T(8,128)S(1)} %fusion.68), channel_id=1, source_target_pairs={{0,4},{4,0},{8,12},{12,8},{1,5},{5,1},{9,13},{13,9},{2,6},{6,2},{1... | collective-permute-start | bytes 402440 | tf_op jit(solution)/shard_map/ppermute | solution.py:42
  109.5 10.4 %collective-permute-start.7 = (f32[128,262]{1,0:T(8,128)S(1)}, f32[128,262]{1,0:T(8,128)S(1)}, u32[]{:S(2)}, u32[]{:S(2)}) collective-permute-start(f32[128,262]{1,0:T(8,128)S(1)} %add.213), channel_id=1, source_target_pairs={{0,8},{4,12},{8,0},{12,4},{1,9},{5,13},{9,1},{13,5},{2,10},{6,14},... | collective-permute-start | bytes 402440 | tf_op jit(solution)/shard_map/ppermute | solution.py:42
  119.9 1.5 collective-permute-start.8

commit v5 on v4

--- a/solution.py
+++ b/solution.py
@@ -2,6 +2,7 @@
 
 import jax
 import jax.numpy as jnp
+import ml_dtypes
 import numpy as np
 from jax import lax
 from jax.sharding import PartitionSpec as P
@@ -65,6 +66,12 @@
     last = lax.slice_in_dim(array, length - width, length, axis=dim)
     leading = lax.slice_in_dim(array, 0, width, axis=dim)
     return (lax.ppermute(last, axis, up), lax.ppermute(leading, axis, down))
+
+
+def split_taps(taps):
+    high = np.asarray(np.float32(taps), dtype=ml_dtypes.bfloat16)
+    rest = np.float32(taps) - high.astype(np.float32)
+    return (high.astype(np.float32), np.asarray(rest, dtype=ml_dtypes.bfloat16).astype(np.float32))
 
 
 def kernel(spread):
@@ -117,25 +124,20 @@
     broad_taps = kernel(3.0)
     guard = jnp.minimum(lax.axis_index("rep"), 0)
     span_table = filter_table(cells_z, narrow_taps, broad_taps, guard, (0, 1, 2))
-    stream_table = filter_table(cells_x, narrow_taps, broad_taps, guard, (1, 0, 2))
     highest = lax.Precision.HIGHEST
-    along_stream = (
-        jnp.einsum(
-            "cpxz,sxm->scpmz",
-            fields.astype(jnp.float32),
-            stream_table[:, width : width + cells_x],
-            precision=highest,
-        )
-        + jnp.einsum(
-            "cpxz,sxm->scpmz", top.astype(jnp.float32), stream_table[:, :width], precision=highest
-        )
-        + jnp.einsum(
-            "cpxz,sxm->scpmz",
-            bottom.astype(jnp.float32),
-            stream_table[:, width + cells_x :],
-            precision=highest,
-        )
-    )
+    stream_pieces = [
+        filter_table(cells_x, first, second, guard, (1, 0, 2)).astype(jnp.bfloat16)
+        for first, second in zip(split_taps(narrow_taps), split_taps(broad_taps))
+    ]
+    stream_input = (top, fields, bottom)
+    stream_bounds = (0, width, width + cells_x, 2 * width + cells_x)
+    along_stream = None
+    for piece in stream_pieces:
+        for part, low, high in zip(stream_input, stream_bounds[:-1], stream_bounds[1:]):
+            term = jnp.einsum(
+                "cpxz,sxm->scpmz", part, piece[:, low:high], preferred_element_type=jnp.float32
+            )
+            along_stream = term if along_stream is None else along_stream + term
     left, right = neighbour_edges(along_stream, "slab", 4, width)
     filtered = (
         jnp.einsum(
@@ -259,7 +261,15 @@
     misfit = lax.fori_loop(
         0, block_count, misfit_step, jnp.zeros((STRESS, chunk_rows, lanes), jnp.bfloat16)
     )
-    misfit = lax.all_gather(misfit, "cols", axis=1, tiled=True)
+    pieces = [misfit] + [
+        lax.ppermute(misfit, "cols", [(i, (i - k) % col_devices) for i in range(col_devices)])
+        for k in range(1, col_devices)
+    ]
+    doubled = jnp.stack(pieces + pieces)
+    misfit = lax.dynamic_slice_in_dim(
+        doubled, (col_devices - column_index) % col_devices, col_devices, 0
+    )
+    misfit = jnp.moveaxis(misfit, 0, 1).reshape(STRESS, col_devices * chunk_rows, lanes)
     misfit = misfit.reshape(STRESS, plane_count, coarse_x, coarse_z)
     return (coefficients, misfit)
 

time: 165 us -> 196 us (1.19)
  matrix products: 52.8 us -> 75.4 us
  waiting for transfers between devices: 50.1 us -> 68.5 us
  blocking collectives: 18 us -> 0 us
  starting transfers between devices: 9.69 us -> 13.6 us
  other arithmetic: 13.2 us -> 15.5 us
    dot_general x3 -> x6, matrix products: 23.9 us -> 51 us  [local(): jnp.einsum('cpxz,sxm->scpmz', part, piece[:, low:high], preferred_element...]
    all_gather x1 -> x0, blocking collectives: 18 us -> none  [local(): misfit = lax.all_gather(misfit, 'cols', axis=1, tiled=True)]
    ppermute x0 -> x3, waiting for transfers between devices: none -> 17.5 us  [local(): lax.ppermute(misfit, 'cols', [(i, (i - k) % col_devices) for i in range(c...]
    ppermute x0 -> x3, starting transfers between devices: none -> 3.86 us  [local(): lax.ppermute(misfit, 'cols', [(i, (i - k) % col_devices) for i in range(c...]
    dot_general x4, matrix products: 5.92 us -> 2.56 us  [gram_step(): jnp.einsum('iqr,kqr->ik', all_terms, weighted_piece, preferred_element_ty...]
    dot_general x4, matrix products: 4.92 us -> 1.6 us  [misfit_step(): jnp.einsum('ki,iqr->kqr', final_weights, all_terms, preferred_element_typ...]
    convert_element_type x0 -> x1, other arithmetic: none -> 2.7 us  [local(): filter_table(cells_x, first, second, guard, (1, 0, 2)).astype(jnp.bfloat16)]
    dot_general x1, matrix products: 5.53 us -> 7.84 us  [local(): jnp.einsum('scpmz,zsn->scpmn', along_stream, span_table[width:width + cel...]
  transfers between devices with their start and end apart: 10 -> 13, of which waited for: 8 -> 9; matrix products, arithmetic and copies ran while one was open for 21% -> 24% of each run, Pallas kernels for 0% -> 0%
where the time goes in v5:
time: 196 us; the launch traced here: 193 us
  matrix products  75.4 us (38%)
  waiting for transfers between devices  68.5 us (35%)
  local copies, waits for them, and re-layouts  18.4 us (9%)
  other arithmetic  15.5 us (8%)
  starting transfers between devices  13.6 us (7%)
    dot_general x6, matrix products, local(): jnp.einsum('cpxz,sxm->scpmz', part, piece[:, low:high], preferred_element...  51 us
    ppermute x3, waiting for transfers between devices, tree_sum(): value = value + lax.ppermute(value, axis, partner)  22.5 us
    all_to_all x1, waiting for transfers between devices, local(): sets = lax.all_to_all(sets, 'cols', 0, 0, tiled=True)  19.2 us
    ppermute x3, waiting for transfers between devices, local(): lax.ppermute(misfit, 'cols', [(i, (i - k) % col_devices) for i in range(c...  17.5 us
    dot_general x1, matrix products, local(): jnp.einsum('scpmz,zsn->scpmn', along_stream, span_table[width:width + cel...  7.84 us
    ppermute x4, waiting for transfers between devices, neighbour_edges(): return (lax.ppermute(last, axis, up), lax.ppermute(leading, axis, down))  6.2 us
    dot_general x12, matrix products, apply_normal(): jnp.einsum('kl,il->ki', active * vector, normal_gram, precision=lax.Preci...  5.19 us
    all_to_all x1, starting transfers between devices, local(): sets = lax.all_to_all(sets, 'cols', 0, 0, tiled=True)  4.87 us
  transfers between devices with their start and end apart: 13, of which 9 were waited for; matrix products, arithmetic and copies ran while one was open for 24% of the time, Pallas kernels for 0%

profile of v5, /device:TPU:0, one launch (start us, length us, event | category | flops | bytes accessed | tf_op | source)
XLA Modules:
  0.0 193.0 jit_solution(11237401684603301521)
XLA Ops:
  2.3 2.7 %select_convert_fusion.1 = (bf16[2,1034,256]{2,1,0:T(8,128)(2,1)S(1)}, bf16[2,1034,256]{2,1,0:T(8,128)(2,1)S(1)}) fusion(bf16[2]{0:T(256)(128)(2,1)S(1)} %get-tuple-element.597, bf16[2]{0:T(256)(128)(2,1)S(1)} %get-tuple-element.598, bf16[2]{0:T(256)(128)(2,1)S(1)} %get-tuple-element.599, bf16[2]{0:T(256)(128)(2,1)S(1)} %get-tuple-element.600, ...), kind=kLoop, calls=%fused_computation.41 | loop fusion | flops 21705728 | bytes 2122852 | tf_op jit(solution)/shard_map/convert_element_type | solution.py:129
  5.0 12.4 %fusion.15 = f32[2,256,4,4,256]{1,4,3,2,0:T(8,128)} fusion(bf16[4,4,1024,256]{3,2,1,0:T(8,128)(2,1)} %param.12, bf16[2,1034,256]{2,1,0:T(8,128)(2,1)S(1)} %get-tuple-element.582), kind=kOutput, calls=%fused_computation.37 | convolution fusion | flops 4294967296 | bytes 17825792 | tf_op jit(solution)/shard_map/cpxz,sxm->scpmz/dot_general | solution.py:137
  17.4 6.9 %fusion.13 = f32[2,256,4,4,256]{1,4,3,2,0:T(8,128)} fusion(bf16[4,4,1024,256]{3,2,1,0:T(8,128)(2,1)S(1)} %bitcast.167, bf16[2,1034,256]{2,1,0:T(8,128)(2,1)S(1)} %get-tuple-element.583), kind=kOutput, calls=%fused_computation.35 | convolution fusion | flops 4294967296 | bytes 17825792 | tf_op jit(solution)/shard_map/cpxz,sxm->scpmz/dot_general | solution.py:137
  24.6 4.5 %fusion.52 = f32[2,256,4,4,256]{1,4,3,2,0:T(8,128)} fusion(bf16[4,4,5,256]{3,2,1,0:T(8,128)(2,1)S(1)} %collective-permute-done, bf16[2,1034,256]{2,1,0:T(8,128)(2,1)S(1)} %get-tuple-element.582), kind=kOutput, calls=%fused_computation.105 | convolution fusion | flops 20971520 | bytes 8462336 | tf_op jit(solution)/shard_map/cpxz,sxm->scpmz/dot_general | solution.py:137
  29.1 4.6 %fusion.50 = f32[2,256,4,4,256]{1,4,3,2,0:T(8,128)} fusion(bf16[4,4,5,256]{3,2,1,0:T(8,128)(2,1)S(1)} %collective-permute-done, bf16[2,1034,256]{2,1,0:T(8,128)(2,1)S(1)} %get-tuple-element.583), kind=kOutput, calls=%fused_computation.103 | convolution fusion | flops 20971520 | bytes 8462336 | tf_op jit(solution)/shard_map/cpxz,sxm->scpmz/dot_general | solution.py:137
  33.6 4.6 %fusion.48 = f32[2,256,4,4,256]{1,4,3,2,0:T(8,128)} fusion(bf16[4,4,5,256]{3,2,1,0:T(8,128)(2,1)S(1)} %collective-permute-done.1, bf16[2,1034,256]{2,1,0:T(8,128)(2,1)S(1)} %get-tuple-element.582), kind=kOutput, calls=%fused_computation.101 | convolution fusion | flops 20971520 | bytes 8462336 | tf_op jit(solution)/shard_map/cpxz,sxm->scpmz/dot_general | solution.py:137
  38.2 18.1 %add_bitcast_fusion = f32[2,4,4,256,256]{3,4,2,1,0:T(8,128)} fusion(f32[2,256,4,4,256]{1,4,3,2,0:T(8,128)} %fusion.13, f32[2,256,4,4,256]{1,4,3,2,0:T(8,128)} %fusion.50, f32[2,256,4,4,256]{1,4,3,2,0:T(8,128)} %fusion.48, f32[2,256,4,4,256]{1,4,3,2,0:T(8,128)} %fusion.52, f32[2,256,4,4,256]{1,4,3,2,0:T(8,128)} %fusion.15, ...), kind=kOutput, calls=%fused_computation.39 | convolution fusion | flops 31457280 | bytes 50405376 | tf_op jit(solution)/shard_map/cpxz,sxm->scpmz/dot_general | solution.py:137
  57.4 3.0 %collective-permute-start.2 = (f32[2,4,4,256,5]{3,4,2,1,0:T(8,128)S(1)}, f32[2,4,4,256,5]{3,4,2,1,0:T(8,128)S(1)}, u32[]{:S(2)}, u32[]{:S(2)}) collective-permute-start(f32[2,4,4,256,5]{3,4,2,1,0:T(8,128)S(1)} %get-tuple-element.577), channel_id=1, source_target_pairs={{0,2},{2,0},{1,3},{3,1},{4,6},{6,4},{5,7},{7,5},{8,10},{10,8},{9,1... | collective-permute-start | bytes 491528 | tf_op jit(solution)/shard_map/ppermute | solution.py:68
  60.4 7.8 %fusion.45 = f32[2,4,4,256,64]{3,4,2,1,0:T(8,128)S(1)} fusion(f32[2,4,4,256,256]{3,4,2,1,0:T(8,128)} %add_bitcast_fusion, f32[266,2,64]{0,2,1:T(8,128)S(1)} %select_select_fusion), kind=kOutput, calls=%fused_computation.96 | convolution fusion | flops 1610612736 | bytes 10616832 | tf_op jit(solution)/shard_map/scpmz,zsn->scpmn/dot_general | solution.py:143
  68.4 1.8 fusion.46
  70.1 6.2 %collective-permute-done.3 = f32[2,4,4,256,5]{3,4,2,1,0:T(8,128)S(1)} collective-permute-done((f32[2,4,4,256,5]{3,4,2,1,0:T(8,128)S(1)}, f32[2,4,4,256,5]{3,4,2,1,0:T(8,128)S(1)}, u32[]{:S(2)}, u32[]{:S(2)}) %collective-permute-start.3) | collective-permute-done | bytes 163872 | tf_op jit(solution)/shard_map/ppermute | solution.py:68
  76.3 2.1 %add_add_fusion = f32[2,4,4,256,64]{3,4,2,1,0:T(8,128)S(1)} fusion(f32[2,4,4,256,64]{3,4,2,1,0:T(8,128)S(1)} %fusion.45, f32[2,4,4,256,64]{3,4,2,1,0:T(8,128)S(1)} %fusion.46, f32[2,4,4,256,5]{3,4,2,1,0:T(8,128)S(1)} %collective-permute-done.3, f32[266,2,64]{0,2,1:T(8,128)S(1)} %select_select_fusion), kind=kOutput, calls=%fused_computation.56 | convolution fusion | flops 32505856 | bytes 6619136 | tf_op jit(solution)/shard_map/scpmz,zsn->scpmn/dot_general | solution.py:150
  83.8 4.9 %all-to-all-start = ((bf16[4,1024,128]{2,1,0:T(8,128)(2,1)}), bf16[4,1024,128]{2,1,0:T(8,128)(2,1)S(1)}, u32[]{:S(2)}, u32[]{:S(2)}) async-start(bf16[4,1024,128]{2,1,0:T(8,128)(2,1)} %bitcast.27), calls=%async_computation | async-start | bytes 2097152 | tf_op jit(solution)/shard_map/all_to_all | solution.py:170
  89.9 1.8 copy.38
  91.7 1.5 reshape_reshape.6
  94.2 19.2 %all-to-all-done = bf16[4,1024,128]{2,1,0:T(8,128)(2,1)S(1)} async-done(((bf16[4,1024,128]{2,1,0:T(8,128)(2,1)}), bf16[4,1024,128]{2,1,0:T(8,128)(2,1)S(1)}, u32[]{:S(2)}, u32[]{:S(2)}) %all-to-all-start) | async-done | bytes 1048608 | tf_op jit(solution)/shard_map/all_to_all | solution.py:170
  114.2 8.4 %while.79 = (s32[]{:T(128)}, f32[256,256]{1,0:T(8,128)S(1)}, f32[256,6]{0,1:T(8,128)S(1)}, bf16[16,128,128]{2,0,1:T(8,128)(2,1)S(1)}, bf16[16,128,128]{2,0,1:T(8...) while((s32[]{:T(128)}, f32[256,256]{1,0:T(8,128)S(1)}, ...), condition=%wide.region_1.2_spmd.clone, body=%wide.region_0.1_spmd.clone.sunk | while | flops 551816192 | bytes 8206510 | solution.py:194
  122.9 1.7 collective-permute-done.4
  125.3 6.4 %collective-permute-done.5 = f32[128,262]{1,0:T(8,128)S(1)} collective-permute-done((f32[128,262]{1,0:T(8,128)S(1)}, f32[128,262]{1,0:T(8,128)S(1)}, u32[]{:S(2)}, u32[]{:S(2)}) %collective-permute-start.5) | collective-permute-done | bytes 134176 | tf_op jit(solution)/shard_map/ppermute | solution.py:43
  131.8 6.1 %collective-permute-done.6 = f32[128,262]{1,0:T(8,128)S(1)} collective-permute-done((f32[128,262]{1,0:T(8,128)S(1)}, f32[128,262]{1,0:T(8,128)S(1)}, u32[]{:S(2)}, u32[]{:S(2)}) %collective-permute-start.6) | collective-permute-done | bytes 134176 | tf_op jit(solution)/shard_map/ppermute | solution.py:43
  138.3 10.0 %collective-permute-done.7 = f32[128,262]{1,0:T(8,128)S(1)} collective-permute-done((f32[128,262]{1,0:T(8,128)S(1)}, f32[128,262]{1,0:T(8,128)S(1)}, u32[]{:S(2)}, u32[]{:S(2)}) %collective-permute-start.7) | collective-permute-done | bytes 134176 | tf_op jit(solution)/shard_map/ppermute | solution.py:43
  149.9 2.3 %gather_fusion = f32[256]{0:T(256)S(1)} fusion(f32[256,256]{1,0:T(8,128)S(1)} %slice.106, s32[256]{0:T(256)S(1)} %bitcast.162), kind=kCustom, calls=%fused_computation | custom fusion | bytes 4096 | tf_op jit(solution)/shard_map/jit(diagonal)/cond/branch_0_fun/gather | solution.py:203
  152.6 12.1 %while.77 = (s32[]{:T(128)}, f32[6,256]{1,0:T(8,128)S(1)}, f32[3,6,64]{2,1,0:T(8,128)}, s32[3,6,256]{2,1,0:T(8,128)}, f32[6,256]{1,0:T(8,128)S(1)}, /*index=5*/f...) while((s32[]{:T(128)}, f32[6,256]{1,0:T(8,128)S(1)}, f32[3,6,64]{2,1,0:T(8,128)}, ...), condition=%wide.region_8.9_spmd, body=%wide.region_2.8_spmd.sunk | while | flops 9474058 | bytes 660066 | solution.py:238
  153.7 2.2 %while.80 = (s32[]{:T(128)}, f32[6,256]{1,0:T(8,128)S(1)}, f32[6,256]{1,0:T(8,128)S(1)}, f32[6,256]{1,0:T(8,128)S(1)}, f32[6]{0:T(128)S(1)}, /*index=5*/f32[6,256]{1,0:T(8,128)S(1)}, f32[256,256]{1,0:T(8,128)S(1)}, s32[]{:T(128)}) while((s32[]{:T(128)}, f32[6,256]{1,0:T(8,128)S(1)}, f32[6,256]{1,0:T(8,128)S(1)}, f32[6,256]{1,0:T(8,128)S(1)}, ...), condition=%wide.region_7.7_spmd, body=%wide.region_4.6_spmd.sunk | while | flops 4740110 | bytes 330125 | solution.py:231
  157.8 2.2 %while.80 = (s32[]{:T(128)}, f32[6,256]{1,0:T(8,128)S(1)}, f32[6,256]{1,0:T(8,128)S(1)}, f32[6,256]{1,0:T(8,128)S(1)}, f32[6]{0:T(128)S(1)}, /*index=5*/f32[6,256]{1,0:T(8,128)S(1)}, f32[256,256]{1,0:T(8,128)S(1)}, s32[]{:T(128)}) while((s32[]{:T(128)}, f32[6,256]{1,0:T(8,128)S(1)}, f32[6,256]{1,0:T(8,128)S(1)}, f32[6,256]{1,0:T(8,128)S(1)}, ...), condition=%wide.region_7.7_spmd, body=%wide.region_4.6_spmd.sunk | while | flops 4740110 | bytes 330125 | solution.py:231
  161.8 2.2 %while.80 = (s32[]{:T(128)}, f32[6,256]{1,0:T(8,128)S(1)}, f32[6,256]{1,0:T(8,128)S(1)}, f32[6,256]{1,0:T(8,128)S(1)}, f32[6]{0:T(128)S(1)}, /*index=5*/f32[6,256]{1,0:T(8,128)S(1)}, f32[256,256]{1,0:T(8,128)S(1)}, s32[]{:T(128)}) while((s32[]{:T(128)}, f32[6,256]{1,0:T(8,128)S(1)}, f32[6,256]{1,0:T(8,128)S(1)}, f32[6,256]{1,0:T(8,128)S(1)}, ...), condition=%wide.region_7.7_spmd, body=%wide.region_4.6_spmd.sunk | while | flops 4740110 | bytes 330125 | solution.py:231
  164.7 4.1 %while.78 = (s32[]{:T(128)}, bf16[6,128,128]{2,0,1:T(8,128)(2,1)S(1)}, bf16[6,128,128]{2,0,1:T(8,128)(2,1)S(1)}, bf16[16,128,128]{2,0,1:T(8,128)(2,1)S(1)}, bf16...) while((s32[]{:T(128)}, ...), condition=%wide.region_10.11_spmd, body=%wide.region_9.10_spmd.sunk | while | flops 14884870 | bytes 5640347 | solution.py:261
  168.9 2.0 %collective-permute-start.10 = (bf16[6,128,128]{2,0,1:T(8,128)(2,1)S(1)}, bf16[6,128,128]{2,0,1:T(8,128)(2,1)S(1)}, u32[]{:S(2)}, u32[]{:S(2)}) collective-permute-start(bf16[6,128,128]{2,0,1:T(8,128)(2,1)S(1)} %get-tuple-element.439), channel_id=1, source_target_pairs={{0,8},{4,12},{8,0},{12,4},{1,9},{5,13},{9,1},{13,5},{2,10},{6,14},... | collective-permute-start | bytes 589832 | tf_op jit(solution)/shard_map/ppermute | solution.py:265
  170.9 1.8 collective-permute-start.9
  172.7 13.6 %collective-permute-done.9 = bf16[6,128,128]{2,0,1:T(8,128)(2,1)S(1)} collective-permute-done((bf16[6,128,128]{2,0,1:T(8,128)(2,1)S(1)}, bf16[6,128,128]{2,0,1:T(8,128)(2,1)S(1)}, u32[]{:S(2)}, u32[]{:S(2)}) %collective-permute-start.9) | collective-permute-done | bytes 196640 | tf_op jit(solution)/shard_map/ppermute | solution.py:265
  186.3 3.9 %collective-permute-done.10 = bf16[6,128,128]{2,0,1:T(8,128)(2,1)S(1)} collective-permute-done((bf16[6,128,128]{2,0,1:T(8,128)(2,1)S(1)}, bf16[6,128,128]{2,0,1:T(8,128)(2,1)S(1)}, u32[]{:S(2)}, u32[]{:S(2)}) %collective-permute-start.10) | collective-permute-done | bytes 196640 | tf_op jit(solution)/shard_map/ppermute | solution.py:265
  191.6 1.4 copy.48
  (182 shorter events, 40.1 us)
Async XLA Ops:
  1.5 32.1 %collective-permute-start.1 = (bf16[4,4,5,256]{3,2,1,0:T(8,128)(2,1)S(1)}, bf16[4,4,5,256]{3,2,1,0:T(8,128)(2,1)S(1)}, u32[]{:S(2)}, u32[]{:S(2)}) collective-permute-start(bf16[4,4,5,256]{3,2,1,0:T(8,128)(2,1)S(1)} %get-tuple-element.578), channel_id=1, source_target_pairs={{1,0},{0,1},{3,2},{2,3},{5,4},{4,5},{7,6},{6,7},{9,8},{8,9},{11,10... | collective-permute-start | bytes 122888 | tf_op jit(solution)/shard_map/ppermute | solution.py:68
  2.0 22.5 %collective-permute-start = (bf16[4,4,5,256]{3,2,1,0:T(8,128)(2,1)S(1)}, bf16[4,4,5,256]{3,2,1,0:T(8,128)(2,1)S(1)}, u32[]{:S(2)}, u32[]{:S(2)}) collective-permute-start(bf16[4,4,5,256]{3,2,1,0:T(8,128)(2,1)S(1)} %get-tuple-element.579), channel_id=1, source_target_pairs={{0,1},{1,0},{2,3},{3,2},{4,5},{5,4},{6,7},{7,6},{8,9},{9,8},{10,11... | collective-permute-start | bytes 122888 | tf_op jit(solution)/shard_map/ppermute | solution.py:68
  2.3 15.1 %slice-start = ((s8[8388608]{0:T(1024)(128)(4,1)}), s8[4194304]{0:T(1024)(128)(4,1)S(1)}, s32[]{:S(2)}) async-start(s8[8388608]{0:T(1024)(128)(4,1)} %bitcast.166), calls=%async_computation.1 | async-start | bytes 8388608
  5.0 12.4 %slice-start.1 = ((s8[8388608]{0:T(1024)(128)(4,1)}), s8[4194304]{0:T(1024)(128)(4,1)S(1)}, s32[]{:S(2)}) async-start(s8[8388608]{0:T(1024)(128)(4,1)} %bitcast.166), calls=%async_computation.2 | async-start | bytes 8388608
  17.4 7.2 %copy-start.1 = (s32[4]{0:T(128)S(1)}, s32[4]{0:T(128)}, u32[]{:S(2)}) copy-start(s32[4]{0:T(128)} %param.14) | copy-start | bytes 52
  57.4 10.9 %collective-permute-start.2 = (f32[2,4,4,256,5]{3,4,2,1,0:T(8,128)S(1)}, f32[2,4,4,256,5]{3,4,2,1,0:T(8,128)S(1)}, u32[]{:S(2)}, u32[]{:S(2)}) collective-permute-start(f32[2,4,4,256,5]{3,4,2,1,0:T(8,128)S(1)} %get-tuple-element.577), channel_id=1, source_target_pairs={{0,2},{2,0},{1,3},{3,1},{4,6},{6,4},{5,7},{7,5},{8,10},{10,8},{9,1... | collective-permute-start | bytes 491528 | tf_op jit(solution)/shard_map/ppermute | solution.py:68
  68.3 8.1 %collective-permute-start.3 = (f32[2,4,4,256,5]{3,4,2,1,0:T(8,128)S(1)}, f32[2,4,4,256,5]{3,4,2,1,0:T(8,128)S(1)}, u32[]{:S(2)}, u32[]{:S(2)}) collective-permute-start(f32[2,4,4,256,5]{3,4,2,1,0:T(8,128)S(1)} %get-tuple-element.576), channel_id=1, source_target_pairs={{2,0},{0,2},{3,1},{1,3},{6,4},{4,6},{7,5},{5,7},{10,8},{8,10},{11,... | collective-permute-start | bytes 491528 | tf_op jit(solution)/shard_map/ppermute | solution.py:68
  82.7 5.9 %copy-start = (bf16[6,4,256,64]{2,3,1,0:T(8,128)(2,1)S(1)}, bf16[6,4,256,64]{2,3,1,0:T(8,128)(2,1)}, u32[]{:S(2)}) copy-start(bf16[6,4,256,64]{2,3,1,0:T(8,128)(2,1)} %param.13) | copy-start | bytes 2359300
  83.8 29.7 %all-to-all-start = ((bf16[4,1024,128]{2,1,0:T(8,128)(2,1)}), bf16[4,1024,128]{2,1,0:T(8,128)(2,1)S(1)}, u32[]{:S(2)}, u32[]{:S(2)}) async-start(bf16[4,1024,128]{2,1,0:T(8,128)(2,1)} %bitcast.27), calls=%async_computation | async-start | bytes 2097152 | tf_op jit(solution)/shard_map/all_to_all | solution.py:170
  122.8 1.8 collective-permute-start.4
  124.7 7.0 %collective-permute-start.5 = (f32[128,262]{1,0:T(8,128)S(1)}, f32[128,262]{1,0:T(8,128)S(1)}, u32[]{:S(2)}, u32[]{:S(2)}) collective-permute-start(f32[128,262]{1,0:T(8,128)S(1)} %slice_select_fusion), channel_id=1, source_target_pairs={{0,2},{2,0},{1,3},{3,1},{4,6},{6,4},{5,7},{7,5},{8,10},{10,8},{9,1... | collective-permute-start | bytes 402440 | tf_op jit(solution)/shard_map/ppermute | solution.py:43
  131.7 6.2 %collective-permute-start.6 = (f32[128,262]{1,0:T(8,128)S(1)}, f32[128,262]{1,0:T(8,128)S(1)}, u32[]{:S(2)}, u32[]{:S(2)}) collective-permute-start(f32[128,262]{1,0:T(8,128)S(1)} %fusion.89), channel_id=1, source_target_pairs={{0,4},{4,0},{8,12},{12,8},{1,5},{5,1},{9,13},{13,9},{2,6},{6,2},{1... | collective-permute-start | bytes 402440 | tf_op jit(solution)/shard_map/ppermute | solution.py:43
  138.0 10.4 %collective-permute-start.7 = (f32[128,262]{1,0:T(8,128)S(1)}, f32[128,262]{1,0:T(8,128)S(1)}, u32[]{:S(2)}, u32[]{:S(2)}) collective-permute-start(f32[128,262]{1,0:T(8,128)S(1)} %add.236), channel_id=1, source_target_pairs={{0,8},{4,12},{8,0},{12,4},{1,9},{5,13},{9,1},{13,5},{2,10},{6,14},... | collective-permute-start | bytes 402440 | tf_op jit(solution)/shard_map/ppermute | solution.py:43
  148.3 1.5 collective-permute-start.8
  168.8 21.5 %collective-permute-start.11 = (bf16[6,128,128]{2,0,1:T(8,128)(2,1)S(1)}, bf16[6,128,128]{2,0,1:T(8,128)(2,1)S(1)}, u32[]{:S(2)}, u32[]{:S(2)}) collective-permute-start(bf16[6,128,128]{2,0,1:T(8,128)(2,1)S(1)} %get-tuple-element.439), channel_id=1, source_target_pairs={{0,4},{4,8},{8,12},{12,0},{1,5},{5,9},{9,13},{13,1},{2,6},{6,10},{... | collective-permute-start | bytes 589832 | tf_op jit(solution)/shard_map/ppermute | solution.py:265
  168.9 21.4 %collective-permute-start.10 = (bf16[6,128,128]{2,0,1:T(8,128)(2,1)S(1)}, bf16[6,128,128]{2,0,1:T(8,128)(2,1)S(1)}, u32[]{:S(2)}, u32[]{:S(2)}) collective-permute-start(bf16[6,128,128]{2,0,1:T(8,128)(2,1)S(1)} %get-tuple-element.439), channel_id=1, source_target_pairs={{0,8},{4,12},{8,0},{12,4},{1,9},{5,13},{9,1},{13,5},{2,10},{6,14},... | collective-permute-start | bytes 589832 | tf_op jit(solution)/shard_map/ppermute | solution.py:265
  170.9 15.4 %collective-permute-start.9 = (bf16[6,128,128]{2,0,1:T(8,128)(2,1)S(1)}, bf16[6,128,128]{2,0,1:T(8,128)(2,1)S(1)}, u32[]{:S(2)}, u32[]{:S(2)}) collective-permute-start(bf16[6,128,128]{2,0,1:T(8,128)(2,1)S(1)} %get-tuple-element.439), channel_id=1, source_target_pairs={{0,12},{4,0},{8,4},{12,8},{1,13},{5,1},{9,5},{13,9},{2,14},{6,2},{... | collective-permute-start | bytes 589832 | tf_op jit(solution)/shard_map/ppermute | solution.py:265

commit v6 on v4

--- a/solution.py
+++ b/solution.py
@@ -4,6 +4,7 @@
 import jax.numpy as jnp
 import numpy as np
 from jax import lax
+from jax.experimental import pallas as pl
 from jax.sharding import PartitionSpec as P
 
 STRESS = 6
@@ -65,6 +66,39 @@
     last = lax.slice_in_dim(array, length - width, length, axis=dim)
     leading = lax.slice_in_dim(array, 0, width, axis=dim)
     return (lax.ppermute(last, axis, up), lax.ppermute(leading, axis, down))
+
+
+def conjugate_passes(gram_ref, target_ref, mask_ref, out_ref):
+    gram = gram_ref[...]
+    target = target_ref[...]
+
+    def apply_normal(vector, active):
+        product = lax.dot_general(
+            active * vector,
+            gram,
+            (((1,), (1,)), ((), ())),
+            precision=lax.Precision.HIGHEST,
+            preferred_element_type=jnp.float32,
+        )
+        return active * product + ridge_weight * vector
+
+    solution_all = jnp.zeros(target.shape, jnp.float32)
+    for pass_index in range(PASSES):
+        active = mask_ref[pass_index]
+        solution_all = active * solution_all
+        remain = active * target - apply_normal(solution_all, active)
+        direction = remain
+        norm_now = jnp.sum(remain * remain, axis=1, keepdims=True)
+        for turn_index in range(ITERS):
+            applied = apply_normal(direction, active)
+            curve_sum = jnp.sum(direction * applied, axis=1, keepdims=True)
+            step_size = norm_now / (curve_sum + epsilon)
+            solution_all = solution_all + step_size * direction
+            remain = remain - step_size * applied
+            norm_next = jnp.sum(remain * remain, axis=1, keepdims=True)
+            direction = remain + (norm_next / (norm_now + epsilon)) * direction
+            norm_now = norm_next
+        out_ref[pass_index] = solution_all
 
 
 def kernel(spread):
@@ -202,46 +236,19 @@
     normal_gram = column_scale[:, None] * gram_matrix * column_scale[None, :] / samples
     target_norm = column_scale[None, :] * rhs_sums.T / samples
 
-    def apply_normal(vector, active):
-        product = jnp.einsum(
-            "kl,il->ki", active * vector, normal_gram, precision=lax.Precision.HIGHEST
-        )
-        return active * product + ridge_weight * vector
-
-    def cg_turn(turn_index, state):
-        solution_all, remain, direction, norm_now, active = state
-        applied = apply_normal(direction, active)
-        curve_sum = jnp.sum(direction * applied, axis=1)
-        step_size = norm_now / (curve_sum + epsilon)
-        solution_all = solution_all + step_size[:, None] * direction
-        remain = remain - step_size[:, None] * applied
-        norm_next = jnp.sum(remain * remain, axis=1)
-        direction = remain + (norm_next / (norm_now + epsilon))[:, None] * direction
-        return (solution_all, remain, direction, norm_next, active)
-
-    def cg_pass(pass_index, state):
-        solution_all, coefficients = state
-        active = lax.dynamic_index_in_dim(active_masks, pass_index, 0, keepdims=False)
-        active = active.astype(jnp.float32)
-        solution_all = active * solution_all
-        remain = active * target_norm - apply_normal(solution_all, active)
-        norm_now = jnp.sum(remain * remain, axis=1)
-        solution_all = lax.fori_loop(
-            0, ITERS, cg_turn, (solution_all, remain, remain, norm_now, active)
-        )[0]
-        own_part = lax.dynamic_slice_in_dim(solution_all, offset, term_dev, 1)
-        coefficients = lax.dynamic_update_index_in_dim(coefficients, own_part, pass_index, 0)
-        return (solution_all, coefficients)
-
-    solution_all, coefficients = lax.fori_loop(
-        0,
-        PASSES,
-        cg_pass,
-        (
-            jnp.zeros((STRESS, TERMS), jnp.float32),
-            jnp.zeros((PASSES, STRESS, term_dev), jnp.float32),
-        ),
-    )
+    padded_rows = -(-STRESS // 8) * 8
+    target_padded = jnp.zeros((padded_rows, TERMS), jnp.float32).at[:STRESS].set(target_norm)
+    masks_padded = (
+        jnp.zeros((PASSES, padded_rows, TERMS), jnp.float32)
+        .at[:, :STRESS]
+        .set(active_masks.astype(jnp.float32))
+    )
+    passes = pl.pallas_call(
+        conjugate_passes,
+        out_shape=jax.ShapeDtypeStruct((PASSES, padded_rows, TERMS), jnp.float32),
+    )(normal_gram, target_padded, masks_padded)
+    coefficients = lax.dynamic_slice_in_dim(passes[:, :STRESS], offset, term_dev, 2)
+    solution_all = passes[PASSES - 1, :STRESS]
     final_weights = (column_scale[None, :] * solution_all).astype(jnp.bfloat16)
 
     def misfit_step(block_index, misfit_acc):

time: 165 us -> 158 us (0.958)
  Pallas kernels: 0 us -> 8.4 us
  waiting for transfers between devices: 50.1 us -> 44.2 us
  matrix products: 52.8 us -> 47.6 us
  other arithmetic: 13.2 us -> 9.2 us
    pallas_call x0 -> x1, Pallas kernels: none -> 8.4 us  [local(): pl.pallas_call(conjugate_passes, out_shape=jax.ShapeDtypeStruct((PASSES,...]
    dot_general x12 -> x0, matrix products: 5.26 us -> none  [apply_normal(): jnp.einsum('kl,il->ki', active * vector, normal_gram, precision=lax.Preci...]
    ppermute x3, waiting for transfers between devices: 22.5 us -> 17.4 us  [tree_sum(): value = value + lax.ppermute(value, axis, partner)]
    mul x3 -> x0, other arithmetic: 2.11 us -> none  [cg_pass(): solution_all = active * solution_all]
    dynamic_update_slice x3 -> x0, local copies, waits for them, and re-layouts: 2.02 us -> none  [cg_pass(): lax.dynamic_update_index_in_dim(coefficients, own_part, pass_index, 0)]
    reduce_sum x9 -> x0, other arithmetic: 1.67 us -> none  [cg_turn(): norm_next = jnp.sum(remain * remain, axis=1)]
  transfers between devices with their start and end apart: 10 -> 10, of which waited for: 8 -> 8; matrix products, arithmetic and copies ran while one was open for 21% -> 23% of each run, Pallas kernels for 0% -> 0%
where the time goes in v6:
time: 158 us; the launch traced here: 157 us
  matrix products  47.6 us (30%)
  waiting for transfers between devices  44.2 us (28%)
  local copies, waits for them, and re-layouts  19.2 us (12%)
  blocking collectives  18 us (11%)
  starting transfers between devices  9.49 us (6%)
  other arithmetic  9.2 us (6%)
  Pallas kernels  8.4 us (5%)
    all_to_all x1, waiting for transfers between devices, local(): sets = lax.all_to_all(sets, 'cols', 0, 0, tiled=True)  18.5 us
    all_gather x1, blocking collectives, local(): misfit = lax.all_gather(misfit, 'cols', axis=1, tiled=True)  18 us
    ppermute x3, waiting for transfers between devices, tree_sum(): value = value + lax.ppermute(value, axis, partner)  17.4 us
    dot_general x1, matrix products, local(): jnp.einsum('cpxz,sxm->scpmz', fields.astype(jnp.float32), stream_table[:,...  16 us
    pallas_call x1, Pallas kernels, local(): pl.pallas_call(conjugate_passes, out_shape=jax.ShapeDtypeStruct((PASSES,...  8.4 us
    ppermute x4, waiting for transfers between devices, neighbour_edges(): return (lax.ppermute(last, axis, up), lax.ppermute(leading, axis, down))  6 us
    dot_general x4, matrix products, gram_step(): jnp.einsum('iqr,kqr->ik', all_terms, weighted_piece, preferred_element_ty...  5.92 us
    dot_general x1, matrix products, local(): jnp.einsum('scpmz,zsn->scpmn', along_stream, span_table[width:width + cel...  5.53 us
  transfers between devices with their start and end apart: 10, of which 8 were waited for; matrix products, arithmetic and copies ran while one was open for 23% of the time, Pallas kernels for 0%

profile of v6, /device:TPU:0, one launch (start us, length us, event | category | flops | bytes accessed | tf_op | source)
XLA Modules:
  0.0 157.3 jit_solution(279525832503433906)
XLA Ops:
  2.2 1.5 select_select_fusion
  3.7 16.0 %fusion.7 = f32[2,256,4,4,256]{1,4,3,2,0:T(8,128)S(1)} fusion(bf16[4,4,1024,256]{3,2,1,0:T(8,128)(2,1)} %param.12, f32[2,1034,256]{2,1,0:T(8,128)S(1)} %select_select_fusion), kind=kOutput, calls=%fused_computation.18 | convolution fusion | flops 25769803776 | bytes 18874368 | tf_op jit(solution)/shard_map/cpxz,sxm->scpmz/dot_general | solution.py:157
  20.0 3.5 %fusion.38 = f32[2,256,4,4,256]{1,4,3,2,0:T(8,128)S(1)} fusion(bf16[4,4,5,256]{3,2,1,0:T(8,128)(2,1)S(1)} %collective-permute-done, f32[2,1034,256]{2,1,0:T(8,128)S(1)} %select_select_fusion), kind=kOutput, calls=%fused_computation.68 | convolution fusion | flops 125829120 | bytes 8470528 | tf_op jit(solution)/shard_map/cpxz,sxm->scpmz/dot_general | solution.py:163
  23.5 4.4 %add_bitcast_fusion = f32[2,4,4,256,256]{3,4,2,1,0:T(8,128)S(1)} fusion(f32[2,256,4,4,256]{1,4,3,2,0:T(8,128)S(1)} %fusion.7, f32[2,256,4,4,256]{1,4,3,2,0:T(8,128)S(1)} %fusion.38, bf16[4,4,5,256]{3,2,1,0:T(8,128)(2,1)S(1)} %collective-permute-done.1, f32[2,1034,256]{2,1,0:T(8,128)S(1)} %select_select_fusion), kind=kOutput, calls=%fused_computation.20 | convolution fusion | flops 130023424 | bytes 25247744 | tf_op jit(solution)/shard_map/cpxz,sxm->scpmz/dot_general | solution.py:166
  28.0 3.0 %collective-permute-start.2 = (f32[2,4,4,256,5]{3,4,2,1,0:T(8,128)S(1)}, f32[2,4,4,256,5]{3,4,2,1,0:T(8,128)S(1)}, u32[]{:S(2)}, u32[]{:S(2)}) collective-permute-start(f32[2,4,4,256,5]{3,4,2,1,0:T(8,128)S(1)} %get-tuple-element.340), channel_id=1, source_target_pairs={{0,2},{2,0},{1,3},{3,1},{4,6},{6,4},{5,7},{7,5},{8,10},{10,8},{9,1... | collective-permute-start | bytes 491528 | tf_op jit(solution)/shard_map/ppermute | solution.py:68
  30.9 5.5 %fusion.35 = f32[2,4,4,256,64]{3,4,2,1,0:T(8,128)S(1)} fusion(f32[2,4,4,256,256]{3,4,2,1,0:T(8,128)S(1)} %add_bitcast_fusion, f32[266,2,64]{0,2,1:T(8,128)S(1)} %select_select_fusion.1), kind=kOutput, calls=%fused_computation.63 | convolution fusion | flops 1610612736 | bytes 10616832 | tf_op jit(solution)/shard_map/scpmz,zsn->scpmn/dot_general | solution.py:175
  37.5 2.0 %fusion.36 = f32[2,4,4,256,64]{3,4,2,1,0:T(8,128)S(1)} fusion(f32[2,4,4,256,5]{3,4,2,1,0:T(8,128)S(1)} %collective-permute-done.2, f32[266,2,64]{0,2,1:T(8,128)S(1)} %select_select_fusion.1), kind=kOutput, calls=%fused_computation.66 | convolution fusion | flops 31457280 | bytes 2424832 | tf_op jit(solution)/shard_map/scpmz,zsn->scpmn/dot_general | solution.py:181
  39.5 5.0 %collective-permute-done.3 = f32[2,4,4,256,5]{3,4,2,1,0:T(8,128)S(1)} collective-permute-done((f32[2,4,4,256,5]{3,4,2,1,0:T(8,128)S(1)}, f32[2,4,4,256,5]{3,4,2,1,0:T(8,128)S(1)}, u32[]{:S(2)}, u32[]{:S(2)}) %collective-permute-start.3) | collective-permute-done | bytes 163872 | tf_op jit(solution)/shard_map/ppermute | solution.py:68
  44.6 2.1 %add_add_fusion = f32[2,4,4,256,64]{3,4,2,1,0:T(8,128)S(1)} fusion(f32[2,4,4,256,64]{3,4,2,1,0:T(8,128)S(1)} %fusion.35, f32[2,4,4,256,64]{3,4,2,1,0:T(8,128)S(1)} %fusion.36, f32[2,4,4,256,5]{3,4,2,1,0:T(8,128)S(1)} %collective-permute-done.3, f32[266,2,64]{0,2,1:T(8,128)S(1)} %select_select_fusion.1), kind=kOutput, calls=%fused_computation.37 | convolution fusion | flops 32505856 | bytes 6619136 | tf_op jit(solution)/shard_map/scpmz,zsn->scpmn/dot_general | solution.py:182
  48.6 1.5 copy.50
  52.0 4.9 %all-to-all-start = ((bf16[4,1024,128]{2,1,0:T(8,128)(2,1)}), bf16[4,1024,128]{2,1,0:T(8,128)(2,1)S(1)}, u32[]{:S(2)}, u32[]{:S(2)}) async-start(bf16[4,1024,128]{2,1,0:T(8,128)(2,1)} %bitcast.18), calls=%async_computation | async-start | bytes 2097152 | tf_op jit(solution)/shard_map/all_to_all | solution.py:202
  56.9 1.2 multiply_convert_fusion.2
  58.2 1.8 %copy.53 = bf16[6,4,256,64]{3,2,1,0:T(8,128)(2,1)S(1)} copy(bf16[6,4,256,64]{2,3,1,0:T(8,128)(2,1)} %multiply_convert_fusion.2) | data formatting | bytes 1572864 | tf_op jit(solution)/shard_map/convert_element_type | solution.py:192
  59.9 1.5 reshape_reshape.3
  63.2 18.5 %all-to-all-done = bf16[4,1024,128]{2,1,0:T(8,128)(2,1)S(1)} async-done(((bf16[4,1024,128]{2,1,0:T(8,128)(2,1)}), bf16[4,1024,128]{2,1,0:T(8,128)(2,1)S(1)}, u32[]{:S(2)}, u32[]{:S(2)}) %all-to-all-start) | async-done | bytes 1048608 | tf_op jit(solution)/shard_map/all_to_all | solution.py:202
  82.5 11.7 %while.32 = (s32[]{:T(128)}, f32[256,256]{1,0:T(8,128)S(1)}, f32[256,6]{0,1:T(8,128)S(1)}, bf16[16,128,128]{2,0,1:T(8,128)(2,1)S(1)}, bf16[16,128,128]{2,0,1:T(8...) while((s32[]{:T(128)}, f32[256,256]{1,0:T(8,128)S(1)}, ...), condition=%wide.region_1.2_spmd.clone, body=%wide.region_0.1_spmd.clone.sunk | while | flops 551816192 | bytes 8204454 | solution.py:226
  83.9 1.5 fusion.80
  86.8 1.5 fusion.80
  89.8 1.5 fusion.80
  92.7 1.5 fusion.80
  94.4 1.5 collective-permute-done.4
  96.6 5.1 %collective-permute-done.5 = f32[128,262]{0,1:T(8,128)S(1)} collective-permute-done((f32[128,262]{0,1:T(8,128)S(1)}, f32[128,262]{0,1:T(8,128)S(1)}, u32[]{:S(2)}, u32[]{:S(2)}) %collective-permute-start.5) | collective-permute-done | bytes 134176 | tf_op jit(solution)/shard_map/ppermute | solution.py:43
  101.8 5.0 %collective-permute-done.6 = f32[128,262]{0,1:T(8,128)S(1)} collective-permute-done((f32[128,262]{0,1:T(8,128)S(1)}, f32[128,262]{0,1:T(8,128)S(1)}, u32[]{:S(2)}, u32[]{:S(2)}) %collective-permute-start.6) | collective-permute-done | bytes 134176 | tf_op jit(solution)/shard_map/ppermute | solution.py:43
  107.0 7.4 %collective-permute-done.7 = f32[128,262]{0,1:T(8,128)S(1)} collective-permute-done((f32[128,262]{0,1:T(8,128)S(1)}, f32[128,262]{0,1:T(8,128)S(1)}, u32[]{:S(2)}, u32[]{:S(2)}) %collective-permute-start.7) | collective-permute-done | bytes 134176 | tf_op jit(solution)/shard_map/ppermute | solution.py:43
  115.8 2.4 %gather_fusion = f32[256]{0:T(256)S(1)} fusion(f32[256,256]{0,1:T(8,128)S(1)} %slice.136, s32[256]{0:T(256)S(1)} %bitcast.116), kind=kCustom, calls=%fused_computation | custom fusion | bytes 4096 | tf_op jit(solution)/shard_map/jit(diagonal)/cond/branch_0_fun/gather | solution.py:235
  119.8 8.4 %shard_map.59 = f32[3,8,256]{2,1,0:T(8,128)} custom-call(f32[256,256]{1,0:T(8,128)} %copy.58.gram_ref, f32[8,256]{1,0:T(8,128)} %scatter.6.target_ref, f32[3,8,256]{2,1,0:T(8,128)} %scatter.9.mask_ref), custom_call_target="tpu_custom_call" | custom-call | tf_op jit(solution)/shard_map/pallas_call | solution.py:246
  128.9 7.6 %while.31 = (s32[]{:T(128)}, bf16[6,128,128]{2,1,0:T(8,128)(2,1)S(1)}, bf16[6,128,128]{2,0,1:T(8,128)(2,1)}, bf16[16,128,128]{2,0,1:T(8,128)(2,1)S(1)}, bf16[16,...) while((s32[]{:T(128)}, ...), condition=%wide.region_3.4_spmd, body=%wide.region_2.3_spmd.sunk | while | flops 14884870 | bytes 5721247 | solution.py:266
  129.6 1.2 fusion.74
  131.5 1.2 fusion.74
  135.3 1.2 fusion.74
  136.5 18.0 %all_gather.3 = bf16[6,512,128]{2,1,0:T(8,128)(2,1)S(1)} all-gather(bf16[6,128,128]{2,1,0:T(8,128)(2,1)S(1)} %get-tuple-element.247), channel_id=1, replica_groups=mesh['groups'=2,'cols'=4,'slab'=2,'rep'=2] {'cols'}, dimensions={1}, use_global_device_ids=true | all-gather | bytes 983040 | tf_op jit(solution)/shard_map/all_gather | solution.py:269
  155.2 1.4 copy.63
  (93 shorter events, 24.8 us)
Async XLA Ops:
  1.5 18.5 %collective-permute-start = (bf16[4,4,5,256]{3,2,1,0:T(8,128)(2,1)S(1)}, bf16[4,4,5,256]{3,2,1,0:T(8,128)(2,1)S(1)}, u32[]{:S(2)}, u32[]{:S(2)}) collective-permute-start(bf16[4,4,5,256]{3,2,1,0:T(8,128)(2,1)S(1)} %get-tuple-element.342), channel_id=1, source_target_pairs={{0,1},{1,0},{2,3},{3,2},{4,5},{5,4},{6,7},{7,6},{8,9},{9,8},{10,11... | collective-permute-start | bytes 122888 | tf_op jit(solution)/shard_map/ppermute | solution.py:68
  2.0 21.5 %collective-permute-start.1 = (bf16[4,4,5,256]{3,2,1,0:T(8,128)(2,1)S(1)}, bf16[4,4,5,256]{3,2,1,0:T(8,128)(2,1)S(1)}, u32[]{:S(2)}, u32[]{:S(2)}) collective-permute-start(bf16[4,4,5,256]{3,2,1,0:T(8,128)(2,1)S(1)} %get-tuple-element.341), channel_id=1, source_target_pairs={{1,0},{0,1},{3,2},{2,3},{5,4},{4,5},{7,6},{6,7},{9,8},{8,9},{11,10... | collective-permute-start | bytes 122888 | tf_op jit(solution)/shard_map/ppermute | solution.py:68
  3.7 16.3 %copy-start.3 = (s32[4]{0:T(128)S(1)}, s32[4]{0:T(128)}, u32[]{:S(2)}) copy-start(s32[4]{0:T(128)} %param.14) | copy-start | bytes 52
  28.0 9.5 %collective-permute-start.2 = (f32[2,4,4,256,5]{3,4,2,1,0:T(8,128)S(1)}, f32[2,4,4,256,5]{3,4,2,1,0:T(8,128)S(1)}, u32[]{:S(2)}, u32[]{:S(2)}) collective-permute-start(f32[2,4,4,256,5]{3,4,2,1,0:T(8,128)S(1)} %get-tuple-element.340), channel_id=1, source_target_pairs={{0,2},{2,0},{1,3},{3,1},{4,6},{6,4},{5,7},{7,5},{8,10},{10,8},{9,1... | collective-permute-start | bytes 491528 | tf_op jit(solution)/shard_map/ppermute | solution.py:68
  36.5 8.1 %collective-permute-start.3 = (f32[2,4,4,256,5]{3,4,2,1,0:T(8,128)S(1)}, f32[2,4,4,256,5]{3,4,2,1,0:T(8,128)S(1)}, u32[]{:S(2)}, u32[]{:S(2)}) collective-permute-start(f32[2,4,4,256,5]{3,4,2,1,0:T(8,128)S(1)} %get-tuple-element.339), channel_id=1, source_target_pairs={{2,0},{0,2},{3,1},{1,3},{6,4},{4,6},{7,5},{5,7},{10,8},{8,10},{11,... | collective-permute-start | bytes 491528 | tf_op jit(solution)/shard_map/ppermute | solution.py:68
  50.9 6.0 %copy-start = (bf16[6,4,256,64]{2,3,1,0:T(8,128)(2,1)S(1)}, bf16[6,4,256,64]{2,3,1,0:T(8,128)(2,1)}, u32[]{:S(2)}) copy-start(bf16[6,4,256,64]{2,3,1,0:T(8,128)(2,1)} %param.13) | copy-start | bytes 2359300
  52.0 29.7 %all-to-all-start = ((bf16[4,1024,128]{2,1,0:T(8,128)(2,1)}), bf16[4,1024,128]{2,1,0:T(8,128)(2,1)S(1)}, u32[]{:S(2)}, u32[]{:S(2)}) async-start(bf16[4,1024,128]{2,1,0:T(8,128)(2,1)} %bitcast.18), calls=%async_computation | async-start | bytes 2097152 | tf_op jit(solution)/shard_map/all_to_all | solution.py:202
  94.2 20.3 %copy-start.2 = (s32[3,6,256]{2,1,0:T(8,128)S(1)}, s32[3,6,256]{2,1,0:T(8,128)}, u32[]{:S(2)}) copy-start(s32[3,6,256]{2,1,0:T(8,128)} %param.15) | copy-start | bytes 55300
  94.3 1.6 %collective-permute-start.4 = (f32[256,262]{0,1:T(8,128)S(1)}, f32[256,262]{0,1:T(8,128)S(1)}, u32[]{:S(2)}, u32[]{:S(2)}) collective-permute-start(f32[256,262]{0,1:T(8,128)S(1)} %pad_maximum_fusion), channel_id=1, source_target_pairs={{0,1},{1,0},{2,3},{3,2},{4,5},{5,4},{6,7},{7,6},{8,9},{9,8},{10,11... | collective-permute-start | bytes 804872 | tf_op jit(solution)/shard_map/ppermute | solution.py:53
  96.0 5.7 %collective-permute-start.5 = (f32[128,262]{0,1:T(8,128)S(1)}, f32[128,262]{0,1:T(8,128)S(1)}, u32[]{:S(2)}, u32[]{:S(2)}) collective-permute-start(f32[128,262]{0,1:T(8,128)S(1)} %slice_select_fusion), channel_id=1, source_target_pairs={{0,2},{2,0},{1,3},{3,1},{4,6},{6,4},{5,7},{7,5},{8,10},{10,8},{9,1... | collective-permute-start | bytes 402440 | tf_op jit(solution)/shard_map/ppermute | solution.py:43
  101.7 5.1 %collective-permute-start.6 = (f32[128,262]{0,1:T(8,128)S(1)}, f32[128,262]{0,1:T(8,128)S(1)}, u32[]{:S(2)}, u32[]{:S(2)}) collective-permute-start(f32[128,262]{0,1:T(8,128)S(1)} %fusion.62), channel_id=1, source_target_pairs={{0,4},{4,0},{8,12},{12,8},{1,5},{5,1},{9,13},{13,9},{2,6},{6,2},{1... | collective-permute-start | bytes 402440 | tf_op jit(solution)/shard_map/ppermute | solution.py:43
  106.8 7.5 %collective-permute-start.7 = (f32[128,262]{0,1:T(8,128)S(1)}, f32[128,262]{0,1:T(8,128)S(1)}, u32[]{:S(2)}, u32[]{:S(2)}) collective-permute-start(f32[128,262]{0,1:T(8,128)S(1)} %add.159), channel_id=1, source_target_pairs={{0,8},{4,12},{8,0},{12,4},{1,9},{5,13},{9,1},{13,5},{2,10},{6,14},... | collective-permute-start | bytes 402440 | tf_op jit(solution)/shard_map/ppermute | solution.py:43
  114.4 1.4 collective-permute-start.8
  154.5 2.1 %copy-start.1 = (f32[3,8,256]{2,1,0:T(8,128)S(1)}, f32[3,8,256]{2,1,0:T(8,128)}, u32[]{:S(2)}) copy-start(f32[3,8,256]{2,1,0:T(8,128)} %shard_map.59) | copy-start | bytes 73732

commit v7 on v6

--- a/solution.py
+++ b/solution.py
@@ -101,6 +101,42 @@
         out_ref[pass_index] = solution_all
 
 
+def filter_fields(fields, stream_table, span_table):
+    width = 5
+    cells_x, cells_z = fields.shape[2:]
+    highest = lax.Precision.HIGHEST
+    top, bottom = neighbour_edges(fields, "rep", 2, width)
+    along_stream = (
+        jnp.einsum(
+            "cpxz,sxm->scpmz",
+            fields.astype(jnp.float32),
+            stream_table[:, width : width + cells_x],
+            precision=highest,
+        )
+        + jnp.einsum(
+            "cpxz,sxm->scpmz", top.astype(jnp.float32), stream_table[:, :width], precision=highest
+        )
+        + jnp.einsum(
+            "cpxz,sxm->scpmz",
+            bottom.astype(jnp.float32),
+            stream_table[:, width + cells_x :],
+            precision=highest,
+        )
+    )
+    left, right = neighbour_edges(along_stream, "slab", 4, width)
+    filtered = (
+        jnp.einsum(
+            "scpmz,zsn->scpmn",
+            along_stream,
+            span_table[width : width + cells_z],
+            precision=highest,
+        )
+        + jnp.einsum("scpmz,zsn->scpmn", left, span_table[:width], precision=highest)
+        + jnp.einsum("scpmz,zsn->scpmn", right, span_table[width + cells_z :], precision=highest)
+    )
+    return (filtered[0], filtered[1])
+
+
 def kernel(spread):
     offsets = np.arange(13) - 6.0
     values = np.exp(-offsets * offsets / (2.0 * spread * spread))
@@ -145,66 +181,44 @@
     samples = float(row_count * lax.axis_size("slab") * lax.axis_size("rep"))
     height = 2.0 * (planes.astype(jnp.float32) + 0.5) / NY - 1.0
     root_weight = jnp.sqrt(1.2 - height * height)
-    width = 5
-    top, bottom = neighbour_edges(fields, "rep", 2, width)
     narrow_taps = kernel(1.5)
     broad_taps = kernel(3.0)
     guard = jnp.minimum(lax.axis_index("rep"), 0)
     span_table = filter_table(cells_z, narrow_taps, broad_taps, guard, (0, 1, 2))
     stream_table = filter_table(cells_x, narrow_taps, broad_taps, guard, (1, 0, 2))
-    highest = lax.Precision.HIGHEST
-    along_stream = (
-        jnp.einsum(
-            "cpxz,sxm->scpmz",
-            fields.astype(jnp.float32),
-            stream_table[:, width : width + cells_x],
-            precision=highest,
-        )
-        + jnp.einsum(
-            "cpxz,sxm->scpmz", top.astype(jnp.float32), stream_table[:, :width], precision=highest
-        )
-        + jnp.einsum(
-            "cpxz,sxm->scpmz",
-            bottom.astype(jnp.float32),
-            stream_table[:, width + cells_x :],
-            precision=highest,
-        )
-    )
-    left, right = neighbour_edges(along_stream, "slab", 4, width)
-    filtered = (
-        jnp.einsum(
-            "scpmz,zsn->scpmn",
-            along_stream,
-            span_table[width : width + cells_z],
-            precision=highest,
-        )
-        + jnp.einsum("scpmz,zsn->scpmn", left, span_table[:width], precision=highest)
-        + jnp.einsum("scpmz,zsn->scpmn", right, span_table[width + cells_z :], precision=highest)
-    )
-    narrow = filtered[0]
-    broader = filtered[1]
-    narrow_set = narrow.astype(jnp.bfloat16).reshape(chan_dev, row_count)
-    broad_set = (
-        (broader * root_weight[None, :, None, None])
-        .astype(jnp.bfloat16)
-        .reshape(chan_dev, row_count)
-    )
+    stages = 2 if plane_count % 2 == 0 and (row_count // 2) % (col_devices * 128) == 0 else 1
+    stage_planes = plane_count // stages
+    stage_rows = row_count // stages
+    lanes = 128
+    stage_chunk_rows = stage_rows // col_devices // lanes
+    chunk_rows = stages * stage_chunk_rows
+    channels = chan_dev * col_devices
+    exchanged = []
+    for stage in range(stages):
+        plane_slice = slice(stage * stage_planes, (stage + 1) * stage_planes)
+        narrow, broader = filter_fields(fields[:, plane_slice], stream_table, span_table)
+        narrow_set = narrow.astype(jnp.bfloat16).reshape(chan_dev, stage_rows)
+        broad_set = (
+            (broader * root_weight[plane_slice][None, :, None, None])
+            .astype(jnp.bfloat16)
+            .reshape(chan_dev, stage_rows)
+        )
+        sets = jnp.stack([narrow_set, broad_set])
+        sets = sets.reshape(2, chan_dev, col_devices, stage_chunk_rows, lanes)
+        sets = jnp.transpose(sets, (2, 0, 1, 3, 4))
+        sets = sets.reshape(col_devices, 2 * chan_dev * stage_chunk_rows, lanes)
+        sets = lax.all_to_all(sets, "cols", 0, 0, tiled=True)
+        sets = sets.reshape(col_devices, 2, chan_dev, stage_chunk_rows, lanes)
+        sets = jnp.transpose(sets, (1, 0, 2, 3, 4))
+        exchanged.append(sets.reshape(2, channels, stage_chunk_rows, lanes))
+    sets = jnp.concatenate(exchanged, axis=2)
+    narrow_all, broad_all = sets[0], sets[1]
     weighted = (stresses.astype(jnp.float32) * root_weight[None, :, None, None]).astype(
         jnp.bfloat16
     )
-    weighted = weighted.reshape(STRESS, row_count)
-    chunk = row_count // col_devices
-    lanes = 128
-    chunk_rows = chunk // lanes
-    channels = chan_dev * col_devices
-    sets = jnp.stack([narrow_set, broad_set]).reshape(2, chan_dev, col_devices, chunk_rows, lanes)
-    sets = jnp.transpose(sets, (2, 0, 1, 3, 4)).reshape(col_devices, 2 * chan_dev * chunk_rows, lanes)
-    sets = lax.all_to_all(sets, "cols", 0, 0, tiled=True)
-    sets = sets.reshape(col_devices, 2, chan_dev, chunk_rows, lanes)
-    sets = jnp.transpose(sets, (1, 0, 2, 3, 4)).reshape(2, channels, chunk_rows, lanes)
-    narrow_all, broad_all = sets[0], sets[1]
-    weighted = weighted.reshape(STRESS, col_devices, chunk_rows, lanes)
-    weighted = lax.dynamic_index_in_dim(weighted, column_index, 1, keepdims=False)
+    weighted = weighted.reshape(STRESS, stages, col_devices, stage_chunk_rows, lanes)
+    weighted = lax.dynamic_index_in_dim(weighted, column_index, 2, keepdims=False)
+    weighted = weighted.reshape(STRESS, chunk_rows, lanes)
     block_rows = math.gcd(chunk_rows, 32)
     block_count = chunk_rows // block_rows
 
@@ -266,7 +280,8 @@
     misfit = lax.fori_loop(
         0, block_count, misfit_step, jnp.zeros((STRESS, chunk_rows, lanes), jnp.bfloat16)
     )
-    misfit = lax.all_gather(misfit, "cols", axis=1, tiled=True)
+    misfit = misfit.reshape(STRESS, stages, stage_chunk_rows, lanes)
+    misfit = lax.all_gather(misfit, "cols", axis=2)
     misfit = misfit.reshape(STRESS, plane_count, coarse_x, coarse_z)
     return (coefficients, misfit)
 

time: 158 us -> 162 us (1.025)
  starting transfers between devices: 9.49 us -> 16.4 us
  waiting for transfers between devices: 44.2 us -> 37.9 us
  matrix products: 47.6 us -> 52.4 us
    dot_general x6 -> x12, matrix products: 33.6 us -> 38.4 us  [the longest x2 18.6 us: filter_fields(): jnp.einsum('cpxz,sxm->scpmz', fields.astype(jnp.float32), stream_table[:,...]
    all_to_all x1 -> x2, starting transfers between devices: 4.86 us -> 9.01 us  [local(): sets = lax.all_to_all(sets, 'cols', 0, 0, tiled=True)]
    all_to_all x1 -> x2, waiting for transfers between devices: 18.5 us -> 15.2 us  [local(): sets = lax.all_to_all(sets, 'cols', 0, 0, tiled=True)]
    ppermute x4 -> x8, waiting for transfers between devices: 6 us -> 3.16 us  [neighbour_edges(): return (lax.ppermute(last, axis, up), lax.ppermute(leading, axis, down))]
    ppermute x4 -> x8, starting transfers between devices: 3.65 us -> 6.37 us  [neighbour_edges(): return (lax.ppermute(last, axis, up), lax.ppermute(leading, axis, down))]
    slice x5 -> x9, local copies, waits for them, and re-layouts: 3.11 us -> 1.41 us  [the longest x8 1.34 us: filter_fields(): return (filtered[0], filtered[1])]
    transpose x1 -> x4, local copies, waits for them, and re-layouts: 1.1 us -> 2.79 us  [the longest x2 1.68 us: local(): sets = jnp.transpose(sets, (2, 0, 1, 3, 4))]
    unnamed x12 -> x20, local copies, waits for them, and re-layouts: 2.95 us -> 3.29 us
  transfers between devices with their start and end apart: 10 -> 15, of which waited for: 8 -> 8; matrix products, arithmetic and copies ran while one was open for 23% -> 30% of each run, Pallas kernels for 0% -> 0%
where the time goes in v7:
time: 162 us; the launch traced here: 161 us
  matrix products  52.4 us (32%)
  waiting for transfers between devices  37.9 us (23%)
  local copies, waits for them, and re-layouts  18 us (11%)
  blocking collectives  18 us (11%)
  starting transfers between devices  16.4 us (10%)
  Pallas kernels  8.39 us (5%)
  other arithmetic  8.33 us (5%)
    dot_general x2, matrix products, filter_fields(): jnp.einsum('cpxz,sxm->scpmz', fields.astype(jnp.float32), stream_table[:,...  18.6 us
    all_gather x1, blocking collectives, local(): misfit = lax.all_gather(misfit, 'cols', axis=2)  18 us
    ppermute x3, waiting for transfers between devices, tree_sum(): value = value + lax.ppermute(value, axis, partner)  17.4 us
    all_to_all x2, waiting for transfers between devices, local(): sets = lax.all_to_all(sets, 'cols', 0, 0, tiled=True)  15.2 us
    all_to_all x2, starting transfers between devices, local(): sets = lax.all_to_all(sets, 'cols', 0, 0, tiled=True)  9.01 us
    pallas_call x1, Pallas kernels, local(): pl.pallas_call(conjugate_passes, out_shape=jax.ShapeDtypeStruct((PASSES,...  8.39 us
    ppermute x8, starting transfers between devices, neighbour_edges(): return (lax.ppermute(last, axis, up), lax.ppermute(leading, axis, down))  6.37 us
    dot_general x4, matrix products, gram_step(): jnp.einsum('iqr,kqr->ik', all_terms, weighted_piece, preferred_element_ty...  5.92 us
  transfers between devices with their start and end apart: 15, of which 8 were waited for; matrix products, arithmetic and copies ran while one was open for 30% of the time, Pallas kernels for 0%

profile of v7, /device:TPU:0, one launch (start us, length us, event | category | flops | bytes accessed | tf_op | source)
XLA Modules:
  0.0 160.9 jit_solution(699999354698214486)
XLA Ops:
  2.7 1.5 select_select_fusion
  4.2 10.2 %fusion.10 = f32[2,256,4,2,256]{1,4,3,2,0:T(8,128)} fusion(bf16[4,4,1024,256]{3,2,1,0:T(8,128)(2,1)} %param.12, f32[2,1034,256]{2,1,0:T(8,128)S(1)} %select_select_fusion), kind=kOutput, calls=%fused_computation.20 | convolution fusion | flops 12884901888 | bytes 10485760 | tf_op jit(solution)/shard_map/cpxz,sxm->scpmz/dot_general | solution.py:110
  14.3 8.4 %fusion.8 = f32[2,256,4,2,256]{1,4,3,2,0:T(8,128)} fusion(bf16[4,4,1024,256]{3,2,1,0:T(8,128)(2,1)S(1)} %bitcast.166, f32[2,1034,256]{2,1,0:T(8,128)S(1)} %select_select_fusion), kind=kOutput, calls=%fused_computation.18 | convolution fusion | flops 12884901888 | bytes 10485760 | tf_op jit(solution)/shard_map/cpxz,sxm->scpmz/dot_general | solution.py:110
  23.6 1.8 %fusion.49 = f32[2,256,4,2,256]{1,4,3,2,0:T(8,128)S(1)} fusion(bf16[4,2,5,256]{3,2,1,0:T(8,128)(2,1)S(1)} %collective-permute-done, f32[2,1034,256]{2,1,0:T(8,128)S(1)} %select_select_fusion), kind=kOutput, calls=%fused_computation.87 | convolution fusion | flops 62914560 | bytes 4243456 | tf_op jit(solution)/shard_map/cpxz,sxm->scpmz/dot_general | solution.py:116
  25.7 2.2 %add_bitcast_fusion.1 = f32[2,4,2,256,256]{3,4,2,1,0:T(8,128)S(1)} fusion(f32[2,256,4,2,256]{1,4,3,2,0:T(8,128)S(1)} %copy-done.1, f32[2,256,4,2,256]{1,4,3,2,0:T(8,128)S(1)} %fusion.49, bf16[4,2,5,256]{3,2,1,0:T(8,128)(2,1)S(1)} %collective-permute-done.1, f32[2,1034,256]{2,1,0:T(8,128)S(1)} %select_select_fusion), kind=kOutput, calls=%fused_computation.24 | convolution fusion | flops 65011712 | bytes 12632064 | tf_op jit(solution)/shard_map/cpxz,sxm->scpmz/dot_general | solution.py:119
  28.0 2.8 %fusion.44 = f32[2,4,2,256,64]{3,4,2,1,0:T(8,128)S(1)} fusion(f32[2,4,2,256,256]{3,4,2,1,0:T(8,128)S(1)} %add_bitcast_fusion.1, f32[266,2,64]{0,2,1:T(8,128)S(1)} %select_select_fusion.1), kind=kOutput, calls=%fused_computation.80 | convolution fusion | flops 805306368 | bytes 5373952 | tf_op jit(solution)/shard_map/scpmz,zsn->scpmn/dot_general | solution.py:128
  30.8 3.0 %collective-permute-start.2 = (f32[2,4,2,256,5]{3,4,2,1,0:T(8,128)S(1)}, f32[2,4,2,256,5]{3,4,2,1,0:T(8,128)S(1)}, u32[]{:S(2)}, u32[]{:S(2)}) collective-permute-start(f32[2,4,2,256,5]{3,4,2,1,0:T(8,128)S(1)} %get-tuple-element.320), channel_id=1, source_target_pairs={{0,2},{2,0},{1,3},{3,1},{4,6},{6,4},{5,7},{7,5},{8,10},{10,8},{9,1... | collective-permute-start | bytes 245768 | tf_op jit(solution)/shard_map/ppermute | solution.py:68
  33.8 1.8 %fusion.46 = f32[2,256,4,2,256]{1,4,3,2,0:T(8,128)S(1)} fusion(bf16[4,2,5,256]{3,2,1,0:T(8,128)(2,1)S(1)} %collective-permute-done.4, f32[2,1034,256]{2,1,0:T(8,128)S(1)} %select_select_fusion), kind=kOutput, calls=%fused_computation.84 | convolution fusion | flops 62914560 | bytes 4243456 | tf_op jit(solution)/shard_map/cpxz,sxm->scpmz/dot_general | solution.py:116
  35.7 2.2 %add_bitcast_fusion = f32[2,4,2,256,256]{3,4,2,1,0:T(8,128)S(1)} fusion(f32[2,256,4,2,256]{1,4,3,2,0:T(8,128)S(1)} %copy-done, f32[2,256,4,2,256]{1,4,3,2,0:T(8,128)S(1)} %fusion.46, bf16[4,2,5,256]{3,2,1,0:T(8,128)(2,1)S(1)} %collective-permute-done.5, f32[2,1034,256]{2,1,0:T(8,128)S(1)} %select_select_fusion), kind=kOutput, calls=%fused_computation.22 | convolution fusion | flops 65011712 | bytes 12632064 | tf_op jit(solution)/shard_map/cpxz,sxm->scpmz/dot_general | solution.py:119
  37.9 3.0 %fusion.43 = f32[2,4,2,256,64]{3,4,2,1,0:T(8,128)S(1)} fusion(f32[2,4,2,256,256]{3,4,2,1,0:T(8,128)S(1)} %add_bitcast_fusion, f32[266,2,64]{0,2,1:T(8,128)S(1)} %select_select_fusion.1), kind=kOutput, calls=%fused_computation.79 | convolution fusion | flops 805306368 | bytes 5373952 | tf_op jit(solution)/shard_map/scpmz,zsn->scpmn/dot_general | solution.py:128
  41.9 1.8 %collective-permute-start.6 = (f32[2,4,2,256,5]{3,4,2,1,0:T(8,128)}, f32[2,4,2,256,5]{3,4,2,1,0:T(8,128)}, u32[]{:S(2)}, u32[]{:S(2)}) collective-permute-start(f32[2,4,2,256,5]{3,4,2,1,0:T(8,128)} %get-tuple-element.318), channel_id=1, source_target_pairs={{0,2},{2,0},{1,3},{3,1},{4,6},{6,4},{5,7},{7,5},{8,10},{10,8},{9,1... | collective-permute-start | bytes 245768 | tf_op jit(solution)/shard_map/ppermute | solution.py:68
  44.9 3.1 %collective-permute-done.3 = f32[2,4,2,256,5]{3,4,2,1,0:T(8,128)S(1)} collective-permute-done((f32[2,4,2,256,5]{3,4,2,1,0:T(8,128)S(1)}, f32[2,4,2,256,5]{3,4,2,1,0:T(8,128)S(1)}, u32[]{:S(2)}, u32[]{:S(2)}) %collective-permute-start.3) | collective-permute-done | bytes 81952 | tf_op jit(solution)/shard_map/ppermute | solution.py:68
  51.2 4.9 %all-to-all-start = ((bf16[4,512,128]{2,1,0:T(8,128)(2,1)}), bf16[4,512,128]{2,1,0:T(8,128)(2,1)S(1)}, u32[]{:S(2)}, u32[]{:S(2)}) async-start(bf16[4,512,128]{2,1,0:T(8,128)(2,1)} %bitcast.18), calls=%async_computation | async-start | bytes 1048576 | tf_op jit(solution)/shard_map/all_to_all | solution.py:210
  56.1 1.9 %convolution_add_fusion.1 = f32[2,4,2,256,64]{3,4,2,1,0:T(8,128)S(1)} fusion(f32[2,4,2,256,64]{3,4,2,1,0:T(8,128)S(1)} %fusion.43, f32[2,4,2,256,5]{3,4,2,1,0:T(8,128)} %collective-permute-done.6, f32[266,2,64]{0,2,1:T(8,128)S(1)} %select_select_fusion.1), kind=kOutput, calls=%fused_computation.44 | convolution fusion | flops 15990784 | bytes 2244608 | tf_op jit(solution)/shard_map/scpmz,zsn->scpmn/dot_general | solution.py:134
  58.0 1.9 %convolution_add_fusion = f32[2,4,2,256,64]{3,4,2,1,0:T(8,128)S(1)} fusion(f32[2,4,2,256,64]{3,4,2,1,0:T(8,128)S(1)} %convolution_add_fusion.1, f32[2,4,2,256,5]{3,4,2,1,0:T(8,128)} %collective-permute-done.7, f32[266,2,64]{0,2,1:T(8,128)S(1)} %select_select_fusion.1), kind=kOutput, calls=%fused_computation.43 | convolution fusion | flops 15990784 | bytes 2244608 | tf_op jit(solution)/shard_map/scpmz,zsn->scpmn/dot_general | solution.py:135
  62.0 6.4 %all-to-all-done = bf16[4,512,128]{2,1,0:T(8,128)(2,1)S(1)} async-done(((bf16[4,512,128]{2,1,0:T(8,128)(2,1)}), bf16[4,512,128]{2,1,0:T(8,128)(2,1)S(1)}, u32[]{:S(2)}, u32[]{:S(2)}) %all-to-all-start) | async-done | bytes 524320 | tf_op jit(solution)/shard_map/all_to_all | solution.py:210
  68.5 4.1 %all-to-all-start.1 = ((bf16[4,512,128]{2,1,0:T(8,128)(2,1)}), bf16[4,512,128]{2,1,0:T(8,128)(2,1)}, u32[]{:S(2)}, u32[]{:S(2)}) async-start(bf16[4,512,128]{2,1,0:T(8,128)(2,1)} %bitcast.33), calls=%async_computation.1 | async-start | bytes 1048576 | tf_op jit(solution)/shard_map/all_to_all | solution.py:210
  75.5 8.8 %all-to-all-done.1 = bf16[4,512,128]{2,1,0:T(8,128)(2,1)} async-done(((bf16[4,512,128]{2,1,0:T(8,128)(2,1)}), bf16[4,512,128]{2,1,0:T(8,128)(2,1)}, u32[]{:S(2)}, u32[]{:S(2)}) %all-to-all-start.1) | async-done | bytes 524320 | tf_op jit(solution)/shard_map/all_to_all | solution.py:210
  86.2 11.7 %while.32 = (s32[]{:T(128)}, f32[256,256]{1,0:T(8,128)S(1)}, f32[256,6]{0,1:T(8,128)S(1)}, bf16[16,128,128]{2,0,1:T(8,128)(2,1)S(1)}, bf16[16,128,128]{2,0,1:T(8...) while((s32[]{:T(128)}, f32[256,256]{1,0:T(8,128)S(1)}, ...), condition=%wide.region_1.2_spmd.clone, body=%wide.region_0.1_spmd.clone.sunk | while | flops 551816192 | bytes 8204454 | solution.py:240
  87.6 1.5 fusion.95
  90.5 1.5 fusion.95
  93.4 1.5 fusion.95
  96.4 1.5 fusion.95
  98.1 1.5 collective-permute-done.8
  100.4 5.0 %collective-permute-done.9 = f32[128,262]{0,1:T(8,128)S(1)} collective-permute-done((f32[128,262]{0,1:T(8,128)S(1)}, f32[128,262]{0,1:T(8,128)S(1)}, u32[]{:S(2)}, u32[]{:S(2)}) %collective-permute-start.9) | collective-permute-done | bytes 134176 | tf_op jit(solution)/shard_map/ppermute | solution.py:43
  105.5 5.0 %collective-permute-done.10 = f32[128,262]{0,1:T(8,128)S(1)} collective-permute-done((f32[128,262]{0,1:T(8,128)S(1)}, f32[128,262]{0,1:T(8,128)S(1)}, u32[]{:S(2)}, u32[]{:S(2)}) %collective-permute-start.10) | collective-permute-done | bytes 134176 | tf_op jit(solution)/shard_map/ppermute | solution.py:43
  110.7 7.4 %collective-permute-done.11 = f32[128,262]{0,1:T(8,128)S(1)} collective-permute-done((f32[128,262]{0,1:T(8,128)S(1)}, f32[128,262]{0,1:T(8,128)S(1)}, u32[]{:S(2)}, u32[]{:S(2)}) %collective-permute-start.11) | collective-permute-done | bytes 134176 | tf_op jit(solution)/shard_map/ppermute | solution.py:43
  119.5 2.4 %gather_fusion = f32[256]{0:T(256)S(1)} fusion(f32[256,256]{0,1:T(8,128)S(1)} %slice.189, s32[256]{0:T(256)S(1)} %bitcast.158), kind=kCustom, calls=%fused_computation | custom fusion | bytes 4096 | tf_op jit(solution)/shard_map/jit(diagonal)/cond/branch_0_fun/gather | solution.py:249
  123.5 8.4 %shard_map.59 = f32[3,8,256]{2,1,0:T(8,128)} custom-call(f32[256,256]{1,0:T(8,128)} %copy.56.gram_ref, f32[8,256]{1,0:T(8,128)} %scatter.6.target_ref, f32[3,8,256]{2,1,0:T(8,128)} %scatter.9.mask_ref), custom_call_target="tpu_custom_call" | custom-call | tf_op jit(solution)/shard_map/pallas_call | solution.py:260
  132.6 7.5 %while.31 = (s32[]{:T(128)}, bf16[6,128,128]{2,0,1:T(8,128)(2,1)S(1)}, bf16[6,128,128]{2,0,1:T(8,128)(2,1)}, bf16[16,128,128]{2,0,1:T(8,128)(2,1)S(1)}, bf16[16,...) while((s32[]{:T(128)}, ...), condition=%wide.region_3.4_spmd, body=%wide.region_2.3_spmd.sunk | while | flops 14884870 | bytes 5623963 | solution.py:280
  140.1 18.0 %all_gather.3 = bf16[6,2,4,64,128]{4,3,2,1,0:T(8,128)(2,1)S(1)} all-gather(bf16[6,2,1,64,128]{4,3,2,1,0:T(8,128)(2,1)S(1)} %copy.60), channel_id=1, replica_groups=mesh['groups'=2,'cols'=4,'slab'=2,'rep'=2] {'cols'}, dimensions={2}, use_global_device_ids=true | all-gather | bytes 983040 | tf_op jit(solution)/shard_map/all_gather | solution.py:284
  158.8 1.4 copy.61
  (132 shorter events, 34.5 us)
Async XLA Ops:
  1.5 22.1 %collective-permute-start = (bf16[4,2,5,256]{3,2,1,0:T(8,128)(2,1)S(1)}, bf16[4,2,5,256]{3,2,1,0:T(8,128)(2,1)S(1)}, u32[]{:S(2)}, u32[]{:S(2)}) collective-permute-start(bf16[4,2,5,256]{3,2,1,0:T(8,128)(2,1)S(1)} %get-tuple-element.315), channel_id=1, source_target_pairs={{0,1},{1,0},{2,3},{3,2},{4,5},{5,4},{6,7},{7,6},{8,9},{9,8},{10,11... | collective-permute-start | bytes 61448 | tf_op jit(solution)/shard_map/ppermute | solution.py:68
  2.0 23.4 %collective-permute-start.1 = (bf16[4,2,5,256]{3,2,1,0:T(8,128)(2,1)S(1)}, bf16[4,2,5,256]{3,2,1,0:T(8,128)(2,1)S(1)}, u32[]{:S(2)}, u32[]{:S(2)}) collective-permute-start(bf16[4,2,5,256]{3,2,1,0:T(8,128)(2,1)S(1)} %get-tuple-element.314), channel_id=1, source_target_pairs={{1,0},{0,1},{3,2},{2,3},{5,4},{4,5},{7,6},{6,7},{9,8},{8,9},{11,10... | collective-permute-start | bytes 61448 | tf_op jit(solution)/shard_map/ppermute | solution.py:68
  2.1 31.8 %collective-permute-start.4 = (bf16[4,2,5,256]{3,2,1,0:T(8,128)(2,1)S(1)}, bf16[4,2,5,256]{3,2,1,0:T(8,128)(2,1)S(1)}, u32[]{:S(2)}, u32[]{:S(2)}) collective-permute-start(bf16[4,2,5,256]{3,2,1,0:T(8,128)(2,1)S(1)} %get-tuple-element.316), channel_id=1, source_target_pairs={{0,1},{1,0},{2,3},{3,2},{4,5},{5,4},{6,7},{7,6},{8,9},{9,8},{10,11... | collective-permute-start | bytes 61448 | tf_op jit(solution)/shard_map/ppermute | solution.py:68
  2.5 33.2 %collective-permute-start.5 = (bf16[4,2,5,256]{3,2,1,0:T(8,128)(2,1)S(1)}, bf16[4,2,5,256]{3,2,1,0:T(8,128)(2,1)S(1)}, u32[]{:S(2)}, u32[]{:S(2)}) collective-permute-start(bf16[4,2,5,256]{3,2,1,0:T(8,128)(2,1)S(1)} %get-tuple-element.313), channel_id=1, source_target_pairs={{1,0},{0,1},{3,2},{2,3},{5,4},{4,5},{7,6},{6,7},{9,8},{8,9},{11,10... | collective-permute-start | bytes 61448 | tf_op jit(solution)/shard_map/ppermute | solution.py:68
  2.6 11.7 %slice-start = ((s8[8388608]{0:T(1024)(128)(4,1)}), s8[4194304]{0:T(1024)(128)(4,1)S(1)}, s32[]{:S(2)}) async-start(s8[8388608]{0:T(1024)(128)(4,1)} %bitcast.165), calls=%async_computation.2 | async-start | bytes 8388608
  4.1 10.2 %slice-start.1 = ((s8[8388608]{0:T(1024)(128)(4,1)}), s8[4194304]{0:T(1024)(128)(4,1)S(1)}, s32[]{:S(2)}) async-start(s8[8388608]{0:T(1024)(128)(4,1)} %bitcast.165), calls=%async_computation.3 | async-start | bytes 8388608
  14.3 8.5 %copy-start.5 = (s32[4]{0:T(128)S(1)}, s32[4]{0:T(128)}, u32[]{:S(2)}) copy-start(s32[4]{0:T(128)} %param.14) | copy-start | bytes 52
  23.5 2.2 %copy-start.1 = (f32[2,256,4,2,256]{1,4,3,2,0:T(8,128)S(1)}, f32[2,256,4,2,256]{1,4,3,2,0:T(8,128)}, u32[]{:S(2)}) copy-start(f32[2,256,4,2,256]{1,4,3,2,0:T(8,128)} %fusion.10) | copy-start | bytes 12582916
  30.8 4.8 %copy-start = (f32[2,256,4,2,256]{1,4,3,2,0:T(8,128)S(1)}, f32[2,256,4,2,256]{1,4,3,2,0:T(8,128)}, u32[]{:S(2)}) copy-start(f32[2,256,4,2,256]{1,4,3,2,0:T(8,128)} %fusion.8) | copy-start | bytes 12582916
  30.8 13.1 %collective-permute-start.2 = (f32[2,4,2,256,5]{3,4,2,1,0:T(8,128)S(1)}, f32[2,4,2,256,5]{3,4,2,1,0:T(8,128)S(1)}, u32[]{:S(2)}, u32[]{:S(2)}) collective-permute-start(f32[2,4,2,256,5]{3,4,2,1,0:T(8,128)S(1)} %get-tuple-element.320), channel_id=1, source_target_pairs={{0,2},{2,0},{1,3},{3,1},{4,6},{6,4},{5,7},{7,5},{8,10},{10,8},{9,1... | collective-permute-start | bytes 245768 | tf_op jit(solution)/shard_map/ppermute | solution.py:68
  41.7 6.4 %collective-permute-start.3 = (f32[2,4,2,256,5]{3,4,2,1,0:T(8,128)S(1)}, f32[2,4,2,256,5]{3,4,2,1,0:T(8,128)S(1)}, u32[]{:S(2)}, u32[]{:S(2)}) collective-permute-start(f32[2,4,2,256,5]{3,4,2,1,0:T(8,128)S(1)} %get-tuple-element.319), channel_id=1, source_target_pairs={{2,0},{0,2},{3,1},{1,3},{6,4},{4,6},{7,5},{5,7},{10,8},{8,10},{11,... | collective-permute-start | bytes 245768 | tf_op jit(solution)/shard_map/ppermute | solution.py:68
  41.9 14.2 %collective-permute-start.6 = (f32[2,4,2,256,5]{3,4,2,1,0:T(8,128)}, f32[2,4,2,256,5]{3,4,2,1,0:T(8,128)}, u32[]{:S(2)}, u32[]{:S(2)}) collective-permute-start(f32[2,4,2,256,5]{3,4,2,1,0:T(8,128)} %get-tuple-element.318), channel_id=1, source_target_pairs={{0,2},{2,0},{1,3},{3,1},{4,6},{6,4},{5,7},{7,5},{8,10},{10,8},{9,1... | collective-permute-start | bytes 245768 | tf_op jit(solution)/shard_map/ppermute | solution.py:68
  43.7 14.3 %collective-permute-start.7 = (f32[2,4,2,256,5]{3,4,2,1,0:T(8,128)}, f32[2,4,2,256,5]{3,4,2,1,0:T(8,128)}, u32[]{:S(2)}, u32[]{:S(2)}) collective-permute-start(f32[2,4,2,256,5]{3,4,2,1,0:T(8,128)} %get-tuple-element.317), channel_id=1, source_target_pairs={{2,0},{0,2},{3,1},{1,3},{6,4},{4,6},{7,5},{5,7},{10,8},{8,10},{11,... | collective-permute-start | bytes 245768 | tf_op jit(solution)/shard_map/ppermute | solution.py:68
  51.2 17.2 %all-to-all-start = ((bf16[4,512,128]{2,1,0:T(8,128)(2,1)}), bf16[4,512,128]{2,1,0:T(8,128)(2,1)S(1)}, u32[]{:S(2)}, u32[]{:S(2)}) async-start(bf16[4,512,128]{2,1,0:T(8,128)(2,1)} %bitcast.18), calls=%async_computation | async-start | bytes 1048576 | tf_op jit(solution)/shard_map/all_to_all | solution.py:210
  61.1 11.6 %copy-start.2 = (bf16[6,4,256,64]{2,3,1,0:T(8,128)(2,1)S(1)}, bf16[6,4,256,64]{2,3,1,0:T(8,128)(2,1)}, u32[]{:S(2)}) copy-start(bf16[6,4,256,64]{2,3,1,0:T(8,128)(2,1)} %param.13) | copy-start | bytes 2359300
  68.5 15.8 %all-to-all-start.1 = ((bf16[4,512,128]{2,1,0:T(8,128)(2,1)}), bf16[4,512,128]{2,1,0:T(8,128)(2,1)}, u32[]{:S(2)}, u32[]{:S(2)}) async-start(bf16[4,512,128]{2,1,0:T(8,128)(2,1)} %bitcast.33), calls=%async_computation.1 | async-start | bytes 1048576 | tf_op jit(solution)/shard_map/all_to_all | solution.py:210
  97.8 20.3 %copy-start.4 = (s32[3,6,256]{2,1,0:T(8,128)S(1)}, s32[3,6,256]{2,1,0:T(8,128)}, u32[]{:S(2)}) copy-start(s32[3,6,256]{2,1,0:T(8,128)} %param.15) | copy-start | bytes 55300
  98.0 1.6 %collective-permute-start.8 = (f32[256,262]{0,1:T(8,128)S(1)}, f32[256,262]{0,1:T(8,128)S(1)}, u32[]{:S(2)}, u32[]{:S(2)}) collective-permute-start(f32[256,262]{0,1:T(8,128)S(1)} %pad_maximum_fusion.1), channel_id=1, source_target_pairs={{0,1},{1,0},{2,3},{3,2},{4,5},{5,4},{6,7},{7,6},{8,9},{9,8},{10,11... | collective-permute-start | bytes 804872 | tf_op jit(solution)/shard_map/ppermute | solution.py:53
  99.7 5.7 %collective-permute-start.9 = (f32[128,262]{0,1:T(8,128)S(1)}, f32[128,262]{0,1:T(8,128)S(1)}, u32[]{:S(2)}, u32[]{:S(2)}) collective-permute-start(f32[128,262]{0,1:T(8,128)S(1)} %slice_select_fusion), channel_id=1, source_target_pairs={{0,2},{2,0},{1,3},{3,1},{4,6},{6,4},{5,7},{7,5},{8,10},{10,8},{9,1... | collective-permute-start | bytes 402440 | tf_op jit(solution)/shard_map/ppermute | solution.py:43
  105.4 5.1 %collective-permute-start.10 = (f32[128,262]{0,1:T(8,128)S(1)}, f32[128,262]{0,1:T(8,128)S(1)}, u32[]{:S(2)}, u32[]{:S(2)}) collective-permute-start(f32[128,262]{0,1:T(8,128)S(1)} %fusion.77), channel_id=1, source_target_pairs={{0,4},{4,0},{8,12},{12,8},{1,5},{5,1},{9,13},{13,9},{2,6},{6,2},{1... | collective-permute-start | bytes 402440 | tf_op jit(solution)/shard_map/ppermute | solution.py:43
  110.5 7.5 %collective-permute-start.11 = (f32[128,262]{0,1:T(8,128)S(1)}, f32[128,262]{0,1:T(8,128)S(1)}, u32[]{:S(2)}, u32[]{:S(2)}) collective-permute-start(f32[128,262]{0,1:T(8,128)S(1)} %add.180), channel_id=1, source_target_pairs={{0,8},{4,12},{8,0},{12,4},{1,9},{5,13},{9,1},{13,5},{2,10},{6,14},... | collective-permute-start | bytes 402440 | tf_op jit(solution)/shard_map/ppermute | solution.py:43
  118.1 1.4 collective-permute-start.12
  158.1 2.1 %copy-start.3 = (f32[3,8,256]{2,1,0:T(8,128)S(1)}, f32[3,8,256]{2,1,0:T(8,128)}, u32[]{:S(2)}) copy-start(f32[3,8,256]{2,1,0:T(8,128)} %shard_map.59) | copy-start | bytes 73732

commit v8 on v6

--- a/solution.py
+++ b/solution.py
@@ -99,6 +99,21 @@
             direction = remain + (norm_next / (norm_now + epsilon)) * direction
             norm_now = norm_next
         out_ref[pass_index] = solution_all
+
+
+def banded_table(out_count, rows, first_taps, second_taps, guard):
+    shape = (2, out_count, rows)
+    which = lax.broadcasted_iota(jnp.int32, shape, 0)
+    out_index = lax.broadcasted_iota(jnp.int32, shape, 1)
+    position = lax.broadcasted_iota(jnp.int32, shape, 2)
+    tap_at = position - 4 * out_index + guard
+    table = jnp.zeros(shape, jnp.float32)
+    for tap_index in range(13):
+        value = jnp.where(
+            which == 0, np.float32(first_taps[tap_index]), np.float32(second_taps[tap_index])
+        )
+        table = jnp.where(tap_at == tap_index, value, table)
+    return table
 
 
 def kernel(spread):
@@ -153,23 +168,42 @@
     span_table = filter_table(cells_z, narrow_taps, broad_taps, guard, (0, 1, 2))
     stream_table = filter_table(cells_x, narrow_taps, broad_taps, guard, (1, 0, 2))
     highest = lax.Precision.HIGHEST
-    along_stream = (
-        jnp.einsum(
-            "cpxz,sxm->scpmz",
-            fields.astype(jnp.float32),
-            stream_table[:, width : width + cells_x],
-            precision=highest,
-        )
-        + jnp.einsum(
-            "cpxz,sxm->scpmz", top.astype(jnp.float32), stream_table[:, :width], precision=highest
-        )
-        + jnp.einsum(
-            "cpxz,sxm->scpmz",
-            bottom.astype(jnp.float32),
-            stream_table[:, width + cells_x :],
-            precision=highest,
-        )
-    )
+    block = 128
+    if cells_x % block == 0:
+        block_count_x = cells_x // block
+        blocked = fields.reshape(chan_dev, plane_count, block_count_x, block, cells_z)
+        before = jnp.concatenate(
+            [top[:, :, None, 1:width], blocked[:, :, :-1, block - width + 1 :]], axis=2
+        )
+        after = jnp.concatenate([blocked[:, :, 1:, :width], bottom[:, :, None]], axis=2)
+        spare = jnp.zeros((chan_dev, plane_count, block_count_x, 7, cells_z), fields.dtype)
+        windows = jnp.concatenate([before, blocked, after, spare], axis=3)
+        window_rows = windows.shape[3]
+        window_table = banded_table(block // 4, window_rows, narrow_taps, broad_taps, guard)
+        along_stream = jnp.einsum(
+            "cpbrz,sir->scpbiz", windows.astype(jnp.float32), window_table, precision=highest
+        ).reshape(2, chan_dev, plane_count, coarse_x, cells_z)
+    else:
+        along_stream = (
+            jnp.einsum(
+                "cpxz,sxm->scpmz",
+                fields.astype(jnp.float32),
+                stream_table[:, width : width + cells_x],
+                precision=highest,
+            )
+            + jnp.einsum(
+                "cpxz,sxm->scpmz",
+                top.astype(jnp.float32),
+                stream_table[:, :width],
+                precision=highest,
+            )
+            + jnp.einsum(
+                "cpxz,sxm->scpmz",
+                bottom.astype(jnp.float32),
+                stream_table[:, width + cells_x :],
+                precision=highest,
+            )
+        )
     left, right = neighbour_edges(along_stream, "slab", 4, width)
     filtered = (
         jnp.einsum(

time: 158 us -> 162 us (1.025)
  local copies, waits for them, and re-layouts: 19.2 us -> 33.1 us
  matrix products: 47.6 us -> 37.9 us
    dot_general x3 -> x1, matrix products: 23.9 us -> 9.53 us  [local(): jnp.einsum('cpbrz,sir->scpbiz', windows.astype(jnp.float32), window_table...]
    unnamed x12 -> x14, local copies, waits for them, and re-layouts: 2.95 us -> 9.31 us
    dot_general x1, matrix products: 5.53 us -> 10.5 us  [local(): jnp.einsum('scpmz,zsn->scpmn', along_stream, span_table[width:width + cel...]
    slice x2 -> x1, local copies, waits for them, and re-layouts: 0.93 us -> 5.25 us  [neighbour_edges(): leading = lax.slice_in_dim(array, 0, width, axis=dim)]
    slice x0 -> x3, local copies, waits for them, and re-layouts: none -> 3.13 us  [the longest x1 1.16 us: local(): blocked[:, :, :-1, block - width + 1:]]
  transfers between devices with their start and end apart: 10 -> 10, of which waited for: 8 -> 7; matrix products, arithmetic and copies ran while one was open for 23% -> 16% of each run, Pallas kernels for 0% -> 0%
where the time goes in v8:
time: 162 us; the launch traced here: 161 us
  waiting for transfers between devices  44.4 us (27%)
  matrix products  37.9 us (23%)
  local copies, waits for them, and re-layouts  33.1 us (20%)
  blocking collectives  18 us (11%)
  starting transfers between devices  9.48 us (6%)
  Pallas kernels  8.4 us (5%)
  other arithmetic  8.36 us (5%)
    all_to_all x1, waiting for transfers between devices, local(): sets = lax.all_to_all(sets, 'cols', 0, 0, tiled=True)  18.5 us
    all_gather x1, blocking collectives, local(): misfit = lax.all_gather(misfit, 'cols', axis=1, tiled=True)  18 us
    ppermute x3, waiting for transfers between devices, tree_sum(): value = value + lax.ppermute(value, axis, partner)  17.5 us
    dot_general x1, matrix products, local(): jnp.einsum('scpmz,zsn->scpmn', along_stream, span_table[width:width + cel...  10.5 us
    dot_general x1, matrix products, local(): jnp.einsum('cpbrz,sir->scpbiz', windows.astype(jnp.float32), window_table...  9.53 us
    unnamed x14, local copies, waits for them, and re-layouts  9.31 us
    pallas_call x1, Pallas kernels, local(): pl.pallas_call(conjugate_passes, out_shape=jax.ShapeDtypeStruct((PASSES,...  8.4 us
    ppermute x4, waiting for transfers between devices, neighbour_edges(): return (lax.ppermute(last, axis, up), lax.ppermute(leading, axis, down))  6.23 us
  transfers between devices with their start and end apart: 10, of which 7 were waited for; matrix products, arithmetic and copies ran while one was open for 16% of the time, Pallas kernels for 0%

profile of v8, /device:TPU:0, one launch (start us, length us, event | category | flops | bytes accessed | tf_op | source)
XLA Modules:
  0.0 160.9 jit_solution(5999608467551533450)
XLA Ops:
  5.5 9.5 %fusion.7 = f32[2,32,4,4,8,256]{5,1,4,3,2,0:T(8,128)S(1)} fusion(bf16[4,4,1,5,256]{4,3,2,1,0:T(8,128)(2,1)S(1)} %bitcast.115, bf16[4,4,7,5,256]{4,3,2,1,0:T(8,128)(2,1)S(1)} %slice.124, bf16[4,4,8,128,256]{4,3,2,1,0:T(8,128)(2,1)} %bitcast.114, bf16[4,4,7,4,256]{4,3,2,1,0:T(4,128)(2,1)S(1)} %slice.123, ...), kind=kOutput, calls=%fused_computation.19 | convolution fusion | flops 3680759808 | bytes 17367516 | tf_op jit(solution)/shard_map/cpbrz,sir->scpbiz/dot_general | solution.py:183
  15.0 5.2 %fusion.123 = (f32[2,4,4,256,5]{4,3,2,1,0:T(8,128)}, f32[2,4,4,256,5]{4,3,2,1,0:T(8,128)}) fusion(f32[2,4,4,256,256]{4,3,2,1,0:T(8,128)S(1)} %bitcast.105), kind=kLoop, calls=%fused_computation.149 | loop fusion | bytes 655360 | tf_op jit(solution)/shard_map/slice | solution.py:67
  20.8 2.8 %copy.74 = f32[2,4,4,256,5]{3,4,2,1,0:T(8,128)S(1)} copy(f32[2,4,4,256,5]{4,3,2,1,0:T(8,128)} %get-tuple-element.340) | data formatting | bytes 327680
  23.6 3.0 %collective-permute-start.2 = (f32[2,4,4,256,5]{3,4,2,1,0:T(8,128)S(1)}, f32[2,4,4,256,5]{3,4,2,1,0:T(8,128)S(1)}, u32[]{:S(2)}, u32[]{:S(2)}) collective-permute-start(f32[2,4,4,256,5]{3,4,2,1,0:T(8,128)S(1)} %copy.74), channel_id=1, source_target_pairs={{0,2},{2,0},{1,3},{3,1},{4,6},{6,4},{5,7},{7,5},{8,10},{10,8},{9,1... | collective-permute-start | bytes 491528 | tf_op jit(solution)/shard_map/ppermute | solution.py:68
  26.6 10.5 %fusion.31 = f32[2,4,4,256,64]{3,4,2,1,0:T(8,128)S(1)} fusion(f32[2,4,4,256,256]{4,3,2,1,0:T(8,128)} %bitcast.106, f32[266,2,64]{0,2,1:T(8,128)S(1)} %select_select_fusion), kind=kOutput, calls=%fused_computation.56 | convolution fusion | flops 1610612736 | bytes 10616832 | tf_op jit(solution)/shard_map/scpmz,zsn->scpmn/dot_general | solution.py:209
  37.2 3.0 %copy.75 = f32[2,4,4,256,5]{3,4,2,1,0:T(8,128)S(1)} copy(f32[2,4,4,256,5]{4,3,2,1,0:T(8,128)} %get-tuple-element.339) | data formatting | bytes 327680
  40.3 1.8 %fusion.32 = f32[2,4,4,256,64]{3,4,2,1,0:T(8,128)S(1)} fusion(f32[2,4,4,256,5]{3,4,2,1,0:T(8,128)S(1)} %collective-permute-done.2, f32[266,2,64]{0,2,1:T(8,128)S(1)} %select_select_fusion), kind=kOutput, calls=%fused_computation.59 | convolution fusion | flops 31457280 | bytes 2424832 | tf_op jit(solution)/shard_map/scpmz,zsn->scpmn/dot_general | solution.py:215
  42.0 6.2 %collective-permute-done.3 = f32[2,4,4,256,5]{3,4,2,1,0:T(8,128)S(1)} collective-permute-done((f32[2,4,4,256,5]{3,4,2,1,0:T(8,128)S(1)}, f32[2,4,4,256,5]{3,4,2,1,0:T(8,128)S(1)}, u32[]{:S(2)}, u32[]{:S(2)}) %collective-permute-start.3) | collective-permute-done | bytes 163872 | tf_op jit(solution)/shard_map/ppermute | solution.py:68
  48.3 2.0 %add_add_fusion = f32[2,4,4,256,64]{3,4,2,1,0:T(8,128)S(1)} fusion(f32[2,4,4,256,64]{3,4,2,1,0:T(8,128)S(1)} %fusion.31, f32[2,4,4,256,64]{3,4,2,1,0:T(8,128)S(1)} %fusion.32, f32[2,4,4,256,5]{3,4,2,1,0:T(8,128)S(1)} %collective-permute-done.3, f32[266,2,64]{0,2,1:T(8,128)S(1)} %select_select_fusion), kind=kOutput, calls=%fused_computation.30 | convolution fusion | flops 32505856 | bytes 6619136 | tf_op jit(solution)/shard_map/scpmz,zsn->scpmn/dot_general | solution.py:216
  52.2 1.5 copy.50
  55.6 4.9 %all-to-all-start = ((bf16[4,1024,128]{2,1,0:T(8,128)(2,1)}), bf16[4,1024,128]{2,1,0:T(8,128)(2,1)S(1)}, u32[]{:S(2)}, u32[]{:S(2)}) async-start(bf16[4,1024,128]{2,1,0:T(8,128)(2,1)} %bitcast.17), calls=%async_computation | async-start | bytes 2097152 | tf_op jit(solution)/shard_map/all_to_all | solution.py:236
  60.5 1.2 multiply_convert_fusion.2
  61.7 1.8 %copy.53 = bf16[6,4,256,64]{3,2,1,0:T(8,128)(2,1)S(1)} copy(bf16[6,4,256,64]{2,3,1,0:T(8,128)(2,1)} %multiply_convert_fusion.2) | data formatting | bytes 1572864 | tf_op jit(solution)/shard_map/convert_element_type | solution.py:226
  63.5 1.5 reshape_reshape.3
  66.8 18.5 %all-to-all-done = bf16[4,1024,128]{2,1,0:T(8,128)(2,1)S(1)} async-done(((bf16[4,1024,128]{2,1,0:T(8,128)(2,1)}), bf16[4,1024,128]{2,1,0:T(8,128)(2,1)S(1)}, u32[]{:S(2)}, u32[]{:S(2)}) %all-to-all-start) | async-done | bytes 1048608 | tf_op jit(solution)/shard_map/all_to_all | solution.py:236
  86.1 11.7 %while.32 = (s32[]{:T(128)}, f32[256,256]{1,0:T(8,128)S(1)}, f32[256,6]{0,1:T(8,128)S(1)}, bf16[16,128,128]{2,0,1:T(8,128)(2,1)S(1)}, bf16[16,128,128]{2,0,1:T(8...) while((s32[]{:T(128)}, f32[256,256]{1,0:T(8,128)S(1)}, ...), condition=%wide.region_1.2_spmd.clone, body=%wide.region_0.1_spmd.clone.sunk | while | flops 551816192 | bytes 8204454 | solution.py:260
  87.5 1.5 fusion.151
  90.4 1.5 fusion.151
  93.4 1.5 fusion.151
  96.3 1.5 fusion.151
  98.0 1.5 collective-permute-done.4
  100.2 5.1 %collective-permute-done.5 = f32[128,262]{0,1:T(8,128)S(1)} collective-permute-done((f32[128,262]{0,1:T(8,128)S(1)}, f32[128,262]{0,1:T(8,128)S(1)}, u32[]{:S(2)}, u32[]{:S(2)}) %collective-permute-start.5) | collective-permute-done | bytes 134176 | tf_op jit(solution)/shard_map/ppermute | solution.py:43
  105.4 5.0 %collective-permute-done.6 = f32[128,262]{0,1:T(8,128)S(1)} collective-permute-done((f32[128,262]{0,1:T(8,128)S(1)}, f32[128,262]{0,1:T(8,128)S(1)}, u32[]{:S(2)}, u32[]{:S(2)}) %collective-permute-start.6) | collective-permute-done | bytes 134176 | tf_op jit(solution)/shard_map/ppermute | solution.py:43
  110.6 7.4 %collective-permute-done.7 = f32[128,262]{0,1:T(8,128)S(1)} collective-permute-done((f32[128,262]{0,1:T(8,128)S(1)}, f32[128,262]{0,1:T(8,128)S(1)}, u32[]{:S(2)}, u32[]{:S(2)}) %collective-permute-start.7) | collective-permute-done | bytes 134176 | tf_op jit(solution)/shard_map/ppermute | solution.py:43
  119.4 2.4 %gather_fusion = f32[256]{0:T(256)S(1)} fusion(f32[256,256]{0,1:T(8,128)S(1)} %slice.136, s32[256]{0:T(256)S(1)} %bitcast.107), kind=kCustom, calls=%fused_computation | custom fusion | bytes 4096 | tf_op jit(solution)/shard_map/jit(diagonal)/cond/branch_0_fun/gather | solution.py:269
  123.4 8.4 %shard_map.59 = f32[3,8,256]{2,1,0:T(8,128)} custom-call(f32[256,256]{1,0:T(8,128)} %copy.58.gram_ref, f32[8,256]{1,0:T(8,128)} %scatter.6.target_ref, f32[3,8,256]{2,1,0:T(8,128)} %scatter.9.mask_ref), custom_call_target="tpu_custom_call" | custom-call | tf_op jit(solution)/shard_map/pallas_call | solution.py:280
  132.5 7.6 %while.31 = (s32[]{:T(128)}, bf16[6,128,128]{2,1,0:T(8,128)(2,1)S(1)}, bf16[6,128,128]{2,0,1:T(8,128)(2,1)}, bf16[16,128,128]{2,0,1:T(8,128)(2,1)S(1)}, bf16[16,...) while((s32[]{:T(128)}, ...), condition=%wide.region_3.4_spmd, body=%wide.region_2.3_spmd.sunk | while | flops 14884870 | bytes 5721247 | solution.py:300
  133.2 1.2 fusion.145
  135.1 1.2 fusion.145
  137.0 1.2 fusion.145
  140.1 18.0 %all_gather.3 = bf16[6,512,128]{2,1,0:T(8,128)(2,1)S(1)} all-gather(bf16[6,128,128]{2,1,0:T(8,128)(2,1)S(1)} %get-tuple-element.247), channel_id=1, replica_groups=mesh['groups'=2,'cols'=4,'slab'=2,'rep'=2] {'cols'}, dimensions={1}, use_global_device_ids=true | all-gather | bytes 983040 | tf_op jit(solution)/shard_map/all_gather | solution.py:303
  158.8 1.4 copy.63
  (96 shorter events, 27.3 us)
Async XLA Ops:
  1.5 3.9 %collective-permute-start = (bf16[4,4,5,256]{3,2,1,0:T(8,128)(2,1)S(1)}, bf16[4,4,5,256]{3,2,1,0:T(8,128)(2,1)S(1)}, u32[]{:S(2)}, u32[]{:S(2)}) collective-permute-start(bf16[4,4,5,256]{3,2,1,0:T(8,128)(2,1)S(1)} %get-tuple-element.341), channel_id=1, source_target_pairs={{0,1},{1,0},{2,3},{3,2},{4,5},{5,4},{6,7},{7,6},{8,9},{9,8},{10,11... | collective-permute-start | bytes 122888 | tf_op jit(solution)/shard_map/ppermute | solution.py:68
  2.0 3.4 %collective-permute-start.1 = (bf16[4,4,5,256]{3,2,1,0:T(8,128)(2,1)S(1)}, bf16[4,4,5,256]{3,2,1,0:T(8,128)(2,1)S(1)}, u32[]{:S(2)}, u32[]{:S(2)}) collective-permute-start(bf16[4,4,5,256]{3,2,1,0:T(8,128)(2,1)S(1)} %get-tuple-element.342), channel_id=1, source_target_pairs={{1,0},{0,1},{3,2},{2,3},{5,4},{4,5},{7,6},{6,7},{9,8},{8,9},{11,10... | collective-permute-start | bytes 122888 | tf_op jit(solution)/shard_map/ppermute | solution.py:68
  15.0 5.8 %copy-start = (f32[2,32,4,4,8,256]{5,1,4,3,2,0:T(8,128)}, f32[2,32,4,4,8,256]{5,1,4,3,2,0:T(8,128)S(1)}, u32[]{:S(2)}) copy-start(f32[2,32,4,4,8,256]{5,1,4,3,2,0:T(8,128)S(1)} %fusion.7) | copy-start | bytes 25165828
  23.6 16.6 %collective-permute-start.2 = (f32[2,4,4,256,5]{3,4,2,1,0:T(8,128)S(1)}, f32[2,4,4,256,5]{3,4,2,1,0:T(8,128)S(1)}, u32[]{:S(2)}, u32[]{:S(2)}) collective-permute-start(f32[2,4,4,256,5]{3,4,2,1,0:T(8,128)S(1)} %copy.74), channel_id=1, source_target_pairs={{0,2},{2,0},{1,3},{3,1},{4,6},{6,4},{5,7},{7,5},{8,10},{10,8},{9,1... | collective-permute-start | bytes 491528 | tf_op jit(solution)/shard_map/ppermute | solution.py:68
  40.2 8.1 %collective-permute-start.3 = (f32[2,4,4,256,5]{3,4,2,1,0:T(8,128)S(1)}, f32[2,4,4,256,5]{3,4,2,1,0:T(8,128)S(1)}, u32[]{:S(2)}, u32[]{:S(2)}) collective-permute-start(f32[2,4,4,256,5]{3,4,2,1,0:T(8,128)S(1)} %copy.75), channel_id=1, source_target_pairs={{2,0},{0,2},{3,1},{1,3},{6,4},{4,6},{7,5},{5,7},{10,8},{8,10},{11,... | collective-permute-start | bytes 491528 | tf_op jit(solution)/shard_map/ppermute | solution.py:68
  54.2 6.2 %copy-start.1 = (bf16[6,4,256,64]{2,3,1,0:T(8,128)(2,1)S(1)}, bf16[6,4,256,64]{2,3,1,0:T(8,128)(2,1)}, u32[]{:S(2)}) copy-start(bf16[6,4,256,64]{2,3,1,0:T(8,128)(2,1)} %param.13) | copy-start | bytes 2359300
  55.6 29.7 %all-to-all-start = ((bf16[4,1024,128]{2,1,0:T(8,128)(2,1)}), bf16[4,1024,128]{2,1,0:T(8,128)(2,1)S(1)}, u32[]{:S(2)}, u32[]{:S(2)}) async-start(bf16[4,1024,128]{2,1,0:T(8,128)(2,1)} %bitcast.17), calls=%async_computation | async-start | bytes 2097152 | tf_op jit(solution)/shard_map/all_to_all | solution.py:236
  86.1 32.0 %copy-start.3 = (s32[3,6,256]{2,1,0:T(8,128)S(1)}, s32[3,6,256]{2,1,0:T(8,128)}, u32[]{:S(2)}) copy-start(s32[3,6,256]{2,1,0:T(8,128)} %param.15) | copy-start | bytes 55300
  97.9 1.6 %collective-permute-start.4 = (f32[256,262]{0,1:T(8,128)S(1)}, f32[256,262]{0,1:T(8,128)S(1)}, u32[]{:S(2)}, u32[]{:S(2)}) collective-permute-start(f32[256,262]{0,1:T(8,128)S(1)} %pad_maximum_fusion), channel_id=1, source_target_pairs={{0,1},{1,0},{2,3},{3,2},{4,5},{5,4},{6,7},{7,6},{8,9},{9,8},{10,11... | collective-permute-start | bytes 804872 | tf_op jit(solution)/shard_map/ppermute | solution.py:53
  99.6 5.7 %collective-permute-start.5 = (f32[128,262]{0,1:T(8,128)S(1)}, f32[128,262]{0,1:T(8,128)S(1)}, u32[]{:S(2)}, u32[]{:S(2)}) collective-permute-start(f32[128,262]{0,1:T(8,128)S(1)} %slice_select_fusion), channel_id=1, source_target_pairs={{0,2},{2,0},{1,3},{3,1},{4,6},{6,4},{5,7},{7,5},{8,10},{10,8},{9,1... | collective-permute-start | bytes 402440 | tf_op jit(solution)/shard_map/ppermute | solution.py:43
  105.3 5.1 %collective-permute-start.6 = (f32[128,262]{0,1:T(8,128)S(1)}, f32[128,262]{0,1:T(8,128)S(1)}, u32[]{:S(2)}, u32[]{:S(2)}) collective-permute-start(f32[128,262]{0,1:T(8,128)S(1)} %fusion.133), channel_id=1, source_target_pairs={{0,4},{4,0},{8,12},{12,8},{1,5},{5,1},{9,13},{13,9},{2,6},{6,2},{1... | collective-permute-start | bytes 402440 | tf_op jit(solution)/shard_map/ppermute | solution.py:43
  110.4 7.5 %collective-permute-start.7 = (f32[128,262]{0,1:T(8,128)S(1)}, f32[128,262]{0,1:T(8,128)S(1)}, u32[]{:S(2)}, u32[]{:S(2)}) collective-permute-start(f32[128,262]{0,1:T(8,128)S(1)} %add.144), channel_id=1, source_target_pairs={{0,8},{4,12},{8,0},{12,4},{1,9},{5,13},{9,1},{13,5},{2,10},{6,14},... | collective-permute-start | bytes 402440 | tf_op jit(solution)/shard_map/ppermute | solution.py:43
  118.0 1.4 collective-permute-start.8
  140.1 20.1 %copy-start.2 = (f32[3,8,256]{2,1,0:T(8,128)S(1)}, f32[3,8,256]{2,1,0:T(8,128)}, u32[]{:S(2)}) copy-start(f32[3,8,256]{2,1,0:T(8,128)} %shard_map.59) | copy-start | bytes 73732

commit v9 on v6

--- a/solution.py
+++ b/solution.py
@@ -266,7 +266,15 @@
     misfit = lax.fori_loop(
         0, block_count, misfit_step, jnp.zeros((STRESS, chunk_rows, lanes), jnp.bfloat16)
     )
-    misfit = lax.all_gather(misfit, "cols", axis=1, tiled=True)
+    pieces = [misfit] + [
+        lax.ppermute(misfit, "cols", [(i, (i - k) % col_devices) for i in range(col_devices)])
+        for k in range(1, col_devices)
+    ]
+    doubled = jnp.stack(pieces + pieces)
+    misfit = lax.dynamic_slice_in_dim(
+        doubled, (col_devices - column_index) % col_devices, col_devices, 0
+    )
+    misfit = jnp.moveaxis(misfit, 0, 1).reshape(STRESS, col_devices * chunk_rows, lanes)
     misfit = misfit.reshape(STRESS, plane_count, coarse_x, coarse_z)
     return (coefficients, misfit)
 

time: 158 us -> 163 us (1.032)
  waiting for transfers between devices: 44.2 us -> 64.6 us
  blocking collectives: 18 us -> 0 us
  starting transfers between devices: 9.49 us -> 11.6 us
    ppermute x0 -> x3, waiting for transfers between devices: none -> 20.5 us  [local(): lax.ppermute(misfit, 'cols', [(i, (i - k) % col_devices) for i in range(c...]
    all_gather x1 -> x0, blocking collectives: 18 us -> none  [local(): misfit = lax.all_gather(misfit, 'cols', axis=1, tiled=True)]
    ppermute x0 -> x3, starting transfers between devices: none -> 2.14 us  [local(): lax.ppermute(misfit, 'cols', [(i, (i - k) % col_devices) for i in range(c...]
  transfers between devices with their start and end apart: 10 -> 13, of which waited for: 8 -> 10; matrix products, arithmetic and copies ran while one was open for 23% -> 22% of each run, Pallas kernels for 0% -> 0%
where the time goes in v9:
time: 163 us
  waiting for transfers between devices  64.6 us (40%)
  matrix products  47.6 us (29%)
  local copies, waits for them, and re-layouts  19.8 us (12%)
  starting transfers between devices  11.6 us (7%)
  other arithmetic  9.2 us (6%)
  Pallas kernels  8.4 us (5%)
    ppermute x3, waiting for transfers between devices, local(): lax.ppermute(misfit, 'cols', [(i, (i - k) % col_devices) for i in range(c...  20.5 us
    all_to_all x1, waiting for transfers between devices, local(): sets = lax.all_to_all(sets, 'cols', 0, 0, tiled=True)  18.5 us
    ppermute x3, waiting for transfers between devices, tree_sum(): value = value + lax.ppermute(value, axis, partner)  17.5 us
    dot_general x1, matrix products, local(): jnp.einsum('cpxz,sxm->scpmz', fields.astype(jnp.float32), stream_table[:,...  16 us
    pallas_call x1, Pallas kernels, local(): pl.pallas_call(conjugate_passes, out_shape=jax.ShapeDtypeStruct((PASSES,...  8.4 us
    ppermute x4, waiting for transfers between devices, neighbour_edges(): return (lax.ppermute(last, axis, up), lax.ppermute(leading, axis, down))  5.99 us
    dot_general x4, matrix products, gram_step(): jnp.einsum('iqr,kqr->ik', all_terms, weighted_piece, preferred_element_ty...  5.92 us
    dot_general x1, matrix products, local(): jnp.einsum('scpmz,zsn->scpmn', along_stream, span_table[width:width + cel...  5.53 us
  transfers between devices with their start and end apart: 13, of which 10 were waited for; matrix products, arithmetic and copies ran while one was open for 22% of the time, Pallas kernels for 0%

profile of v9, /device:TPU:0, one launch (start us, length us, event | category | flops | bytes accessed | tf_op | source)
XLA Modules:
  0.0 162.5 jit_solution(4991205581538058773)
XLA Ops:
  2.2 1.5 select_select_fusion
  3.7 16.0 %fusion.8 = f32[2,256,4,4,256]{1,4,3,2,0:T(8,128)S(1)} fusion(bf16[4,4,1024,256]{3,2,1,0:T(8,128)(2,1)} %param.12, f32[2,1034,256]{2,1,0:T(8,128)S(1)} %select_select_fusion), kind=kOutput, calls=%fused_computation.18 | convolution fusion | flops 25769803776 | bytes 18874368 | tf_op jit(solution)/shard_map/cpxz,sxm->scpmz/dot_general | solution.py:157
  20.0 3.5 %fusion.39 = f32[2,256,4,4,256]{1,4,3,2,0:T(8,128)S(1)} fusion(bf16[4,4,5,256]{3,2,1,0:T(8,128)(2,1)S(1)} %collective-permute-done, f32[2,1034,256]{2,1,0:T(8,128)S(1)} %select_select_fusion), kind=kOutput, calls=%fused_computation.77 | convolution fusion | flops 125829120 | bytes 8470528 | tf_op jit(solution)/shard_map/cpxz,sxm->scpmz/dot_general | solution.py:163
  23.5 4.4 %add_bitcast_fusion = f32[2,4,4,256,256]{3,4,2,1,0:T(8,128)S(1)} fusion(f32[2,256,4,4,256]{1,4,3,2,0:T(8,128)S(1)} %fusion.8, f32[2,256,4,4,256]{1,4,3,2,0:T(8,128)S(1)} %fusion.39, bf16[4,4,5,256]{3,2,1,0:T(8,128)(2,1)S(1)} %collective-permute-done.1, f32[2,1034,256]{2,1,0:T(8,128)S(1)} %select_select_fusion), kind=kOutput, calls=%fused_computation.20 | convolution fusion | flops 130023424 | bytes 25247744 | tf_op jit(solution)/shard_map/cpxz,sxm->scpmz/dot_general | solution.py:166
  28.0 3.0 %collective-permute-start.2 = (f32[2,4,4,256,5]{3,4,2,1,0:T(8,128)S(1)}, f32[2,4,4,256,5]{3,4,2,1,0:T(8,128)S(1)}, u32[]{:S(2)}, u32[]{:S(2)}) collective-permute-start(f32[2,4,4,256,5]{3,4,2,1,0:T(8,128)S(1)} %get-tuple-element.326), channel_id=1, source_target_pairs={{0,2},{2,0},{1,3},{3,1},{4,6},{6,4},{5,7},{7,5},{8,10},{10,8},{9,1... | collective-permute-start | bytes 491528 | tf_op jit(solution)/shard_map/ppermute | solution.py:68
  31.0 5.5 %fusion.36 = f32[2,4,4,256,64]{3,4,2,1,0:T(8,128)S(1)} fusion(f32[2,4,4,256,256]{3,4,2,1,0:T(8,128)S(1)} %add_bitcast_fusion, f32[266,2,64]{0,2,1:T(8,128)S(1)} %select_select_fusion.1), kind=kOutput, calls=%fused_computation.72 | convolution fusion | flops 1610612736 | bytes 10616832 | tf_op jit(solution)/shard_map/scpmz,zsn->scpmn/dot_general | solution.py:175
  37.5 2.0 %fusion.37 = f32[2,4,4,256,64]{3,4,2,1,0:T(8,128)S(1)} fusion(f32[2,4,4,256,5]{3,4,2,1,0:T(8,128)S(1)} %collective-permute-done.2, f32[266,2,64]{0,2,1:T(8,128)S(1)} %select_select_fusion.1), kind=kOutput, calls=%fused_computation.75 | convolution fusion | flops 31457280 | bytes 2424832 | tf_op jit(solution)/shard_map/scpmz,zsn->scpmn/dot_general | solution.py:181
  39.5 5.0 %collective-permute-done.3 = f32[2,4,4,256,5]{3,4,2,1,0:T(8,128)S(1)} collective-permute-done((f32[2,4,4,256,5]{3,4,2,1,0:T(8,128)S(1)}, f32[2,4,4,256,5]{3,4,2,1,0:T(8,128)S(1)}, u32[]{:S(2)}, u32[]{:S(2)}) %collective-permute-start.3) | collective-permute-done | bytes 163872 | tf_op jit(solution)/shard_map/ppermute | solution.py:68
  44.6 2.1 %add_add_fusion = f32[2,4,4,256,64]{3,4,2,1,0:T(8,128)S(1)} fusion(f32[2,4,4,256,64]{3,4,2,1,0:T(8,128)S(1)} %fusion.36, f32[2,4,4,256,64]{3,4,2,1,0:T(8,128)S(1)} %fusion.37, f32[2,4,4,256,5]{3,4,2,1,0:T(8,128)S(1)} %collective-permute-done.3, f32[266,2,64]{0,2,1:T(8,128)S(1)} %select_select_fusion.1), kind=kOutput, calls=%fused_computation.37 | convolution fusion | flops 32505856 | bytes 6619136 | tf_op jit(solution)/shard_map/scpmz,zsn->scpmn/dot_general | solution.py:182
  48.6 1.5 copy.32
  52.0 4.9 %all-to-all-start = ((bf16[4,1024,128]{2,1,0:T(8,128)(2,1)}), bf16[4,1024,128]{2,1,0:T(8,128)(2,1)S(1)}, u32[]{:S(2)}, u32[]{:S(2)}) async-start(bf16[4,1024,128]{2,1,0:T(8,128)(2,1)} %bitcast.18), calls=%async_computation | async-start | bytes 2097152 | tf_op jit(solution)/shard_map/all_to_all | solution.py:202
  56.9 1.2 multiply_convert_fusion.2
  58.1 1.8 %copy.35 = bf16[6,4,256,64]{3,2,1,0:T(8,128)(2,1)S(1)} copy(bf16[6,4,256,64]{2,3,1,0:T(8,128)(2,1)} %multiply_convert_fusion.2) | data formatting | bytes 1572864 | tf_op jit(solution)/shard_map/convert_element_type | solution.py:192
  59.9 1.5 reshape_reshape.6
  63.2 18.5 %all-to-all-done = bf16[4,1024,128]{2,1,0:T(8,128)(2,1)S(1)} async-done(((bf16[4,1024,128]{2,1,0:T(8,128)(2,1)}), bf16[4,1024,128]{2,1,0:T(8,128)(2,1)S(1)}, u32[]{:S(2)}, u32[]{:S(2)}) %all-to-all-start) | async-done | bytes 1048608 | tf_op jit(solution)/shard_map/all_to_all | solution.py:202
  82.5 11.7 %while.32 = (s32[]{:T(128)}, f32[256,256]{1,0:T(8,128)S(1)}, f32[256,6]{0,1:T(8,128)S(1)}, bf16[16,128,128]{2,0,1:T(8,128)(2,1)S(1)}, bf16[16,128,128]{2,0,1:T(8...) while((s32[]{:T(128)}, f32[256,256]{1,0:T(8,128)S(1)}, ...), condition=%wide.region_1.2_spmd.clone, body=%wide.region_0.1_spmd.clone.sunk | while | flops 551816192 | bytes 8204454 | solution.py:226
  84.0 1.5 fusion.81
  86.9 1.5 fusion.81
  89.8 1.5 fusion.81
  92.7 1.5 fusion.81
  94.5 1.5 collective-permute-done.4
  96.6 5.1 %collective-permute-done.5 = f32[128,262]{0,1:T(8,128)S(1)} collective-permute-done((f32[128,262]{0,1:T(8,128)S(1)}, f32[128,262]{0,1:T(8,128)S(1)}, u32[]{:S(2)}, u32[]{:S(2)}) %collective-permute-start.5) | collective-permute-done | bytes 134176 | tf_op jit(solution)/shard_map/ppermute | solution.py:43
  101.9 5.0 %collective-permute-done.6 = f32[128,262]{0,1:T(8,128)S(1)} collective-permute-done((f32[128,262]{0,1:T(8,128)S(1)}, f32[128,262]{0,1:T(8,128)S(1)}, u32[]{:S(2)}, u32[]{:S(2)}) %collective-permute-start.6) | collective-permute-done | bytes 134176 | tf_op jit(solution)/shard_map/ppermute | solution.py:43
  107.0 7.4 %collective-permute-done.7 = f32[128,262]{0,1:T(8,128)S(1)} collective-permute-done((f32[128,262]{0,1:T(8,128)S(1)}, f32[128,262]{0,1:T(8,128)S(1)}, u32[]{:S(2)}, u32[]{:S(2)}) %collective-permute-start.7) | collective-permute-done | bytes 134176 | tf_op jit(solution)/shard_map/ppermute | solution.py:43
  115.9 2.4 %gather_fusion = f32[256]{0:T(256)S(1)} fusion(f32[256,256]{0,1:T(8,128)S(1)} %slice.136, s32[256]{0:T(256)S(1)} %bitcast.134), kind=kCustom, calls=%fused_computation | custom fusion | bytes 4096 | tf_op jit(solution)/shard_map/jit(diagonal)/cond/branch_0_fun/gather | solution.py:235
  119.8 8.4 %shard_map.59 = f32[3,8,256]{2,1,0:T(8,128)} custom-call(f32[256,256]{1,0:T(8,128)} %copy.40.gram_ref, f32[8,256]{1,0:T(8,128)} %scatter.6.target_ref, f32[3,8,256]{2,1,0:T(8,128)} %scatter.9.mask_ref), custom_call_target="tpu_custom_call" | custom-call | tf_op jit(solution)/shard_map/pallas_call | solution.py:246
  129.0 7.5 %while.31 = (s32[]{:T(128)}, bf16[6,128,128]{2,0,1:T(8,128)(2,1)S(1)}, bf16[6,128,128]{2,0,1:T(8,128)(2,1)}, bf16[16,128,128]{2,0,1:T(8,128)(2,1)S(1)}, bf16[16,...) while((s32[]{:T(128)}, ...), condition=%wide.region_3.4_spmd, body=%wide.region_2.3_spmd.sunk | while | flops 14884870 | bytes 5623963 | solution.py:266
  129.6 1.2 fusion.75
  136.4 1.5 collective-permute-start.9
  139.3 7.3 %collective-permute-done.9 = bf16[6,128,128]{2,0,1:T(8,128)(2,1)S(1)} collective-permute-done((bf16[6,128,128]{2,0,1:T(8,128)(2,1)S(1)}, bf16[6,128,128]{2,0,1:T(8,128)(2,1)S(1)}, u32[]{:S(2)}, u32[]{:S(2)}) %collective-permute-start.9) | collective-permute-done | bytes 196640 | tf_op jit(solution)/shard_map/ppermute | solution.py:270
  146.6 13.1 %collective-permute-done.10 = bf16[6,128,128]{2,0,1:T(8,128)(2,1)S(1)} collective-permute-done((bf16[6,128,128]{2,0,1:T(8,128)(2,1)S(1)}, bf16[6,128,128]{2,0,1:T(8,128)(2,1)S(1)}, u32[]{:S(2)}, u32[]{:S(2)}) %collective-permute-start.10) | collective-permute-done | bytes 196640 | tf_op jit(solution)/shard_map/ppermute | solution.py:270
  161.1 1.4 copy.45
  (104 shorter events, 28.5 us)
Async XLA Ops:
  1.5 18.5 %collective-permute-start = (bf16[4,4,5,256]{3,2,1,0:T(8,128)(2,1)S(1)}, bf16[4,4,5,256]{3,2,1,0:T(8,128)(2,1)S(1)}, u32[]{:S(2)}, u32[]{:S(2)}) collective-permute-start(bf16[4,4,5,256]{3,2,1,0:T(8,128)(2,1)S(1)} %get-tuple-element.328), channel_id=1, source_target_pairs={{0,1},{1,0},{2,3},{3,2},{4,5},{5,4},{6,7},{7,6},{8,9},{9,8},{10,11... | collective-permute-start | bytes 122888 | tf_op jit(solution)/shard_map/ppermute | solution.py:68
  2.0 21.5 %collective-permute-start.1 = (bf16[4,4,5,256]{3,2,1,0:T(8,128)(2,1)S(1)}, bf16[4,4,5,256]{3,2,1,0:T(8,128)(2,1)S(1)}, u32[]{:S(2)}, u32[]{:S(2)}) collective-permute-start(bf16[4,4,5,256]{3,2,1,0:T(8,128)(2,1)S(1)} %get-tuple-element.327), channel_id=1, source_target_pairs={{1,0},{0,1},{3,2},{2,3},{5,4},{4,5},{7,6},{6,7},{9,8},{8,9},{11,10... | collective-permute-start | bytes 122888 | tf_op jit(solution)/shard_map/ppermute | solution.py:68
  3.7 16.3 %copy-start.3 = (s32[4]{0:T(128)S(1)}, s32[4]{0:T(128)}, u32[]{:S(2)}) copy-start(s32[4]{0:T(128)} %param.14) | copy-start | bytes 52
  28.0 9.5 %collective-permute-start.2 = (f32[2,4,4,256,5]{3,4,2,1,0:T(8,128)S(1)}, f32[2,4,4,256,5]{3,4,2,1,0:T(8,128)S(1)}, u32[]{:S(2)}, u32[]{:S(2)}) collective-permute-start(f32[2,4,4,256,5]{3,4,2,1,0:T(8,128)S(1)} %get-tuple-element.326), channel_id=1, source_target_pairs={{0,2},{2,0},{1,3},{3,1},{4,6},{6,4},{5,7},{7,5},{8,10},{10,8},{9,1... | collective-permute-start | bytes 491528 | tf_op jit(solution)/shard_map/ppermute | solution.py:68
  36.5 8.1 %collective-permute-start.3 = (f32[2,4,4,256,5]{3,4,2,1,0:T(8,128)S(1)}, f32[2,4,4,256,5]{3,4,2,1,0:T(8,128)S(1)}, u32[]{:S(2)}, u32[]{:S(2)}) collective-permute-start(f32[2,4,4,256,5]{3,4,2,1,0:T(8,128)S(1)} %get-tuple-element.325), channel_id=1, source_target_pairs={{2,0},{0,2},{3,1},{1,3},{6,4},{4,6},{7,5},{5,7},{10,8},{8,10},{11,... | collective-permute-start | bytes 491528 | tf_op jit(solution)/shard_map/ppermute | solution.py:68
  50.9 6.0 %copy-start = (bf16[6,4,256,64]{2,3,1,0:T(8,128)(2,1)S(1)}, bf16[6,4,256,64]{2,3,1,0:T(8,128)(2,1)}, u32[]{:S(2)}) copy-start(bf16[6,4,256,64]{2,3,1,0:T(8,128)(2,1)} %param.13) | copy-start | bytes 2359300
  52.0 29.7 %all-to-all-start = ((bf16[4,1024,128]{2,1,0:T(8,128)(2,1)}), bf16[4,1024,128]{2,1,0:T(8,128)(2,1)S(1)}, u32[]{:S(2)}, u32[]{:S(2)}) async-start(bf16[4,1024,128]{2,1,0:T(8,128)(2,1)} %bitcast.18), calls=%async_computation | async-start | bytes 2097152 | tf_op jit(solution)/shard_map/all_to_all | solution.py:202
  94.2 20.3 %copy-start.2 = (s32[3,6,256]{2,1,0:T(8,128)S(1)}, s32[3,6,256]{2,1,0:T(8,128)}, u32[]{:S(2)}) copy-start(s32[3,6,256]{2,1,0:T(8,128)} %param.15) | copy-start | bytes 55300
  94.4 1.6 collective-permute-start.4
  96.1 5.7 %collective-permute-start.5 = (f32[128,262]{0,1:T(8,128)S(1)}, f32[128,262]{0,1:T(8,128)S(1)}, u32[]{:S(2)}, u32[]{:S(2)}) collective-permute-start(f32[128,262]{0,1:T(8,128)S(1)} %slice_select_fusion), channel_id=1, source_target_pairs={{0,2},{2,0},{1,3},{3,1},{4,6},{6,4},{5,7},{7,5},{8,10},{10,8},{9,1... | collective-permute-start | bytes 402440 | tf_op jit(solution)/shard_map/ppermute | solution.py:43
  101.8 5.1 %collective-permute-start.6 = (f32[128,262]{0,1:T(8,128)S(1)}, f32[128,262]{0,1:T(8,128)S(1)}, u32[]{:S(2)}, u32[]{:S(2)}) collective-permute-start(f32[128,262]{0,1:T(8,128)S(1)} %fusion.63), channel_id=1, source_target_pairs={{0,4},{4,0},{8,12},{12,8},{1,5},{5,1},{9,13},{13,9},{2,6},{6,2},{1... | collective-permute-start | bytes 402440 | tf_op jit(solution)/shard_map/ppermute | solution.py:43
  106.9 7.5 %collective-permute-start.7 = (f32[128,262]{0,1:T(8,128)S(1)}, f32[128,262]{0,1:T(8,128)S(1)}, u32[]{:S(2)}, u32[]{:S(2)}) collective-permute-start(f32[128,262]{0,1:T(8,128)S(1)} %add.166), channel_id=1, source_target_pairs={{0,8},{4,12},{8,0},{12,4},{1,9},{5,13},{9,1},{13,5},{2,10},{6,14},... | collective-permute-start | bytes 402440 | tf_op jit(solution)/shard_map/ppermute | solution.py:43
  114.4 1.4 collective-permute-start.8
  129.0 9.6 %copy-start.1 = (f32[3,8,256]{2,1,0:T(8,128)S(1)}, f32[3,8,256]{2,1,0:T(8,128)}, u32[]{:S(2)}) copy-start(f32[3,8,256]{2,1,0:T(8,128)} %shard_map.59) | copy-start | bytes 73732
  136.4 10.1 %collective-permute-start.9 = (bf16[6,128,128]{2,0,1:T(8,128)(2,1)S(1)}, bf16[6,128,128]{2,0,1:T(8,128)(2,1)S(1)}, u32[]{:S(2)}, u32[]{:S(2)}) collective-permute-start(bf16[6,128,128]{2,0,1:T(8,128)(2,1)S(1)} %get-tuple-element.247), channel_id=1, source_target_pairs={{0,12},{4,0},{8,4},{12,8},{1,13},{5,1},{9,5},{13,9},{2,14},{6,2},{... | collective-permute-start | bytes 589832 | tf_op jit(solution)/shard_map/ppermute | solution.py:270
  137.9 21.8 %collective-permute-start.10 = (bf16[6,128,128]{2,0,1:T(8,128)(2,1)S(1)}, bf16[6,128,128]{2,0,1:T(8,128)(2,1)S(1)}, u32[]{:S(2)}, u32[]{:S(2)}) collective-permute-start(bf16[6,128,128]{2,0,1:T(8,128)(2,1)S(1)} %get-tuple-element.247), channel_id=1, source_target_pairs={{0,8},{4,12},{8,0},{12,4},{1,9},{5,13},{9,1},{13,5},{2,10},{6,14},... | collective-permute-start | bytes 589832 | tf_op jit(solution)/shard_map/ppermute | solution.py:270
  137.9 21.9 %collective-permute-start.11 = (bf16[6,128,128]{2,0,1:T(8,128)(2,1)S(1)}, bf16[6,128,128]{2,0,1:T(8,128)(2,1)S(1)}, u32[]{:S(2)}, u32[]{:S(2)}) collective-permute-start(bf16[6,128,128]{2,0,1:T(8,128)(2,1)S(1)} %get-tuple-element.247), channel_id=1, source_target_pairs={{0,4},{4,8},{8,12},{12,0},{1,5},{5,9},{9,13},{13,1},{2,6},{6,10},{... | collective-permute-start | bytes 589832 | tf_op jit(solution)/shard_map/ppermute | solution.py:270

commit v10 on v6

--- a/solution.py
+++ b/solution.py
@@ -205,7 +205,7 @@
     narrow_all, broad_all = sets[0], sets[1]
     weighted = weighted.reshape(STRESS, col_devices, chunk_rows, lanes)
     weighted = lax.dynamic_index_in_dim(weighted, column_index, 1, keepdims=False)
-    block_rows = math.gcd(chunk_rows, 32)
+    block_rows = chunk_rows
     block_count = chunk_rows // block_rows
 
     def gram_step(block_index, carry):

time: 158 us -> 155 us (0.981)
  matrix products: 47.6 us -> 42.8 us
  waiting for transfers between devices: 44.2 us -> 46.8 us
    dot_general x4 -> x1, matrix products: 5.92 us -> 2.25 us  [gram_step(): jnp.einsum('iqr,kqr->ik', all_terms, weighted_piece, preferred_element_ty...]
    all_to_all x1, waiting for transfers between devices: 18.5 us -> 21.1 us  [local(): sets = lax.all_to_all(sets, 'cols', 0, 0, tiled=True)]
    convert_element_type x0 -> x3, local copies, waits for them, and re-layouts: none -> 2.26 us  [the longest x1 1.61 us: library(): broad_part.astype(jnp.float32)[None, :]]
    convert_element_type x8 -> x1, other arithmetic: 4.52 us -> 4.06 us  [library(): product.astype(jnp.bfloat16)]
    dot_general x4 -> x1, matrix products: 4.92 us -> 4.6 us  [misfit_step(): jnp.einsum('ki,iqr->kqr', final_weights, all_terms, preferred_element_typ...]
  transfers between devices with their start and end apart: 10 -> 10, of which waited for: 8 -> 8; matrix products, arithmetic and copies ran while one was open for 23% -> 21% of each run, Pallas kernels for 0% -> 0%
where the time goes in v10:
time: 155 us; the launch traced here: 154 us
  waiting for transfers between devices  46.8 us (30%)
  matrix products  42.8 us (28%)
  local copies, waits for them, and re-layouts  20.2 us (13%)
  blocking collectives  18 us (12%)
  starting transfers between devices  9.44 us (6%)
  Pallas kernels  8.41 us (5%)
  other arithmetic  7.75 us (5%)
    all_to_all x1, waiting for transfers between devices, local(): sets = lax.all_to_all(sets, 'cols', 0, 0, tiled=True)  21.1 us
    all_gather x1, blocking collectives, local(): misfit = lax.all_gather(misfit, 'cols', axis=1, tiled=True)  18 us
    ppermute x3, waiting for transfers between devices, tree_sum(): value = value + lax.ppermute(value, axis, partner)  17.5 us
    dot_general x1, matrix products, local(): jnp.einsum('cpxz,sxm->scpmz', fields.astype(jnp.float32), stream_table[:,...  16 us
    pallas_call x1, Pallas kernels, local(): pl.pallas_call(conjugate_passes, out_shape=jax.ShapeDtypeStruct((PASSES,...  8.41 us
    ppermute x4, waiting for transfers between devices, neighbour_edges(): return (lax.ppermute(last, axis, up), lax.ppermute(leading, axis, down))  5.99 us
    dot_general x1, matrix products, local(): jnp.einsum('scpmz,zsn->scpmn', along_stream, span_table[width:width + cel...  5.53 us
    all_to_all x1, starting transfers between devices, local(): sets = lax.all_to_all(sets, 'cols', 0, 0, tiled=True)  4.86 us
  transfers between devices with their start and end apart: 10, of which 8 were waited for; matrix products, arithmetic and copies ran while one was open for 21% of the time, Pallas kernels for 0%

profile of v10, /device:TPU:0, one launch (start us, length us, event | category | flops | bytes accessed | tf_op | source)
XLA Modules:
  0.0 154.5 jit_solution(9146818852837158305)
XLA Ops:
  0.6 0.9 fusion.51
  2.2 1.5 select_select_fusion
  3.7 16.0 %fusion = f32[2,256,4,4,256]{1,4,3,2,0:T(8,128)S(1)} fusion(bf16[4,4,1024,256]{3,2,1,0:T(8,128)(2,1)} %param.8, f32[2,1034,256]{2,1,0:T(8,128)S(1)} %select_select_fusion), kind=kOutput, calls=%fused_computation.2 | convolution fusion | flops 25769803776 | bytes 18874368 | tf_op jit(solution)/shard_map/cpxz,sxm->scpmz/dot_general | solution.py:157
  20.0 3.5 %fusion.34 = f32[2,256,4,4,256]{1,4,3,2,0:T(8,128)S(1)} fusion(bf16[4,4,5,256]{3,2,1,0:T(8,128)(2,1)S(1)} %collective-permute-done, f32[2,1034,256]{2,1,0:T(8,128)S(1)} %select_select_fusion), kind=kOutput, calls=%fused_computation.59 | convolution fusion | flops 125829120 | bytes 8470528 | tf_op jit(solution)/shard_map/cpxz,sxm->scpmz/dot_general | solution.py:163
  23.5 4.4 %add_bitcast_fusion = f32[2,4,4,256,256]{3,4,2,1,0:T(8,128)S(1)} fusion(f32[2,256,4,4,256]{1,4,3,2,0:T(8,128)S(1)} %fusion, f32[2,256,4,4,256]{1,4,3,2,0:T(8,128)S(1)} %fusion.34, bf16[4,4,5,256]{3,2,1,0:T(8,128)(2,1)S(1)} %collective-permute-done.1, f32[2,1034,256]{2,1,0:T(8,128)S(1)} %select_select_fusion), kind=kOutput, calls=%fused_computation.4 | convolution fusion | flops 130023424 | bytes 25247744 | tf_op jit(solution)/shard_map/cpxz,sxm->scpmz/dot_general | solution.py:166
  28.0 3.0 %collective-permute-start.2 = (f32[2,4,4,256,5]{3,4,2,1,0:T(8,128)S(1)}, f32[2,4,4,256,5]{3,4,2,1,0:T(8,128)S(1)}, u32[]{:S(2)}, u32[]{:S(2)}) collective-permute-start(f32[2,4,4,256,5]{3,4,2,1,0:T(8,128)S(1)} %get-tuple-element.73), channel_id=1, source_target_pairs={{0,2},{2,0},{1,3},{3,1},{4,6},{6,4},{5,7},{7,5},{8,10},{10,8},{9,1... | collective-permute-start | bytes 491528 | tf_op jit(solution)/shard_map/ppermute | solution.py:68
  31.0 5.5 %fusion.31 = f32[2,4,4,256,64]{3,4,2,1,0:T(8,128)S(1)} fusion(f32[2,4,4,256,256]{3,4,2,1,0:T(8,128)S(1)} %add_bitcast_fusion, f32[266,2,64]{0,2,1:T(8,128)S(1)} %select_select_fusion.1), kind=kOutput, calls=%fused_computation.54 | convolution fusion | flops 1610612736 | bytes 10616832 | tf_op jit(solution)/shard_map/scpmz,zsn->scpmn/dot_general | solution.py:175
  36.6 0.9 collective-permute-done.2
  37.5 2.0 %fusion.32 = f32[2,4,4,256,64]{3,4,2,1,0:T(8,128)S(1)} fusion(f32[2,4,4,256,5]{3,4,2,1,0:T(8,128)S(1)} %collective-permute-done.2, f32[266,2,64]{0,2,1:T(8,128)S(1)} %select_select_fusion.1), kind=kOutput, calls=%fused_computation.57 | convolution fusion | flops 31457280 | bytes 2424832 | tf_op jit(solution)/shard_map/scpmz,zsn->scpmn/dot_general | solution.py:181
  39.5 5.0 %collective-permute-done.3 = f32[2,4,4,256,5]{3,4,2,1,0:T(8,128)S(1)} collective-permute-done((f32[2,4,4,256,5]{3,4,2,1,0:T(8,128)S(1)}, f32[2,4,4,256,5]{3,4,2,1,0:T(8,128)S(1)}, u32[]{:S(2)}, u32[]{:S(2)}) %collective-permute-start.3) | collective-permute-done | bytes 163872 | tf_op jit(solution)/shard_map/ppermute | solution.py:68
  44.6 2.1 %add_add_fusion = f32[2,4,4,256,64]{3,4,2,1,0:T(8,128)S(1)} fusion(f32[2,4,4,256,64]{3,4,2,1,0:T(8,128)S(1)} %fusion.31, f32[2,4,4,256,64]{3,4,2,1,0:T(8,128)S(1)} %fusion.32, f32[2,4,4,256,5]{3,4,2,1,0:T(8,128)S(1)} %collective-permute-done.3, f32[266,2,64]{0,2,1:T(8,128)S(1)} %select_select_fusion.1), kind=kOutput, calls=%fused_computation.21 | convolution fusion | flops 32505856 | bytes 6619136 | tf_op jit(solution)/shard_map/scpmz,zsn->scpmn/dot_general | solution.py:182
  46.8 0.9 slice.167
  48.6 1.5 copy.29
  51.0 1.1 copy.31
  52.0 4.9 %all-to-all-start = ((bf16[4,1024,128]{2,1,0:T(8,128)(2,1)}), bf16[4,1024,128]{2,1,0:T(8,128)(2,1)S(1)}, u32[]{:S(2)}, u32[]{:S(2)}) async-start(bf16[4,1024,128]{2,1,0:T(8,128)(2,1)} %bitcast.15), calls=%async_computation | async-start | bytes 2097152 | tf_op jit(solution)/shard_map/all_to_all | solution.py:202
  58.1 1.5 reshape_reshape.3
  59.6 0.9 constant_dynamic-slice_fusion.1
  60.6 21.1 %all-to-all-done = bf16[4,1024,128]{2,1,0:T(8,128)(2,1)S(1)} async-done(((bf16[4,1024,128]{2,1,0:T(8,128)(2,1)}), bf16[4,1024,128]{2,1,0:T(8,128)(2,1)S(1)}, u32[]{:S(2)}, u32[]{:S(2)}) %all-to-all-start) | async-done | bytes 1048608 | tf_op jit(solution)/shard_map/all_to_all | solution.py:202
  82.7 1.6 %copy.33 = f32[16,128,128]{2,0,1:T(8,128)} copy(f32[16,128,128]{2,1,0:T(8,128)S(1)} %bitcast_convert_fusion) | data formatting | bytes 2097152 | tf_op jit(solution)/shard_map/while/body/eval_jaxpr/convert_element_type | solution.py:129
  84.3 4.1 %multiply_convert_fusion = bf16[16,16,128,128]{3,1,0,2:T(8,128)(2,1)S(1)} fusion(f32[16,128,128]{2,0,1:T(8,128)} %copy.33, f32[16,128,128]{2,0,1:T(8,128)S(1)} %copy.32), kind=kLoop, calls=%fused_computation.1 | loop fusion | flops 8388608 | bytes 10485760 | tf_op jit(solution)/shard_map/while/body/eval_jaxpr/convert_element_type | solution.py:131
  88.4 2.4 %convolution_bitcast_fusion = f32[256,256]{0,1:T(8,128)S(1)} fusion(bf16[256,128,128]{2,0,1:T(8,128)(2,1)S(1)} %bitcast.83), kind=kOutput, calls=%fused_computation.25 | convolution fusion | flops 2147483648 | bytes 8650752 | tf_op jit(solution)/shard_map/while/body/eval_jaxpr/iqr,jqr->ij/dot_general | solution.py:218
  90.7 0.9 copy-done
  91.6 2.3 %convolution_bitcast_fusion.1 = f32[256,6]{0,1:T(8,128)S(1)} fusion(bf16[256,128,128]{2,0,1:T(8,128)(2,1)S(1)} %bitcast.84, bf16[6,1,128,128]{3,2,1,0:T(8,128)(2,1)S(1)} %constant_dynamic-slice_fusion.1), kind=kOutput, calls=%fused_computation.26 | convolution fusion | flops 50331648 | bytes 8591360 | tf_op jit(solution)/shard_map/while/body/eval_jaxpr/iqr,kqr->ik/dot_general | solution.py:221
  94.6 1.5 collective-permute-done.4
  97.5 5.1 %collective-permute-done.5 = f32[128,262]{0,1:T(8,128)S(1)} collective-permute-done((f32[128,262]{0,1:T(8,128)S(1)}, f32[128,262]{0,1:T(8,128)S(1)}, u32[]{:S(2)}, u32[]{:S(2)}) %collective-permute-start.5) | collective-permute-done | bytes 134176 | tf_op jit(solution)/shard_map/ppermute | solution.py:43
  102.7 5.0 %collective-permute-done.6 = f32[128,262]{0,1:T(8,128)S(1)} collective-permute-done((f32[128,262]{0,1:T(8,128)S(1)}, f32[128,262]{0,1:T(8,128)S(1)}, u32[]{:S(2)}, u32[]{:S(2)}) %collective-permute-start.6) | collective-permute-done | bytes 134176 | tf_op jit(solution)/shard_map/ppermute | solution.py:43
  107.8 7.4 %collective-permute-done.7 = f32[128,262]{0,1:T(8,128)S(1)} collective-permute-done((f32[128,262]{0,1:T(8,128)S(1)}, f32[128,262]{0,1:T(8,128)S(1)}, u32[]{:S(2)}, u32[]{:S(2)}) %collective-permute-start.7) | collective-permute-done | bytes 134176 | tf_op jit(solution)/shard_map/ppermute | solution.py:43
  116.7 2.4 %gather_fusion = f32[256]{0:T(256)S(1)} fusion(f32[256,256]{0,1:T(8,128)S(1)} %slice.136, s32[256]{0:T(256)S(1)} %bitcast.86), kind=kCustom, calls=%fused_computation | custom fusion | bytes 4096 | tf_op jit(solution)/shard_map/jit(diagonal)/cond/branch_0_fun/gather | solution.py:235
  120.7 8.4 %shard_map.59 = f32[3,8,256]{2,1,0:T(8,128)} custom-call(f32[256,256]{1,0:T(8,128)} %copy.36.gram_ref, f32[8,256]{1,0:T(8,128)} %scatter.6.target_ref, f32[3,8,256]{2,1,0:T(8,128)} %scatter.9.mask_ref), custom_call_target="tpu_custom_call" | custom-call | tf_op jit(solution)/shard_map/pallas_call | solution.py:246
  129.1 4.6 %fusion.15 = bf16[6,128,128]{2,0,1:T(8,128)(2,1)S(1)} fusion(bf16[256,128,128]{2,0,1:T(8,128)(2,1)} %bitcast.85, bf16[6,1,128,128]{3,2,1,0:T(8,128)(2,1)S(1)} %constant_dynamic-slice_fusion.1, f32[3,8,256]{2,1,0:T(8,128)} %shard_map.59, f32[256]{0:T(256)S(1)} %add_rsqrt_fusion), kind=kOutput, calls=%fused_computation.24 | convolution fusion | flops 50629632 | bytes 8791040 | tf_op jit(solution)/shard_map/while/body/eval_jaxpr/ki,iqr->kqr/dot_general | solution.py:259
  133.7 18.0 %all_gather.3 = bf16[6,512,128]{2,1,0:T(8,128)(2,1)S(1)} all-gather(bf16[6,128,128]{2,1,0:T(8,128)(2,1)S(1)} %copy.37), channel_id=1, replica_groups=mesh['groups'=2,'cols'=4,'slab'=2,'rep'=2] {'cols'}, dimensions={1}, use_global_device_ids=true | all-gather | bytes 983040 | tf_op jit(solution)/shard_map/all_gather | solution.py:269
  152.4 1.4 copy.38
  (64 shorter events, 11.7 us)
Async XLA Ops:
  1.5 18.5 %collective-permute-start = (bf16[4,4,5,256]{3,2,1,0:T(8,128)(2,1)S(1)}, bf16[4,4,5,256]{3,2,1,0:T(8,128)(2,1)S(1)}, u32[]{:S(2)}, u32[]{:S(2)}) collective-permute-start(bf16[4,4,5,256]{3,2,1,0:T(8,128)(2,1)S(1)} %get-tuple-element.75), channel_id=1, source_target_pairs={{0,1},{1,0},{2,3},{3,2},{4,5},{5,4},{6,7},{7,6},{8,9},{9,8},{10,11... | collective-permute-start | bytes 122888 | tf_op jit(solution)/shard_map/ppermute | solution.py:68
  2.0 21.5 %collective-permute-start.1 = (bf16[4,4,5,256]{3,2,1,0:T(8,128)(2,1)S(1)}, bf16[4,4,5,256]{3,2,1,0:T(8,128)(2,1)S(1)}, u32[]{:S(2)}, u32[]{:S(2)}) collective-permute-start(bf16[4,4,5,256]{3,2,1,0:T(8,128)(2,1)S(1)} %get-tuple-element.74), channel_id=1, source_target_pairs={{1,0},{0,1},{3,2},{2,3},{5,4},{4,5},{7,6},{6,7},{9,8},{8,9},{11,10... | collective-permute-start | bytes 122888 | tf_op jit(solution)/shard_map/ppermute | solution.py:68
  3.7 16.3 %copy-start.5 = (s32[4]{0:T(128)S(1)}, s32[4]{0:T(128)}, u32[]{:S(2)}) copy-start(s32[4]{0:T(128)} %param.10) | copy-start | bytes 52
  28.0 9.5 %collective-permute-start.2 = (f32[2,4,4,256,5]{3,4,2,1,0:T(8,128)S(1)}, f32[2,4,4,256,5]{3,4,2,1,0:T(8,128)S(1)}, u32[]{:S(2)}, u32[]{:S(2)}) collective-permute-start(f32[2,4,4,256,5]{3,4,2,1,0:T(8,128)S(1)} %get-tuple-element.73), channel_id=1, source_target_pairs={{0,2},{2,0},{1,3},{3,1},{4,6},{6,4},{5,7},{7,5},{8,10},{10,8},{9,1... | collective-permute-start | bytes 491528 | tf_op jit(solution)/shard_map/ppermute | solution.py:68
  36.5 8.1 %collective-permute-start.3 = (f32[2,4,4,256,5]{3,4,2,1,0:T(8,128)S(1)}, f32[2,4,4,256,5]{3,4,2,1,0:T(8,128)S(1)}, u32[]{:S(2)}, u32[]{:S(2)}) collective-permute-start(f32[2,4,4,256,5]{3,4,2,1,0:T(8,128)S(1)} %get-tuple-element.72), channel_id=1, source_target_pairs={{2,0},{0,2},{3,1},{1,3},{6,4},{4,6},{7,5},{5,7},{10,8},{8,10},{11,... | collective-permute-start | bytes 491528 | tf_op jit(solution)/shard_map/ppermute | solution.py:68
  50.9 6.0 %copy-start.1 = (bf16[6,4,256,64]{2,3,1,0:T(8,128)(2,1)S(1)}, bf16[6,4,256,64]{2,3,1,0:T(8,128)(2,1)}, u32[]{:S(2)}) copy-start(bf16[6,4,256,64]{2,3,1,0:T(8,128)(2,1)} %param.9) | copy-start | bytes 2359300
  52.0 29.7 %all-to-all-start = ((bf16[4,1024,128]{2,1,0:T(8,128)(2,1)}), bf16[4,1024,128]{2,1,0:T(8,128)(2,1)S(1)}, u32[]{:S(2)}, u32[]{:S(2)}) async-start(bf16[4,1024,128]{2,1,0:T(8,128)(2,1)} %bitcast.15), calls=%async_computation | async-start | bytes 2097152 | tf_op jit(solution)/shard_map/all_to_all | solution.py:202
  88.4 3.3 %copy-start = (bf16[16,16,128,128]{3,1,0,2:T(8,128)(2,1)}, bf16[16,16,128,128]{3,1,0,2:T(8,128)(2,1)S(1)}, u32[]{:S(2)}) copy-start(bf16[16,16,128,128]{3,1,0,2:T(8,128)(2,1)S(1)} %multiply_convert_fusion) | copy-start | bytes 25165828
  93.9 0.6 copy-start.3
  94.5 20.8 %copy-start.4 = (s32[3,6,256]{2,1,0:T(8,128)S(1)}, s32[3,6,256]{2,1,0:T(8,128)}, u32[]{:S(2)}) copy-start(s32[3,6,256]{2,1,0:T(8,128)} %param.11) | copy-start | bytes 55300
  94.5 1.6 %collective-permute-start.4 = (f32[256,262]{0,1:T(8,128)S(1)}, f32[256,262]{0,1:T(8,128)S(1)}, u32[]{:S(2)}, u32[]{:S(2)}) collective-permute-start(f32[256,262]{0,1:T(8,128)S(1)} %pad_maximum_fusion), channel_id=1, source_target_pairs={{0,1},{1,0},{2,3},{3,2},{4,5},{5,4},{6,7},{7,6},{8,9},{9,8},{10,11... | collective-permute-start | bytes 804872 | tf_op jit(solution)/shard_map/ppermute | solution.py:53
  96.9 5.7 %collective-permute-start.5 = (f32[128,262]{0,1:T(8,128)S(1)}, f32[128,262]{0,1:T(8,128)S(1)}, u32[]{:S(2)}, u32[]{:S(2)}) collective-permute-start(f32[128,262]{0,1:T(8,128)S(1)} %slice_select_fusion), channel_id=1, source_target_pairs={{0,2},{2,0},{1,3},{3,1},{4,6},{6,4},{5,7},{7,5},{8,10},{10,8},{9,1... | collective-permute-start | bytes 402440 | tf_op jit(solution)/shard_map/ppermute | solution.py:43
  102.6 5.1 %collective-permute-start.6 = (f32[128,262]{0,1:T(8,128)S(1)}, f32[128,262]{0,1:T(8,128)S(1)}, u32[]{:S(2)}, u32[]{:S(2)}) collective-permute-start(f32[128,262]{0,1:T(8,128)S(1)} %fusion.60), channel_id=1, source_target_pairs={{0,4},{4,0},{8,12},{12,8},{1,5},{5,1},{9,13},{13,9},{2,6},{6,2},{1... | collective-permute-start | bytes 402440 | tf_op jit(solution)/shard_map/ppermute | solution.py:43
  107.7 7.5 %collective-permute-start.7 = (f32[128,262]{0,1:T(8,128)S(1)}, f32[128,262]{0,1:T(8,128)S(1)}, u32[]{:S(2)}, u32[]{:S(2)}) collective-permute-start(f32[128,262]{0,1:T(8,128)S(1)} %add.115), channel_id=1, source_target_pairs={{0,8},{4,12},{8,0},{12,4},{1,9},{5,13},{9,1},{13,5},{2,10},{6,14},... | collective-permute-start | bytes 402440 | tf_op jit(solution)/shard_map/ppermute | solution.py:43
  115.2 1.4 collective-permute-start.8
  151.7 2.1 %copy-start.2 = (f32[3,8,256]{2,1,0:T(8,128)S(1)}, f32[3,8,256]{2,1,0:T(8,128)}, u32[]{:S(2)}) copy-start(f32[3,8,256]{2,1,0:T(8,128)} %shard_map.59) | copy-start | bytes 73732

commit v11 on v10

--- a/solution.py
+++ b/solution.py
@@ -71,14 +71,22 @@
 def conjugate_passes(gram_ref, target_ref, mask_ref, out_ref):
     gram = gram_ref[...]
     target = target_ref[...]
+    gram_high = gram.astype(jnp.bfloat16)
+    gram_low = (gram - gram_high.astype(jnp.float32)).astype(jnp.bfloat16)
+
+    def product_with(left, right):
+        return lax.dot_general(
+            left, right, (((1,), (1,)), ((), ())), preferred_element_type=jnp.float32
+        )
 
     def apply_normal(vector, active):
-        product = lax.dot_general(
-            active * vector,
-            gram,
-            (((1,), (1,)), ((), ())),
-            precision=lax.Precision.HIGHEST,
-            preferred_element_type=jnp.float32,
+        masked = active * vector
+        masked_high = masked.astype(jnp.bfloat16)
+        masked_low = (masked - masked_high.astype(jnp.float32)).astype(jnp.bfloat16)
+        product = (
+            product_with(masked_high, gram_high)
+            + product_with(masked_low, gram_high)
+            + product_with(masked_high, gram_low)
         )
         return active * product + ridge_weight * vector
 

time: 155 us -> 152 us (0.981)
  Pallas kernels: 8.41 us -> 5.98 us
    pallas_call x1, Pallas kernels: 8.41 us -> 5.98 us  [local(): pl.pallas_call(conjugate_passes, out_shape=jax.ShapeDtypeStruct((PASSES,...]
  transfers between devices with their start and end apart: 10 -> 10, of which waited for: 8 -> 8; matrix products, arithmetic and copies ran while one was open for 21% -> 22% of each run, Pallas kernels for 0% -> 0%
where the time goes in v11:
time: 152 us
  waiting for transfers between devices  46.8 us (31%)
  matrix products  42.8 us (28%)
  local copies, waits for them, and re-layouts  20.2 us (13%)
  blocking collectives  18 us (12%)
  starting transfers between devices  9.44 us (6%)
  other arithmetic  7.75 us (5%)
  Pallas kernels  5.98 us (4%)
    all_to_all x1, waiting for transfers between devices, local(): sets = lax.all_to_all(sets, 'cols', 0, 0, tiled=True)  21.1 us
    all_gather x1, blocking collectives, local(): misfit = lax.all_gather(misfit, 'cols', axis=1, tiled=True)  18 us
    ppermute x3, waiting for transfers between devices, tree_sum(): value = value + lax.ppermute(value, axis, partner)  17.5 us
    dot_general x1, matrix products, local(): jnp.einsum('cpxz,sxm->scpmz', fields.astype(jnp.float32), stream_table[:,...  16 us
    ppermute x4, waiting for transfers between devices, neighbour_edges(): return (lax.ppermute(last, axis, up), lax.ppermute(leading, axis, down))  5.99 us
    pallas_call x1, Pallas kernels, local(): pl.pallas_call(conjugate_passes, out_shape=jax.ShapeDtypeStruct((PASSES,...  5.98 us
    dot_general x1, matrix products, local(): jnp.einsum('scpmz,zsn->scpmn', along_stream, span_table[width:width + cel...  5.53 us
    all_to_all x1, starting transfers between devices, local(): sets = lax.all_to_all(sets, 'cols', 0, 0, tiled=True)  4.86 us
  transfers between devices with their start and end apart: 10, of which 8 were waited for; matrix products, arithmetic and copies ran while one was open for 22% of the time, Pallas kernels for 0%

profile of v11, /device:TPU:0, one launch (start us, length us, event | category | flops | bytes accessed | tf_op | source)
XLA Modules:
  0.0 152.1 jit_solution(10198033528695483666)
XLA Ops:
  0.6 0.9 fusion.51
  2.2 1.5 select_select_fusion
  3.7 16.0 %fusion = f32[2,256,4,4,256]{1,4,3,2,0:T(8,128)S(1)} fusion(bf16[4,4,1024,256]{3,2,1,0:T(8,128)(2,1)} %param.8, f32[2,1034,256]{2,1,0:T(8,128)S(1)} %select_select_fusion), kind=kOutput, calls=%fused_computation.2 | convolution fusion | flops 25769803776 | bytes 18874368 | tf_op jit(solution)/shard_map/cpxz,sxm->scpmz/dot_general | solution.py:165
  20.0 3.5 %fusion.34 = f32[2,256,4,4,256]{1,4,3,2,0:T(8,128)S(1)} fusion(bf16[4,4,5,256]{3,2,1,0:T(8,128)(2,1)S(1)} %collective-permute-done, f32[2,1034,256]{2,1,0:T(8,128)S(1)} %select_select_fusion), kind=kOutput, calls=%fused_computation.59 | convolution fusion | flops 125829120 | bytes 8470528 | tf_op jit(solution)/shard_map/cpxz,sxm->scpmz/dot_general | solution.py:171
  23.5 4.4 %add_bitcast_fusion = f32[2,4,4,256,256]{3,4,2,1,0:T(8,128)S(1)} fusion(f32[2,256,4,4,256]{1,4,3,2,0:T(8,128)S(1)} %fusion, f32[2,256,4,4,256]{1,4,3,2,0:T(8,128)S(1)} %fusion.34, bf16[4,4,5,256]{3,2,1,0:T(8,128)(2,1)S(1)} %collective-permute-done.1, f32[2,1034,256]{2,1,0:T(8,128)S(1)} %select_select_fusion), kind=kOutput, calls=%fused_computation.4 | convolution fusion | flops 130023424 | bytes 25247744 | tf_op jit(solution)/shard_map/cpxz,sxm->scpmz/dot_general | solution.py:174
  28.0 3.0 %collective-permute-start.2 = (f32[2,4,4,256,5]{3,4,2,1,0:T(8,128)S(1)}, f32[2,4,4,256,5]{3,4,2,1,0:T(8,128)S(1)}, u32[]{:S(2)}, u32[]{:S(2)}) collective-permute-start(f32[2,4,4,256,5]{3,4,2,1,0:T(8,128)S(1)} %get-tuple-element.73), channel_id=1, source_target_pairs={{0,2},{2,0},{1,3},{3,1},{4,6},{6,4},{5,7},{7,5},{8,10},{10,8},{9,1... | collective-permute-start | bytes 491528 | tf_op jit(solution)/shard_map/ppermute | solution.py:68
  31.0 5.5 %fusion.31 = f32[2,4,4,256,64]{3,4,2,1,0:T(8,128)S(1)} fusion(f32[2,4,4,256,256]{3,4,2,1,0:T(8,128)S(1)} %add_bitcast_fusion, f32[266,2,64]{0,2,1:T(8,128)S(1)} %select_select_fusion.1), kind=kOutput, calls=%fused_computation.54 | convolution fusion | flops 1610612736 | bytes 10616832 | tf_op jit(solution)/shard_map/scpmz,zsn->scpmn/dot_general | solution.py:183
  36.6 0.9 collective-permute-done.2
  37.5 2.0 %fusion.32 = f32[2,4,4,256,64]{3,4,2,1,0:T(8,128)S(1)} fusion(f32[2,4,4,256,5]{3,4,2,1,0:T(8,128)S(1)} %collective-permute-done.2, f32[266,2,64]{0,2,1:T(8,128)S(1)} %select_select_fusion.1), kind=kOutput, calls=%fused_computation.57 | convolution fusion | flops 31457280 | bytes 2424832 | tf_op jit(solution)/shard_map/scpmz,zsn->scpmn/dot_general | solution.py:189
  39.5 5.0 %collective-permute-done.3 = f32[2,4,4,256,5]{3,4,2,1,0:T(8,128)S(1)} collective-permute-done((f32[2,4,4,256,5]{3,4,2,1,0:T(8,128)S(1)}, f32[2,4,4,256,5]{3,4,2,1,0:T(8,128)S(1)}, u32[]{:S(2)}, u32[]{:S(2)}) %collective-permute-start.3) | collective-permute-done | bytes 163872 | tf_op jit(solution)/shard_map/ppermute | solution.py:68
  44.6 2.1 %add_add_fusion = f32[2,4,4,256,64]{3,4,2,1,0:T(8,128)S(1)} fusion(f32[2,4,4,256,64]{3,4,2,1,0:T(8,128)S(1)} %fusion.31, f32[2,4,4,256,64]{3,4,2,1,0:T(8,128)S(1)} %fusion.32, f32[2,4,4,256,5]{3,4,2,1,0:T(8,128)S(1)} %collective-permute-done.3, f32[266,2,64]{0,2,1:T(8,128)S(1)} %select_select_fusion.1), kind=kOutput, calls=%fused_computation.21 | convolution fusion | flops 32505856 | bytes 6619136 | tf_op jit(solution)/shard_map/scpmz,zsn->scpmn/dot_general | solution.py:190
  46.8 0.9 slice.167
  48.6 1.5 copy.29
  51.0 1.1 copy.31
  52.0 4.9 %all-to-all-start = ((bf16[4,1024,128]{2,1,0:T(8,128)(2,1)}), bf16[4,1024,128]{2,1,0:T(8,128)(2,1)S(1)}, u32[]{:S(2)}, u32[]{:S(2)}) async-start(bf16[4,1024,128]{2,1,0:T(8,128)(2,1)} %bitcast.15), calls=%async_computation | async-start | bytes 2097152 | tf_op jit(solution)/shard_map/all_to_all | solution.py:210
  58.1 1.5 reshape_reshape.3
  59.6 0.9 constant_dynamic-slice_fusion.1
  60.6 21.1 %all-to-all-done = bf16[4,1024,128]{2,1,0:T(8,128)(2,1)S(1)} async-done(((bf16[4,1024,128]{2,1,0:T(8,128)(2,1)}), bf16[4,1024,128]{2,1,0:T(8,128)(2,1)S(1)}, u32[]{:S(2)}, u32[]{:S(2)}) %all-to-all-start) | async-done | bytes 1048608 | tf_op jit(solution)/shard_map/all_to_all | solution.py:210
  82.7 1.6 %copy.33 = f32[16,128,128]{2,0,1:T(8,128)} copy(f32[16,128,128]{2,1,0:T(8,128)S(1)} %bitcast_convert_fusion) | data formatting | bytes 2097152 | tf_op jit(solution)/shard_map/while/body/eval_jaxpr/convert_element_type | solution.py:137
  84.3 4.1 %multiply_convert_fusion = bf16[16,16,128,128]{3,1,0,2:T(8,128)(2,1)S(1)} fusion(f32[16,128,128]{2,0,1:T(8,128)} %copy.33, f32[16,128,128]{2,0,1:T(8,128)S(1)} %copy.32), kind=kLoop, calls=%fused_computation.1 | loop fusion | flops 8388608 | bytes 10485760 | tf_op jit(solution)/shard_map/while/body/eval_jaxpr/convert_element_type | solution.py:139
  88.4 2.4 %convolution_bitcast_fusion = f32[256,256]{0,1:T(8,128)S(1)} fusion(bf16[256,128,128]{2,0,1:T(8,128)(2,1)S(1)} %bitcast.83), kind=kOutput, calls=%fused_computation.25 | convolution fusion | flops 2147483648 | bytes 8650752 | tf_op jit(solution)/shard_map/while/body/eval_jaxpr/iqr,jqr->ij/dot_general | solution.py:226
  90.7 0.9 copy-done
  91.6 2.3 %convolution_bitcast_fusion.1 = f32[256,6]{0,1:T(8,128)S(1)} fusion(bf16[256,128,128]{2,0,1:T(8,128)(2,1)S(1)} %bitcast.84, bf16[6,1,128,128]{3,2,1,0:T(8,128)(2,1)S(1)} %constant_dynamic-slice_fusion.1), kind=kOutput, calls=%fused_computation.26 | convolution fusion | flops 50331648 | bytes 8591360 | tf_op jit(solution)/shard_map/while/body/eval_jaxpr/iqr,kqr->ik/dot_general | solution.py:229
  94.6 1.5 %collective-permute-done.4 = f32[256,262]{0,1:T(8,128)S(1)} collective-permute-done((f32[256,262]{0,1:T(8,128)S(1)}, f32[256,262]{0,1:T(8,128)S(1)}, u32[]{:S(2)}, u32[]{:S(2)}) %collective-permute-start.4) | collective-permute-done | bytes 268320 | tf_op jit(solution)/shard_map/ppermute | solution.py:53
  97.5 5.1 %collective-permute-done.5 = f32[128,262]{0,1:T(8,128)S(1)} collective-permute-done((f32[128,262]{0,1:T(8,128)S(1)}, f32[128,262]{0,1:T(8,128)S(1)}, u32[]{:S(2)}, u32[]{:S(2)}) %collective-permute-start.5) | collective-permute-done | bytes 134176 | tf_op jit(solution)/shard_map/ppermute | solution.py:43
  102.7 5.0 %collective-permute-done.6 = f32[128,262]{0,1:T(8,128)S(1)} collective-permute-done((f32[128,262]{0,1:T(8,128)S(1)}, f32[128,262]{0,1:T(8,128)S(1)}, u32[]{:S(2)}, u32[]{:S(2)}) %collective-permute-start.6) | collective-permute-done | bytes 134176 | tf_op jit(solution)/shard_map/ppermute | solution.py:43
  107.8 7.4 %collective-permute-done.7 = f32[128,262]{0,1:T(8,128)S(1)} collective-permute-done((f32[128,262]{0,1:T(8,128)S(1)}, f32[128,262]{0,1:T(8,128)S(1)}, u32[]{:S(2)}, u32[]{:S(2)}) %collective-permute-start.7) | collective-permute-done | bytes 134176 | tf_op jit(solution)/shard_map/ppermute | solution.py:43
  116.7 2.4 %gather_fusion = f32[256]{0:T(256)S(1)} fusion(f32[256,256]{0,1:T(8,128)S(1)} %slice.136, s32[256]{0:T(256)S(1)} %bitcast.86), kind=kCustom, calls=%fused_computation | custom fusion | bytes 4096 | tf_op jit(solution)/shard_map/jit(diagonal)/cond/branch_0_fun/gather | solution.py:243
  120.7 6.0 %shard_map.59 = f32[3,8,256]{2,1,0:T(8,128)} custom-call(f32[256,256]{1,0:T(8,128)} %copy.36.gram_ref, f32[8,256]{1,0:T(8,128)} %scatter.6.target_ref, f32[3,8,256]{2,1,0:T(8,128)} %scatter.9.mask_ref), custom_call_target="tpu_custom_call" | custom-call | tf_op jit(solution)/shard_map/pallas_call | solution.py:254
  126.6 4.6 %fusion.15 = bf16[6,128,128]{2,0,1:T(8,128)(2,1)S(1)} fusion(bf16[256,128,128]{2,0,1:T(8,128)(2,1)} %bitcast.85, bf16[6,1,128,128]{3,2,1,0:T(8,128)(2,1)S(1)} %constant_dynamic-slice_fusion.1, f32[3,8,256]{2,1,0:T(8,128)} %shard_map.59, f32[256]{0:T(256)S(1)} %add_rsqrt_fusion), kind=kOutput, calls=%fused_computation.24 | convolution fusion | flops 50629632 | bytes 8791040 | tf_op jit(solution)/shard_map/while/body/eval_jaxpr/ki,iqr->kqr/dot_general | solution.py:267
  131.3 18.0 %all_gather.3 = bf16[6,512,128]{2,1,0:T(8,128)(2,1)S(1)} all-gather(bf16[6,128,128]{2,1,0:T(8,128)(2,1)S(1)} %copy.37), channel_id=1, replica_groups=mesh['groups'=2,'cols'=4,'slab'=2,'rep'=2] {'cols'}, dimensions={1}, use_global_device_ids=true | all-gather | bytes 983040 | tf_op jit(solution)/shard_map/all_gather | solution.py:277
  150.0 1.4 copy.38
  (64 shorter events, 11.7 us)
Async XLA Ops:
  1.5 18.5 %collective-permute-start = (bf16[4,4,5,256]{3,2,1,0:T(8,128)(2,1)S(1)}, bf16[4,4,5,256]{3,2,1,0:T(8,128)(2,1)S(1)}, u32[]{:S(2)}, u32[]{:S(2)}) collective-permute-start(bf16[4,4,5,256]{3,2,1,0:T(8,128)(2,1)S(1)} %get-tuple-element.75), channel_id=1, source_target_pairs={{0,1},{1,0},{2,3},{3,2},{4,5},{5,4},{6,7},{7,6},{8,9},{9,8},{10,11... | collective-permute-start | bytes 122888 | tf_op jit(solution)/shard_map/ppermute | solution.py:68
  2.0 21.5 %collective-permute-start.1 = (bf16[4,4,5,256]{3,2,1,0:T(8,128)(2,1)S(1)}, bf16[4,4,5,256]{3,2,1,0:T(8,128)(2,1)S(1)}, u32[]{:S(2)}, u32[]{:S(2)}) collective-permute-start(bf16[4,4,5,256]{3,2,1,0:T(8,128)(2,1)S(1)} %get-tuple-element.74), channel_id=1, source_target_pairs={{1,0},{0,1},{3,2},{2,3},{5,4},{4,5},{7,6},{6,7},{9,8},{8,9},{11,10... | collective-permute-start | bytes 122888 | tf_op jit(solution)/shard_map/ppermute | solution.py:68
  3.7 16.3 %copy-start.5 = (s32[4]{0:T(128)S(1)}, s32[4]{0:T(128)}, u32[]{:S(2)}) copy-start(s32[4]{0:T(128)} %param.10) | copy-start | bytes 52
  28.0 9.5 %collective-permute-start.2 = (f32[2,4,4,256,5]{3,4,2,1,0:T(8,128)S(1)}, f32[2,4,4,256,5]{3,4,2,1,0:T(8,128)S(1)}, u32[]{:S(2)}, u32[]{:S(2)}) collective-permute-start(f32[2,4,4,256,5]{3,4,2,1,0:T(8,128)S(1)} %get-tuple-element.73), channel_id=1, source_target_pairs={{0,2},{2,0},{1,3},{3,1},{4,6},{6,4},{5,7},{7,5},{8,10},{10,8},{9,1... | collective-permute-start | bytes 491528 | tf_op jit(solution)/shard_map/ppermute | solution.py:68
  36.5 8.1 %collective-permute-start.3 = (f32[2,4,4,256,5]{3,4,2,1,0:T(8,128)S(1)}, f32[2,4,4,256,5]{3,4,2,1,0:T(8,128)S(1)}, u32[]{:S(2)}, u32[]{:S(2)}) collective-permute-start(f32[2,4,4,256,5]{3,4,2,1,0:T(8,128)S(1)} %get-tuple-element.72), channel_id=1, source_target_pairs={{2,0},{0,2},{3,1},{1,3},{6,4},{4,6},{7,5},{5,7},{10,8},{8,10},{11,... | collective-permute-start | bytes 491528 | tf_op jit(solution)/shard_map/ppermute | solution.py:68
  50.9 6.0 %copy-start.1 = (bf16[6,4,256,64]{2,3,1,0:T(8,128)(2,1)S(1)}, bf16[6,4,256,64]{2,3,1,0:T(8,128)(2,1)}, u32[]{:S(2)}) copy-start(bf16[6,4,256,64]{2,3,1,0:T(8,128)(2,1)} %param.9) | copy-start | bytes 2359300
  52.0 29.7 %all-to-all-start = ((bf16[4,1024,128]{2,1,0:T(8,128)(2,1)}), bf16[4,1024,128]{2,1,0:T(8,128)(2,1)S(1)}, u32[]{:S(2)}, u32[]{:S(2)}) async-start(bf16[4,1024,128]{2,1,0:T(8,128)(2,1)} %bitcast.15), calls=%async_computation | async-start | bytes 2097152 | tf_op jit(solution)/shard_map/all_to_all | solution.py:210
  88.4 3.3 %copy-start = (bf16[16,16,128,128]{3,1,0,2:T(8,128)(2,1)}, bf16[16,16,128,128]{3,1,0,2:T(8,128)(2,1)S(1)}, u32[]{:S(2)}) copy-start(bf16[16,16,128,128]{3,1,0,2:T(8,128)(2,1)S(1)} %multiply_convert_fusion) | copy-start | bytes 25165828
  93.9 0.6 copy-start.3
  94.5 20.8 %copy-start.4 = (s32[3,6,256]{2,1,0:T(8,128)S(1)}, s32[3,6,256]{2,1,0:T(8,128)}, u32[]{:S(2)}) copy-start(s32[3,6,256]{2,1,0:T(8,128)} %param.11) | copy-start | bytes 55300
  94.5 1.6 %collective-permute-start.4 = (f32[256,262]{0,1:T(8,128)S(1)}, f32[256,262]{0,1:T(8,128)S(1)}, u32[]{:S(2)}, u32[]{:S(2)}) collective-permute-start(f32[256,262]{0,1:T(8,128)S(1)} %pad_maximum_fusion), channel_id=1, source_target_pairs={{0,1},{1,0},{2,3},{3,2},{4,5},{5,4},{6,7},{7,6},{8,9},{9,8},{10,11... | collective-permute-start | bytes 804872 | tf_op jit(solution)/shard_map/ppermute | solution.py:53
  96.9 5.7 %collective-permute-start.5 = (f32[128,262]{0,1:T(8,128)S(1)}, f32[128,262]{0,1:T(8,128)S(1)}, u32[]{:S(2)}, u32[]{:S(2)}) collective-permute-start(f32[128,262]{0,1:T(8,128)S(1)} %slice_select_fusion), channel_id=1, source_target_pairs={{0,2},{2,0},{1,3},{3,1},{4,6},{6,4},{5,7},{7,5},{8,10},{10,8},{9,1... | collective-permute-start | bytes 402440 | tf_op jit(solution)/shard_map/ppermute | solution.py:43
  102.6 5.1 %collective-permute-start.6 = (f32[128,262]{0,1:T(8,128)S(1)}, f32[128,262]{0,1:T(8,128)S(1)}, u32[]{:S(2)}, u32[]{:S(2)}) collective-permute-start(f32[128,262]{0,1:T(8,128)S(1)} %fusion.60), channel_id=1, source_target_pairs={{0,4},{4,0},{8,12},{12,8},{1,5},{5,1},{9,13},{13,9},{2,6},{6,2},{1... | collective-permute-start | bytes 402440 | tf_op jit(solution)/shard_map/ppermute | solution.py:43
  107.7 7.5 %collective-permute-start.7 = (f32[128,262]{0,1:T(8,128)S(1)}, f32[128,262]{0,1:T(8,128)S(1)}, u32[]{:S(2)}, u32[]{:S(2)}) collective-permute-start(f32[128,262]{0,1:T(8,128)S(1)} %add.115), channel_id=1, source_target_pairs={{0,8},{4,12},{8,0},{12,4},{1,9},{5,13},{9,1},{13,5},{2,10},{6,14},... | collective-permute-start | bytes 402440 | tf_op jit(solution)/shard_map/ppermute | solution.py:43
  115.2 1.4 collective-permute-start.8
  149.3 2.1 %copy-start.2 = (f32[3,8,256]{2,1,0:T(8,128)S(1)}, f32[3,8,256]{2,1,0:T(8,128)}, u32[]{:S(2)}) copy-start(f32[3,8,256]{2,1,0:T(8,128)} %shard_map.59) | copy-start | bytes 73732

commit v12 on v11

--- a/solution.py
+++ b/solution.py
@@ -178,7 +178,7 @@
             precision=highest,
         )
     )
-    left, right = neighbour_edges(along_stream, "slab", 4, width)
+    left, right = neighbour_edges(jnp.swapaxes(along_stream, 3, 4), "slab", 3, width)
     filtered = (
         jnp.einsum(
             "scpmz,zsn->scpmn",
@@ -186,8 +186,8 @@
             span_table[width : width + cells_z],
             precision=highest,
         )
-        + jnp.einsum("scpmz,zsn->scpmn", left, span_table[:width], precision=highest)
-        + jnp.einsum("scpmz,zsn->scpmn", right, span_table[width + cells_z :], precision=highest)
+        + jnp.einsum("scpzm,zsn->scpmn", left, span_table[:width], precision=highest)
+        + jnp.einsum("scpzm,zsn->scpmn", right, span_table[width + cells_z :], precision=highest)
     )
     narrow = filtered[0]
     broader = filtered[1]
@@ -240,7 +240,11 @@
     full_rows = split_sum(jnp.concatenate([gram_part, rhs_part], axis=1), "rep", ("slab", "cols"))
     gram_matrix = full_rows[:, :TERMS]
     rhs_sums = full_rows[:, TERMS:]
-    column_scale = 1.0 / jnp.sqrt(jnp.diagonal(gram_matrix) / samples + epsilon)
+    on_diagonal = lax.broadcasted_iota(jnp.int32, (TERMS, TERMS), 0) == lax.broadcasted_iota(
+        jnp.int32, (TERMS, TERMS), 1
+    )
+    diagonal = jnp.sum(jnp.where(on_diagonal, gram_matrix, 0.0), axis=1)
+    column_scale = 1.0 / jnp.sqrt(diagonal / samples + epsilon)
     normal_gram = column_scale[:, None] * gram_matrix * column_scale[None, :] / samples
     target_norm = column_scale[None, :] * rhs_sums.T / samples
 

time: 152 us -> 150 us (0.987)
  local copies, waits for them, and re-layouts: 20.2 us -> 17.8 us
    gather x1 -> x0, local copies, waits for them, and re-layouts: 2.37 us -> none  [local(): column_scale = 1.0 / jnp.sqrt(jnp.diagonal(gram_matrix) / samples + epsilon)]
where the time goes in v12:
time: 150 us
  waiting for transfers between devices  46.8 us (31%)
  matrix products  42.8 us (29%)
  blocking collectives  18 us (12%)
  local copies, waits for them, and re-layouts  17.8 us (12%)
  starting transfers between devices  9.44 us (6%)
  other arithmetic  7.79 us (5%)
  Pallas kernels  5.98 us (4%)
    all_to_all x1, waiting for transfers between devices, local(): sets = lax.all_to_all(sets, 'cols', 0, 0, tiled=True)  21.1 us
    all_gather x1, blocking collectives, local(): misfit = lax.all_gather(misfit, 'cols', axis=1, tiled=True)  18 us
    ppermute x3, waiting for transfers between devices, tree_sum(): value = value + lax.ppermute(value, axis, partner)  17.5 us
    dot_general x1, matrix products, local(): jnp.einsum('cpxz,sxm->scpmz', fields.astype(jnp.float32), stream_table[:,...  16 us
    ppermute x4, waiting for transfers between devices, neighbour_edges(): return (lax.ppermute(last, axis, up), lax.ppermute(leading, axis, down))  5.99 us
    pallas_call x1, Pallas kernels, local(): pl.pallas_call(conjugate_passes, out_shape=jax.ShapeDtypeStruct((PASSES,...  5.98 us
    dot_general x1, matrix products, local(): jnp.einsum('scpmz,zsn->scpmn', along_stream, span_table[width:width + cel...  5.53 us
    all_to_all x1, starting transfers between devices, local(): sets = lax.all_to_all(sets, 'cols', 0, 0, tiled=True)  4.86 us
  transfers between devices with their start and end apart: 10, of which 8 were waited for; matrix products, arithmetic and copies ran while one was open for 22% of the time, Pallas kernels for 0%

profile of v12, /device:TPU:0, one launch (start us, length us, event | category | flops | bytes accessed | tf_op | source)
XLA Modules:
  0.0 149.7 jit_solution(662933163460418017)
XLA Ops:
  0.6 0.9 fusion.52
  2.2 1.5 select_select_fusion
  3.7 16.0 %fusion.2 = f32[2,256,4,4,256]{1,4,3,2,0:T(8,128)S(1)} fusion(bf16[4,4,1024,256]{3,2,1,0:T(8,128)(2,1)} %param.8, f32[2,1034,256]{2,1,0:T(8,128)S(1)} %select_select_fusion), kind=kOutput, calls=%fused_computation.3 | convolution fusion | flops 25769803776 | bytes 18874368 | tf_op jit(solution)/shard_map/cpxz,sxm->scpmz/dot_general | solution.py:165
  20.0 3.5 %fusion.35 = f32[2,256,4,4,256]{1,4,3,2,0:T(8,128)S(1)} fusion(bf16[4,4,5,256]{3,2,1,0:T(8,128)(2,1)S(1)} %collective-permute-done, f32[2,1034,256]{2,1,0:T(8,128)S(1)} %select_select_fusion), kind=kOutput, calls=%fused_computation.61 | convolution fusion | flops 125829120 | bytes 8470528 | tf_op jit(solution)/shard_map/cpxz,sxm->scpmz/dot_general | solution.py:171
  23.5 4.4 %add_add_fusion = f32[2,256,4,4,256]{1,4,3,2,0:T(8,128)S(1)} fusion(f32[2,256,4,4,256]{1,4,3,2,0:T(8,128)S(1)} %fusion.2, f32[2,256,4,4,256]{1,4,3,2,0:T(8,128)S(1)} %fusion.35, bf16[4,4,5,256]{3,2,1,0:T(8,128)(2,1)S(1)} %collective-permute-done.1, f32[2,1034,256]{2,1,0:T(8,128)S(1)} %select_select_fusion), kind=kOutput, calls=%fused_computation.5 | convolution fusion | flops 130023424 | bytes 25247744 | tf_op jit(solution)/shard_map/cpxz,sxm->scpmz/dot_general | solution.py:174
  28.0 3.0 %collective-permute-start.2 = (f32[2,4,4,5,256]{4,3,2,1,0:T(8,128)S(1)}, f32[2,4,4,5,256]{4,3,2,1,0:T(8,128)S(1)}, u32[]{:S(2)}, u32[]{:S(2)}) collective-permute-start(f32[2,4,4,5,256]{4,3,2,1,0:T(8,128)S(1)} %get-tuple-element.73), channel_id=1, source_target_pairs={{0,2},{2,0},{1,3},{3,1},{4,6},{6,4},{5,7},{7,5},{8,10},{10,8},{9,1... | collective-permute-start | bytes 491528 | tf_op jit(solution)/shard_map/ppermute | solution.py:68
  31.0 5.5 %fusion = f32[2,4,4,256,64]{3,4,2,1,0:T(8,128)S(1)} fusion(f32[2,256,4,4,256]{1,4,3,2,0:T(8,128)S(1)} %add_add_fusion, f32[266,2,64]{0,2,1:T(8,128)S(1)} %select_select_fusion.1), kind=kOutput, calls=%fused_computation.1 | convolution fusion | flops 1610612736 | bytes 10616832 | tf_op jit(solution)/shard_map/scpmz,zsn->scpmn/dot_general | solution.py:183
  36.6 0.9 collective-permute-done.2
  37.5 2.0 %fusion.33 = f32[2,4,4,256,64]{3,4,2,1,0:T(8,128)S(1)} fusion(f32[2,4,4,5,256]{4,3,2,1,0:T(8,128)S(1)} %collective-permute-done.2, f32[266,2,64]{0,2,1:T(8,128)S(1)} %select_select_fusion.1), kind=kOutput, calls=%fused_computation.59 | convolution fusion | flops 31457280 | bytes 2424832 | tf_op jit(solution)/shard_map/scpzm,zsn->scpmn/dot_general | solution.py:189
  39.5 5.0 %collective-permute-done.3 = f32[2,4,4,5,256]{4,3,2,1,0:T(8,128)S(1)} collective-permute-done((f32[2,4,4,5,256]{4,3,2,1,0:T(8,128)S(1)}, f32[2,4,4,5,256]{4,3,2,1,0:T(8,128)S(1)}, u32[]{:S(2)}, u32[]{:S(2)}) %collective-permute-start.3) | collective-permute-done | bytes 163872 | tf_op jit(solution)/shard_map/ppermute | solution.py:68
  44.6 2.1 %add_add_fusion.1 = f32[2,4,4,256,64]{3,4,2,1,0:T(8,128)S(1)} fusion(f32[2,4,4,256,64]{3,4,2,1,0:T(8,128)S(1)} %fusion, f32[2,4,4,256,64]{3,4,2,1,0:T(8,128)S(1)} %fusion.33, f32[2,4,4,5,256]{4,3,2,1,0:T(8,128)S(1)} %collective-permute-done.3, f32[266,2,64]{0,2,1:T(8,128)S(1)} %select_select_fusion.1), kind=kOutput, calls=%fused_computation.22 | convolution fusion | flops 32505856 | bytes 6619136 | tf_op jit(solution)/shard_map/scpzm,zsn->scpmn/dot_general | solution.py:190
  46.8 0.9 slice.166
  48.6 1.5 %copy.29 = bf16[1,4,4,256,64]{4,3,2,1,0:T(8,128)(2,1)S(1)} copy(bf16[1,4,4,256,64]{3,4,2,1,0:T(8,128)(2,1)} %slice.166) | data formatting | bytes 1048576 | tf_op jit(solution)/shard_map/slice | solution.py:192
  51.0 1.1 copy.31
  52.0 4.9 %all-to-all-start = ((bf16[4,1024,128]{2,1,0:T(8,128)(2,1)}), bf16[4,1024,128]{2,1,0:T(8,128)(2,1)S(1)}, u32[]{:S(2)}, u32[]{:S(2)}) async-start(bf16[4,1024,128]{2,1,0:T(8,128)(2,1)} %bitcast.16), calls=%async_computation | async-start | bytes 2097152 | tf_op jit(solution)/shard_map/all_to_all | solution.py:210
  57.3 0.9 copy.34
  58.1 1.5 reshape_reshape.3
  59.6 0.9 constant_dynamic-slice_fusion.1
  60.5 21.1 %all-to-all-done = bf16[4,1024,128]{2,1,0:T(8,128)(2,1)S(1)} async-done(((bf16[4,1024,128]{2,1,0:T(8,128)(2,1)}), bf16[4,1024,128]{2,1,0:T(8,128)(2,1)S(1)}, u32[]{:S(2)}, u32[]{:S(2)}) %all-to-all-start) | async-done | bytes 1048608 | tf_op jit(solution)/shard_map/all_to_all | solution.py:210
  82.7 1.6 %copy.33 = f32[16,128,128]{2,0,1:T(8,128)} copy(f32[16,128,128]{2,1,0:T(8,128)S(1)} %bitcast_convert_fusion) | data formatting | bytes 2097152 | tf_op jit(solution)/shard_map/while/body/eval_jaxpr/convert_element_type | solution.py:137
  84.3 4.1 %multiply_convert_fusion = bf16[16,16,128,128]{3,1,0,2:T(8,128)(2,1)S(1)} fusion(f32[16,128,128]{2,0,1:T(8,128)} %copy.33, f32[16,128,128]{2,0,1:T(8,128)S(1)} %copy.32), kind=kLoop, calls=%fused_computation | loop fusion | flops 8388608 | bytes 10485760 | tf_op jit(solution)/shard_map/while/body/eval_jaxpr/convert_element_type | solution.py:139
  88.4 2.4 %convolution_bitcast_fusion = f32[256,256]{0,1:T(8,128)S(1)} fusion(bf16[256,128,128]{2,0,1:T(8,128)(2,1)S(1)} %bitcast.83), kind=kOutput, calls=%fused_computation.26 | convolution fusion | flops 2147483648 | bytes 8650752 | tf_op jit(solution)/shard_map/while/body/eval_jaxpr/iqr,jqr->ij/dot_general | solution.py:226
  90.7 0.9 copy-done
  91.6 2.3 %convolution_bitcast_fusion.1 = f32[256,6]{0,1:T(8,128)S(1)} fusion(bf16[256,128,128]{2,0,1:T(8,128)(2,1)S(1)} %bitcast.84, bf16[6,1,128,128]{3,2,1,0:T(8,128)(2,1)S(1)} %constant_dynamic-slice_fusion.1), kind=kOutput, calls=%fused_computation.27 | convolution fusion | flops 50331648 | bytes 8591360 | tf_op jit(solution)/shard_map/while/body/eval_jaxpr/iqr,kqr->ik/dot_general | solution.py:229
  94.6 1.5 %collective-permute-done.4 = f32[256,262]{0,1:T(8,128)S(1)} collective-permute-done((f32[256,262]{0,1:T(8,128)S(1)}, f32[256,262]{0,1:T(8,128)S(1)}, u32[]{:S(2)}, u32[]{:S(2)}) %collective-permute-start.4) | collective-permute-done | bytes 268320 | tf_op jit(solution)/shard_map/ppermute | solution.py:53
  97.4 5.1 %collective-permute-done.5 = f32[128,262]{0,1:T(8,128)S(1)} collective-permute-done((f32[128,262]{0,1:T(8,128)S(1)}, f32[128,262]{0,1:T(8,128)S(1)}, u32[]{:S(2)}, u32[]{:S(2)}) %collective-permute-start.5) | collective-permute-done | bytes 134176 | tf_op jit(solution)/shard_map/ppermute | solution.py:43
  102.6 5.0 %collective-permute-done.6 = f32[128,262]{0,1:T(8,128)S(1)} collective-permute-done((f32[128,262]{0,1:T(8,128)S(1)}, f32[128,262]{0,1:T(8,128)S(1)}, u32[]{:S(2)}, u32[]{:S(2)}) %collective-permute-start.6) | collective-permute-done | bytes 134176 | tf_op jit(solution)/shard_map/ppermute | solution.py:43
  107.8 7.4 %collective-permute-done.7 = f32[128,262]{0,1:T(8,128)S(1)} collective-permute-done((f32[128,262]{0,1:T(8,128)S(1)}, f32[128,262]{0,1:T(8,128)S(1)}, u32[]{:S(2)}, u32[]{:S(2)}) %collective-permute-start.7) | collective-permute-done | bytes 134176 | tf_op jit(solution)/shard_map/ppermute | solution.py:43
  118.3 6.0 %shard_map.59 = f32[3,8,256]{2,1,0:T(8,128)} custom-call(f32[256,256]{1,0:T(8,128)} %copy.36.gram_ref, f32[8,256]{1,0:T(8,128)} %scatter.6.target_ref, f32[3,8,256]{2,1,0:T(8,128)} %scatter.9.mask_ref), custom_call_target="tpu_custom_call" | custom-call | tf_op jit(solution)/shard_map/pallas_call | solution.py:258
  124.3 4.6 %fusion.17 = bf16[6,128,128]{2,0,1:T(8,128)(2,1)S(1)} fusion(bf16[256,128,128]{2,0,1:T(8,128)(2,1)} %bitcast.85, bf16[6,1,128,128]{3,2,1,0:T(8,128)(2,1)S(1)} %constant_dynamic-slice_fusion.1, f32[3,8,256]{2,1,0:T(8,128)} %shard_map.59, f32[256]{0:T(256)S(1)} %add_rsqrt_fusion), kind=kOutput, calls=%fused_computation.25 | convolution fusion | flops 50629632 | bytes 8791040 | tf_op jit(solution)/shard_map/while/body/eval_jaxpr/ki,iqr->kqr/dot_general | solution.py:271
  128.9 18.0 %all_gather.3 = bf16[6,512,128]{2,1,0:T(8,128)(2,1)S(1)} all-gather(bf16[6,128,128]{2,1,0:T(8,128)(2,1)S(1)} %copy.37), channel_id=1, replica_groups=mesh['groups'=2,'cols'=4,'slab'=2,'rep'=2] {'cols'}, dimensions={1}, use_global_device_ids=true | all-gather | bytes 983040 | tf_op jit(solution)/shard_map/all_gather | solution.py:281
  147.6 1.4 copy.38
  (62 shorter events, 10.9 us)
Async XLA Ops:
  1.5 18.5 %collective-permute-start = (bf16[4,4,5,256]{3,2,1,0:T(8,128)(2,1)S(1)}, bf16[4,4,5,256]{3,2,1,0:T(8,128)(2,1)S(1)}, u32[]{:S(2)}, u32[]{:S(2)}) collective-permute-start(bf16[4,4,5,256]{3,2,1,0:T(8,128)(2,1)S(1)} %get-tuple-element.75), channel_id=1, source_target_pairs={{0,1},{1,0},{2,3},{3,2},{4,5},{5,4},{6,7},{7,6},{8,9},{9,8},{10,11... | collective-permute-start | bytes 122888 | tf_op jit(solution)/shard_map/ppermute | solution.py:68
  2.0 21.5 %collective-permute-start.1 = (bf16[4,4,5,256]{3,2,1,0:T(8,128)(2,1)S(1)}, bf16[4,4,5,256]{3,2,1,0:T(8,128)(2,1)S(1)}, u32[]{:S(2)}, u32[]{:S(2)}) collective-permute-start(bf16[4,4,5,256]{3,2,1,0:T(8,128)(2,1)S(1)} %get-tuple-element.74), channel_id=1, source_target_pairs={{1,0},{0,1},{3,2},{2,3},{5,4},{4,5},{7,6},{6,7},{9,8},{8,9},{11,10... | collective-permute-start | bytes 122888 | tf_op jit(solution)/shard_map/ppermute | solution.py:68
  3.7 16.3 %copy-start.5 = (s32[4]{0:T(128)S(1)}, s32[4]{0:T(128)}, u32[]{:S(2)}) copy-start(s32[4]{0:T(128)} %param.10) | copy-start | bytes 52
  28.0 9.5 %collective-permute-start.2 = (f32[2,4,4,5,256]{4,3,2,1,0:T(8,128)S(1)}, f32[2,4,4,5,256]{4,3,2,1,0:T(8,128)S(1)}, u32[]{:S(2)}, u32[]{:S(2)}) collective-permute-start(f32[2,4,4,5,256]{4,3,2,1,0:T(8,128)S(1)} %get-tuple-element.73), channel_id=1, source_target_pairs={{0,2},{2,0},{1,3},{3,1},{4,6},{6,4},{5,7},{7,5},{8,10},{10,8},{9,1... | collective-permute-start | bytes 491528 | tf_op jit(solution)/shard_map/ppermute | solution.py:68
  36.5 8.1 %collective-permute-start.3 = (f32[2,4,4,5,256]{4,3,2,1,0:T(8,128)S(1)}, f32[2,4,4,5,256]{4,3,2,1,0:T(8,128)S(1)}, u32[]{:S(2)}, u32[]{:S(2)}) collective-permute-start(f32[2,4,4,5,256]{4,3,2,1,0:T(8,128)S(1)} %get-tuple-element.72), channel_id=1, source_target_pairs={{2,0},{0,2},{3,1},{1,3},{6,4},{4,6},{7,5},{5,7},{10,8},{8,10},{11,... | collective-permute-start | bytes 491528 | tf_op jit(solution)/shard_map/ppermute | solution.py:68
  50.9 5.9 %copy-start.1 = (bf16[6,4,256,64]{2,3,1,0:T(8,128)(2,1)S(1)}, bf16[6,4,256,64]{2,3,1,0:T(8,128)(2,1)}, u32[]{:S(2)}) copy-start(bf16[6,4,256,64]{2,3,1,0:T(8,128)(2,1)} %param.9) | copy-start | bytes 2359300
  52.0 29.7 %all-to-all-start = ((bf16[4,1024,128]{2,1,0:T(8,128)(2,1)}), bf16[4,1024,128]{2,1,0:T(8,128)(2,1)S(1)}, u32[]{:S(2)}, u32[]{:S(2)}) async-start(bf16[4,1024,128]{2,1,0:T(8,128)(2,1)} %bitcast.16), calls=%async_computation | async-start | bytes 2097152 | tf_op jit(solution)/shard_map/all_to_all | solution.py:210
  88.3 3.2 %copy-start = (bf16[16,16,128,128]{3,1,0,2:T(8,128)(2,1)}, bf16[16,16,128,128]{3,1,0,2:T(8,128)(2,1)S(1)}, u32[]{:S(2)}) copy-start(bf16[16,16,128,128]{3,1,0,2:T(8,128)(2,1)S(1)} %multiply_convert_fusion) | copy-start | bytes 25165828
  93.8 0.6 copy-start.3
  94.4 20.8 %copy-start.4 = (s32[3,6,256]{2,1,0:T(8,128)S(1)}, s32[3,6,256]{2,1,0:T(8,128)}, u32[]{:S(2)}) copy-start(s32[3,6,256]{2,1,0:T(8,128)} %param.11) | copy-start | bytes 55300
  94.5 1.6 %collective-permute-start.4 = (f32[256,262]{0,1:T(8,128)S(1)}, f32[256,262]{0,1:T(8,128)S(1)}, u32[]{:S(2)}, u32[]{:S(2)}) collective-permute-start(f32[256,262]{0,1:T(8,128)S(1)} %pad_maximum_fusion), channel_id=1, source_target_pairs={{0,1},{1,0},{2,3},{3,2},{4,5},{5,4},{6,7},{7,6},{8,9},{9,8},{10,11... | collective-permute-start | bytes 804872 | tf_op jit(solution)/shard_map/ppermute | solution.py:53
  96.8 5.7 %collective-permute-start.5 = (f32[128,262]{0,1:T(8,128)S(1)}, f32[128,262]{0,1:T(8,128)S(1)}, u32[]{:S(2)}, u32[]{:S(2)}) collective-permute-start(f32[128,262]{0,1:T(8,128)S(1)} %slice_select_fusion), channel_id=1, source_target_pairs={{0,2},{2,0},{1,3},{3,1},{4,6},{6,4},{5,7},{7,5},{8,10},{10,8},{9,1... | collective-permute-start | bytes 402440 | tf_op jit(solution)/shard_map/ppermute | solution.py:43
  102.6 5.1 %collective-permute-start.6 = (f32[128,262]{0,1:T(8,128)S(1)}, f32[128,262]{0,1:T(8,128)S(1)}, u32[]{:S(2)}, u32[]{:S(2)}) collective-permute-start(f32[128,262]{0,1:T(8,128)S(1)} %fusion.60), channel_id=1, source_target_pairs={{0,4},{4,0},{8,12},{12,8},{1,5},{5,1},{9,13},{13,9},{2,6},{6,2},{1... | collective-permute-start | bytes 402440 | tf_op jit(solution)/shard_map/ppermute | solution.py:43
  107.7 7.5 %collective-permute-start.7 = (f32[128,262]{0,1:T(8,128)S(1)}, f32[128,262]{0,1:T(8,128)S(1)}, u32[]{:S(2)}, u32[]{:S(2)}) collective-permute-start(f32[128,262]{0,1:T(8,128)S(1)} %add.118), channel_id=1, source_target_pairs={{0,8},{4,12},{8,0},{12,4},{1,9},{5,13},{9,1},{13,5},{2,10},{6,14},... | collective-permute-start | bytes 402440 | tf_op jit(solution)/shard_map/ppermute | solution.py:43
  115.2 1.4 collective-permute-start.8
  146.9 2.1 %copy-start.2 = (f32[3,8,256]{2,1,0:T(8,128)S(1)}, f32[3,8,256]{2,1,0:T(8,128)}, u32[]{:S(2)}) copy-start(f32[3,8,256]{2,1,0:T(8,128)} %shard_map.59) | copy-start | bytes 73732

commit v13 on v12

--- a/solution.py
+++ b/solution.py
@@ -107,6 +107,23 @@
             direction = remain + (norm_next / (norm_now + epsilon)) * direction
             norm_now = norm_next
         out_ref[pass_index] = solution_all
+
+
+def halving_sum(value, scatter_axes, rest_axes):
+    if not scatter_axes:
+        return tree_sum(value, rest_axes)
+    axis = scatter_axes[0]
+    if lax.axis_size(axis) != 2 or value.shape[0] % 16:
+        return tree_sum(value, scatter_axes + rest_axes)
+    swap = [(0, 1), (1, 0)]
+    first = lax.axis_index(axis) == 0
+    half = value.shape[0] // 2
+    keep = jnp.where(first, value[:half], value[half:])
+    give = jnp.where(first, value[half:], value[:half])
+    keep = keep + lax.ppermute(give, axis, swap)
+    keep = halving_sum(keep, scatter_axes[1:], rest_axes)
+    other = lax.ppermute(keep, axis, swap)
+    return jnp.where(first, jnp.concatenate([keep, other]), jnp.concatenate([other, keep]))
 
 
 def kernel(spread):
@@ -237,7 +254,9 @@
         gram_step,
         (jnp.zeros((TERMS, TERMS), jnp.float32), jnp.zeros((TERMS, STRESS), jnp.float32)),
     )
-    full_rows = split_sum(jnp.concatenate([gram_part, rhs_part], axis=1), "rep", ("slab", "cols"))
+    full_rows = halving_sum(
+        jnp.concatenate([gram_part, rhs_part], axis=1), ("rep", "slab"), ("cols",)
+    )
     gram_matrix = full_rows[:, :TERMS]
     rhs_sums = full_rows[:, TERMS:]
     on_diagonal = lax.broadcasted_iota(jnp.int32, (TERMS, TERMS), 0) == lax.broadcasted_iota(

time: 150 us -> 155 us (1.033)
  waiting for transfers between devices: 46.8 us -> 51.2 us
    ppermute x2 -> x4, waiting for transfers between devices: 2.23 us -> 11.7 us  [the longest x2 6.45 us: halving_sum(): keep = keep + lax.ppermute(give, axis, swap)]
    ppermute x3 -> x2, waiting for transfers between devices: 17.5 us -> 12.4 us  [tree_sum(): value = value + lax.ppermute(value, axis, partner)]
  transfers between devices with their start and end apart: 10 -> 11, of which waited for: 8 -> 9; matrix products, arithmetic and copies ran while one was open for 22% -> 21% of each run, Pallas kernels for 0% -> 0%
where the time goes in v13:
time: 155 us
  waiting for transfers between devices  51.2 us (33%)
  matrix products  42.8 us (28%)
  blocking collectives  18 us (12%)
  local copies, waits for them, and re-layouts  17.8 us (11%)
  starting transfers between devices  10 us (6%)
  other arithmetic  8.08 us (5%)
  Pallas kernels  5.98 us (4%)
    all_to_all x1, waiting for transfers between devices, local(): sets = lax.all_to_all(sets, 'cols', 0, 0, tiled=True)  21.1 us
    all_gather x1, blocking collectives, local(): misfit = lax.all_gather(misfit, 'cols', axis=1, tiled=True)  18 us
    dot_general x1, matrix products, local(): jnp.einsum('cpxz,sxm->scpmz', fields.astype(jnp.float32), stream_table[:,...  16 us
    ppermute x2, waiting for transfers between devices, tree_sum(): value = value + lax.ppermute(value, axis, partner)  12.4 us
    ppermute x2, waiting for transfers between devices, halving_sum(): keep = keep + lax.ppermute(give, axis, swap)  6.45 us
    ppermute x4, waiting for transfers between devices, neighbour_edges(): return (lax.ppermute(last, axis, up), lax.ppermute(leading, axis, down))  5.99 us
    pallas_call x1, Pallas kernels, local(): pl.pallas_call(conjugate_passes, out_shape=jax.ShapeDtypeStruct((PASSES,...  5.98 us
    dot_general x1, matrix products, local(): jnp.einsum('scpmz,zsn->scpmn', along_stream, span_table[width:width + cel...  5.53 us
  transfers between devices with their start and end apart: 11, of which 9 were waited for; matrix products, arithmetic and copies ran while one was open for 21% of the time, Pallas kernels for 0%

profile of v13, /device:TPU:0, one launch (start us, length us, event | category | flops | bytes accessed | tf_op | source)
XLA Modules:
  0.0 154.9 jit_solution(3849953156713192878)
XLA Ops:
  0.6 0.9 fusion.52
  2.2 1.5 select_select_fusion
  3.7 16.0 %fusion.2 = f32[2,256,4,4,256]{1,4,3,2,0:T(8,128)S(1)} fusion(bf16[4,4,1024,256]{3,2,1,0:T(8,128)(2,1)} %param.8, f32[2,1034,256]{2,1,0:T(8,128)S(1)} %select_select_fusion), kind=kOutput, calls=%fused_computation.3 | convolution fusion | flops 25769803776 | bytes 18874368 | tf_op jit(solution)/shard_map/cpxz,sxm->scpmz/dot_general | solution.py:182
  20.0 3.5 %fusion.36 = f32[2,256,4,4,256]{1,4,3,2,0:T(8,128)S(1)} fusion(bf16[4,4,5,256]{3,2,1,0:T(8,128)(2,1)S(1)} %collective-permute-done, f32[2,1034,256]{2,1,0:T(8,128)S(1)} %select_select_fusion), kind=kOutput, calls=%fused_computation.68 | convolution fusion | flops 125829120 | bytes 8470528 | tf_op jit(solution)/shard_map/cpxz,sxm->scpmz/dot_general | solution.py:188
  23.5 4.4 %add_add_fusion = f32[2,256,4,4,256]{1,4,3,2,0:T(8,128)S(1)} fusion(f32[2,256,4,4,256]{1,4,3,2,0:T(8,128)S(1)} %fusion.2, f32[2,256,4,4,256]{1,4,3,2,0:T(8,128)S(1)} %fusion.36, bf16[4,4,5,256]{3,2,1,0:T(8,128)(2,1)S(1)} %collective-permute-done.1, f32[2,1034,256]{2,1,0:T(8,128)S(1)} %select_select_fusion), kind=kOutput, calls=%fused_computation.5 | convolution fusion | flops 130023424 | bytes 25247744 | tf_op jit(solution)/shard_map/cpxz,sxm->scpmz/dot_general | solution.py:191
  28.0 3.0 %collective-permute-start.2 = (f32[2,4,4,5,256]{4,3,2,1,0:T(8,128)S(1)}, f32[2,4,4,5,256]{4,3,2,1,0:T(8,128)S(1)}, u32[]{:S(2)}, u32[]{:S(2)}) collective-permute-start(f32[2,4,4,5,256]{4,3,2,1,0:T(8,128)S(1)} %get-tuple-element.73), channel_id=1, source_target_pairs={{0,2},{2,0},{1,3},{3,1},{4,6},{6,4},{5,7},{7,5},{8,10},{10,8},{9,1... | collective-permute-start | bytes 491528 | tf_op jit(solution)/shard_map/ppermute | solution.py:68
  31.0 5.5 %fusion = f32[2,4,4,256,64]{3,4,2,1,0:T(8,128)S(1)} fusion(f32[2,256,4,4,256]{1,4,3,2,0:T(8,128)S(1)} %add_add_fusion, f32[266,2,64]{0,2,1:T(8,128)S(1)} %select_select_fusion.1), kind=kOutput, calls=%fused_computation.1 | convolution fusion | flops 1610612736 | bytes 10616832 | tf_op jit(solution)/shard_map/scpmz,zsn->scpmn/dot_general | solution.py:200
  36.6 0.9 collective-permute-done.2
  37.5 2.0 %fusion.34 = f32[2,4,4,256,64]{3,4,2,1,0:T(8,128)S(1)} fusion(f32[2,4,4,5,256]{4,3,2,1,0:T(8,128)S(1)} %collective-permute-done.2, f32[266,2,64]{0,2,1:T(8,128)S(1)} %select_select_fusion.1), kind=kOutput, calls=%fused_computation.66 | convolution fusion | flops 31457280 | bytes 2424832 | tf_op jit(solution)/shard_map/scpzm,zsn->scpmn/dot_general | solution.py:206
  39.5 5.0 %collective-permute-done.3 = f32[2,4,4,5,256]{4,3,2,1,0:T(8,128)S(1)} collective-permute-done((f32[2,4,4,5,256]{4,3,2,1,0:T(8,128)S(1)}, f32[2,4,4,5,256]{4,3,2,1,0:T(8,128)S(1)}, u32[]{:S(2)}, u32[]{:S(2)}) %collective-permute-start.3) | collective-permute-done | bytes 163872 | tf_op jit(solution)/shard_map/ppermute | solution.py:68
  44.6 2.1 %add_add_fusion.1 = f32[2,4,4,256,64]{3,4,2,1,0:T(8,128)S(1)} fusion(f32[2,4,4,256,64]{3,4,2,1,0:T(8,128)S(1)} %fusion, f32[2,4,4,256,64]{3,4,2,1,0:T(8,128)S(1)} %fusion.34, f32[2,4,4,5,256]{4,3,2,1,0:T(8,128)S(1)} %collective-permute-done.3, f32[266,2,64]{0,2,1:T(8,128)S(1)} %select_select_fusion.1), kind=kOutput, calls=%fused_computation.22 | convolution fusion | flops 32505856 | bytes 6619136 | tf_op jit(solution)/shard_map/scpzm,zsn->scpmn/dot_general | solution.py:207
  46.8 0.9 slice.196
  48.6 1.5 copy.29
  51.0 1.1 copy.31
  52.0 4.9 %all-to-all-start = ((bf16[4,1024,128]{2,1,0:T(8,128)(2,1)}), bf16[4,1024,128]{2,1,0:T(8,128)(2,1)S(1)}, u32[]{:S(2)}, u32[]{:S(2)}) async-start(bf16[4,1024,128]{2,1,0:T(8,128)(2,1)} %bitcast.16), calls=%async_computation | async-start | bytes 2097152 | tf_op jit(solution)/shard_map/all_to_all | solution.py:227
  58.1 1.5 reshape_reshape.3
  59.6 0.9 constant_dynamic-slice_fusion.1
  60.5 21.1 %all-to-all-done = bf16[4,1024,128]{2,1,0:T(8,128)(2,1)S(1)} async-done(((bf16[4,1024,128]{2,1,0:T(8,128)(2,1)}), bf16[4,1024,128]{2,1,0:T(8,128)(2,1)S(1)}, u32[]{:S(2)}, u32[]{:S(2)}) %all-to-all-start) | async-done | bytes 1048608 | tf_op jit(solution)/shard_map/all_to_all | solution.py:227
  82.7 1.6 %copy.33 = f32[16,128,128]{2,0,1:T(8,128)} copy(f32[16,128,128]{2,1,0:T(8,128)S(1)} %bitcast_convert_fusion) | data formatting | bytes 2097152 | tf_op jit(solution)/shard_map/while/body/eval_jaxpr/convert_element_type | solution.py:154
  84.3 4.1 %multiply_convert_fusion = bf16[16,16,128,128]{3,1,0,2:T(8,128)(2,1)S(1)} fusion(f32[16,128,128]{2,0,1:T(8,128)} %copy.33, f32[16,128,128]{2,0,1:T(8,128)S(1)} %copy.32), kind=kLoop, calls=%fused_computation | loop fusion | flops 8388608 | bytes 10485760 | tf_op jit(solution)/shard_map/while/body/eval_jaxpr/convert_element_type | solution.py:156
  88.3 2.4 %convolution_bitcast_fusion = f32[256,256]{0,1:T(8,128)S(1)} fusion(bf16[256,128,128]{2,0,1:T(8,128)(2,1)S(1)} %bitcast.83), kind=kOutput, calls=%fused_computation.26 | convolution fusion | flops 2147483648 | bytes 8650752 | tf_op jit(solution)/shard_map/while/body/eval_jaxpr/iqr,jqr->ij/dot_general | solution.py:243
  90.7 0.9 copy-done
  91.6 2.3 %convolution_bitcast_fusion.1 = f32[256,6]{0,1:T(8,128)S(1)} fusion(bf16[256,128,128]{2,0,1:T(8,128)(2,1)S(1)} %bitcast.84, bf16[6,1,128,128]{3,2,1,0:T(8,128)(2,1)S(1)} %constant_dynamic-slice_fusion.1), kind=kOutput, calls=%fused_computation.27 | convolution fusion | flops 50331648 | bytes 8591360 | tf_op jit(solution)/shard_map/while/body/eval_jaxpr/iqr,kqr->ik/dot_general | solution.py:246
  94.6 1.3 collective-permute-done.4
  97.3 5.1 %collective-permute-done.5 = f32[64,262]{0,1:T(8,128)S(1)} collective-permute-done((f32[64,262]{0,1:T(8,128)S(1)}, f32[64,262]{0,1:T(8,128)S(1)}, u32[]{:S(2)}, u32[]{:S(2)}) %collective-permute-start.5) | collective-permute-done | bytes 67104 | tf_op jit(solution)/shard_map/ppermute | solution.py:123
  102.6 5.0 %collective-permute-done.6 = f32[64,262]{0,1:T(8,128)S(1)} collective-permute-done((f32[64,262]{0,1:T(8,128)S(1)}, f32[64,262]{0,1:T(8,128)S(1)}, u32[]{:S(2)}, u32[]{:S(2)}) %collective-permute-start.6) | collective-permute-done | bytes 67104 | tf_op jit(solution)/shard_map/ppermute | solution.py:43
  107.8 7.4 %collective-permute-done.7 = f32[64,262]{0,1:T(8,128)S(1)} collective-permute-done((f32[64,262]{0,1:T(8,128)S(1)}, f32[64,262]{0,1:T(8,128)S(1)}, u32[]{:S(2)}, u32[]{:S(2)}) %collective-permute-start.7) | collective-permute-done | bytes 67104 | tf_op jit(solution)/shard_map/ppermute | solution.py:43
  115.8 4.5 %collective-permute-done.8 = f32[64,262]{0,1:T(8,128)S(1)} collective-permute-done((f32[64,262]{0,1:T(8,128)S(1)}, f32[64,262]{0,1:T(8,128)S(1)}, u32[]{:S(2)}, u32[]{:S(2)}) %collective-permute-start.8) | collective-permute-done | bytes 67104 | tf_op jit(solution)/shard_map/ppermute | solution.py:125
  123.5 6.0 %shard_map.59 = f32[3,8,256]{2,1,0:T(8,128)} custom-call(f32[256,256]{1,0:T(8,128)} %copy.36.gram_ref, f32[8,256]{1,0:T(8,128)} %scatter.6.target_ref, f32[3,8,256]{2,1,0:T(8,128)} %scatter.9.mask_ref), custom_call_target="tpu_custom_call" | custom-call | tf_op jit(solution)/shard_map/pallas_call | solution.py:277
  129.4 4.6 %fusion.17 = bf16[6,128,128]{2,0,1:T(8,128)(2,1)S(1)} fusion(bf16[256,128,128]{2,0,1:T(8,128)(2,1)} %bitcast.85, bf16[6,1,128,128]{3,2,1,0:T(8,128)(2,1)S(1)} %constant_dynamic-slice_fusion.1, f32[3,8,256]{2,1,0:T(8,128)} %shard_map.59, f32[256]{0:T(256)S(1)} %add_rsqrt_fusion), kind=kOutput, calls=%fused_computation.25 | convolution fusion | flops 50629632 | bytes 8791040 | tf_op jit(solution)/shard_map/while/body/eval_jaxpr/ki,iqr->kqr/dot_general | solution.py:290
  134.1 18.0 %all_gather.3 = bf16[6,512,128]{2,1,0:T(8,128)(2,1)S(1)} all-gather(bf16[6,128,128]{2,1,0:T(8,128)(2,1)S(1)} %copy.37), channel_id=1, replica_groups=mesh['groups'=2,'cols'=4,'slab'=2,'rep'=2] {'cols'}, dimensions={1}, use_global_device_ids=true | all-gather | bytes 983040 | tf_op jit(solution)/shard_map/all_gather | solution.py:300
  152.8 1.4 copy.38
  (65 shorter events, 12.6 us)
Async XLA Ops:
  1.5 18.5 %collective-permute-start = (bf16[4,4,5,256]{3,2,1,0:T(8,128)(2,1)S(1)}, bf16[4,4,5,256]{3,2,1,0:T(8,128)(2,1)S(1)}, u32[]{:S(2)}, u32[]{:S(2)}) collective-permute-start(bf16[4,4,5,256]{3,2,1,0:T(8,128)(2,1)S(1)} %get-tuple-element.75), channel_id=1, source_target_pairs={{0,1},{1,0},{2,3},{3,2},{4,5},{5,4},{6,7},{7,6},{8,9},{9,8},{10,11... | collective-permute-start | bytes 122888 | tf_op jit(solution)/shard_map/ppermute | solution.py:68
  2.0 21.5 %collective-permute-start.1 = (bf16[4,4,5,256]{3,2,1,0:T(8,128)(2,1)S(1)}, bf16[4,4,5,256]{3,2,1,0:T(8,128)(2,1)S(1)}, u32[]{:S(2)}, u32[]{:S(2)}) collective-permute-start(bf16[4,4,5,256]{3,2,1,0:T(8,128)(2,1)S(1)} %get-tuple-element.74), channel_id=1, source_target_pairs={{1,0},{0,1},{3,2},{2,3},{5,4},{4,5},{7,6},{6,7},{9,8},{8,9},{11,10... | collective-permute-start | bytes 122888 | tf_op jit(solution)/shard_map/ppermute | solution.py:68
  3.7 16.3 %copy-start.5 = (s32[4]{0:T(128)S(1)}, s32[4]{0:T(128)}, u32[]{:S(2)}) copy-start(s32[4]{0:T(128)} %param.10) | copy-start | bytes 52
  28.0 9.5 %collective-permute-start.2 = (f32[2,4,4,5,256]{4,3,2,1,0:T(8,128)S(1)}, f32[2,4,4,5,256]{4,3,2,1,0:T(8,128)S(1)}, u32[]{:S(2)}, u32[]{:S(2)}) collective-permute-start(f32[2,4,4,5,256]{4,3,2,1,0:T(8,128)S(1)} %get-tuple-element.73), channel_id=1, source_target_pairs={{0,2},{2,0},{1,3},{3,1},{4,6},{6,4},{5,7},{7,5},{8,10},{10,8},{9,1... | collective-permute-start | bytes 491528 | tf_op jit(solution)/shard_map/ppermute | solution.py:68
  36.5 8.1 %collective-permute-start.3 = (f32[2,4,4,5,256]{4,3,2,1,0:T(8,128)S(1)}, f32[2,4,4,5,256]{4,3,2,1,0:T(8,128)S(1)}, u32[]{:S(2)}, u32[]{:S(2)}) collective-permute-start(f32[2,4,4,5,256]{4,3,2,1,0:T(8,128)S(1)} %get-tuple-element.72), channel_id=1, source_target_pairs={{2,0},{0,2},{3,1},{1,3},{6,4},{4,6},{7,5},{5,7},{10,8},{8,10},{11,... | collective-permute-start | bytes 491528 | tf_op jit(solution)/shard_map/ppermute | solution.py:68
  50.9 5.9 %copy-start.1 = (bf16[6,4,256,64]{2,3,1,0:T(8,128)(2,1)S(1)}, bf16[6,4,256,64]{2,3,1,0:T(8,128)(2,1)}, u32[]{:S(2)}) copy-start(bf16[6,4,256,64]{2,3,1,0:T(8,128)(2,1)} %param.9) | copy-start | bytes 2359300
  52.0 29.7 %all-to-all-start = ((bf16[4,1024,128]{2,1,0:T(8,128)(2,1)}), bf16[4,1024,128]{2,1,0:T(8,128)(2,1)S(1)}, u32[]{:S(2)}, u32[]{:S(2)}) async-start(bf16[4,1024,128]{2,1,0:T(8,128)(2,1)} %bitcast.16), calls=%async_computation | async-start | bytes 2097152 | tf_op jit(solution)/shard_map/all_to_all | solution.py:227
  88.3 3.2 %copy-start = (bf16[16,16,128,128]{3,1,0,2:T(8,128)(2,1)}, bf16[16,16,128,128]{3,1,0,2:T(8,128)(2,1)S(1)}, u32[]{:S(2)}) copy-start(bf16[16,16,128,128]{3,1,0,2:T(8,128)(2,1)S(1)} %multiply_convert_fusion) | copy-start | bytes 25165828
  93.8 0.6 copy-start.3
  94.4 26.0 %copy-start.4 = (s32[3,6,256]{2,1,0:T(8,128)S(1)}, s32[3,6,256]{2,1,0:T(8,128)}, u32[]{:S(2)}) copy-start(s32[3,6,256]{2,1,0:T(8,128)} %param.11) | copy-start | bytes 55300
  94.5 1.4 collective-permute-start.4
  96.7 5.7 %collective-permute-start.5 = (f32[64,262]{0,1:T(8,128)S(1)}, f32[64,262]{0,1:T(8,128)S(1)}, u32[]{:S(2)}, u32[]{:S(2)}) collective-permute-start(f32[64,262]{0,1:T(8,128)S(1)} %slice_select_fusion), channel_id=1, source_target_pairs={{0,2},{2,0},{1,3},{3,1},{4,6},{6,4},{5,7},{7,5},{8,10},{10,8},{9,1... | collective-permute-start | bytes 201224 | tf_op jit(solution)/shard_map/ppermute | solution.py:123
  102.5 5.1 %collective-permute-start.6 = (f32[64,262]{0,1:T(8,128)S(1)}, f32[64,262]{0,1:T(8,128)S(1)}, u32[]{:S(2)}, u32[]{:S(2)}) collective-permute-start(f32[64,262]{0,1:T(8,128)S(1)} %select_add_fusion), channel_id=1, source_target_pairs={{0,4},{4,0},{8,12},{12,8},{1,5},{5,1},{9,13},{13,9},{2,6},{6,2},{1... | collective-permute-start | bytes 201224 | tf_op jit(solution)/shard_map/ppermute | solution.py:43
  107.6 7.5 %collective-permute-start.7 = (f32[64,262]{0,1:T(8,128)S(1)}, f32[64,262]{0,1:T(8,128)S(1)}, u32[]{:S(2)}, u32[]{:S(2)}) collective-permute-start(f32[64,262]{0,1:T(8,128)S(1)} %add.118), channel_id=1, source_target_pairs={{0,8},{4,12},{8,0},{12,4},{1,9},{5,13},{9,1},{13,5},{2,10},{6,14},... | collective-permute-start | bytes 201224 | tf_op jit(solution)/shard_map/ppermute | solution.py:43
  115.2 5.1 %collective-permute-start.8 = (f32[64,262]{0,1:T(8,128)S(1)}, f32[64,262]{0,1:T(8,128)S(1)}, u32[]{:S(2)}, u32[]{:S(2)}) collective-permute-start(f32[64,262]{0,1:T(8,128)S(1)} %add.119), channel_id=1, source_target_pairs={{0,2},{2,0},{1,3},{3,1},{4,6},{6,4},{5,7},{7,5},{8,10},{10,8},{9,1... | collective-permute-start | bytes 201224 | tf_op jit(solution)/shard_map/ppermute | solution.py:125
  120.4 1.4 collective-permute-start.9
  152.1 2.1 %copy-start.2 = (f32[3,8,256]{2,1,0:T(8,128)S(1)}, f32[3,8,256]{2,1,0:T(8,128)}, u32[]{:S(2)}) copy-start(f32[3,8,256]{2,1,0:T(8,128)} %shard_map.59) | copy-start | bytes 73732

commit v14 on v12

--- a/solution.py
+++ b/solution.py
@@ -65,6 +65,9 @@
     down = [(j, i) for i, j in up]
     last = lax.slice_in_dim(array, length - width, length, axis=dim)
     leading = lax.slice_in_dim(array, 0, width, axis=dim)
+    if count == 2:
+        both = lax.ppermute(jnp.stack([last, leading]), axis, up)
+        return (both[0], both[1])
     return (lax.ppermute(last, axis, up), lax.ppermute(leading, axis, down))
 
 

time: 150 us -> 152 us (1.013)
    ppermute x4 -> x2, waiting for transfers between devices: 5.99 us -> 7.03 us  [neighbour_edges(): both = lax.ppermute(jnp.stack([last, leading]), axis, up)]
    ppermute x4 -> x2, starting transfers between devices: 3.64 us -> 3.11 us  [neighbour_edges(): both = lax.ppermute(jnp.stack([last, leading]), axis, up)]
  transfers between devices with their start and end apart: 10 -> 8, of which waited for: 8 -> 7; matrix products, arithmetic and copies ran while one was open for 22% -> 18% of each run, Pallas kernels for 0% -> 0%
where the time goes in v14:
time: 152 us; the launch traced here: 151 us
  waiting for transfers between devices  47.7 us (31%)
  matrix products  42.8 us (28%)
  blocking collectives  18 us (12%)
  local copies, waits for them, and re-layouts  17.8 us (12%)
  starting transfers between devices  10.1 us (7%)
  other arithmetic  7.88 us (5%)
  Pallas kernels  5.97 us (4%)
    all_to_all x1, waiting for transfers between devices, local(): sets = lax.all_to_all(sets, 'cols', 0, 0, tiled=True)  21.9 us
    all_gather x1, blocking collectives, local(): misfit = lax.all_gather(misfit, 'cols', axis=1, tiled=True)  18 us
    ppermute x3, waiting for transfers between devices, tree_sum(): value = value + lax.ppermute(value, axis, partner)  16.5 us
    dot_general x1, matrix products, local(): jnp.einsum('cpxz,sxm->scpmz', fields.astype(jnp.float32), stream_table[:,...  16 us
    ppermute x2, waiting for transfers between devices, neighbour_edges(): both = lax.ppermute(jnp.stack([last, leading]), axis, up)  7.03 us
    pallas_call x1, Pallas kernels, local(): pl.pallas_call(conjugate_passes, out_shape=jax.ShapeDtypeStruct((PASSES,...  5.97 us
    dot_general x1, matrix products, local(): jnp.einsum('scpmz,zsn->scpmn', along_stream, span_table[width:width + cel...  5.53 us
    all_to_all x1, starting transfers between devices, local(): sets = lax.all_to_all(sets, 'cols', 0, 0, tiled=True)  5.12 us
  transfers between devices with their start and end apart: 8, of which 7 were waited for; matrix products, arithmetic and copies ran while one was open for 18% of the time, Pallas kernels for 0%

profile of v14, /device:TPU:0, one launch (start us, length us, event | category | flops | bytes accessed | tf_op | source)
XLA Modules:
  0.0 151.3 jit_solution(10967210480522247115)
XLA Ops:
  0.6 0.9 slice_bitcast_fusion.19
  2.1 1.5 select_select_fusion
  3.6 16.0 %fusion.2 = f32[2,256,4,4,256]{1,4,3,2,0:T(8,128)S(1)} fusion(bf16[4,4,1024,256]{3,2,1,0:T(8,128)(2,1)} %param.8, f32[2,1034,256]{2,1,0:T(8,128)S(1)} %select_select_fusion), kind=kOutput, calls=%fused_computation.3 | convolution fusion | flops 25769803776 | bytes 18874368 | tf_op jit(solution)/shard_map/cpxz,sxm->scpmz/dot_general | solution.py:168
  20.0 3.5 %fusion.34 = f32[2,256,4,4,256]{1,4,3,2,0:T(8,128)S(1)} fusion(bf16[2,4,4,5,256]{4,3,2,1,0:T(8,128)(2,1)S(1)} %collective-permute-done, f32[2,1034,256]{2,1,0:T(8,128)S(1)} %select_select_fusion), kind=kOutput, calls=%fused_computation.68 | convolution fusion | flops 125829120 | bytes 8470528 | tf_op jit(solution)/shard_map/cpxz,sxm->scpmz/dot_general | solution.py:174
  23.5 4.4 %add_add_fusion = f32[2,256,4,4,256]{1,4,3,2,0:T(8,128)S(1)} fusion(f32[2,256,4,4,256]{1,4,3,2,0:T(8,128)S(1)} %fusion.2, f32[2,256,4,4,256]{1,4,3,2,0:T(8,128)S(1)} %fusion.34, bf16[2,4,4,5,256]{4,3,2,1,0:T(8,128)(2,1)S(1)} %collective-permute-done, f32[2,1034,256]{2,1,0:T(8,128)S(1)} %select_select_fusion), kind=kOutput, calls=%fused_computation.5 | convolution fusion | flops 130023424 | bytes 25247744 | tf_op jit(solution)/shard_map/cpxz,sxm->scpmz/dot_general | solution.py:177
  28.0 2.6 %collective-permute-start.1 = (f32[2,2,4,4,5,256]{5,4,3,2,1,0:T(8,128)S(1)}, f32[2,2,4,4,5,256]{5,4,3,2,1,0:T(8,128)S(1)}, u32[]{:S(2)}, u32[]{:S(2)}) collective-permute-start(f32[2,2,4,4,5,256]{5,4,3,2,1,0:T(8,128)S(1)} %pad_maximum_fusion), channel_id=1, source_target_pairs={{0,2},{2,0},{1,3},{3,1},{4,6},{6,4},{5,7},{7,5},{8,10},{10,8},{9,1... | collective-permute-start | bytes 983048 | tf_op jit(solution)/shard_map/ppermute | solution.py:69
  30.6 5.5 %fusion = f32[2,4,4,256,64]{3,4,2,1,0:T(8,128)S(1)} fusion(f32[2,256,4,4,256]{1,4,3,2,0:T(8,128)S(1)} %add_add_fusion, f32[266,2,64]{0,2,1:T(8,128)S(1)} %select_select_fusion.1), kind=kOutput, calls=%fused_computation.1 | convolution fusion | flops 1610612736 | bytes 10616832 | tf_op jit(solution)/shard_map/scpmz,zsn->scpmn/dot_general | solution.py:186
  36.1 7.0 %collective-permute-done.1 = f32[2,2,4,4,5,256]{5,4,3,2,1,0:T(8,128)S(1)} collective-permute-done((f32[2,2,4,4,5,256]{5,4,3,2,1,0:T(8,128)S(1)}, f32[2,2,4,4,5,256]{5,4,3,2,1,0:T(8,128)S(1)}, u32[]{:S(2)}, u32[]{:S(2)}) %collective-permute-start.1) | collective-permute-done | bytes 327712 | tf_op jit(solution)/shard_map/ppermute | solution.py:69
  43.1 2.0 %fusion.18 = f32[2,4,4,256,64]{3,4,2,1,0:T(8,128)S(1)} fusion(f32[2,2,4,4,5,256]{5,4,3,2,1,0:T(8,128)S(1)} %collective-permute-done.1, f32[266,2,64]{0,2,1:T(8,128)S(1)} %select_select_fusion.1), kind=kOutput, calls=%fused_computation.38 | convolution fusion | flops 31457280 | bytes 2424832 | tf_op jit(solution)/shard_map/scpzm,zsn->scpmn/dot_general | solution.py:192
  45.2 2.1 %add_add_fusion.1 = f32[2,4,4,256,64]{3,4,2,1,0:T(8,128)S(1)} fusion(f32[2,4,4,256,64]{3,4,2,1,0:T(8,128)S(1)} %fusion, f32[2,4,4,256,64]{3,4,2,1,0:T(8,128)S(1)} %fusion.18, f32[2,2,4,4,5,256]{5,4,3,2,1,0:T(8,128)S(1)} %collective-permute-done.1, f32[266,2,64]{0,2,1:T(8,128)S(1)} %select_select_fusion.1), kind=kOutput, calls=%fused_computation.22 | convolution fusion | flops 32505856 | bytes 6619136 | tf_op jit(solution)/shard_map/scpzm,zsn->scpmn/dot_general | solution.py:193
  47.4 0.9 slice.198
  49.2 1.5 %copy.29 = bf16[1,4,4,256,64]{4,3,2,1,0:T(8,128)(2,1)S(1)} copy(bf16[1,4,4,256,64]{3,4,2,1,0:T(8,128)(2,1)} %slice.198) | data formatting | bytes 1048576 | tf_op jit(solution)/shard_map/slice | solution.py:195
  51.5 1.1 copy.31
  52.6 5.1 %all-to-all-start = ((bf16[4,1024,128]{2,1,0:T(8,128)(2,1)}), bf16[4,1024,128]{2,1,0:T(8,128)(2,1)S(1)}, u32[]{:S(2)}, u32[]{:S(2)}) async-start(bf16[4,1024,128]{2,1,0:T(8,128)(2,1)} %bitcast.24), calls=%async_computation | async-start | bytes 2097152 | tf_op jit(solution)/shard_map/all_to_all | solution.py:213
  58.1 0.9 copy.34
  59.0 1.5 reshape_reshape.3
  60.4 0.9 constant_dynamic-slice_fusion.1
  61.4 21.9 %all-to-all-done = bf16[4,1024,128]{2,1,0:T(8,128)(2,1)S(1)} async-done(((bf16[4,1024,128]{2,1,0:T(8,128)(2,1)}), bf16[4,1024,128]{2,1,0:T(8,128)(2,1)S(1)}, u32[]{:S(2)}, u32[]{:S(2)}) %all-to-all-start) | async-done | bytes 1048608 | tf_op jit(solution)/shard_map/all_to_all | solution.py:213
  84.3 1.6 %copy.33 = f32[16,128,128]{2,0,1:T(8,128)} copy(f32[16,128,128]{2,1,0:T(8,128)S(1)} %bitcast_convert_fusion) | data formatting | bytes 2097152 | tf_op jit(solution)/shard_map/while/body/eval_jaxpr/convert_element_type | solution.py:140
  85.9 4.1 %multiply_convert_fusion = bf16[16,16,128,128]{3,1,0,2:T(8,128)(2,1)S(1)} fusion(f32[16,128,128]{2,0,1:T(8,128)} %copy.33, f32[16,128,128]{2,0,1:T(8,128)S(1)} %copy.32), kind=kLoop, calls=%fused_computation | loop fusion | flops 8388608 | bytes 10485760 | tf_op jit(solution)/shard_map/while/body/eval_jaxpr/convert_element_type | solution.py:142
  90.0 2.4 %convolution_bitcast_fusion = f32[256,256]{0,1:T(8,128)S(1)} fusion(bf16[256,128,128]{2,0,1:T(8,128)(2,1)S(1)} %bitcast.97), kind=kOutput, calls=%fused_computation.26 | convolution fusion | flops 2147483648 | bytes 8650752 | tf_op jit(solution)/shard_map/while/body/eval_jaxpr/iqr,jqr->ij/dot_general | solution.py:229
  92.3 0.9 copy-done
  93.2 2.3 %convolution_bitcast_fusion.1 = f32[256,6]{0,1:T(8,128)S(1)} fusion(bf16[256,128,128]{2,0,1:T(8,128)(2,1)S(1)} %bitcast.98, bf16[6,1,128,128]{3,2,1,0:T(8,128)(2,1)S(1)} %constant_dynamic-slice_fusion.1), kind=kOutput, calls=%fused_computation.27 | convolution fusion | flops 50331648 | bytes 8591360 | tf_op jit(solution)/shard_map/while/body/eval_jaxpr/iqr,kqr->ik/dot_general | solution.py:232
  96.2 1.5 %collective-permute-done.2 = f32[256,262]{0,1:T(8,128)S(1)} collective-permute-done((f32[256,262]{0,1:T(8,128)S(1)}, f32[256,262]{0,1:T(8,128)S(1)}, u32[]{:S(2)}, u32[]{:S(2)}) %collective-permute-start.2) | collective-permute-done | bytes 268320 | tf_op jit(solution)/shard_map/ppermute | solution.py:53
  98.5 1.6 %collective-permute-start.3 = (f32[128,262]{0,1:T(8,128)S(1)}, f32[128,262]{0,1:T(8,128)S(1)}, u32[]{:S(2)}, u32[]{:S(2)}) collective-permute-start(f32[128,262]{0,1:T(8,128)S(1)} %slice_select_fusion), channel_id=1, source_target_pairs={{0,2},{2,0},{1,3},{3,1},{4,6},{6,4},{5,7},{7,5},{8,10},{10,8},{9,1... | collective-permute-start | bytes 402440 | tf_op jit(solution)/shard_map/ppermute | solution.py:43
  100.0 4.1 %collective-permute-done.3 = f32[128,262]{0,1:T(8,128)S(1)} collective-permute-done((f32[128,262]{0,1:T(8,128)S(1)}, f32[128,262]{0,1:T(8,128)S(1)}, u32[]{:S(2)}, u32[]{:S(2)}) %collective-permute-start.3) | collective-permute-done | bytes 134176 | tf_op jit(solution)/shard_map/ppermute | solution.py:43
  104.3 5.0 %collective-permute-done.4 = f32[128,262]{0,1:T(8,128)S(1)} collective-permute-done((f32[128,262]{0,1:T(8,128)S(1)}, f32[128,262]{0,1:T(8,128)S(1)}, u32[]{:S(2)}, u32[]{:S(2)}) %collective-permute-start.4) | collective-permute-done | bytes 134176 | tf_op jit(solution)/shard_map/ppermute | solution.py:43
  109.4 7.4 %collective-permute-done.5 = f32[128,262]{0,1:T(8,128)S(1)} collective-permute-done((f32[128,262]{0,1:T(8,128)S(1)}, f32[128,262]{0,1:T(8,128)S(1)}, u32[]{:S(2)}, u32[]{:S(2)}) %collective-permute-start.5) | collective-permute-done | bytes 134176 | tf_op jit(solution)/shard_map/ppermute | solution.py:43
  119.9 6.0 %shard_map.59 = f32[3,8,256]{2,1,0:T(8,128)} custom-call(f32[256,256]{1,0:T(8,128)} %copy.36.gram_ref, f32[8,256]{1,0:T(8,128)} %scatter.6.target_ref, f32[3,8,256]{2,1,0:T(8,128)} %scatter.9.mask_ref), custom_call_target="tpu_custom_call" | custom-call | tf_op jit(solution)/shard_map/pallas_call | solution.py:261
  125.9 4.6 %fusion.17 = bf16[6,128,128]{2,0,1:T(8,128)(2,1)S(1)} fusion(bf16[256,128,128]{2,0,1:T(8,128)(2,1)} %bitcast.99, bf16[6,1,128,128]{3,2,1,0:T(8,128)(2,1)S(1)} %constant_dynamic-slice_fusion.1, f32[3,8,256]{2,1,0:T(8,128)} %shard_map.59, f32[256]{0:T(256)S(1)} %add_rsqrt_fusion), kind=kOutput, calls=%fused_computation.25 | convolution fusion | flops 50629632 | bytes 8791040 | tf_op jit(solution)/shard_map/while/body/eval_jaxpr/ki,iqr->kqr/dot_general | solution.py:274
  130.5 18.0 %all_gather.3 = bf16[6,512,128]{2,1,0:T(8,128)(2,1)S(1)} all-gather(bf16[6,128,128]{2,1,0:T(8,128)(2,1)S(1)} %copy.37), channel_id=1, replica_groups=mesh['groups'=2,'cols'=4,'slab'=2,'rep'=2] {'cols'}, dimensions={1}, use_global_device_ids=true | all-gather | bytes 983040 | tf_op jit(solution)/shard_map/all_gather | solution.py:284
  149.2 1.4 copy.38
  (60 shorter events, 10.2 us)
Async XLA Ops:
  1.6 18.4 %collective-permute-start = (bf16[2,4,4,5,256]{4,3,2,1,0:T(8,128)(2,1)S(1)}, bf16[2,4,4,5,256]{4,3,2,1,0:T(8,128)(2,1)S(1)}, u32[]{:S(2)}, u32[]{:S(2)}) collective-permute-start(bf16[2,4,4,5,256]{4,3,2,1,0:T(8,128)(2,1)S(1)} %pad_maximum_fusion.2), channel_id=1, source_target_pairs={{0,1},{1,0},{2,3},{3,2},{4,5},{5,4},{6,7},{7,6},{8,9},{9,8},{10,11... | collective-permute-start | bytes 245768 | tf_op jit(solution)/shard_map/ppermute | solution.py:69
  3.6 16.3 %copy-start.5 = (s32[4]{0:T(128)S(1)}, s32[4]{0:T(128)}, u32[]{:S(2)}) copy-start(s32[4]{0:T(128)} %param.10) | copy-start | bytes 52
  28.0 15.1 %collective-permute-start.1 = (f32[2,2,4,4,5,256]{5,4,3,2,1,0:T(8,128)S(1)}, f32[2,2,4,4,5,256]{5,4,3,2,1,0:T(8,128)S(1)}, u32[]{:S(2)}, u32[]{:S(2)}) collective-permute-start(f32[2,2,4,4,5,256]{5,4,3,2,1,0:T(8,128)S(1)} %pad_maximum_fusion), channel_id=1, source_target_pairs={{0,2},{2,0},{1,3},{3,1},{4,6},{6,4},{5,7},{7,5},{8,10},{10,8},{9,1... | collective-permute-start | bytes 983048 | tf_op jit(solution)/shard_map/ppermute | solution.py:69
  51.5 6.2 %copy-start.1 = (bf16[6,4,256,64]{2,3,1,0:T(8,128)(2,1)S(1)}, bf16[6,4,256,64]{2,3,1,0:T(8,128)(2,1)}, u32[]{:S(2)}) copy-start(bf16[6,4,256,64]{2,3,1,0:T(8,128)(2,1)} %param.9) | copy-start | bytes 2359300
  52.6 30.7 %all-to-all-start = ((bf16[4,1024,128]{2,1,0:T(8,128)(2,1)}), bf16[4,1024,128]{2,1,0:T(8,128)(2,1)S(1)}, u32[]{:S(2)}, u32[]{:S(2)}) async-start(bf16[4,1024,128]{2,1,0:T(8,128)(2,1)} %bitcast.24), calls=%async_computation | async-start | bytes 2097152 | tf_op jit(solution)/shard_map/all_to_all | solution.py:213
  90.0 3.2 %copy-start = (bf16[16,16,128,128]{3,1,0,2:T(8,128)(2,1)}, bf16[16,16,128,128]{3,1,0,2:T(8,128)(2,1)S(1)}, u32[]{:S(2)}) copy-start(bf16[16,16,128,128]{3,1,0,2:T(8,128)(2,1)S(1)} %multiply_convert_fusion) | copy-start | bytes 25165828
  95.4 0.6 copy-start.3
  96.1 20.8 %copy-start.4 = (s32[3,6,256]{2,1,0:T(8,128)S(1)}, s32[3,6,256]{2,1,0:T(8,128)}, u32[]{:S(2)}) copy-start(s32[3,6,256]{2,1,0:T(8,128)} %param.11) | copy-start | bytes 55300
  96.1 1.6 %collective-permute-start.2 = (f32[256,262]{0,1:T(8,128)S(1)}, f32[256,262]{0,1:T(8,128)S(1)}, u32[]{:S(2)}, u32[]{:S(2)}) collective-permute-start(f32[256,262]{0,1:T(8,128)S(1)} %pad_maximum_fusion.1), channel_id=1, source_target_pairs={{0,1},{1,0},{2,3},{3,2},{4,5},{5,4},{6,7},{7,6},{8,9},{9,8},{10,11... | collective-permute-start | bytes 804872 | tf_op jit(solution)/shard_map/ppermute | solution.py:53
  98.5 5.7 %collective-permute-start.3 = (f32[128,262]{0,1:T(8,128)S(1)}, f32[128,262]{0,1:T(8,128)S(1)}, u32[]{:S(2)}, u32[]{:S(2)}) collective-permute-start(f32[128,262]{0,1:T(8,128)S(1)} %slice_select_fusion), channel_id=1, source_target_pairs={{0,2},{2,0},{1,3},{3,1},{4,6},{6,4},{5,7},{7,5},{8,10},{10,8},{9,1... | collective-permute-start | bytes 402440 | tf_op jit(solution)/shard_map/ppermute | solution.py:43
  104.2 5.1 %collective-permute-start.4 = (f32[128,262]{0,1:T(8,128)S(1)}, f32[128,262]{0,1:T(8,128)S(1)}, u32[]{:S(2)}, u32[]{:S(2)}) collective-permute-start(f32[128,262]{0,1:T(8,128)S(1)} %fusion.54), channel_id=1, source_target_pairs={{0,4},{4,0},{8,12},{12,8},{1,5},{5,1},{9,13},{13,9},{2,6},{6,2},{1... | collective-permute-start | bytes 402440 | tf_op jit(solution)/shard_map/ppermute | solution.py:43
  109.3 7.5 %collective-permute-start.5 = (f32[128,262]{0,1:T(8,128)S(1)}, f32[128,262]{0,1:T(8,128)S(1)}, u32[]{:S(2)}, u32[]{:S(2)}) collective-permute-start(f32[128,262]{0,1:T(8,128)S(1)} %add.118), channel_id=1, source_target_pairs={{0,8},{4,12},{8,0},{12,4},{1,9},{5,13},{9,1},{13,5},{2,10},{6,14},... | collective-permute-start | bytes 402440 | tf_op jit(solution)/shard_map/ppermute | solution.py:43
  116.8 1.4 collective-permute-start.6
  148.5 2.1 %copy-start.2 = (f32[3,8,256]{2,1,0:T(8,128)S(1)}, f32[3,8,256]{2,1,0:T(8,128)}, u32[]{:S(2)}) copy-start(f32[3,8,256]{2,1,0:T(8,128)} %shard_map.59) | copy-start | bytes 73732

commit v15 on v12

--- a/solution.py
+++ b/solution.py
@@ -166,16 +166,16 @@
             "cpxz,sxm->scpmz",
             fields.astype(jnp.float32),
             stream_table[:, width : width + cells_x],
-            precision=highest,
+            precision=lax.Precision.HIGH,
         )
         + jnp.einsum(
-            "cpxz,sxm->scpmz", top.astype(jnp.float32), stream_table[:, :width], precision=highest
+            "cpxz,sxm->scpmz", top.astype(jnp.float32), stream_table[:, :width], precision=lax.Precision.HIGH
         )
         + jnp.einsum(
             "cpxz,sxm->scpmz",
             bottom.astype(jnp.float32),
             stream_table[:, width + cells_x :],
-            precision=highest,
+            precision=lax.Precision.HIGH,
         )
     )
     left, right = neighbour_edges(jnp.swapaxes(along_stream, 3, 4), "slab", 3, width)

time: 150 us -> 147 us (0.980)
  matrix products: 42.8 us -> 37.8 us
    dot_general x1, matrix products: 16 us -> 11.6 us  [local(): jnp.einsum('cpxz,sxm->scpmz', fields.astype(jnp.float32), stream_table[:,...]
  transfers between devices with their start and end apart: 10 -> 10, of which waited for: 8 -> 7; matrix products, arithmetic and copies ran while one was open for 22% -> 21% of each run, Pallas kernels for 0% -> 0%
where the time goes in v15:
time: 147 us
  waiting for transfers between devices  46.9 us (32%)
  matrix products  37.8 us (26%)
  local copies, waits for them, and re-layouts  18.5 us (13%)
  blocking collectives  18 us (12%)
  starting transfers between devices  9.39 us (6%)
  other arithmetic  9 us (6%)
  Pallas kernels  5.98 us (4%)
    all_to_all x1, waiting for transfers between devices, local(): sets = lax.all_to_all(sets, 'cols', 0, 0, tiled=True)  21.1 us
    all_gather x1, blocking collectives, local(): misfit = lax.all_gather(misfit, 'cols', axis=1, tiled=True)  18 us
    ppermute x3, waiting for transfers between devices, tree_sum(): value = value + lax.ppermute(value, axis, partner)  17.5 us
    dot_general x1, matrix products, local(): jnp.einsum('cpxz,sxm->scpmz', fields.astype(jnp.float32), stream_table[:,...  11.6 us
    dot_general x1, matrix products, local(): jnp.einsum('scpmz,zsn->scpmn', along_stream, span_table[width:width + cel...  6.6 us
    ppermute x4, waiting for transfers between devices, neighbour_edges(): return (lax.ppermute(last, axis, up), lax.ppermute(leading, axis, down))  6.13 us
    pallas_call x1, Pallas kernels, local(): pl.pallas_call(conjugate_passes, out_shape=jax.ShapeDtypeStruct((PASSES,...  5.98 us
    all_to_all x1, starting transfers between devices, local(): sets = lax.all_to_all(sets, 'cols', 0, 0, tiled=True)  4.87 us
  transfers between devices with their start and end apart: 10, of which 7 were waited for; matrix products, arithmetic and copies ran while one was open for 21% of the time, Pallas kernels for 0%

profile of v15, /device:TPU:0, one launch (start us, length us, event | category | flops | bytes accessed | tf_op | source)
XLA Modules:
  0.0 146.5 jit_solution(13496476664041483681)
XLA Ops:
  0.6 1.5 %fusion.52 = (bf16[4,4,5,256]{3,2,1,0:T(8,128)(2,1)}, bf16[4,4,5,256]{3,2,1,0:T(8,128)(2,1)S(1)}) fusion(bf16[4,4,1024,256]{3,2,1,0:T(8,128)(2,1)} %param.8), kind=kLoop, calls=%fused_computation.90 | loop fusion | bytes 163840 | tf_op jit(solution)/shard_map/slice | solution.py:67
  2.7 1.5 %select_select_fusion = f32[2,1034,256]{2,1,0:T(8,128)S(1)} fusion(f32[2]{0:T(128)S(1)} %get-tuple-element.78, f32[2]{0:T(128)S(1)} %get-tuple-element.79, f32[2]{0:T(128)S(1)} %get-tuple-element.80, f32[2]{0:T(128)S(1)} %get-tuple-element.81, f32[2]{0:T(128)S(1)} %get-tuple-element.82, f32[2]{0:T(128)S(1)} %get-tuple-element.83, f32[2]{0:T(128)S(1)} %fusion.49, ...), kind=kLoop, calls=%fused_computation.6 | loop fusion | flops 14823424 | bytes 2122852 | tf_op jit(solution)/shard_map/jit(_where)/select_n | solution.py:131
  4.2 11.6 %fusion.2 = f32[2,256,4,4,256]{1,4,3,2,0:T(8,128)S(1)} fusion(bf16[4,4,1024,256]{3,2,1,0:T(8,128)(2,1)} %param.8, f32[2,1034,256]{2,1,0:T(8,128)S(1)} %select_select_fusion), kind=kOutput, calls=%fused_computation.3 | convolution fusion | flops 12884901888 | bytes 18874368 | tf_op jit(solution)/shard_map/cpxz,sxm->scpmz/dot_general | solution.py:165
  15.8 1.0 select_select_fusion.1
  17.3 3.2 %fusion.35 = f32[2,256,4,4,256]{1,4,3,2,0:T(8,128)S(1)} fusion(bf16[4,4,5,256]{3,2,1,0:T(8,128)(2,1)} %collective-permute-done, f32[2,1034,256]{2,1,0:T(8,128)S(1)} %select_select_fusion), kind=kOutput, calls=%fused_computation.61 | convolution fusion | flops 62914560 | bytes 8445952 | tf_op jit(solution)/shard_map/cpxz,sxm->scpmz/dot_general | solution.py:171
  20.5 3.0 %add_add_fusion = f32[2,256,4,4,256]{1,4,3,2,0:T(8,128)S(1)} fusion(f32[2,256,4,4,256]{1,4,3,2,0:T(8,128)S(1)} %fusion.2, f32[2,256,4,4,256]{1,4,3,2,0:T(8,128)S(1)} %fusion.35, bf16[4,4,5,256]{3,2,1,0:T(8,128)(2,1)S(1)} %collective-permute-done.1, f32[2,1034,256]{2,1,0:T(8,128)S(1)} %select_select_fusion), kind=kOutput, calls=%fused_computation.5 | convolution fusion | flops 67108864 | bytes 25247744 | tf_op jit(solution)/shard_map/cpxz,sxm->scpmz/dot_general | solution.py:174
  23.6 3.0 %collective-permute-start.2 = (f32[2,4,4,5,256]{4,3,2,1,0:T(8,128)S(1)}, f32[2,4,4,5,256]{4,3,2,1,0:T(8,128)S(1)}, u32[]{:S(2)}, u32[]{:S(2)}) collective-permute-start(f32[2,4,4,5,256]{4,3,2,1,0:T(8,128)S(1)} %get-tuple-element.73), channel_id=1, source_target_pairs={{0,2},{2,0},{1,3},{3,1},{4,6},{6,4},{5,7},{7,5},{8,10},{10,8},{9,1... | collective-permute-start | bytes 491528 | tf_op jit(solution)/shard_map/ppermute | solution.py:68
  26.6 6.6 %fusion = f32[2,4,4,256,64]{3,4,2,1,0:T(8,128)S(1)} fusion(f32[2,256,4,4,256]{1,4,3,2,0:T(8,128)S(1)} %add_add_fusion, f32[266,2,64]{0,2,1:T(8,128)} %select_select_fusion.1), kind=kOutput, calls=%fused_computation.1 | convolution fusion | flops 1610612736 | bytes 10616832 | tf_op jit(solution)/shard_map/scpmz,zsn->scpmn/dot_general | solution.py:183
  33.3 1.8 %fusion.33 = f32[2,4,4,256,64]{3,4,2,1,0:T(8,128)S(1)} fusion(f32[2,4,4,5,256]{4,3,2,1,0:T(8,128)S(1)} %collective-permute-done.2, f32[266,2,64]{0,2,1:T(8,128)S(1)} %copy-done.1), kind=kOutput, calls=%fused_computation.59 | convolution fusion | flops 31457280 | bytes 2424832 | tf_op jit(solution)/shard_map/scpzm,zsn->scpmn/dot_general | solution.py:189
  35.1 6.1 %collective-permute-done.3 = f32[2,4,4,5,256]{4,3,2,1,0:T(8,128)S(1)} collective-permute-done((f32[2,4,4,5,256]{4,3,2,1,0:T(8,128)S(1)}, f32[2,4,4,5,256]{4,3,2,1,0:T(8,128)S(1)}, u32[]{:S(2)}, u32[]{:S(2)}) %collective-permute-start.3) | collective-permute-done | bytes 163872 | tf_op jit(solution)/shard_map/ppermute | solution.py:68
  41.2 2.4 %add_add_fusion.1 = f32[2,4,4,256,64]{3,4,2,1,0:T(8,128)S(1)} fusion(f32[2,4,4,256,64]{3,4,2,1,0:T(8,128)S(1)} %fusion, f32[2,4,4,256,64]{3,4,2,1,0:T(8,128)S(1)} %fusion.33, f32[2,4,4,5,256]{4,3,2,1,0:T(8,128)S(1)} %collective-permute-done.3, f32[266,2,64]{0,2,1:T(8,128)S(1)} %copy-done.1), kind=kOutput, calls=%fused_computation.22 | convolution fusion | flops 32505856 | bytes 6619136 | tf_op jit(solution)/shard_map/scpzm,zsn->scpmn/dot_general | solution.py:190
  43.7 0.9 slice.166
  45.5 1.5 %copy.29 = bf16[1,4,4,256,64]{4,3,2,1,0:T(8,128)(2,1)S(1)} copy(bf16[1,4,4,256,64]{3,4,2,1,0:T(8,128)(2,1)} %slice.166) | data formatting | bytes 1048576 | tf_op jit(solution)/shard_map/slice | solution.py:192
  47.9 1.1 copy.31
  48.9 4.9 %all-to-all-start = ((bf16[4,1024,128]{2,1,0:T(8,128)(2,1)}), bf16[4,1024,128]{2,1,0:T(8,128)(2,1)S(1)}, u32[]{:S(2)}, u32[]{:S(2)}) async-start(bf16[4,1024,128]{2,1,0:T(8,128)(2,1)} %bitcast.16), calls=%async_computation | async-start | bytes 2097152 | tf_op jit(solution)/shard_map/all_to_all | solution.py:210
  54.2 0.9 copy.34
  55.0 1.5 %reshape_reshape.3 = bf16[6,4,128,128]{3,2,1,0:T(8,128)(2,1)} reshape(bf16[6,4,256,64]{3,2,1,0:T(8,128)(2,1)S(1)} %copy.34) | data formatting | bytes 1572864 | tf_op jit(solution)/shard_map/reshape;reshape | solution.py:214
  56.5 0.9 constant_dynamic-slice_fusion.1
  57.5 21.1 %all-to-all-done = bf16[4,1024,128]{2,1,0:T(8,128)(2,1)S(1)} async-done(((bf16[4,1024,128]{2,1,0:T(8,128)(2,1)}), bf16[4,1024,128]{2,1,0:T(8,128)(2,1)S(1)}, u32[]{:S(2)}, u32[]{:S(2)}) %all-to-all-start) | async-done | bytes 1048608 | tf_op jit(solution)/shard_map/all_to_all | solution.py:210
  79.5 1.6 %copy.33 = f32[16,128,128]{2,0,1:T(8,128)} copy(f32[16,128,128]{2,1,0:T(8,128)S(1)} %bitcast_convert_fusion) | data formatting | bytes 2097152 | tf_op jit(solution)/shard_map/while/body/eval_jaxpr/convert_element_type | solution.py:137
  81.1 4.1 %multiply_convert_fusion = bf16[16,16,128,128]{3,1,0,2:T(8,128)(2,1)S(1)} fusion(f32[16,128,128]{2,0,1:T(8,128)} %copy.33, f32[16,128,128]{2,0,1:T(8,128)S(1)} %copy.32), kind=kLoop, calls=%fused_computation | loop fusion | flops 8388608 | bytes 10485760 | tf_op jit(solution)/shard_map/while/body/eval_jaxpr/convert_element_type | solution.py:139
  85.2 2.4 %convolution_bitcast_fusion = f32[256,256]{0,1:T(8,128)S(1)} fusion(bf16[256,128,128]{2,0,1:T(8,128)(2,1)S(1)} %bitcast.83), kind=kOutput, calls=%fused_computation.26 | convolution fusion | flops 2147483648 | bytes 8650752 | tf_op jit(solution)/shard_map/while/body/eval_jaxpr/iqr,jqr->ij/dot_general | solution.py:226
  87.6 0.9 copy-done
  88.5 2.3 %convolution_bitcast_fusion.1 = f32[256,6]{0,1:T(8,128)S(1)} fusion(bf16[256,128,128]{2,0,1:T(8,128)(2,1)S(1)} %bitcast.84, bf16[6,1,128,128]{3,2,1,0:T(8,128)(2,1)S(1)} %constant_dynamic-slice_fusion.1), kind=kOutput, calls=%fused_computation.27 | convolution fusion | flops 50331648 | bytes 8591360 | tf_op jit(solution)/shard_map/while/body/eval_jaxpr/iqr,kqr->ik/dot_general | solution.py:229
  91.4 1.5 %collective-permute-done.4 = f32[256,262]{0,1:T(8,128)S(1)} collective-permute-done((f32[256,262]{0,1:T(8,128)S(1)}, f32[256,262]{0,1:T(8,128)S(1)}, u32[]{:S(2)}, u32[]{:S(2)}) %collective-permute-start.4) | collective-permute-done | bytes 268320 | tf_op jit(solution)/shard_map/ppermute | solution.py:53
  94.3 5.1 %collective-permute-done.5 = f32[128,262]{0,1:T(8,128)S(1)} collective-permute-done((f32[128,262]{0,1:T(8,128)S(1)}, f32[128,262]{0,1:T(8,128)S(1)}, u32[]{:S(2)}, u32[]{:S(2)}) %collective-permute-start.5) | collective-permute-done | bytes 134176 | tf_op jit(solution)/shard_map/ppermute | solution.py:43
  99.5 5.0 %collective-permute-done.6 = f32[128,262]{0,1:T(8,128)S(1)} collective-permute-done((f32[128,262]{0,1:T(8,128)S(1)}, f32[128,262]{0,1:T(8,128)S(1)}, u32[]{:S(2)}, u32[]{:S(2)}) %collective-permute-start.6) | collective-permute-done | bytes 134176 | tf_op jit(solution)/shard_map/ppermute | solution.py:43
  104.7 7.4 %collective-permute-done.7 = f32[128,262]{0,1:T(8,128)S(1)} collective-permute-done((f32[128,262]{0,1:T(8,128)S(1)}, f32[128,262]{0,1:T(8,128)S(1)}, u32[]{:S(2)}, u32[]{:S(2)}) %collective-permute-start.7) | collective-permute-done | bytes 134176 | tf_op jit(solution)/shard_map/ppermute | solution.py:43
  115.1 6.0 %shard_map.59 = f32[3,8,256]{2,1,0:T(8,128)} custom-call(f32[256,256]{1,0:T(8,128)} %copy.36.gram_ref, f32[8,256]{1,0:T(8,128)} %scatter.6.target_ref, f32[3,8,256]{2,1,0:T(8,128)} %scatter.9.mask_ref), custom_call_target="tpu_custom_call" | custom-call | tf_op jit(solution)/shard_map/pallas_call | solution.py:258
  121.1 4.6 %fusion.17 = bf16[6,128,128]{2,0,1:T(8,128)(2,1)S(1)} fusion(bf16[256,128,128]{2,0,1:T(8,128)(2,1)} %bitcast.85, bf16[6,1,128,128]{3,2,1,0:T(8,128)(2,1)S(1)} %constant_dynamic-slice_fusion.1, f32[3,8,256]{2,1,0:T(8,128)} %shard_map.59, f32[256]{0:T(256)S(1)} %add_rsqrt_fusion), kind=kOutput, calls=%fused_computation.25 | convolution fusion | flops 50629632 | bytes 8791040 | tf_op jit(solution)/shard_map/while/body/eval_jaxpr/ki,iqr->kqr/dot_general | solution.py:271
  125.8 18.0 %all_gather.3 = bf16[6,512,128]{2,1,0:T(8,128)(2,1)S(1)} all-gather(bf16[6,128,128]{2,1,0:T(8,128)(2,1)S(1)} %copy.37), channel_id=1, replica_groups=mesh['groups'=2,'cols'=4,'slab'=2,'rep'=2] {'cols'}, dimensions={1}, use_global_device_ids=true | all-gather | bytes 983040 | tf_op jit(solution)/shard_map/all_gather | solution.py:281
  144.5 1.4 copy.38
  (66 shorter events, 11.1 us)
Async XLA Ops:
  2.1 15.1 %collective-permute-start = (bf16[4,4,5,256]{3,2,1,0:T(8,128)(2,1)S(1)}, bf16[4,4,5,256]{3,2,1,0:T(8,128)(2,1)}, u32[]{:S(2)}, u32[]{:S(2)}) collective-permute-start(bf16[4,4,5,256]{3,2,1,0:T(8,128)(2,1)S(1)} %get-tuple-element.75), channel_id=1, source_target_pairs={{0,1},{1,0},{2,3},{3,2},{4,5},{5,4},{6,7},{7,6},{8,9},{9,8},{10,11... | collective-permute-start | bytes 122888 | tf_op jit(solution)/shard_map/ppermute | solution.py:68
  2.6 17.9 %collective-permute-start.1 = (bf16[4,4,5,256]{3,2,1,0:T(8,128)(2,1)}, bf16[4,4,5,256]{3,2,1,0:T(8,128)(2,1)S(1)}, u32[]{:S(2)}, u32[]{:S(2)}) collective-permute-start(bf16[4,4,5,256]{3,2,1,0:T(8,128)(2,1)} %get-tuple-element.74), channel_id=1, source_target_pairs={{1,0},{0,1},{3,2},{2,3},{5,4},{4,5},{7,6},{6,7},{9,8},{8,9},{11,10... | collective-permute-start | bytes 122888 | tf_op jit(solution)/shard_map/ppermute | solution.py:68
  4.2 12.6 %copy-start.7 = (s32[4]{0:T(128)S(1)}, s32[4]{0:T(128)}, u32[]{:S(2)}) copy-start(s32[4]{0:T(128)} %param.10) | copy-start | bytes 52
  23.6 9.7 %copy-start.1 = (f32[266,2,64]{0,2,1:T(8,128)S(1)}, f32[266,2,64]{0,2,1:T(8,128)}, u32[]{:S(2)}) copy-start(f32[266,2,64]{0,2,1:T(8,128)} %select_select_fusion.1) | copy-start | bytes 408580
  23.6 9.7 %collective-permute-start.2 = (f32[2,4,4,5,256]{4,3,2,1,0:T(8,128)S(1)}, f32[2,4,4,5,256]{4,3,2,1,0:T(8,128)S(1)}, u32[]{:S(2)}, u32[]{:S(2)}) collective-permute-start(f32[2,4,4,5,256]{4,3,2,1,0:T(8,128)S(1)} %get-tuple-element.73), channel_id=1, source_target_pairs={{0,2},{2,0},{1,3},{3,1},{4,6},{6,4},{5,7},{7,5},{8,10},{10,8},{9,1... | collective-permute-start | bytes 491528 | tf_op jit(solution)/shard_map/ppermute | solution.py:68
  33.2 8.0 %collective-permute-start.3 = (f32[2,4,4,5,256]{4,3,2,1,0:T(8,128)S(1)}, f32[2,4,4,5,256]{4,3,2,1,0:T(8,128)S(1)}, u32[]{:S(2)}, u32[]{:S(2)}) collective-permute-start(f32[2,4,4,5,256]{4,3,2,1,0:T(8,128)S(1)} %get-tuple-element.72), channel_id=1, source_target_pairs={{2,0},{0,2},{3,1},{1,3},{6,4},{4,6},{7,5},{5,7},{10,8},{8,10},{11,... | collective-permute-start | bytes 491528 | tf_op jit(solution)/shard_map/ppermute | solution.py:68
  45.5 2.0 %copy-start.6 = (f32[4]{0:T(128)S(1)}, f32[4]{0:T(128)}, u32[]{:S(2)}) copy-start(f32[4]{0:T(128)} %subtract_sqrt_fusion) | copy-start | bytes 52
  47.8 6.0 %copy-start.2 = (bf16[6,4,256,64]{2,3,1,0:T(8,128)(2,1)S(1)}, bf16[6,4,256,64]{2,3,1,0:T(8,128)(2,1)}, u32[]{:S(2)}) copy-start(bf16[6,4,256,64]{2,3,1,0:T(8,128)(2,1)} %param.9) | copy-start | bytes 2359300
  48.9 29.6 %all-to-all-start = ((bf16[4,1024,128]{2,1,0:T(8,128)(2,1)}), bf16[4,1024,128]{2,1,0:T(8,128)(2,1)S(1)}, u32[]{:S(2)}, u32[]{:S(2)}) async-start(bf16[4,1024,128]{2,1,0:T(8,128)(2,1)} %bitcast.16), calls=%async_computation | async-start | bytes 2097152 | tf_op jit(solution)/shard_map/all_to_all | solution.py:210
  85.2 3.3 %copy-start = (bf16[16,16,128,128]{3,1,0,2:T(8,128)(2,1)}, bf16[16,16,128,128]{3,1,0,2:T(8,128)(2,1)S(1)}, u32[]{:S(2)}) copy-start(bf16[16,16,128,128]{3,1,0,2:T(8,128)(2,1)S(1)} %multiply_convert_fusion) | copy-start | bytes 25165828
  90.7 0.6 copy-start.4
  91.3 20.8 %copy-start.5 = (s32[3,6,256]{2,1,0:T(8,128)S(1)}, s32[3,6,256]{2,1,0:T(8,128)}, u32[]{:S(2)}) copy-start(s32[3,6,256]{2,1,0:T(8,128)} %param.11) | copy-start | bytes 55300
  91.3 1.6 %collective-permute-start.4 = (f32[256,262]{0,1:T(8,128)S(1)}, f32[256,262]{0,1:T(8,128)S(1)}, u32[]{:S(2)}, u32[]{:S(2)}) collective-permute-start(f32[256,262]{0,1:T(8,128)S(1)} %pad_maximum_fusion), channel_id=1, source_target_pairs={{0,1},{1,0},{2,3},{3,2},{4,5},{5,4},{6,7},{7,6},{8,9},{9,8},{10,11... | collective-permute-start | bytes 804872 | tf_op jit(solution)/shard_map/ppermute | solution.py:53
  93.7 5.7 %collective-permute-start.5 = (f32[128,262]{0,1:T(8,128)S(1)}, f32[128,262]{0,1:T(8,128)S(1)}, u32[]{:S(2)}, u32[]{:S(2)}) collective-permute-start(f32[128,262]{0,1:T(8,128)S(1)} %slice_select_fusion), channel_id=1, source_target_pairs={{0,2},{2,0},{1,3},{3,1},{4,6},{6,4},{5,7},{7,5},{8,10},{10,8},{9,1... | collective-permute-start | bytes 402440 | tf_op jit(solution)/shard_map/ppermute | solution.py:43
  99.4 5.1 %collective-permute-start.6 = (f32[128,262]{0,1:T(8,128)S(1)}, f32[128,262]{0,1:T(8,128)S(1)}, u32[]{:S(2)}, u32[]{:S(2)}) collective-permute-start(f32[128,262]{0,1:T(8,128)S(1)} %fusion.60), channel_id=1, source_target_pairs={{0,4},{4,0},{8,12},{12,8},{1,5},{5,1},{9,13},{13,9},{2,6},{6,2},{1... | collective-permute-start | bytes 402440 | tf_op jit(solution)/shard_map/ppermute | solution.py:43
  104.5 7.5 %collective-permute-start.7 = (f32[128,262]{0,1:T(8,128)S(1)}, f32[128,262]{0,1:T(8,128)S(1)}, u32[]{:S(2)}, u32[]{:S(2)}) collective-permute-start(f32[128,262]{0,1:T(8,128)S(1)} %add.118), channel_id=1, source_target_pairs={{0,8},{4,12},{8,0},{12,4},{1,9},{5,13},{9,1},{13,5},{2,10},{6,14},... | collective-permute-start | bytes 402440 | tf_op jit(solution)/shard_map/ppermute | solution.py:43
  112.1 1.4 collective-permute-start.8
  143.7 2.1 %copy-start.3 = (f32[3,8,256]{2,1,0:T(8,128)S(1)}, f32[3,8,256]{2,1,0:T(8,128)}, u32[]{:S(2)}) copy-start(f32[3,8,256]{2,1,0:T(8,128)} %shard_map.59) | copy-start | bytes 73732

commit v16 on v15

--- a/solution.py
+++ b/solution.py
@@ -184,10 +184,10 @@
             "scpmz,zsn->scpmn",
             along_stream,
             span_table[width : width + cells_z],
-            precision=highest,
-        )
-        + jnp.einsum("scpzm,zsn->scpmn", left, span_table[:width], precision=highest)
-        + jnp.einsum("scpzm,zsn->scpmn", right, span_table[width + cells_z :], precision=highest)
+            precision=lax.Precision.HIGH,
+        )
+        + jnp.einsum("scpzm,zsn->scpmn", left, span_table[:width], precision=lax.Precision.HIGH)
+        + jnp.einsum("scpzm,zsn->scpmn", right, span_table[width + cells_z :], precision=lax.Precision.HIGH)
     )
     narrow = filtered[0]
     broader = filtered[1]

time: 147 us -> 144 us (0.980)
  matrix products: 37.8 us -> 32.9 us
    dot_general x1, matrix products: 6.6 us -> 3.6 us  [local(): jnp.einsum('scpmz,zsn->scpmn', along_stream, span_table[width:width + cel...]
  transfers between devices with their start and end apart: 10 -> 10, of which waited for: 7 -> 8; matrix products, arithmetic and copies ran while one was open for 21% -> 18% of each run, Pallas kernels for 0% -> 0%
where the time goes in v16:
time: 144 us
  waiting for transfers between devices  48.1 us (33%)
  matrix products  32.9 us (23%)
  local copies, waits for them, and re-layouts  18.5 us (13%)
  blocking collectives  18 us (12%)
  starting transfers between devices  10.3 us (7%)
  other arithmetic  9 us (6%)
  Pallas kernels  5.98 us (4%)
    all_to_all x1, waiting for transfers between devices, local(): sets = lax.all_to_all(sets, 'cols', 0, 0, tiled=True)  21.7 us
    all_gather x1, blocking collectives, local(): misfit = lax.all_gather(misfit, 'cols', axis=1, tiled=True)  18 us
    ppermute x3, waiting for transfers between devices, tree_sum(): value = value + lax.ppermute(value, axis, partner)  16.8 us
    dot_general x1, matrix products, local(): jnp.einsum('cpxz,sxm->scpmz', fields.astype(jnp.float32), stream_table[:,...  11.6 us
    ppermute x4, waiting for transfers between devices, neighbour_edges(): return (lax.ppermute(last, axis, up), lax.ppermute(leading, axis, down))  7.44 us
    pallas_call x1, Pallas kernels, local(): pl.pallas_call(conjugate_passes, out_shape=jax.ShapeDtypeStruct((PASSES,...  5.98 us
    all_to_all x1, starting transfers between devices, local(): sets = lax.all_to_all(sets, 'cols', 0, 0, tiled=True)  5.11 us
    dot_general x1, matrix products, misfit_step(): jnp.einsum('ki,iqr->kqr', final_weights, all_terms, preferred_element_typ...  4.6 us
  transfers between devices with their start and end apart: 10, of which 8 were waited for; matrix products, arithmetic and copies ran while one was open for 18% of the time, Pallas kernels for 0%

profile of v16, /device:TPU:0, one launch (start us, length us, event | category | flops | bytes accessed | tf_op | source)
XLA Modules:
  0.0 143.8 jit_solution(12932756568605635066)
XLA Ops:
  0.6 1.5 %fusion.52 = (bf16[4,4,5,256]{3,2,1,0:T(8,128)(2,1)}, bf16[4,4,5,256]{3,2,1,0:T(8,128)(2,1)S(1)}) fusion(bf16[4,4,1024,256]{3,2,1,0:T(8,128)(2,1)} %param.8), kind=kLoop, calls=%fused_computation.90 | loop fusion | bytes 163840 | tf_op jit(solution)/shard_map/slice | solution.py:67
  2.7 1.5 %select_select_fusion = f32[2,1034,256]{2,1,0:T(8,128)S(1)} fusion(f32[2]{0:T(128)S(1)} %get-tuple-element.78, f32[2]{0:T(128)S(1)} %get-tuple-element.79, f32[2]{0:T(128)S(1)} %get-tuple-element.80, f32[2]{0:T(128)S(1)} %get-tuple-element.81, f32[2]{0:T(128)S(1)} %get-tuple-element.82, f32[2]{0:T(128)S(1)} %get-tuple-element.83, f32[2]{0:T(128)S(1)} %fusion.49, ...), kind=kLoop, calls=%fused_computation.6 | loop fusion | flops 14823424 | bytes 2122852 | tf_op jit(solution)/shard_map/jit(_where)/select_n | solution.py:131
  4.2 11.6 %fusion.2 = f32[2,256,4,4,256]{1,4,3,2,0:T(8,128)S(1)} fusion(bf16[4,4,1024,256]{3,2,1,0:T(8,128)(2,1)} %param.8, f32[2,1034,256]{2,1,0:T(8,128)S(1)} %select_select_fusion), kind=kOutput, calls=%fused_computation.3 | convolution fusion | flops 12884901888 | bytes 18874368 | tf_op jit(solution)/shard_map/cpxz,sxm->scpmz/dot_general | solution.py:165
  15.8 1.0 select_select_fusion.1
  17.3 3.2 %fusion.35 = f32[2,256,4,4,256]{1,4,3,2,0:T(8,128)S(1)} fusion(bf16[4,4,5,256]{3,2,1,0:T(8,128)(2,1)} %collective-permute-done, f32[2,1034,256]{2,1,0:T(8,128)S(1)} %select_select_fusion), kind=kOutput, calls=%fused_computation.61 | convolution fusion | flops 62914560 | bytes 8445952 | tf_op jit(solution)/shard_map/cpxz,sxm->scpmz/dot_general | solution.py:171
  20.5 3.0 %add_add_fusion = f32[2,256,4,4,256]{1,4,3,2,0:T(8,128)S(1)} fusion(f32[2,256,4,4,256]{1,4,3,2,0:T(8,128)S(1)} %fusion.2, f32[2,256,4,4,256]{1,4,3,2,0:T(8,128)S(1)} %fusion.35, bf16[4,4,5,256]{3,2,1,0:T(8,128)(2,1)S(1)} %collective-permute-done.1, f32[2,1034,256]{2,1,0:T(8,128)S(1)} %select_select_fusion), kind=kOutput, calls=%fused_computation.5 | convolution fusion | flops 67108864 | bytes 25247744 | tf_op jit(solution)/shard_map/cpxz,sxm->scpmz/dot_general | solution.py:174
  23.6 3.0 %collective-permute-start.2 = (f32[2,4,4,5,256]{4,3,2,1,0:T(8,128)S(1)}, f32[2,4,4,5,256]{4,3,2,1,0:T(8,128)S(1)}, u32[]{:S(2)}, u32[]{:S(2)}) collective-permute-start(f32[2,4,4,5,256]{4,3,2,1,0:T(8,128)S(1)} %get-tuple-element.73), channel_id=1, source_target_pairs={{0,2},{2,0},{1,3},{3,1},{4,6},{6,4},{5,7},{7,5},{8,10},{10,8},{9,1... | collective-permute-start | bytes 491528 | tf_op jit(solution)/shard_map/ppermute | solution.py:68
  26.6 3.6 %fusion = f32[2,4,4,256,64]{3,4,2,1,0:T(8,128)S(1)} fusion(f32[2,256,4,4,256]{1,4,3,2,0:T(8,128)S(1)} %add_add_fusion, f32[266,2,64]{0,2,1:T(8,128)} %select_select_fusion.1), kind=kOutput, calls=%fused_computation.1 | convolution fusion | flops 805306368 | bytes 10616832 | tf_op jit(solution)/shard_map/scpmz,zsn->scpmn/dot_general | solution.py:183
  30.3 3.2 %collective-permute-done.2 = f32[2,4,4,5,256]{4,3,2,1,0:T(8,128)S(1)} collective-permute-done((f32[2,4,4,5,256]{4,3,2,1,0:T(8,128)S(1)}, f32[2,4,4,5,256]{4,3,2,1,0:T(8,128)S(1)}, u32[]{:S(2)}, u32[]{:S(2)}) %collective-permute-start.2) | collective-permute-done | bytes 163872 | tf_op jit(solution)/shard_map/ppermute | solution.py:68
  33.5 1.0 fusion.33
  34.5 4.2 %collective-permute-done.3 = f32[2,4,4,5,256]{4,3,2,1,0:T(8,128)S(1)} collective-permute-done((f32[2,4,4,5,256]{4,3,2,1,0:T(8,128)S(1)}, f32[2,4,4,5,256]{4,3,2,1,0:T(8,128)S(1)}, u32[]{:S(2)}, u32[]{:S(2)}) %collective-permute-start.3) | collective-permute-done | bytes 163872 | tf_op jit(solution)/shard_map/ppermute | solution.py:68
  38.7 1.3 add_add_fusion.1
  42.0 1.5 %copy.29 = bf16[1,4,4,256,64]{4,3,2,1,0:T(8,128)(2,1)S(1)} copy(bf16[1,4,4,256,64]{3,4,2,1,0:T(8,128)(2,1)} %slice.166) | data formatting | bytes 1048576 | tf_op jit(solution)/shard_map/slice | solution.py:192
  44.3 1.1 copy.31
  45.4 5.1 %all-to-all-start = ((bf16[4,1024,128]{2,1,0:T(8,128)(2,1)}), bf16[4,1024,128]{2,1,0:T(8,128)(2,1)S(1)}, u32[]{:S(2)}, u32[]{:S(2)}) async-start(bf16[4,1024,128]{2,1,0:T(8,128)(2,1)} %bitcast.16), calls=%async_computation | async-start | bytes 2097152 | tf_op jit(solution)/shard_map/all_to_all | solution.py:210
  51.7 1.5 %reshape_reshape.3 = bf16[6,4,128,128]{3,2,1,0:T(8,128)(2,1)} reshape(bf16[6,4,256,64]{3,2,1,0:T(8,128)(2,1)S(1)} %copy.34) | data formatting | bytes 1572864 | tf_op jit(solution)/shard_map/reshape;reshape | solution.py:214
  53.2 0.9 constant_dynamic-slice_fusion.1
  54.1 21.7 %all-to-all-done = bf16[4,1024,128]{2,1,0:T(8,128)(2,1)S(1)} async-done(((bf16[4,1024,128]{2,1,0:T(8,128)(2,1)}), bf16[4,1024,128]{2,1,0:T(8,128)(2,1)S(1)}, u32[]{:S(2)}, u32[]{:S(2)}) %all-to-all-start) | async-done | bytes 1048608 | tf_op jit(solution)/shard_map/all_to_all | solution.py:210
  76.8 1.6 %copy.33 = f32[16,128,128]{2,0,1:T(8,128)} copy(f32[16,128,128]{2,1,0:T(8,128)S(1)} %bitcast_convert_fusion) | data formatting | bytes 2097152 | tf_op jit(solution)/shard_map/while/body/eval_jaxpr/convert_element_type | solution.py:137
  78.4 4.1 %multiply_convert_fusion = bf16[16,16,128,128]{3,1,0,2:T(8,128)(2,1)S(1)} fusion(f32[16,128,128]{2,0,1:T(8,128)} %copy.33, f32[16,128,128]{2,0,1:T(8,128)S(1)} %copy.32), kind=kLoop, calls=%fused_computation | loop fusion | flops 8388608 | bytes 10485760 | tf_op jit(solution)/shard_map/while/body/eval_jaxpr/convert_element_type | solution.py:139
  82.5 2.4 %convolution_bitcast_fusion = f32[256,256]{0,1:T(8,128)S(1)} fusion(bf16[256,128,128]{2,0,1:T(8,128)(2,1)S(1)} %bitcast.83), kind=kOutput, calls=%fused_computation.26 | convolution fusion | flops 2147483648 | bytes 8650752 | tf_op jit(solution)/shard_map/while/body/eval_jaxpr/iqr,jqr->ij/dot_general | solution.py:226
  84.9 0.9 copy-done
  85.7 2.3 %convolution_bitcast_fusion.1 = f32[256,6]{0,1:T(8,128)S(1)} fusion(bf16[256,128,128]{2,0,1:T(8,128)(2,1)S(1)} %bitcast.84, bf16[6,1,128,128]{3,2,1,0:T(8,128)(2,1)S(1)} %constant_dynamic-slice_fusion.1), kind=kOutput, calls=%fused_computation.27 | convolution fusion | flops 50331648 | bytes 8591360 | tf_op jit(solution)/shard_map/while/body/eval_jaxpr/iqr,kqr->ik/dot_general | solution.py:229
  88.7 1.5 %collective-permute-done.4 = f32[256,262]{0,1:T(8,128)S(1)} collective-permute-done((f32[256,262]{0,1:T(8,128)S(1)}, f32[256,262]{0,1:T(8,128)S(1)}, u32[]{:S(2)}, u32[]{:S(2)}) %collective-permute-start.4) | collective-permute-done | bytes 268320 | tf_op jit(solution)/shard_map/ppermute | solution.py:53
  91.0 1.3 collective-permute-start.5
  92.3 4.4 %collective-permute-done.5 = f32[128,262]{0,1:T(8,128)S(1)} collective-permute-done((f32[128,262]{0,1:T(8,128)S(1)}, f32[128,262]{0,1:T(8,128)S(1)}, u32[]{:S(2)}, u32[]{:S(2)}) %collective-permute-start.5) | collective-permute-done | bytes 134176 | tf_op jit(solution)/shard_map/ppermute | solution.py:43
  96.8 5.0 %collective-permute-done.6 = f32[128,262]{0,1:T(8,128)S(1)} collective-permute-done((f32[128,262]{0,1:T(8,128)S(1)}, f32[128,262]{0,1:T(8,128)S(1)}, u32[]{:S(2)}, u32[]{:S(2)}) %collective-permute-start.6) | collective-permute-done | bytes 134176 | tf_op jit(solution)/shard_map/ppermute | solution.py:43
  102.0 7.4 %collective-permute-done.7 = f32[128,262]{0,1:T(8,128)S(1)} collective-permute-done((f32[128,262]{0,1:T(8,128)S(1)}, f32[128,262]{0,1:T(8,128)S(1)}, u32[]{:S(2)}, u32[]{:S(2)}) %collective-permute-start.7) | collective-permute-done | bytes 134176 | tf_op jit(solution)/shard_map/ppermute | solution.py:43
  112.4 6.0 %shard_map.59 = f32[3,8,256]{2,1,0:T(8,128)} custom-call(f32[256,256]{1,0:T(8,128)} %copy.36.gram_ref, f32[8,256]{1,0:T(8,128)} %scatter.6.target_ref, f32[3,8,256]{2,1,0:T(8,128)} %scatter.9.mask_ref), custom_call_target="tpu_custom_call" | custom-call | tf_op jit(solution)/shard_map/pallas_call | solution.py:258
  118.4 4.6 %fusion.17 = bf16[6,128,128]{2,0,1:T(8,128)(2,1)S(1)} fusion(bf16[256,128,128]{2,0,1:T(8,128)(2,1)} %bitcast.85, bf16[6,1,128,128]{3,2,1,0:T(8,128)(2,1)S(1)} %constant_dynamic-slice_fusion.1, f32[3,8,256]{2,1,0:T(8,128)} %shard_map.59, f32[256]{0:T(256)S(1)} %add_rsqrt_fusion), kind=kOutput, calls=%fused_computation.25 | convolution fusion | flops 50629632 | bytes 8791040 | tf_op jit(solution)/shard_map/while/body/eval_jaxpr/ki,iqr->kqr/dot_general | solution.py:271
  123.1 18.0 %all_gather.3 = bf16[6,512,128]{2,1,0:T(8,128)(2,1)S(1)} all-gather(bf16[6,128,128]{2,1,0:T(8,128)(2,1)S(1)} %copy.37), channel_id=1, replica_groups=mesh['groups'=2,'cols'=4,'slab'=2,'rep'=2] {'cols'}, dimensions={1}, use_global_device_ids=true | all-gather | bytes 983040 | tf_op jit(solution)/shard_map/all_gather | solution.py:281
  141.7 1.4 copy.38
  (66 shorter events, 12.2 us)
Async XLA Ops:
  2.1 15.1 %collective-permute-start = (bf16[4,4,5,256]{3,2,1,0:T(8,128)(2,1)S(1)}, bf16[4,4,5,256]{3,2,1,0:T(8,128)(2,1)}, u32[]{:S(2)}, u32[]{:S(2)}) collective-permute-start(bf16[4,4,5,256]{3,2,1,0:T(8,128)(2,1)S(1)} %get-tuple-element.75), channel_id=1, source_target_pairs={{0,1},{1,0},{2,3},{3,2},{4,5},{5,4},{6,7},{7,6},{8,9},{9,8},{10,11... | collective-permute-start | bytes 122888 | tf_op jit(solution)/shard_map/ppermute | solution.py:68
  2.6 17.9 %collective-permute-start.1 = (bf16[4,4,5,256]{3,2,1,0:T(8,128)(2,1)}, bf16[4,4,5,256]{3,2,1,0:T(8,128)(2,1)S(1)}, u32[]{:S(2)}, u32[]{:S(2)}) collective-permute-start(bf16[4,4,5,256]{3,2,1,0:T(8,128)(2,1)} %get-tuple-element.74), channel_id=1, source_target_pairs={{1,0},{0,1},{3,2},{2,3},{5,4},{4,5},{7,6},{6,7},{9,8},{8,9},{11,10... | collective-permute-start | bytes 122888 | tf_op jit(solution)/shard_map/ppermute | solution.py:68
  4.2 12.6 %copy-start.7 = (s32[4]{0:T(128)S(1)}, s32[4]{0:T(128)}, u32[]{:S(2)}) copy-start(s32[4]{0:T(128)} %param.10) | copy-start | bytes 52
  23.6 9.9 %copy-start.1 = (f32[266,2,64]{0,2,1:T(8,128)S(1)}, f32[266,2,64]{0,2,1:T(8,128)}, u32[]{:S(2)}) copy-start(f32[266,2,64]{0,2,1:T(8,128)} %select_select_fusion.1) | copy-start | bytes 408580
  23.6 9.9 %collective-permute-start.2 = (f32[2,4,4,5,256]{4,3,2,1,0:T(8,128)S(1)}, f32[2,4,4,5,256]{4,3,2,1,0:T(8,128)S(1)}, u32[]{:S(2)}, u32[]{:S(2)}) collective-permute-start(f32[2,4,4,5,256]{4,3,2,1,0:T(8,128)S(1)} %get-tuple-element.73), channel_id=1, source_target_pairs={{0,2},{2,0},{1,3},{3,1},{4,6},{6,4},{5,7},{7,5},{8,10},{10,8},{9,1... | collective-permute-start | bytes 491528 | tf_op jit(solution)/shard_map/ppermute | solution.py:68
  30.2 8.5 %collective-permute-start.3 = (f32[2,4,4,5,256]{4,3,2,1,0:T(8,128)S(1)}, f32[2,4,4,5,256]{4,3,2,1,0:T(8,128)S(1)}, u32[]{:S(2)}, u32[]{:S(2)}) collective-permute-start(f32[2,4,4,5,256]{4,3,2,1,0:T(8,128)S(1)} %get-tuple-element.72), channel_id=1, source_target_pairs={{2,0},{0,2},{3,1},{1,3},{6,4},{4,6},{7,5},{5,7},{10,8},{8,10},{11,... | collective-permute-start | bytes 491528 | tf_op jit(solution)/shard_map/ppermute | solution.py:68
  41.9 2.0 %copy-start.6 = (f32[4]{0:T(128)S(1)}, f32[4]{0:T(128)}, u32[]{:S(2)}) copy-start(f32[4]{0:T(128)} %subtract_sqrt_fusion) | copy-start | bytes 52
  44.3 6.2 %copy-start.2 = (bf16[6,4,256,64]{2,3,1,0:T(8,128)(2,1)S(1)}, bf16[6,4,256,64]{2,3,1,0:T(8,128)(2,1)}, u32[]{:S(2)}) copy-start(bf16[6,4,256,64]{2,3,1,0:T(8,128)(2,1)} %param.9) | copy-start | bytes 2359300
  45.4 30.5 %all-to-all-start = ((bf16[4,1024,128]{2,1,0:T(8,128)(2,1)}), bf16[4,1024,128]{2,1,0:T(8,128)(2,1)S(1)}, u32[]{:S(2)}, u32[]{:S(2)}) async-start(bf16[4,1024,128]{2,1,0:T(8,128)(2,1)} %bitcast.16), calls=%async_computation | async-start | bytes 2097152 | tf_op jit(solution)/shard_map/all_to_all | solution.py:210
  82.5 3.3 %copy-start = (bf16[16,16,128,128]{3,1,0,2:T(8,128)(2,1)}, bf16[16,16,128,128]{3,1,0,2:T(8,128)(2,1)S(1)}, u32[]{:S(2)}) copy-start(bf16[16,16,128,128]{3,1,0,2:T(8,128)(2,1)S(1)} %multiply_convert_fusion) | copy-start | bytes 25165828
  88.0 0.6 copy-start.4
  88.6 20.8 %copy-start.5 = (s32[3,6,256]{2,1,0:T(8,128)S(1)}, s32[3,6,256]{2,1,0:T(8,128)}, u32[]{:S(2)}) copy-start(s32[3,6,256]{2,1,0:T(8,128)} %param.11) | copy-start | bytes 55300
  88.6 1.6 %collective-permute-start.4 = (f32[256,262]{0,1:T(8,128)S(1)}, f32[256,262]{0,1:T(8,128)S(1)}, u32[]{:S(2)}, u32[]{:S(2)}) collective-permute-start(f32[256,262]{0,1:T(8,128)S(1)} %pad_maximum_fusion), channel_id=1, source_target_pairs={{0,1},{1,0},{2,3},{3,2},{4,5},{5,4},{6,7},{7,6},{8,9},{9,8},{10,11... | collective-permute-start | bytes 804872 | tf_op jit(solution)/shard_map/ppermute | solution.py:53
  91.0 5.7 %collective-permute-start.5 = (f32[128,262]{0,1:T(8,128)S(1)}, f32[128,262]{0,1:T(8,128)S(1)}, u32[]{:S(2)}, u32[]{:S(2)}) collective-permute-start(f32[128,262]{0,1:T(8,128)S(1)} %slice_select_fusion), channel_id=1, source_target_pairs={{0,2},{2,0},{1,3},{3,1},{4,6},{6,4},{5,7},{7,5},{8,10},{10,8},{9,1... | collective-permute-start | bytes 402440 | tf_op jit(solution)/shard_map/ppermute | solution.py:43
  96.7 5.1 %collective-permute-start.6 = (f32[128,262]{0,1:T(8,128)S(1)}, f32[128,262]{0,1:T(8,128)S(1)}, u32[]{:S(2)}, u32[]{:S(2)}) collective-permute-start(f32[128,262]{0,1:T(8,128)S(1)} %fusion.60), channel_id=1, source_target_pairs={{0,4},{4,0},{8,12},{12,8},{1,5},{5,1},{9,13},{13,9},{2,6},{6,2},{1... | collective-permute-start | bytes 402440 | tf_op jit(solution)/shard_map/ppermute | solution.py:43
  101.8 7.5 %collective-permute-start.7 = (f32[128,262]{0,1:T(8,128)S(1)}, f32[128,262]{0,1:T(8,128)S(1)}, u32[]{:S(2)}, u32[]{:S(2)}) collective-permute-start(f32[128,262]{0,1:T(8,128)S(1)} %add.118), channel_id=1, source_target_pairs={{0,8},{4,12},{8,0},{12,4},{1,9},{5,13},{9,1},{13,5},{2,10},{6,14},... | collective-permute-start | bytes 402440 | tf_op jit(solution)/shard_map/ppermute | solution.py:43
  109.4 1.4 collective-permute-start.8
  141.0 2.1 %copy-start.3 = (f32[3,8,256]{2,1,0:T(8,128)S(1)}, f32[3,8,256]{2,1,0:T(8,128)}, u32[]{:S(2)}) copy-start(f32[3,8,256]{2,1,0:T(8,128)} %shard_map.59) | copy-start | bytes 73732

commit v17 on v16

--- a/solution.py
+++ b/solution.py
@@ -248,17 +248,10 @@
     normal_gram = column_scale[:, None] * gram_matrix * column_scale[None, :] / samples
     target_norm = column_scale[None, :] * rhs_sums.T / samples
 
-    padded_rows = -(-STRESS // 8) * 8
-    target_padded = jnp.zeros((padded_rows, TERMS), jnp.float32).at[:STRESS].set(target_norm)
-    masks_padded = (
-        jnp.zeros((PASSES, padded_rows, TERMS), jnp.float32)
-        .at[:, :STRESS]
-        .set(active_masks.astype(jnp.float32))
-    )
     passes = pl.pallas_call(
         conjugate_passes,
-        out_shape=jax.ShapeDtypeStruct((PASSES, padded_rows, TERMS), jnp.float32),
-    )(normal_gram, target_padded, masks_padded)
+        out_shape=jax.ShapeDtypeStruct((PASSES, STRESS, TERMS), jnp.float32),
+    )(normal_gram, target_norm, active_masks.astype(jnp.float32))
     coefficients = lax.dynamic_slice_in_dim(passes[:, :STRESS], offset, term_dev, 2)
     solution_all = passes[PASSES - 1, :STRESS]
     final_weights = (column_scale[None, :] * solution_all).astype(jnp.bfloat16)

time: 144 us -> 144 us (level)
  no operation moved by 1% of the time
where the time goes in v17:
time: 144 us
  waiting for transfers between devices  48.2 us (33%)
  matrix products  32.9 us (23%)
  blocking collectives  18 us (12%)
  local copies, waits for them, and re-layouts  17.3 us (12%)
  starting transfers between devices  10.3 us (7%)
  other arithmetic  10.2 us (7%)
  Pallas kernels  5.99 us (4%)
    all_to_all x1, waiting for transfers between devices, local(): sets = lax.all_to_all(sets, 'cols', 0, 0, tiled=True)  21.7 us
    all_gather x1, blocking collectives, local(): misfit = lax.all_gather(misfit, 'cols', axis=1, tiled=True)  18 us
    ppermute x3, waiting for transfers between devices, tree_sum(): value = value + lax.ppermute(value, axis, partner)  16.8 us
    dot_general x1, matrix products, local(): jnp.einsum('cpxz,sxm->scpmz', fields.astype(jnp.float32), stream_table[:,...  11.6 us
    ppermute x4, waiting for transfers between devices, neighbour_edges(): return (lax.ppermute(last, axis, up), lax.ppermute(leading, axis, down))  7.44 us
    pallas_call x1, Pallas kernels, local(): pl.pallas_call(conjugate_passes, out_shape=jax.ShapeDtypeStruct((PASSES,...  5.99 us
    all_to_all x1, starting transfers between devices, local(): sets = lax.all_to_all(sets, 'cols', 0, 0, tiled=True)  5.11 us
    dot_general x1, matrix products, misfit_step(): jnp.einsum('ki,iqr->kqr', final_weights, all_terms, preferred_element_typ...  4.6 us
  transfers between devices with their start and end apart: 10, of which 8 were waited for; matrix products, arithmetic and copies ran while one was open for 18% of the time, Pallas kernels for 0%

profile of v17, /device:TPU:0, one launch (start us, length us, event | category | flops | bytes accessed | tf_op | source)
XLA Modules:
  0.0 143.8 jit_solution(12677495304408330632)
XLA Ops:
  0.6 1.5 %fusion.52 = (bf16[4,4,5,256]{3,2,1,0:T(8,128)(2,1)}, bf16[4,4,5,256]{3,2,1,0:T(8,128)(2,1)S(1)}) fusion(bf16[4,4,1024,256]{3,2,1,0:T(8,128)(2,1)} %param.4), kind=kLoop, calls=%fused_computation.90 | loop fusion | bytes 163840 | tf_op jit(solution)/shard_map/slice | solution.py:67
  2.7 1.5 %select_select_fusion = f32[2,1034,256]{2,1,0:T(8,128)S(1)} fusion(f32[2]{0:T(128)S(1)} %get-tuple-element.47, f32[2]{0:T(128)S(1)} %get-tuple-element.48, f32[2]{0:T(128)S(1)} %get-tuple-element.56, f32[2]{0:T(128)S(1)} %get-tuple-element.57, f32[2]{0:T(128)S(1)} %get-tuple-element.58, f32[2]{0:T(128)S(1)} %get-tuple-element.59, f32[2]{0:T(128)S(1)} %fusion.49, ...), kind=kLoop, calls=%fused_computation.6 | loop fusion | flops 14823424 | bytes 2122852 | tf_op jit(solution)/shard_map/jit(_where)/select_n | solution.py:131
  4.2 11.6 %fusion.2 = f32[2,256,4,4,256]{1,4,3,2,0:T(8,128)S(1)} fusion(bf16[4,4,1024,256]{3,2,1,0:T(8,128)(2,1)} %param.4, f32[2,1034,256]{2,1,0:T(8,128)S(1)} %select_select_fusion), kind=kOutput, calls=%fused_computation.3 | convolution fusion | flops 12884901888 | bytes 18874368 | tf_op jit(solution)/shard_map/cpxz,sxm->scpmz/dot_general | solution.py:165
  15.8 1.0 select_select_fusion.1
  17.3 3.2 %fusion.35 = f32[2,256,4,4,256]{1,4,3,2,0:T(8,128)S(1)} fusion(bf16[4,4,5,256]{3,2,1,0:T(8,128)(2,1)} %collective-permute-done, f32[2,1034,256]{2,1,0:T(8,128)S(1)} %select_select_fusion), kind=kOutput, calls=%fused_computation.61 | convolution fusion | flops 62914560 | bytes 8445952 | tf_op jit(solution)/shard_map/cpxz,sxm->scpmz/dot_general | solution.py:171
  20.5 3.0 %add_add_fusion = f32[2,256,4,4,256]{1,4,3,2,0:T(8,128)S(1)} fusion(f32[2,256,4,4,256]{1,4,3,2,0:T(8,128)S(1)} %fusion.2, f32[2,256,4,4,256]{1,4,3,2,0:T(8,128)S(1)} %fusion.35, bf16[4,4,5,256]{3,2,1,0:T(8,128)(2,1)S(1)} %collective-permute-done.1, f32[2,1034,256]{2,1,0:T(8,128)S(1)} %select_select_fusion), kind=kOutput, calls=%fused_computation.5 | convolution fusion | flops 67108864 | bytes 25247744 | tf_op jit(solution)/shard_map/cpxz,sxm->scpmz/dot_general | solution.py:174
  23.6 3.0 %collective-permute-start.2 = (f32[2,4,4,5,256]{4,3,2,1,0:T(8,128)S(1)}, f32[2,4,4,5,256]{4,3,2,1,0:T(8,128)S(1)}, u32[]{:S(2)}, u32[]{:S(2)}) collective-permute-start(f32[2,4,4,5,256]{4,3,2,1,0:T(8,128)S(1)} %get-tuple-element.42), channel_id=1, source_target_pairs={{0,2},{2,0},{1,3},{3,1},{4,6},{6,4},{5,7},{7,5},{8,10},{10,8},{9,1... | collective-permute-start | bytes 491528 | tf_op jit(solution)/shard_map/ppermute | solution.py:68
  26.6 3.6 %fusion = f32[2,4,4,256,64]{3,4,2,1,0:T(8,128)S(1)} fusion(f32[2,256,4,4,256]{1,4,3,2,0:T(8,128)S(1)} %add_add_fusion, f32[266,2,64]{0,2,1:T(8,128)} %select_select_fusion.1), kind=kOutput, calls=%fused_computation.1 | convolution fusion | flops 805306368 | bytes 10616832 | tf_op jit(solution)/shard_map/scpmz,zsn->scpmn/dot_general | solution.py:183
  30.3 3.2 %collective-permute-done.2 = f32[2,4,4,5,256]{4,3,2,1,0:T(8,128)S(1)} collective-permute-done((f32[2,4,4,5,256]{4,3,2,1,0:T(8,128)S(1)}, f32[2,4,4,5,256]{4,3,2,1,0:T(8,128)S(1)}, u32[]{:S(2)}, u32[]{:S(2)}) %collective-permute-start.2) | collective-permute-done | bytes 163872 | tf_op jit(solution)/shard_map/ppermute | solution.py:68
  33.5 1.0 fusion.33
  34.5 4.2 %collective-permute-done.3 = f32[2,4,4,5,256]{4,3,2,1,0:T(8,128)S(1)} collective-permute-done((f32[2,4,4,5,256]{4,3,2,1,0:T(8,128)S(1)}, f32[2,4,4,5,256]{4,3,2,1,0:T(8,128)S(1)}, u32[]{:S(2)}, u32[]{:S(2)}) %collective-permute-start.3) | collective-permute-done | bytes 163872 | tf_op jit(solution)/shard_map/ppermute | solution.py:68
  38.7 1.3 add_add_fusion.1
  42.0 1.5 %copy.29 = bf16[1,4,4,256,64]{4,3,2,1,0:T(8,128)(2,1)S(1)} copy(bf16[1,4,4,256,64]{3,4,2,1,0:T(8,128)(2,1)} %slice.124) | data formatting | bytes 1048576 | tf_op jit(solution)/shard_map/slice | solution.py:192
  44.3 1.1 copy.31
  45.4 5.1 %all-to-all-start = ((bf16[4,1024,128]{2,1,0:T(8,128)(2,1)}), bf16[4,1024,128]{2,1,0:T(8,128)(2,1)S(1)}, u32[]{:S(2)}, u32[]{:S(2)}) async-start(bf16[4,1024,128]{2,1,0:T(8,128)(2,1)} %bitcast.16), calls=%async_computation | async-start | bytes 2097152 | tf_op jit(solution)/shard_map/all_to_all | solution.py:210
  51.7 1.5 %reshape_reshape.3 = bf16[6,4,128,128]{3,2,1,0:T(8,128)(2,1)} reshape(bf16[6,4,256,64]{3,2,1,0:T(8,128)(2,1)S(1)} %copy.34) | data formatting | bytes 1572864 | tf_op jit(solution)/shard_map/reshape;reshape | solution.py:214
  53.2 0.9 constant_dynamic-slice_fusion.1
  54.1 21.7 %all-to-all-done = bf16[4,1024,128]{2,1,0:T(8,128)(2,1)S(1)} async-done(((bf16[4,1024,128]{2,1,0:T(8,128)(2,1)}), bf16[4,1024,128]{2,1,0:T(8,128)(2,1)S(1)}, u32[]{:S(2)}, u32[]{:S(2)}) %all-to-all-start) | async-done | bytes 1048608 | tf_op jit(solution)/shard_map/all_to_all | solution.py:210
  76.8 1.6 %copy.33 = f32[16,128,128]{2,0,1:T(8,128)} copy(f32[16,128,128]{2,1,0:T(8,128)S(1)} %bitcast_convert_fusion) | data formatting | bytes 2097152 | tf_op jit(solution)/shard_map/while/body/eval_jaxpr/convert_element_type | solution.py:137
  78.4 4.1 %multiply_convert_fusion = bf16[16,16,128,128]{3,1,0,2:T(8,128)(2,1)S(1)} fusion(f32[16,128,128]{2,0,1:T(8,128)} %copy.33, f32[16,128,128]{2,0,1:T(8,128)S(1)} %copy.32), kind=kLoop, calls=%fused_computation | loop fusion | flops 8388608 | bytes 10485760 | tf_op jit(solution)/shard_map/while/body/eval_jaxpr/convert_element_type | solution.py:139
  82.5 2.4 %convolution_bitcast_fusion = f32[256,256]{0,1:T(8,128)S(1)} fusion(bf16[256,128,128]{2,0,1:T(8,128)(2,1)S(1)} %bitcast.82), kind=kOutput, calls=%fused_computation.26 | convolution fusion | flops 2147483648 | bytes 8650752 | tf_op jit(solution)/shard_map/while/body/eval_jaxpr/iqr,jqr->ij/dot_general | solution.py:226
  84.9 0.9 copy-done
  85.7 2.3 %convolution_bitcast_fusion.1 = f32[256,6]{0,1:T(8,128)S(1)} fusion(bf16[256,128,128]{2,0,1:T(8,128)(2,1)S(1)} %bitcast.83, bf16[6,1,128,128]{3,2,1,0:T(8,128)(2,1)S(1)} %constant_dynamic-slice_fusion.1), kind=kOutput, calls=%fused_computation.27 | convolution fusion | flops 50331648 | bytes 8591360 | tf_op jit(solution)/shard_map/while/body/eval_jaxpr/iqr,kqr->ik/dot_general | solution.py:229
  88.7 1.5 %collective-permute-done.4 = f32[256,262]{0,1:T(8,128)S(1)} collective-permute-done((f32[256,262]{0,1:T(8,128)S(1)}, f32[256,262]{0,1:T(8,128)S(1)}, u32[]{:S(2)}, u32[]{:S(2)}) %collective-permute-start.4) | collective-permute-done | bytes 268320 | tf_op jit(solution)/shard_map/ppermute | solution.py:53
  91.0 1.3 collective-permute-start.5
  92.3 4.4 %collective-permute-done.5 = f32[128,262]{0,1:T(8,128)S(1)} collective-permute-done((f32[128,262]{0,1:T(8,128)S(1)}, f32[128,262]{0,1:T(8,128)S(1)}, u32[]{:S(2)}, u32[]{:S(2)}) %collective-permute-start.5) | collective-permute-done | bytes 134176 | tf_op jit(solution)/shard_map/ppermute | solution.py:43
  96.8 5.0 %collective-permute-done.6 = f32[128,262]{0,1:T(8,128)S(1)} collective-permute-done((f32[128,262]{0,1:T(8,128)S(1)}, f32[128,262]{0,1:T(8,128)S(1)}, u32[]{:S(2)}, u32[]{:S(2)}) %collective-permute-start.6) | collective-permute-done | bytes 134176 | tf_op jit(solution)/shard_map/ppermute | solution.py:43
  102.0 7.4 %collective-permute-done.7 = f32[128,262]{0,1:T(8,128)S(1)} collective-permute-done((f32[128,262]{0,1:T(8,128)S(1)}, f32[128,262]{0,1:T(8,128)S(1)}, u32[]{:S(2)}, u32[]{:S(2)}) %collective-permute-start.7) | collective-permute-done | bytes 134176 | tf_op jit(solution)/shard_map/ppermute | solution.py:43
  112.4 6.0 %shard_map.59 = f32[3,6,256]{2,1,0:T(8,128)} custom-call(f32[256,256]{1,0:T(8,128)} %copy.36.gram_ref, f32[6,256]{1,0:T(8,128)} %fusion.39.target_ref, f32[3,6,256]{2,1,0:T(8,128)} %convert_element_type.117.mask_ref), custom_call_target="tpu_custom_call" | custom-call | tf_op jit(solution)/shard_map/pallas_call | solution.py:251
  118.4 4.6 %fusion.17 = bf16[6,128,128]{2,0,1:T(8,128)(2,1)S(1)} fusion(bf16[256,128,128]{2,0,1:T(8,128)(2,1)} %bitcast.84, bf16[6,1,128,128]{3,2,1,0:T(8,128)(2,1)S(1)} %constant_dynamic-slice_fusion.1, f32[3,6,256]{2,1,0:T(8,128)} %shard_map.59, f32[256]{0:T(256)S(1)} %add_rsqrt_fusion), kind=kOutput, calls=%fused_computation.25 | convolution fusion | flops 50629632 | bytes 8791040 | tf_op jit(solution)/shard_map/while/body/eval_jaxpr/ki,iqr->kqr/dot_general | solution.py:264
  123.1 18.0 %all_gather.3 = bf16[6,512,128]{2,1,0:T(8,128)(2,1)S(1)} all-gather(bf16[6,128,128]{2,1,0:T(8,128)(2,1)S(1)} %copy.37), channel_id=1, replica_groups=mesh['groups'=2,'cols'=4,'slab'=2,'rep'=2] {'cols'}, dimensions={1}, use_global_device_ids=true | all-gather | bytes 983040 | tf_op jit(solution)/shard_map/all_gather | solution.py:274
  141.7 1.4 copy.38
  (64 shorter events, 12.2 us)
Async XLA Ops:
  2.1 15.1 %collective-permute-start = (bf16[4,4,5,256]{3,2,1,0:T(8,128)(2,1)S(1)}, bf16[4,4,5,256]{3,2,1,0:T(8,128)(2,1)}, u32[]{:S(2)}, u32[]{:S(2)}) collective-permute-start(bf16[4,4,5,256]{3,2,1,0:T(8,128)(2,1)S(1)} %get-tuple-element.44), channel_id=1, source_target_pairs={{0,1},{1,0},{2,3},{3,2},{4,5},{5,4},{6,7},{7,6},{8,9},{9,8},{10,11... | collective-permute-start | bytes 122888 | tf_op jit(solution)/shard_map/ppermute | solution.py:68
  2.6 17.9 %collective-permute-start.1 = (bf16[4,4,5,256]{3,2,1,0:T(8,128)(2,1)}, bf16[4,4,5,256]{3,2,1,0:T(8,128)(2,1)S(1)}, u32[]{:S(2)}, u32[]{:S(2)}) collective-permute-start(bf16[4,4,5,256]{3,2,1,0:T(8,128)(2,1)} %get-tuple-element.43), channel_id=1, source_target_pairs={{1,0},{0,1},{3,2},{2,3},{5,4},{4,5},{7,6},{6,7},{9,8},{8,9},{11,10... | collective-permute-start | bytes 122888 | tf_op jit(solution)/shard_map/ppermute | solution.py:68
  4.2 12.6 %copy-start.7 = (s32[4]{0:T(128)S(1)}, s32[4]{0:T(128)}, u32[]{:S(2)}) copy-start(s32[4]{0:T(128)} %param.6) | copy-start | bytes 52
  23.6 9.9 %copy-start.1 = (f32[266,2,64]{0,2,1:T(8,128)S(1)}, f32[266,2,64]{0,2,1:T(8,128)}, u32[]{:S(2)}) copy-start(f32[266,2,64]{0,2,1:T(8,128)} %select_select_fusion.1) | copy-start | bytes 408580
  23.6 9.9 %collective-permute-start.2 = (f32[2,4,4,5,256]{4,3,2,1,0:T(8,128)S(1)}, f32[2,4,4,5,256]{4,3,2,1,0:T(8,128)S(1)}, u32[]{:S(2)}, u32[]{:S(2)}) collective-permute-start(f32[2,4,4,5,256]{4,3,2,1,0:T(8,128)S(1)} %get-tuple-element.42), channel_id=1, source_target_pairs={{0,2},{2,0},{1,3},{3,1},{4,6},{6,4},{5,7},{7,5},{8,10},{10,8},{9,1... | collective-permute-start | bytes 491528 | tf_op jit(solution)/shard_map/ppermute | solution.py:68
  30.2 8.5 %collective-permute-start.3 = (f32[2,4,4,5,256]{4,3,2,1,0:T(8,128)S(1)}, f32[2,4,4,5,256]{4,3,2,1,0:T(8,128)S(1)}, u32[]{:S(2)}, u32[]{:S(2)}) collective-permute-start(f32[2,4,4,5,256]{4,3,2,1,0:T(8,128)S(1)} %get-tuple-element.34), channel_id=1, source_target_pairs={{2,0},{0,2},{3,1},{1,3},{6,4},{4,6},{7,5},{5,7},{10,8},{8,10},{11,... | collective-permute-start | bytes 491528 | tf_op jit(solution)/shard_map/ppermute | solution.py:68
  41.9 2.0 %copy-start.6 = (f32[4]{0:T(128)S(1)}, f32[4]{0:T(128)}, u32[]{:S(2)}) copy-start(f32[4]{0:T(128)} %subtract_sqrt_fusion) | copy-start | bytes 52
  44.3 6.2 %copy-start.2 = (bf16[6,4,256,64]{2,3,1,0:T(8,128)(2,1)S(1)}, bf16[6,4,256,64]{2,3,1,0:T(8,128)(2,1)}, u32[]{:S(2)}) copy-start(bf16[6,4,256,64]{2,3,1,0:T(8,128)(2,1)} %param.5) | copy-start | bytes 2359300
  45.4 30.5 %all-to-all-start = ((bf16[4,1024,128]{2,1,0:T(8,128)(2,1)}), bf16[4,1024,128]{2,1,0:T(8,128)(2,1)S(1)}, u32[]{:S(2)}, u32[]{:S(2)}) async-start(bf16[4,1024,128]{2,1,0:T(8,128)(2,1)} %bitcast.16), calls=%async_computation | async-start | bytes 2097152 | tf_op jit(solution)/shard_map/all_to_all | solution.py:210
  82.5 3.3 %copy-start = (bf16[16,16,128,128]{3,1,0,2:T(8,128)(2,1)}, bf16[16,16,128,128]{3,1,0,2:T(8,128)(2,1)S(1)}, u32[]{:S(2)}) copy-start(bf16[16,16,128,128]{3,1,0,2:T(8,128)(2,1)S(1)} %multiply_convert_fusion) | copy-start | bytes 25165828
  88.0 0.6 copy-start.4
  88.6 20.8 %copy-start.5 = (s32[3,6,256]{2,1,0:T(8,128)S(1)}, s32[3,6,256]{2,1,0:T(8,128)}, u32[]{:S(2)}) copy-start(s32[3,6,256]{2,1,0:T(8,128)} %param.7) | copy-start | bytes 55300
  88.6 1.6 %collective-permute-start.4 = (f32[256,262]{0,1:T(8,128)S(1)}, f32[256,262]{0,1:T(8,128)S(1)}, u32[]{:S(2)}, u32[]{:S(2)}) collective-permute-start(f32[256,262]{0,1:T(8,128)S(1)} %pad_maximum_fusion), channel_id=1, source_target_pairs={{0,1},{1,0},{2,3},{3,2},{4,5},{5,4},{6,7},{7,6},{8,9},{9,8},{10,11... | collective-permute-start | bytes 804872 | tf_op jit(solution)/shard_map/ppermute | solution.py:53
  91.0 5.7 %collective-permute-start.5 = (f32[128,262]{0,1:T(8,128)S(1)}, f32[128,262]{0,1:T(8,128)S(1)}, u32[]{:S(2)}, u32[]{:S(2)}) collective-permute-start(f32[128,262]{0,1:T(8,128)S(1)} %slice_select_fusion), channel_id=1, source_target_pairs={{0,2},{2,0},{1,3},{3,1},{4,6},{6,4},{5,7},{7,5},{8,10},{10,8},{9,1... | collective-permute-start | bytes 402440 | tf_op jit(solution)/shard_map/ppermute | solution.py:43
  96.7 5.1 %collective-permute-start.6 = (f32[128,262]{0,1:T(8,128)S(1)}, f32[128,262]{0,1:T(8,128)S(1)}, u32[]{:S(2)}, u32[]{:S(2)}) collective-permute-start(f32[128,262]{0,1:T(8,128)S(1)} %fusion.60), channel_id=1, source_target_pairs={{0,4},{4,0},{8,12},{12,8},{1,5},{5,1},{9,13},{13,9},{2,6},{6,2},{1... | collective-permute-start | bytes 402440 | tf_op jit(solution)/shard_map/ppermute | solution.py:43
  101.8 7.5 %collective-permute-start.7 = (f32[128,262]{0,1:T(8,128)S(1)}, f32[128,262]{0,1:T(8,128)S(1)}, u32[]{:S(2)}, u32[]{:S(2)}) collective-permute-start(f32[128,262]{0,1:T(8,128)S(1)} %add.110), channel_id=1, source_target_pairs={{0,8},{4,12},{8,0},{12,4},{1,9},{5,13},{9,1},{13,5},{2,10},{6,14},... | collective-permute-start | bytes 402440 | tf_op jit(solution)/shard_map/ppermute | solution.py:43
  109.4 1.4 collective-permute-start.8
  141.0 2.1 %copy-start.3 = (f32[3,6,256]{2,1,0:T(8,128)S(1)}, f32[3,6,256]{2,1,0:T(8,128)}, u32[]{:S(2)}) copy-start(f32[3,6,256]{2,1,0:T(8,128)} %shard_map.59) | copy-start | bytes 55300

commit v18 on v17

--- a/solution.py
+++ b/solution.py
@@ -123,13 +123,18 @@
     which = lax.broadcasted_iota(jnp.int32, shape, where[1])
     out_index = lax.broadcasted_iota(jnp.int32, shape, where[2])
     tap_at = position - 1 - 4 * out_index + guard
-    table = jnp.zeros(shape, jnp.float32)
-    for tap_index in range(13):
-        value = jnp.where(
-            which == 0, np.float32(first_taps[tap_index]), np.float32(second_taps[tap_index])
-        )
-        table = jnp.where(tap_at == tap_index, value, table)
-    return table
+    spread = jnp.where(which == 0, np.float32(1.5), np.float32(3.0))
+    total = jnp.where(
+        which == 0, np.float32(gauss_total(1.5)), np.float32(gauss_total(3.0))
+    )
+    offset = (tap_at - 6).astype(jnp.float32)
+    value = jnp.exp(-offset * offset / (2.0 * spread * spread)) / total
+    return jnp.where((tap_at >= 0) & (tap_at <= 12), value, 0.0)
+
+
+def gauss_total(spread):
+    offsets = np.arange(13) - 6.0
+    return np.exp(-offsets * offsets / (2.0 * spread * spread)).sum()
 
 
 def library(narrow_part, broad_part):

time: 144 us -> 143 us (level)
  no operation moved by 1% of the time
where the time goes in v18:
time: 143 us
  waiting for transfers between devices  48.1 us (34%)
  matrix products  32.9 us (23%)
  blocking collectives  18 us (13%)
  local copies, waits for them, and re-layouts  17.2 us (12%)
  starting transfers between devices  10.4 us (7%)
  other arithmetic  9.34 us (7%)
  Pallas kernels  5.99 us (4%)
    all_to_all x1, waiting for transfers between devices, local(): sets = lax.all_to_all(sets, 'cols', 0, 0, tiled=True)  21.7 us
    all_gather x1, blocking collectives, local(): misfit = lax.all_gather(misfit, 'cols', axis=1, tiled=True)  18 us
    ppermute x3, waiting for transfers between devices, tree_sum(): value = value + lax.ppermute(value, axis, partner)  16.8 us
    dot_general x1, matrix products, local(): jnp.einsum('cpxz,sxm->scpmz', fields.astype(jnp.float32), stream_table[:,...  11.6 us
    ppermute x4, waiting for transfers between devices, neighbour_edges(): return (lax.ppermute(last, axis, up), lax.ppermute(leading, axis, down))  7.43 us
    pallas_call x1, Pallas kernels, local(): pl.pallas_call(conjugate_passes, out_shape=jax.ShapeDtypeStruct((PASSES,...  5.99 us
    all_to_all x1, starting transfers between devices, local(): sets = lax.all_to_all(sets, 'cols', 0, 0, tiled=True)  5.12 us
    dot_general x1, matrix products, misfit_step(): jnp.einsum('ki,iqr->kqr', final_weights, all_terms, preferred_element_typ...  4.6 us
  transfers between devices with their start and end apart: 10, of which 8 were waited for; matrix products, arithmetic and copies ran while one was open for 18% of the time, Pallas kernels for 0%

profile of v18, /device:TPU:0, one launch (start us, length us, event | category | flops | bytes accessed | tf_op | source)
XLA Modules:
  0.0 142.9 jit_solution(12087864347580775339)
XLA Ops:
  0.6 1.5 %fusion.33 = (bf16[4,4,5,256]{3,2,1,0:T(8,128)(2,1)}, bf16[4,4,5,256]{3,2,1,0:T(8,128)(2,1)S(1)}) fusion(bf16[4,4,1024,256]{3,2,1,0:T(8,128)(2,1)} %param.4), kind=kLoop, calls=%fused_computation.73 | loop fusion | bytes 163840 | tf_op jit(solution)/shard_map/slice | solution.py:67
  3.5 11.6 %fusion.2 = f32[2,256,4,4,256]{1,4,3,2,0:T(8,128)S(1)} fusion(bf16[4,4,1024,256]{3,2,1,0:T(8,128)(2,1)} %param.4, f32[2,1034,256]{2,1,0:T(8,128)S(1)} %fusion.7), kind=kOutput, calls=%fused_computation.3 | convolution fusion | flops 12884901888 | bytes 18874368 | tf_op jit(solution)/shard_map/cpxz,sxm->scpmz/dot_general | solution.py:170
  16.4 3.2 %fusion.23 = f32[2,256,4,4,256]{1,4,3,2,0:T(8,128)S(1)} fusion(bf16[4,4,5,256]{3,2,1,0:T(8,128)(2,1)} %collective-permute-done, f32[2,1034,256]{2,1,0:T(8,128)S(1)} %fusion.7), kind=kOutput, calls=%fused_computation.49 | convolution fusion | flops 62914560 | bytes 8445952 | tf_op jit(solution)/shard_map/cpxz,sxm->scpmz/dot_general | solution.py:176
  19.6 3.0 %add_add_fusion = f32[2,256,4,4,256]{1,4,3,2,0:T(8,128)S(1)} fusion(f32[2,256,4,4,256]{1,4,3,2,0:T(8,128)S(1)} %fusion.2, f32[2,256,4,4,256]{1,4,3,2,0:T(8,128)S(1)} %fusion.23, bf16[4,4,5,256]{3,2,1,0:T(8,128)(2,1)S(1)} %collective-permute-done.1, f32[2,1034,256]{2,1,0:T(8,128)S(1)} %fusion.7), kind=kOutput, calls=%fused_computation.5 | convolution fusion | flops 67108864 | bytes 25247744 | tf_op jit(solution)/shard_map/cpxz,sxm->scpmz/dot_general | solution.py:179
  22.7 3.0 %collective-permute-start.2 = (f32[2,4,4,5,256]{4,3,2,1,0:T(8,128)S(1)}, f32[2,4,4,5,256]{4,3,2,1,0:T(8,128)S(1)}, u32[]{:S(2)}, u32[]{:S(2)}) collective-permute-start(f32[2,4,4,5,256]{4,3,2,1,0:T(8,128)S(1)} %get-tuple-element.42), channel_id=1, source_target_pairs={{0,2},{2,0},{1,3},{3,1},{4,6},{6,4},{5,7},{7,5},{8,10},{10,8},{9,1... | collective-permute-start | bytes 491528 | tf_op jit(solution)/shard_map/ppermute | solution.py:68
  25.7 3.6 %fusion = f32[2,4,4,256,64]{3,4,2,1,0:T(8,128)S(1)} fusion(f32[2,256,4,4,256]{1,4,3,2,0:T(8,128)S(1)} %add_add_fusion, f32[266,2,64]{0,2,1:T(8,128)} %fusion.17), kind=kOutput, calls=%fused_computation.1 | convolution fusion | flops 805306368 | bytes 10616832 | tf_op jit(solution)/shard_map/scpmz,zsn->scpmn/dot_general | solution.py:188
  29.4 3.2 %collective-permute-done.2 = f32[2,4,4,5,256]{4,3,2,1,0:T(8,128)S(1)} collective-permute-done((f32[2,4,4,5,256]{4,3,2,1,0:T(8,128)S(1)}, f32[2,4,4,5,256]{4,3,2,1,0:T(8,128)S(1)}, u32[]{:S(2)}, u32[]{:S(2)}) %collective-permute-start.2) | collective-permute-done | bytes 163872 | tf_op jit(solution)/shard_map/ppermute | solution.py:68
  32.6 1.0 fusion.21
  33.6 4.2 %collective-permute-done.3 = f32[2,4,4,5,256]{4,3,2,1,0:T(8,128)S(1)} collective-permute-done((f32[2,4,4,5,256]{4,3,2,1,0:T(8,128)S(1)}, f32[2,4,4,5,256]{4,3,2,1,0:T(8,128)S(1)}, u32[]{:S(2)}, u32[]{:S(2)}) %collective-permute-start.3) | collective-permute-done | bytes 163872 | tf_op jit(solution)/shard_map/ppermute | solution.py:68
  37.8 1.3 add_add_fusion.1
  39.2 0.9 slice.124
  41.1 1.5 %copy.29 = bf16[1,4,4,256,64]{4,3,2,1,0:T(8,128)(2,1)S(1)} copy(bf16[1,4,4,256,64]{3,4,2,1,0:T(8,128)(2,1)} %slice.124) | data formatting | bytes 1048576 | tf_op jit(solution)/shard_map/slice | solution.py:197
  43.4 1.1 copy.31
  44.5 5.1 %all-to-all-start = ((bf16[4,1024,128]{2,1,0:T(8,128)(2,1)}), bf16[4,1024,128]{2,1,0:T(8,128)(2,1)S(1)}, u32[]{:S(2)}, u32[]{:S(2)}) async-start(bf16[4,1024,128]{2,1,0:T(8,128)(2,1)} %bitcast.16), calls=%async_computation | async-start | bytes 2097152 | tf_op jit(solution)/shard_map/all_to_all | solution.py:215
  50.0 0.9 copy.34
  50.8 1.5 %reshape_reshape.3 = bf16[6,4,128,128]{3,2,1,0:T(8,128)(2,1)} reshape(bf16[6,4,256,64]{3,2,1,0:T(8,128)(2,1)S(1)} %copy.34) | data formatting | bytes 1572864 | tf_op jit(solution)/shard_map/reshape;reshape | solution.py:219
  52.3 0.9 constant_dynamic-slice_fusion.1
  53.2 21.7 %all-to-all-done = bf16[4,1024,128]{2,1,0:T(8,128)(2,1)S(1)} async-done(((bf16[4,1024,128]{2,1,0:T(8,128)(2,1)}), bf16[4,1024,128]{2,1,0:T(8,128)(2,1)S(1)}, u32[]{:S(2)}, u32[]{:S(2)}) %all-to-all-start) | async-done | bytes 1048608 | tf_op jit(solution)/shard_map/all_to_all | solution.py:215
  75.9 1.6 %copy.33 = f32[16,128,128]{2,0,1:T(8,128)} copy(f32[16,128,128]{2,1,0:T(8,128)S(1)} %bitcast_convert_fusion) | data formatting | bytes 2097152 | tf_op jit(solution)/shard_map/while/body/eval_jaxpr/convert_element_type | solution.py:142
  77.5 4.1 %multiply_convert_fusion = bf16[16,16,128,128]{3,1,0,2:T(8,128)(2,1)S(1)} fusion(f32[16,128,128]{2,0,1:T(8,128)} %copy.33, f32[16,128,128]{2,0,1:T(8,128)S(1)} %copy.32), kind=kLoop, calls=%fused_computation | loop fusion | flops 8388608 | bytes 10485760 | tf_op jit(solution)/shard_map/while/body/eval_jaxpr/convert_element_type | solution.py:144
  81.6 2.4 %convolution_bitcast_fusion = f32[256,256]{0,1:T(8,128)S(1)} fusion(bf16[256,128,128]{2,0,1:T(8,128)(2,1)S(1)} %bitcast.82), kind=kOutput, calls=%fused_computation.20 | convolution fusion | flops 2147483648 | bytes 8650752 | tf_op jit(solution)/shard_map/while/body/eval_jaxpr/iqr,jqr->ij/dot_general | solution.py:231
  83.9 0.9 copy-done
  84.8 2.3 %convolution_bitcast_fusion.1 = f32[256,6]{0,1:T(8,128)S(1)} fusion(bf16[256,128,128]{2,0,1:T(8,128)(2,1)S(1)} %bitcast.83, bf16[6,1,128,128]{3,2,1,0:T(8,128)(2,1)S(1)} %constant_dynamic-slice_fusion.1), kind=kOutput, calls=%fused_computation.21 | convolution fusion | flops 50331648 | bytes 8591360 | tf_op jit(solution)/shard_map/while/body/eval_jaxpr/iqr,kqr->ik/dot_general | solution.py:234
  87.8 1.5 %collective-permute-done.4 = f32[256,262]{0,1:T(8,128)S(1)} collective-permute-done((f32[256,262]{0,1:T(8,128)S(1)}, f32[256,262]{0,1:T(8,128)S(1)}, u32[]{:S(2)}, u32[]{:S(2)}) %collective-permute-start.4) | collective-permute-done | bytes 268320 | tf_op jit(solution)/shard_map/ppermute | solution.py:53
  90.1 1.3 collective-permute-start.5
  91.4 4.4 %collective-permute-done.5 = f32[128,262]{0,1:T(8,128)S(1)} collective-permute-done((f32[128,262]{0,1:T(8,128)S(1)}, f32[128,262]{0,1:T(8,128)S(1)}, u32[]{:S(2)}, u32[]{:S(2)}) %collective-permute-start.5) | collective-permute-done | bytes 134176 | tf_op jit(solution)/shard_map/ppermute | solution.py:43
  95.9 5.0 %collective-permute-done.6 = f32[128,262]{0,1:T(8,128)S(1)} collective-permute-done((f32[128,262]{0,1:T(8,128)S(1)}, f32[128,262]{0,1:T(8,128)S(1)}, u32[]{:S(2)}, u32[]{:S(2)}) %collective-permute-start.6) | collective-permute-done | bytes 134176 | tf_op jit(solution)/shard_map/ppermute | solution.py:43
  101.0 7.4 %collective-permute-done.7 = f32[128,262]{0,1:T(8,128)S(1)} collective-permute-done((f32[128,262]{0,1:T(8,128)S(1)}, f32[128,262]{0,1:T(8,128)S(1)}, u32[]{:S(2)}, u32[]{:S(2)}) %collective-permute-start.7) | collective-permute-done | bytes 134176 | tf_op jit(solution)/shard_map/ppermute | solution.py:43
  111.5 6.0 %shard_map.59 = f32[3,6,256]{2,1,0:T(8,128)} custom-call(f32[256,256]{1,0:T(8,128)} %copy.36.gram_ref, f32[6,256]{1,0:T(8,128)} %fusion.27.target_ref, f32[3,6,256]{2,1,0:T(8,128)} %convert_element_type.125.mask_ref), custom_call_target="tpu_custom_call" | custom-call | tf_op jit(solution)/shard_map/pallas_call | solution.py:256
  117.5 4.6 %fusion.11 = bf16[6,128,128]{2,0,1:T(8,128)(2,1)S(1)} fusion(bf16[256,128,128]{2,0,1:T(8,128)(2,1)} %bitcast.84, bf16[6,1,128,128]{3,2,1,0:T(8,128)(2,1)S(1)} %constant_dynamic-slice_fusion.1, f32[3,6,256]{2,1,0:T(8,128)} %shard_map.59, f32[256]{0:T(256)S(1)} %add_rsqrt_fusion), kind=kOutput, calls=%fused_computation.19 | convolution fusion | flops 50629632 | bytes 8791040 | tf_op jit(solution)/shard_map/while/body/eval_jaxpr/ki,iqr->kqr/dot_general | solution.py:269
  122.1 18.0 %all_gather.3 = bf16[6,512,128]{2,1,0:T(8,128)(2,1)S(1)} all-gather(bf16[6,128,128]{2,1,0:T(8,128)(2,1)S(1)} %copy.37), channel_id=1, replica_groups=mesh['groups'=2,'cols'=4,'slab'=2,'rep'=2] {'cols'}, dimensions={1}, use_global_device_ids=true | all-gather | bytes 983040 | tf_op jit(solution)/shard_map/all_gather | solution.py:279
  140.8 1.4 copy.38
  (61 shorter events, 12.1 us)
Async XLA Ops:
  2.1 14.3 %collective-permute-start = (bf16[4,4,5,256]{3,2,1,0:T(8,128)(2,1)S(1)}, bf16[4,4,5,256]{3,2,1,0:T(8,128)(2,1)}, u32[]{:S(2)}, u32[]{:S(2)}) collective-permute-start(bf16[4,4,5,256]{3,2,1,0:T(8,128)(2,1)S(1)} %get-tuple-element.44), channel_id=1, source_target_pairs={{0,1},{1,0},{2,3},{3,2},{4,5},{5,4},{6,7},{7,6},{8,9},{9,8},{10,11... | collective-permute-start | bytes 122888 | tf_op jit(solution)/shard_map/ppermute | solution.py:68
  2.6 17.0 %collective-permute-start.1 = (bf16[4,4,5,256]{3,2,1,0:T(8,128)(2,1)}, bf16[4,4,5,256]{3,2,1,0:T(8,128)(2,1)S(1)}, u32[]{:S(2)}, u32[]{:S(2)}) collective-permute-start(bf16[4,4,5,256]{3,2,1,0:T(8,128)(2,1)} %get-tuple-element.43), channel_id=1, source_target_pairs={{1,0},{0,1},{3,2},{2,3},{5,4},{4,5},{7,6},{6,7},{9,8},{8,9},{11,10... | collective-permute-start | bytes 122888 | tf_op jit(solution)/shard_map/ppermute | solution.py:68
  3.4 12.4 %copy-start.7 = (s32[4]{0:T(128)S(1)}, s32[4]{0:T(128)}, u32[]{:S(2)}) copy-start(s32[4]{0:T(128)} %param.6) | copy-start | bytes 52
  22.7 9.9 %copy-start.1 = (f32[266,2,64]{0,2,1:T(8,128)S(1)}, f32[266,2,64]{0,2,1:T(8,128)}, u32[]{:S(2)}) copy-start(f32[266,2,64]{0,2,1:T(8,128)} %fusion.17) | copy-start | bytes 408580
  22.7 9.9 %collective-permute-start.2 = (f32[2,4,4,5,256]{4,3,2,1,0:T(8,128)S(1)}, f32[2,4,4,5,256]{4,3,2,1,0:T(8,128)S(1)}, u32[]{:S(2)}, u32[]{:S(2)}) collective-permute-start(f32[2,4,4,5,256]{4,3,2,1,0:T(8,128)S(1)} %get-tuple-element.42), channel_id=1, source_target_pairs={{0,2},{2,0},{1,3},{3,1},{4,6},{6,4},{5,7},{7,5},{8,10},{10,8},{9,1... | collective-permute-start | bytes 491528 | tf_op jit(solution)/shard_map/ppermute | solution.py:68
  29.3 8.5 %collective-permute-start.3 = (f32[2,4,4,5,256]{4,3,2,1,0:T(8,128)S(1)}, f32[2,4,4,5,256]{4,3,2,1,0:T(8,128)S(1)}, u32[]{:S(2)}, u32[]{:S(2)}) collective-permute-start(f32[2,4,4,5,256]{4,3,2,1,0:T(8,128)S(1)} %get-tuple-element.34), channel_id=1, source_target_pairs={{2,0},{0,2},{3,1},{1,3},{6,4},{4,6},{7,5},{5,7},{10,8},{8,10},{11,... | collective-permute-start | bytes 491528 | tf_op jit(solution)/shard_map/ppermute | solution.py:68
  41.0 2.0 %copy-start.6 = (f32[4]{0:T(128)S(1)}, f32[4]{0:T(128)}, u32[]{:S(2)}) copy-start(f32[4]{0:T(128)} %subtract_sqrt_fusion) | copy-start | bytes 52
  43.4 6.2 %copy-start.2 = (bf16[6,4,256,64]{2,3,1,0:T(8,128)(2,1)S(1)}, bf16[6,4,256,64]{2,3,1,0:T(8,128)(2,1)}, u32[]{:S(2)}) copy-start(bf16[6,4,256,64]{2,3,1,0:T(8,128)(2,1)} %param.5) | copy-start | bytes 2359300
  44.5 30.5 %all-to-all-start = ((bf16[4,1024,128]{2,1,0:T(8,128)(2,1)}), bf16[4,1024,128]{2,1,0:T(8,128)(2,1)S(1)}, u32[]{:S(2)}, u32[]{:S(2)}) async-start(bf16[4,1024,128]{2,1,0:T(8,128)(2,1)} %bitcast.16), calls=%async_computation | async-start | bytes 2097152 | tf_op jit(solution)/shard_map/all_to_all | solution.py:215
  81.6 3.2 %copy-start = (bf16[16,16,128,128]{3,1,0,2:T(8,128)(2,1)}, bf16[16,16,128,128]{3,1,0,2:T(8,128)(2,1)S(1)}, u32[]{:S(2)}) copy-start(bf16[16,16,128,128]{3,1,0,2:T(8,128)(2,1)S(1)} %multiply_convert_fusion) | copy-start | bytes 25165828
  87.1 0.6 copy-start.4
  87.7 20.8 %copy-start.5 = (s32[3,6,256]{2,1,0:T(8,128)S(1)}, s32[3,6,256]{2,1,0:T(8,128)}, u32[]{:S(2)}) copy-start(s32[3,6,256]{2,1,0:T(8,128)} %param.7) | copy-start | bytes 55300
  87.7 1.6 %collective-permute-start.4 = (f32[256,262]{0,1:T(8,128)S(1)}, f32[256,262]{0,1:T(8,128)S(1)}, u32[]{:S(2)}, u32[]{:S(2)}) collective-permute-start(f32[256,262]{0,1:T(8,128)S(1)} %pad_maximum_fusion), channel_id=1, source_target_pairs={{0,1},{1,0},{2,3},{3,2},{4,5},{5,4},{6,7},{7,6},{8,9},{9,8},{10,11... | collective-permute-start | bytes 804872 | tf_op jit(solution)/shard_map/ppermute | solution.py:53
  90.1 5.7 %collective-permute-start.5 = (f32[128,262]{0,1:T(8,128)S(1)}, f32[128,262]{0,1:T(8,128)S(1)}, u32[]{:S(2)}, u32[]{:S(2)}) collective-permute-start(f32[128,262]{0,1:T(8,128)S(1)} %slice_select_fusion), channel_id=1, source_target_pairs={{0,2},{2,0},{1,3},{3,1},{4,6},{6,4},{5,7},{7,5},{8,10},{10,8},{9,1... | collective-permute-start | bytes 402440 | tf_op jit(solution)/shard_map/ppermute | solution.py:43
  95.8 5.1 %collective-permute-start.6 = (f32[128,262]{0,1:T(8,128)S(1)}, f32[128,262]{0,1:T(8,128)S(1)}, u32[]{:S(2)}, u32[]{:S(2)}) collective-permute-start(f32[128,262]{0,1:T(8,128)S(1)} %fusion.41), channel_id=1, source_target_pairs={{0,4},{4,0},{8,12},{12,8},{1,5},{5,1},{9,13},{13,9},{2,6},{6,2},{1... | collective-permute-start | bytes 402440 | tf_op jit(solution)/shard_map/ppermute | solution.py:43
  100.9 7.5 %collective-permute-start.7 = (f32[128,262]{0,1:T(8,128)S(1)}, f32[128,262]{0,1:T(8,128)S(1)}, u32[]{:S(2)}, u32[]{:S(2)}) collective-permute-start(f32[128,262]{0,1:T(8,128)S(1)} %add.112), channel_id=1, source_target_pairs={{0,8},{4,12},{8,0},{12,4},{1,9},{5,13},{9,1},{13,5},{2,10},{6,14},... | collective-permute-start | bytes 402440 | tf_op jit(solution)/shard_map/ppermute | solution.py:43
  108.4 1.4 collective-permute-start.8
  140.1 2.1 %copy-start.3 = (f32[3,6,256]{2,1,0:T(8,128)S(1)}, f32[3,6,256]{2,1,0:T(8,128)}, u32[]{:S(2)}) copy-start(f32[3,6,256]{2,1,0:T(8,128)} %shard_map.59) | copy-start | bytes 55300
